TPU v7x, 32 devices: a whole 2x2x4 slice. The times are simulated.
32 devices in a mesh: cond: 2 (over x), gx: 4 (over z), gy: 4 (over y, core).
Axes of the slice: x: 2, y: 2, z: 4, core: 2. Of those that a mesh axis runs over, the one named last changes fastest.
Arguments:
- psi_old: float32 [32, 4, 6, 2048], P('gx', 'cond', None, 'gy'), may hold values from -6 to 6
- objective_grad: float32 [32, 4, 6, 2048], P('gx', 'cond', None, 'gy'), may hold values from -6 to 6
- near_upper: float32 [32, 4, 6, 6, 2048], P('gx', 'cond', None, None, 'gy'), may hold values from -1 to 0.06
- far_upper: float32 [32, 4, 6, 6, 2048], P('gx', 'cond', None, None, 'gy'), may hold values from -1 to 0.03
- inverse_diag: float32 [32, 4, 6, 6, 2048], P('gx', 'cond', None, None, 'gy'), may hold values from -0.06 to 1
- near_lower: float32 [32, 4, 6, 6, 2048], P('gx', 'cond', None, None, 'gy'), may hold values from -1 to 0.06
- far_lower: float32 [32, 4, 6, 6, 2048], P('gx', 'cond', None, None, 'gy'), may hold values from -1 to 0.03
- y_inverse: float32 [32, 4, 6, 6, 2048], P('gx', 'cond', None, None, 'gy'), may hold values from -0.1 to 1.5
- z_inverse: float32 [4, 6, 32, 32], P('cond'), may hold values from -1 to 1
- sens_terms: float32 [32, 4, 3, 6, 2048], P('gx', 'cond', None, None, 'gy'), may hold values from -1.25 to 1.25
- wall_mask: int32 [32, 2048], P('gx', 'gy'), may hold values 0 or 1
- cond_index: int32 [4], P('cond'), may hold values from 0 to 7
- weight_table: float32 [8], replicated, may hold values from 0.5 to 2
Outputs:
- psi_new: float32 [32, 4, 6, 2048], P('gx', 'cond', None, 'gy')
- mesh_sens: float32 [32, 3, 2048], P('gx', None, 'gy')
All inputs are finite; a program needn't handle non-finite values. No bound on the sum of `wall_mask` on one device may be relied on, other than what follows from the above.
Results may differ from a plain program's by a relative error of at most 0.0001.
Values sent between devices are 32-bit elements; how exact they have to be, the bound alone decides.
No kernel may reach another device: no remote copies, remote signals or barrier semaphores. Data moves between devices by JAX's collectives and lax.ppermute only.
A program may use at most 128 MiB of HBM per device.

v0:
```python
import jax
import jax.numpy as jnp
from jax import lax
from jax.sharding import PartitionSpec as P

NZ = 32
ITERS = 2


def extended(value, sides, width):
    for axis, dim in sides:
        size, length = (lax.axis_size(axis), value.shape[dim])
        up = [(i, (i + 1) % size) for i in range(size - 1)]
        down = [(j, i) for i, j in up]
        last = lax.slice_in_dim(value, length - width, length, axis=dim)
        first = lax.slice_in_dim(value, 0, width, axis=dim)
        before = lax.ppermute(last, axis, up)
        after = lax.ppermute(first, axis, down)
        value = jnp.concatenate([before, value, after], axis=dim)
    return value


def from_behind(value, axis, steps):
    count = lax.axis_size(axis)
    first, last = (max(0, -steps), min(count, count - steps))
    return lax.ppermute(value, axis, [(source, source + steps) for source in range(first, last)])


def apply_block(blocks, vector):
    return jnp.sum(blocks * vector[..., None, :, :], axis=-2)


def apply_transpose(blocks, vector):
    return jnp.sum(blocks * vector[..., :, None, :], axis=-3)


def upper_sweep(rhs, near, far, incoming):

    def step(carry, item):
        last, before = carry
        value, near_cell, far_cell = item
        now = value - apply_block(near_cell, last) - apply_block(far_cell, before)
        return ((now, last), now)

    carry, values = lax.scan(step, (incoming[0], incoming[1]), (rhs, near, far))
    return (values, jnp.stack([carry[0], carry[1]]))


def lower_sweep(rhs, inverse, near, far, incoming):

    def step(carry, item):
        pending, partial_value = carry
        value, inverse_cell, near_cell, far_cell = item
        now = apply_transpose(inverse_cell, value - pending)
        return (
            (partial_value + apply_transpose(near_cell, now), apply_transpose(far_cell, now)),
            now,
        )

    carry, values = lax.scan(
        step, (incoming[0], incoming[1]), (rhs, inverse, near, far), reverse=True
    )
    return (values, jnp.stack([carry[0], carry[1]]))


def unit_carries(shape):
    width = 2 * shape[1]
    table = jnp.eye(width, dtype=jnp.float32).reshape(width, 2, shape[1]).transpose(1, 0, 2)
    return jnp.broadcast_to(table[:, :, None, :, None], (2, width, shape[0], shape[1], shape[2]))


def as_matrix(response):
    width = response.shape[1]
    return jnp.transpose(response, (1, 0, 3, 2, 4)).reshape(
        width, width, response.shape[2], response.shape[4]
    )


def as_vector(carry):
    return jnp.transpose(carry, (0, 2, 1, 3)).reshape(-1, carry.shape[1], carry.shape[3])


def from_vector(vector, count):
    return vector.reshape(2, count, vector.shape[1], vector.shape[2]).transpose(0, 2, 1, 3)


def carry_through(vector, matrix, offset):
    return jnp.einsum("kcl,kmcl->mcl", vector, matrix, precision=lax.Precision.HIGHEST) + offset


def on_device(
    psi_old,
    objective_grad,
    near_upper,
    far_upper,
    inverse_diag,
    near_lower,
    far_lower,
    y_inverse,
    z_inverse,
    sens_terms,
    wall_mask,
    cond_index,
    weight_table,
):
    keep = (1.0 - wall_mask.astype(jnp.float32))[:, None, None, :]
    carry_shape = psi_old.shape[1:]
    zeros = jnp.zeros((2,) + carry_shape, jnp.float32)
    psi = psi_old
    for step in range(ITERS):
        stream_pad = extended(psi, (("gx", 0),), 1)
        span_pad = extended(psi, (("gy", 3),), NZ)
        beside_all = (
            stream_pad[2:] + stream_pad[:-2] + span_pad[..., 2 * NZ :] + span_pad[..., : -2 * NZ]
        )
        rhs = objective_grad + 0.5 * beside_all - 2.0 * psi
        grid = rhs.reshape(rhs.shape[0], rhs.shape[1], rhs.shape[2], rhs.shape[3] // NZ, NZ)
        zres = jnp.einsum(
            "icvjq,cvqk->icvjk", grid, z_inverse, precision=lax.Precision.HIGHEST
        ).reshape(rhs.shape)
        yres = apply_transpose(y_inverse, zres)
        blank = jnp.zeros((yres.shape[0], 1) + carry_shape, jnp.float32)
        units = unit_carries(carry_shape)
        values, offset = upper_sweep(yres, near_upper, far_upper, zeros)
        values, response = upper_sweep(blank, near_upper, far_upper, units)
        matrix = as_matrix(response)
        vector = as_vector(offset)

        def upper_reversal(turn, incoming):
            return from_behind(carry_through(incoming, matrix, vector), "gx", 1)

        entering = lax.fori_loop(0, lax.axis_size("gx") - 1, upper_reversal, jnp.zeros_like(vector))
        upper, leaving = upper_sweep(
            yres, near_upper, far_upper, from_vector(entering, carry_shape[1])
        )
        values, offset = lower_sweep(upper, inverse_diag, near_lower, far_lower, zeros)
        values, response = lower_sweep(blank, inverse_diag, near_lower, far_lower, units)
        reverse_matrix = as_matrix(response)
        vector_back = as_vector(offset)

        def lower_turn(turn, incoming):
            return from_behind(carry_through(incoming, reverse_matrix, vector_back), "gx", -1)

        entering = lax.fori_loop(
            0, lax.axis_size("gx") - 1, lower_turn, jnp.zeros_like(vector_back)
        )
        lower, leaving = lower_sweep(
            upper, inverse_diag, near_lower, far_lower, from_vector(entering, carry_shape[1])
        )
        psi = (psi + 0.05 * lower) * keep
    onehot = (cond_index[:, None] == jnp.arange(weight_table.shape[0])[None, :]).astype(jnp.float32)
    weights = jnp.sum(onehot * weight_table[None, :], axis=1)
    local_sens = jnp.einsum(
        "icvl,icmvl->iml",
        psi * weights[None, :, None, None],
        sens_terms,
        precision=lax.Precision.HIGHEST,
    )
    mesh_sens = lax.psum(local_sens, "cond")
    return (psi, mesh_sens)


def solution(mesh):
    placed = (
        P("gx", "cond", None, "gy"),
        P("gx", "cond", None, "gy"),
        P("gx", "cond", None, None, "gy"),
        P("gx", "cond", None, None, "gy"),
        P("gx", "cond", None, None, "gy"),
        P("gx", "cond", None, None, "gy"),
        P("gx", "cond", None, None, "gy"),
        P("gx", "cond", None, None, "gy"),
        P("cond", None, None, None),
        P("gx", "cond", None, None, "gy"),
        P("gx", "gy"),
        P("cond"),
        P(),
    )
    return jax.shard_map(
        on_device,
        mesh=mesh,
        in_specs=placed,
        out_specs=(P("gx", "cond", None, "gy"), P("gx", None, "gy")),
        check_vma=False,
    )
```

profile of v0, /device:TPU:0, one launch (start us, length us, event | category | flops | bytes accessed | tf_op | source)
XLA Modules:
  0.0 314.0 jit_solution(5735646118887496638)
XLA Ops:
  0.6 1.5 fusion.47
  3.4 3.0 collective-permute-start.7
  6.5 1.4 fusion.46
  9.1 6.2 %collective-permute-start.5 = (f32[1,2,6,512]{3,1,2,0:T(2,128)}, f32[1,2,6,512]{3,1,2,0:T(2,128)}, u32[]{:S(2)}, u32[]{:S(2)}) collective-permute-start(f32[1,2,6,512]{3,1,2,0:T(2,128)} %get-tuple-element.1342), channel_id=1, source_target_pairs={{0,4},{4,8},{8,12},{1,5},{5,9},{9,13},{2,6},{6,10},{10,14},{3,7},{... | collective-permute-start | bytes 73736 | tf_op jit(solution)/shard_map/ppermute | solution.py:17
  15.9 34.7 %while.203 = (s32[]{:T(128)}, f32[12,2,6,512]{3,1,2,0:T(2,128)S(1)}, f32[12,2,6,512]{3,1,2,0:T(2,128)S(1)}, f32[8,2,6,6,512]{4,1,3,2,0:T(2,128)}, f32[8,2,6,6,512]{4,1,3,2,0:T(2,128)}, /*index=5*/s32[]{:T(128)}) while((s32[]{:T(128)}, f32[12,2,6,512]{3,1,2,0:T(2,128)S(1)}, f32[12,2,6,512]{3,1,2,0:T(2,128)S(1)}, ...), condition=%wide.region_8.9_spmd, body=%wide.region_5.8_spmd.sunk | while | flops 1769474 | bytes 3539021 | solution.py:45
  17.8 2.2 multiply_reduce_fusion.21
  22.1 2.2 multiply_reduce_fusion.21
  26.4 2.2 multiply_reduce_fusion.21
  30.8 2.2 multiply_reduce_fusion.21
  35.1 2.2 multiply_reduce_fusion.21
  39.4 2.2 multiply_reduce_fusion.21
  43.8 2.2 multiply_reduce_fusion.21
  48.1 2.2 multiply_reduce_fusion.21
  50.9 38.1 %while.202 = (s32[]{:T(128)}, f32[12,2,6,512]{3,1,2,0:T(2,128)S(1)}, f32[12,2,6,512]{3,1,2,0:T(2,128)S(1)}, f32[8,2,6,6,512]{4,1,3,2,0:T(2,128)}, f32[8,2,6,6,51...) while((s32[]{:T(128)}, f32[12,2,6,512]{3,1,2,0:T(2,128)S(1)}, ...), condition=%wide.region_4.5_spmd, body=%wide.region_0.4_spmd.sunk | while | flops 2580483 | bytes 4866153 | solution.py:60
  53.8 1.6 multiply_reduce_fusion.20
  58.6 1.6 multiply_reduce_fusion.20
  63.3 1.6 multiply_reduce_fusion.20
  68.1 1.6 multiply_reduce_fusion.20
  72.8 1.6 multiply_reduce_fusion.20
  77.6 1.6 multiply_reduce_fusion.20
  82.4 1.6 multiply_reduce_fusion.20
  87.1 1.6 multiply_reduce_fusion.20
  95.2 2.0 multiply_reduce_fusion.10
  97.2 9.2 %while.212 = (s32[]{:T(128)}, f32[2,6,512]{2,0,1:T(2,128)S(1)}, f32[2,6,512]{2,0,1:T(2,128)S(1)}, f32[8,2,6,512]{3,1,2,0:T(2,128)S(1)}, f32[8,2,6,6,512]{4,1,3,2...) while((s32[]{:T(128)}, f32[2,6,512]{2,0,1:T(2,128)S(1)}, ...), condition=%wide.region_13.14_spmd.clone, body=%wide.region_10.13_spmd.clone.sunk | while | flops 153603 | bytes 589927 | solution.py:45
  106.5 18.1 %while.204 = (s32[]{:T(128)}, f32[12,2,512]{2,1,0:T(2,128)S(1)}, f32[12,12,2,512]{3,2,1,0:T(2,128)S(1)}, f32[12,2,512]{2,1,0:T(2,128)S(1)}, s32[]{:T(128)}) while((s32[]{:T(128)}, f32[12,2,512]{2,1,0:T(2,128)S(1)}, f32[12,12,2,512]{3,2,1,0:T(2,128)S(1)}, f32[12,2,512]{2,1,0:T(2,128)S(1)}, s32[]{:T(128)}) %tuple.404), condition=%wide.region_15.16_spmd, body=%wide.region_14.15_spmd.sunk | while | flops 294914 | bytes 1032293 | solution.py:132
  106.8 3.3 %collective-permute-start = (f32[12,2,512]{2,1,0:T(2,128)S(1)}, f32[12,2,512]{2,1,0:T(2,128)S(1)}, u32[]{:S(2)}, u32[]{:S(2)}) collective-permute-start(f32[12,2,512]{2,1,0:T(2,128)S(1)} %bitcast_add_fusion.8), channel_id=1, source_target_pairs={{0,4},{4,8},{8,12},{1,5},{5,9},{9,13},{2,6},{6,10},{10,14},{3,7},{... | collective-permute-start | bytes 147464 | tf_op jit(solution)/shard_map/while/body/eval_jaxpr/ppermute | solution.py:26
  110.1 1.7 collective-permute-done
  112.1 4.4 %collective-permute-start = (f32[12,2,512]{2,1,0:T(2,128)S(1)}, f32[12,2,512]{2,1,0:T(2,128)S(1)}, u32[]{:S(2)}, u32[]{:S(2)}) collective-permute-start(f32[12,2,512]{2,1,0:T(2,128)S(1)} %bitcast_add_fusion.8), channel_id=1, source_target_pairs={{0,4},{4,8},{8,12},{1,5},{5,9},{9,13},{2,6},{6,10},{10,14},{3,7},{... | collective-permute-start | bytes 147464 | tf_op jit(solution)/shard_map/while/body/eval_jaxpr/ppermute | solution.py:26
  116.5 1.7 collective-permute-done
  118.6 4.2 %collective-permute-start = (f32[12,2,512]{2,1,0:T(2,128)S(1)}, f32[12,2,512]{2,1,0:T(2,128)S(1)}, u32[]{:S(2)}, u32[]{:S(2)}) collective-permute-start(f32[12,2,512]{2,1,0:T(2,128)S(1)} %bitcast_add_fusion.8), channel_id=1, source_target_pairs={{0,4},{4,8},{8,12},{1,5},{5,9},{9,13},{2,6},{6,10},{10,14},{3,7},{... | collective-permute-start | bytes 147464 | tf_op jit(solution)/shard_map/while/body/eval_jaxpr/ppermute | solution.py:26
  122.8 1.7 collective-permute-done
  124.6 9.3 %while.205 = (s32[]{:T(128)}, f32[2,6,512]{2,0,1:T(2,128)S(1)}, f32[2,6,512]{2,0,1:T(2,128)S(1)}, f32[8,2,6,512]{3,1,2,0:T(2,128)S(1)}, f32[8,2,6,512]{3,1,2,0:T...) while((s32[]{:T(128)}, f32[2,6,512]{2,0,1:T(2,128)S(1)}, ...), condition=%wide.region_19.20_spmd, body=%wide.region_16.19_spmd.sunk | while | flops 159746 | bytes 639073 | solution.py:45
  134.0 17.8 %while.213 = (s32[]{:T(128)}, f32[2,6,512]{2,0,1:T(2,128)S(1)}, f32[2,6,512]{2,0,1:T(2,128)S(1)}, f32[8,2,6,6,512]{4,1,3,2,0:T(2,128)}, f32[8,2,6,6,512]{4,1,3,2...) while((s32[]{:T(128)}, f32[2,6,512]{2,0,1:T(2,128)S(1)}, ...), condition=%wide.region_24.25_spmd.clone, body=%wide.region_20.24_spmd.clone.sunk | while | flops 221188 | bytes 761991 | solution.py:60
  151.8 19.3 %while.206 = (s32[]{:T(128)}, f32[12,2,512]{2,1,0:T(2,128)S(1)}, f32[12,12,2,512]{3,2,1,0:T(2,128)S(1)}, f32[12,2,512]{2,1,0:T(2,128)S(1)}, s32[]{:T(128)}) while((s32[]{:T(128)}, f32[12,2,512]{2,1,0:T(2,128)S(1)}, f32[12,12,2,512]{3,2,1,0:T(2,128)S(1)}, f32[12,2,512]{2,1,0:T(2,128)S(1)}, s32[]{:T(128)}) %tuple.405), condition=%wide.region_26.27_spmd, body=%wide.region_25.26_spmd.sunk | while | flops 294914 | bytes 1032293 | solution.py:144
  152.1 1.3 collective-permute-start.1
  153.4 5.0 %collective-permute-done.1 = f32[12,2,512]{2,1,0:T(2,128)S(1)} collective-permute-done((f32[12,2,512]{2,1,0:T(2,128)S(1)}, f32[12,2,512]{2,1,0:T(2,128)S(1)}, u32[]{:S(2)}, u32[]{:S(2)}) %collective-permute-start.1) | collective-permute-done | bytes 49184 | tf_op jit(solution)/shard_map/while/body/eval_jaxpr/ppermute | solution.py:26
  158.7 1.3 collective-permute-start.1
  160.0 4.8 %collective-permute-done.1 = f32[12,2,512]{2,1,0:T(2,128)S(1)} collective-permute-done((f32[12,2,512]{2,1,0:T(2,128)S(1)}, f32[12,2,512]{2,1,0:T(2,128)S(1)}, u32[]{:S(2)}, u32[]{:S(2)}) %collective-permute-start.1) | collective-permute-done | bytes 49184 | tf_op jit(solution)/shard_map/while/body/eval_jaxpr/ppermute | solution.py:26
  166.5 4.7 %collective-permute-done.1 = f32[12,2,512]{2,1,0:T(2,128)S(1)} collective-permute-done((f32[12,2,512]{2,1,0:T(2,128)S(1)}, f32[12,2,512]{2,1,0:T(2,128)S(1)}, u32[]{:S(2)}, u32[]{:S(2)}) %collective-permute-start.1) | collective-permute-done | bytes 49184 | tf_op jit(solution)/shard_map/while/body/eval_jaxpr/ppermute | solution.py:26
  171.2 18.1 %while.207 = (s32[]{:T(128)}, f32[2,6,512]{2,0,1:T(2,128)S(1)}, f32[2,6,512]{2,0,1:T(2,128)S(1)}, f32[8,2,6,512]{3,1,2,0:T(2,128)S(1)}, f32[8,2,6,6,512]{4,1,3,2...) while((s32[]{:T(128)}, f32[2,6,512]{2,0,1:T(2,128)S(1)}, ...), condition=%wide.region_31.32_spmd, body=%wide.region_27.31_spmd.sunk | while | flops 215043 | bytes 811137 | solution.py:60
  191.0 3.0 collective-permute-start.11
  195.3 4.6 %collective-permute-start.9 = (f32[1,2,6,512]{3,1,2,0:T(2,128)S(1)}, f32[1,2,6,512]{3,1,2,0:T(2,128)S(1)}, u32[]{:S(2)}, u32[]{:S(2)}) collective-permute-start(f32[1,2,6,512]{3,1,2,0:T(2,128)S(1)} %get-tuple-element.1338), channel_id=1, source_target_pairs={{0,4},{4,8},{8,12},{1,5},{5,9},{9,13},{2,6},{6,10},{10,14},{3,7},{... | collective-permute-start | bytes 73736 | tf_op jit(solution)/shard_map/ppermute | solution.py:17
  201.5 2.1 fusion.31
  204.9 1.7 convolution_bitcast_fusion
  206.6 1.4 mul.524
  208.1 1.9 multiply_reduce_fusion.9
  210.1 9.2 %while.214 = (s32[]{:T(128)}, f32[2,6,512]{2,0,1:T(2,128)S(1)}, f32[2,6,512]{2,0,1:T(2,128)S(1)}, f32[8,2,6,512]{3,1,2,0:T(2,128)S(1)}, f32[8,2,6,6,512]{4,1,3,2...) while((s32[]{:T(128)}, f32[2,6,512]{2,0,1:T(2,128)S(1)}, ...), condition=%wide.region_36.37_spmd.clone, body=%wide.region_33.36_spmd.clone.sunk | while | flops 153603 | bytes 589927 | solution.py:45
  219.4 18.8 %while.208 = (s32[]{:T(128)}, f32[12,2,512]{2,1,0:T(2,128)S(1)}, f32[12,12,2,512]{3,2,1,0:T(2,128)S(1)}, f32[12,2,512]{2,1,0:T(2,128)S(1)}, s32[]{:T(128)}) while((s32[]{:T(128)}, f32[12,2,512]{2,1,0:T(2,128)S(1)}, f32[12,12,2,512]{3,2,1,0:T(2,128)S(1)}, f32[12,2,512]{2,1,0:T(2,128)S(1)}, s32[]{:T(128)}) %tuple.402), condition=%wide.region_38.39_spmd, body=%wide.region_37.38_spmd.sunk | while | flops 294914 | bytes 1032293 | solution.py:132
  219.7 4.2 %collective-permute-start.2 = (f32[12,2,512]{2,1,0:T(2,128)S(1)}, f32[12,2,512]{2,1,0:T(2,128)S(1)}, u32[]{:S(2)}, u32[]{:S(2)}) collective-permute-start(f32[12,2,512]{2,1,0:T(2,128)S(1)} %bitcast_add_fusion.10), channel_id=1, source_target_pairs={{0,4},{4,8},{8,12},{1,5},{5,9},{9,13},{2,6},{6,10},{10,14},{3,7},{... | collective-permute-start | bytes 147464 | tf_op jit(solution)/shard_map/while/body/eval_jaxpr/ppermute | solution.py:26
  223.9 1.7 collective-permute-done.2
  225.9 4.2 %collective-permute-start.2 = (f32[12,2,512]{2,1,0:T(2,128)S(1)}, f32[12,2,512]{2,1,0:T(2,128)S(1)}, u32[]{:S(2)}, u32[]{:S(2)}) collective-permute-start(f32[12,2,512]{2,1,0:T(2,128)S(1)} %bitcast_add_fusion.10), channel_id=1, source_target_pairs={{0,4},{4,8},{8,12},{1,5},{5,9},{9,13},{2,6},{6,10},{10,14},{3,7},{... | collective-permute-start | bytes 147464 | tf_op jit(solution)/shard_map/while/body/eval_jaxpr/ppermute | solution.py:26
  230.2 1.7 collective-permute-done.2
  232.2 4.2 %collective-permute-start.2 = (f32[12,2,512]{2,1,0:T(2,128)S(1)}, f32[12,2,512]{2,1,0:T(2,128)S(1)}, u32[]{:S(2)}, u32[]{:S(2)}) collective-permute-start(f32[12,2,512]{2,1,0:T(2,128)S(1)} %bitcast_add_fusion.10), channel_id=1, source_target_pairs={{0,4},{4,8},{8,12},{1,5},{5,9},{9,13},{2,6},{6,10},{10,14},{3,7},{... | collective-permute-start | bytes 147464 | tf_op jit(solution)/shard_map/while/body/eval_jaxpr/ppermute | solution.py:26
  236.5 1.7 collective-permute-done.2
  238.3 9.3 %while.209 = (s32[]{:T(128)}, f32[2,6,512]{2,0,1:T(2,128)S(1)}, f32[2,6,512]{2,0,1:T(2,128)S(1)}, f32[8,2,6,512]{3,1,2,0:T(2,128)S(1)}, f32[8,2,6,512]{3,1,2,0:T...) while((s32[]{:T(128)}, f32[2,6,512]{2,0,1:T(2,128)S(1)}, ...), condition=%wide.region_42.43_spmd, body=%wide.region_39.42_spmd.sunk | while | flops 159746 | bytes 639073 | solution.py:45
  247.6 17.8 %while.215 = (s32[]{:T(128)}, f32[2,6,512]{2,0,1:T(2,128)S(1)}, f32[2,6,512]{2,0,1:T(2,128)S(1)}, f32[8,2,6,6,512]{4,1,3,2,0:T(2,128)}, f32[8,2,6,6,512]{4,1,3,2...) while((s32[]{:T(128)}, f32[2,6,512]{2,0,1:T(2,128)S(1)}, ...), condition=%wide.region_47.48_spmd.clone, body=%wide.region_43.47_spmd.clone.sunk | while | flops 221188 | bytes 761991 | solution.py:60
  265.5 19.9 %while.210 = (s32[]{:T(128)}, f32[12,2,512]{2,1,0:T(2,128)S(1)}, f32[12,12,2,512]{3,2,1,0:T(2,128)S(1)}, f32[12,2,512]{2,1,0:T(2,128)S(1)}, s32[]{:T(128)}) while((s32[]{:T(128)}, f32[12,2,512]{2,1,0:T(2,128)S(1)}, f32[12,12,2,512]{3,2,1,0:T(2,128)S(1)}, f32[12,2,512]{2,1,0:T(2,128)S(1)}, s32[]{:T(128)}) %tuple.403), condition=%wide.region_49.50_spmd, body=%wide.region_48.49_spmd.sunk | while | flops 294914 | bytes 1032293 | solution.py:144
  265.8 1.3 collective-permute-start.3
  267.1 5.0 %collective-permute-done.3 = f32[12,2,512]{2,1,0:T(2,128)S(1)} collective-permute-done((f32[12,2,512]{2,1,0:T(2,128)S(1)}, f32[12,2,512]{2,1,0:T(2,128)S(1)}, u32[]{:S(2)}, u32[]{:S(2)}) %collective-permute-start.3) | collective-permute-done | bytes 49184 | tf_op jit(solution)/shard_map/while/body/eval_jaxpr/ppermute | solution.py:26
  272.4 1.3 collective-permute-start.3
  273.7 5.2 %collective-permute-done.3 = f32[12,2,512]{2,1,0:T(2,128)S(1)} collective-permute-done((f32[12,2,512]{2,1,0:T(2,128)S(1)}, f32[12,2,512]{2,1,0:T(2,128)S(1)}, u32[]{:S(2)}, u32[]{:S(2)}) %collective-permute-start.3) | collective-permute-done | bytes 49184 | tf_op jit(solution)/shard_map/while/body/eval_jaxpr/ppermute | solution.py:26
  280.5 4.8 %collective-permute-done.3 = f32[12,2,512]{2,1,0:T(2,128)S(1)} collective-permute-done((f32[12,2,512]{2,1,0:T(2,128)S(1)}, f32[12,2,512]{2,1,0:T(2,128)S(1)}, u32[]{:S(2)}, u32[]{:S(2)}) %collective-permute-start.3) | collective-permute-done | bytes 49184 | tf_op jit(solution)/shard_map/while/body/eval_jaxpr/ppermute | solution.py:26
  285.4 17.9 %while.211 = (s32[]{:T(128)}, f32[2,6,512]{2,0,1:T(2,128)S(1)}, f32[2,6,512]{2,0,1:T(2,128)S(1)}, f32[8,2,6,512]{3,1,2,0:T(2,128)S(1)}, f32[8,2,6,6,512]{4,1,3,2...) while((s32[]{:T(128)}, f32[2,6,512]{2,0,1:T(2,128)S(1)}, ...), condition=%wide.region_54.55_spmd, body=%wide.region_50.0_spmd.sunk | while | flops 215043 | bytes 811137 | solution.py:60
  304.8 9.2 %psum.7 = f32[8,3,512]{2,0,1:T(8,128)} all-reduce(f32[8,3,512]{2,0,1:T(8,128)S(1)} %bitcast.356), channel_id=1, replica_groups=mesh['cond'=2,'gx'=4,'gy'=4] {'cond'}, use_global_device_ids=true, to_apply=%region_56.57 | all-reduce | flops 12288 | bytes 98304 | tf_op jit(solution)/shard_map/psum | solution.py:159
  (498 shorter events, 170.1 us)
Async XLA Ops:
  0.6 91.6 %copy-start = (f32[2,6,32,32]{3,2,1,0:T(8,128)S(1)}, f32[2,6,32,32]{3,2,1,0:T(8,128)}, u32[]{:S(2)}) copy-start(f32[2,6,32,32]{3,2,1,0:T(8,128)} %param.49) | copy-start | bytes 147460
  2.2 88.0 %collective-permute-start.6 = (f32[8,2,6,32]{3,1,2,0:T(2,128)}, f32[8,2,6,32]{3,1,2,0:T(2,128)S(1)}, u32[]{:S(2)}, u32[]{:S(2)}) collective-permute-start(f32[8,2,6,32]{3,1,2,0:T(2,128)} %get-tuple-element.1343), channel_id=1, source_target_pairs={{1,0},{2,1},{3,2},{5,4},{6,5},{7,6},{9,8},{10,9},{11,10},{13,12},{... | collective-permute-start | bytes 36872 | tf_op jit(solution)/shard_map/ppermute | solution.py:18
  3.4 86.7 %collective-permute-start.7 = (f32[8,2,6,32]{3,1,2,0:T(2,128)S(1)}, f32[8,2,6,32]{3,1,2,0:T(2,128)S(1)}, u32[]{:S(2)}, u32[]{:S(2)}) collective-permute-start(f32[8,2,6,32]{3,1,2,0:T(2,128)S(1)} %get-tuple-element.1344), channel_id=1, source_target_pairs={{0,1},{1,2},{2,3},{4,5},{5,6},{6,7},{8,9},{9,10},{10,11},{12,13},{... | collective-permute-start | bytes 36872 | tf_op jit(solution)/shard_map/ppermute | solution.py:17
  7.9 82.3 %collective-permute-start.4 = (f32[1,2,6,512]{3,1,2,0:T(2,128)}, f32[1,2,6,512]{3,1,2,0:T(2,128)}, u32[]{:S(2)}, u32[]{:S(2)}) collective-permute-start(f32[1,2,6,512]{3,1,2,0:T(2,128)} %get-tuple-element.1341), channel_id=1, source_target_pairs={{4,0},{8,4},{12,8},{5,1},{9,5},{13,9},{6,2},{10,6},{14,10},{7,3},{... | collective-permute-start | bytes 73736 | tf_op jit(solution)/shard_map/ppermute | solution.py:18
  9.1 81.0 %collective-permute-start.5 = (f32[1,2,6,512]{3,1,2,0:T(2,128)}, f32[1,2,6,512]{3,1,2,0:T(2,128)}, u32[]{:S(2)}, u32[]{:S(2)}) collective-permute-start(f32[1,2,6,512]{3,1,2,0:T(2,128)} %get-tuple-element.1342), channel_id=1, source_target_pairs={{0,4},{4,8},{8,12},{1,5},{5,9},{9,13},{2,6},{6,10},{10,14},{3,7},{... | collective-permute-start | bytes 73736 | tf_op jit(solution)/shard_map/ppermute | solution.py:17
  50.9 38.1 %copy-start.8 = (s32[8,512]{1,0:T(8,128)S(1)}, s32[8,512]{1,0:T(8,128)}, u32[]{:S(2)}) copy-start(s32[8,512]{1,0:T(8,128)} %param.51) | copy-start | bytes 49156
  89.5 0.9 copy-start.2
  89.6 1.0 copy-start.6
  94.0 3.2 %copy-start.1 = (f32[8,2,6,6,512]{4,1,3,2,0:T(2,128)S(1)}, f32[8,2,6,6,512]{4,1,3,2,0:T(2,128)}, u32[]{:S(2)}) copy-start(f32[8,2,6,6,512]{4,1,3,2,0:T(2,128)} %get-tuple-element.2231) | copy-start | bytes 3538948
  106.8 5.1 %collective-permute-start = (f32[12,2,512]{2,1,0:T(2,128)S(1)}, f32[12,2,512]{2,1,0:T(2,128)S(1)}, u32[]{:S(2)}, u32[]{:S(2)}) collective-permute-start(f32[12,2,512]{2,1,0:T(2,128)S(1)} %bitcast_add_fusion.8), channel_id=1, source_target_pairs={{0,4},{4,8},{8,12},{1,5},{5,9},{9,13},{2,6},{6,10},{10,14},{3,7},{... | collective-permute-start | bytes 147464 | tf_op jit(solution)/shard_map/while/body/eval_jaxpr/ppermute | solution.py:26
  112.1 6.1 %collective-permute-start = (f32[12,2,512]{2,1,0:T(2,128)S(1)}, f32[12,2,512]{2,1,0:T(2,128)S(1)}, u32[]{:S(2)}, u32[]{:S(2)}) collective-permute-start(f32[12,2,512]{2,1,0:T(2,128)S(1)} %bitcast_add_fusion.8), channel_id=1, source_target_pairs={{0,4},{4,8},{8,12},{1,5},{5,9},{9,13},{2,6},{6,10},{10,14},{3,7},{... | collective-permute-start | bytes 147464 | tf_op jit(solution)/shard_map/while/body/eval_jaxpr/ppermute | solution.py:26
  118.6 6.0 %collective-permute-start = (f32[12,2,512]{2,1,0:T(2,128)S(1)}, f32[12,2,512]{2,1,0:T(2,128)S(1)}, u32[]{:S(2)}, u32[]{:S(2)}) collective-permute-start(f32[12,2,512]{2,1,0:T(2,128)S(1)} %bitcast_add_fusion.8), channel_id=1, source_target_pairs={{0,4},{4,8},{8,12},{1,5},{5,9},{9,13},{2,6},{6,10},{10,14},{3,7},{... | collective-permute-start | bytes 147464 | tf_op jit(solution)/shard_map/while/body/eval_jaxpr/ppermute | solution.py:26
  152.1 6.3 %collective-permute-start.1 = (f32[12,2,512]{2,1,0:T(2,128)S(1)}, f32[12,2,512]{2,1,0:T(2,128)S(1)}, u32[]{:S(2)}, u32[]{:S(2)}) collective-permute-start(f32[12,2,512]{2,1,0:T(2,128)S(1)} %bitcast_add_fusion.9), channel_id=1, source_target_pairs={{4,0},{8,4},{12,8},{5,1},{9,5},{13,9},{6,2},{10,6},{14,10},{7,3},{... | collective-permute-start | bytes 147464 | tf_op jit(solution)/shard_map/while/body/eval_jaxpr/ppermute | solution.py:26
  158.7 6.1 %collective-permute-start.1 = (f32[12,2,512]{2,1,0:T(2,128)S(1)}, f32[12,2,512]{2,1,0:T(2,128)S(1)}, u32[]{:S(2)}, u32[]{:S(2)}) collective-permute-start(f32[12,2,512]{2,1,0:T(2,128)S(1)} %bitcast_add_fusion.9), channel_id=1, source_target_pairs={{4,0},{8,4},{12,8},{5,1},{9,5},{13,9},{6,2},{10,6},{14,10},{7,3},{... | collective-permute-start | bytes 147464 | tf_op jit(solution)/shard_map/while/body/eval_jaxpr/ppermute | solution.py:26
  165.1 6.0 %collective-permute-start.1 = (f32[12,2,512]{2,1,0:T(2,128)S(1)}, f32[12,2,512]{2,1,0:T(2,128)S(1)}, u32[]{:S(2)}, u32[]{:S(2)}) collective-permute-start(f32[12,2,512]{2,1,0:T(2,128)S(1)} %bitcast_add_fusion.9), channel_id=1, source_target_pairs={{4,0},{8,4},{12,8},{5,1},{9,5},{13,9},{6,2},{10,6},{14,10},{7,3},{... | collective-permute-start | bytes 147464 | tf_op jit(solution)/shard_map/while/body/eval_jaxpr/ppermute | solution.py:26
  171.2 18.2 %copy-start.3 = (f32[8,2,6,512]{3,1,2,0:T(2,128)S(1)}, f32[8,2,6,512]{3,1,2,0:T(2,128)}, u32[]{:S(2)}) copy-start(f32[8,2,6,512]{3,1,2,0:T(2,128)} %param.41) | copy-start | bytes 589828
  171.2 28.8 %copy-start.10 = (f32[8]{0:T(128)S(1)}, f32[8]{0:T(128)}, u32[]{:S(2)}) copy-start(f32[8]{0:T(128)} %param.53) | copy-start | bytes 100
  171.2 28.8 %copy-start.11 = (s32[2]{0:T(128)S(1)}, s32[2]{0:T(128)}, u32[]{:S(2)}) copy-start(s32[2]{0:T(128)} %param.52) | copy-start | bytes 28
  189.7 11.1 %collective-permute-start.10 = (f32[8,2,6,32]{3,1,2,0:T(2,128)S(1)}, f32[8,2,6,32]{3,1,2,0:T(2,128)S(1)}, u32[]{:S(2)}, u32[]{:S(2)}) collective-permute-start(f32[8,2,6,32]{3,1,2,0:T(2,128)S(1)} %get-tuple-element.1339), channel_id=1, source_target_pairs={{1,0},{2,1},{3,2},{5,4},{6,5},{7,6},{9,8},{10,9},{11,10},{13,12},{... | collective-permute-start | bytes 36872 | tf_op jit(solution)/shard_map/ppermute | solution.py:18
  191.0 9.8 %collective-permute-start.11 = (f32[8,2,6,32]{3,1,2,0:T(2,128)S(1)}, f32[8,2,6,32]{3,1,2,0:T(2,128)S(1)}, u32[]{:S(2)}, u32[]{:S(2)}) collective-permute-start(f32[8,2,6,32]{3,1,2,0:T(2,128)S(1)} %get-tuple-element.1340), channel_id=1, source_target_pairs={{0,1},{1,2},{2,3},{4,5},{5,6},{6,7},{8,9},{9,10},{10,11},{12,13},{... | collective-permute-start | bytes 36872 | tf_op jit(solution)/shard_map/ppermute | solution.py:17
  194.0 6.7 %collective-permute-start.8 = (f32[1,2,6,512]{3,1,2,0:T(2,128)S(1)}, f32[1,2,6,512]{3,1,2,0:T(2,128)S(1)}, u32[]{:S(2)}, u32[]{:S(2)}) collective-permute-start(f32[1,2,6,512]{3,1,2,0:T(2,128)S(1)} %get-tuple-element.1337), channel_id=1, source_target_pairs={{4,0},{8,4},{12,8},{5,1},{9,5},{13,9},{6,2},{10,6},{14,10},{7,3},{... | collective-permute-start | bytes 73736 | tf_op jit(solution)/shard_map/ppermute | solution.py:18
  195.3 6.2 %collective-permute-start.9 = (f32[1,2,6,512]{3,1,2,0:T(2,128)S(1)}, f32[1,2,6,512]{3,1,2,0:T(2,128)S(1)}, u32[]{:S(2)}, u32[]{:S(2)}) collective-permute-start(f32[1,2,6,512]{3,1,2,0:T(2,128)S(1)} %get-tuple-element.1338), channel_id=1, source_target_pairs={{0,4},{4,8},{8,12},{1,5},{5,9},{9,13},{2,6},{6,10},{10,14},{3,7},{... | collective-permute-start | bytes 73736 | tf_op jit(solution)/shard_map/ppermute | solution.py:17
  208.0 2.1 copy-start.4
  219.7 6.0 %collective-permute-start.2 = (f32[12,2,512]{2,1,0:T(2,128)S(1)}, f32[12,2,512]{2,1,0:T(2,128)S(1)}, u32[]{:S(2)}, u32[]{:S(2)}) collective-permute-start(f32[12,2,512]{2,1,0:T(2,128)S(1)} %bitcast_add_fusion.10), channel_id=1, source_target_pairs={{0,4},{4,8},{8,12},{1,5},{5,9},{9,13},{2,6},{6,10},{10,14},{3,7},{... | collective-permute-start | bytes 147464 | tf_op jit(solution)/shard_map/while/body/eval_jaxpr/ppermute | solution.py:26
  225.9 6.0 %collective-permute-start.2 = (f32[12,2,512]{2,1,0:T(2,128)S(1)}, f32[12,2,512]{2,1,0:T(2,128)S(1)}, u32[]{:S(2)}, u32[]{:S(2)}) collective-permute-start(f32[12,2,512]{2,1,0:T(2,128)S(1)} %bitcast_add_fusion.10), channel_id=1, source_target_pairs={{0,4},{4,8},{8,12},{1,5},{5,9},{9,13},{2,6},{6,10},{10,14},{3,7},{... | collective-permute-start | bytes 147464 | tf_op jit(solution)/shard_map/while/body/eval_jaxpr/ppermute | solution.py:26
  232.2 6.0 %collective-permute-start.2 = (f32[12,2,512]{2,1,0:T(2,128)S(1)}, f32[12,2,512]{2,1,0:T(2,128)S(1)}, u32[]{:S(2)}, u32[]{:S(2)}) collective-permute-start(f32[12,2,512]{2,1,0:T(2,128)S(1)} %bitcast_add_fusion.10), channel_id=1, source_target_pairs={{0,4},{4,8},{8,12},{1,5},{5,9},{9,13},{2,6},{6,10},{10,14},{3,7},{... | collective-permute-start | bytes 147464 | tf_op jit(solution)/shard_map/while/body/eval_jaxpr/ppermute | solution.py:26
  238.2 9.4 %copy-start.5 = (f32[2,6,512]{2,0,1:T(2,128)S(1)}, f32[2,6,512]{2,0,1:T(2,128)}, u32[]{:S(2)}) copy-start(f32[2,6,512]{2,0,1:T(2,128)} %custom-call.3) | copy-start | bytes 73732
  265.8 6.3 %collective-permute-start.3 = (f32[12,2,512]{2,1,0:T(2,128)S(1)}, f32[12,2,512]{2,1,0:T(2,128)S(1)}, u32[]{:S(2)}, u32[]{:S(2)}) collective-permute-start(f32[12,2,512]{2,1,0:T(2,128)S(1)} %bitcast_add_fusion.11), channel_id=1, source_target_pairs={{4,0},{8,4},{12,8},{5,1},{9,5},{13,9},{6,2},{10,6},{14,10},{7,3},{... | collective-permute-start | bytes 147464 | tf_op jit(solution)/shard_map/while/body/eval_jaxpr/ppermute | solution.py:26
  272.4 6.5 %collective-permute-start.3 = (f32[12,2,512]{2,1,0:T(2,128)S(1)}, f32[12,2,512]{2,1,0:T(2,128)S(1)}, u32[]{:S(2)}, u32[]{:S(2)}) collective-permute-start(f32[12,2,512]{2,1,0:T(2,128)S(1)} %bitcast_add_fusion.11), channel_id=1, source_target_pairs={{4,0},{8,4},{12,8},{5,1},{9,5},{13,9},{6,2},{10,6},{14,10},{7,3},{... | collective-permute-start | bytes 147464 | tf_op jit(solution)/shard_map/while/body/eval_jaxpr/ppermute | solution.py:26
  279.2 6.1 %collective-permute-start.3 = (f32[12,2,512]{2,1,0:T(2,128)S(1)}, f32[12,2,512]{2,1,0:T(2,128)S(1)}, u32[]{:S(2)}, u32[]{:S(2)}) collective-permute-start(f32[12,2,512]{2,1,0:T(2,128)S(1)} %bitcast_add_fusion.11), channel_id=1, source_target_pairs={{4,0},{8,4},{12,8},{5,1},{9,5},{13,9},{6,2},{10,6},{14,10},{7,3},{... | collective-permute-start | bytes 147464 | tf_op jit(solution)/shard_map/while/body/eval_jaxpr/ppermute | solution.py:26
  285.4 17.9 %copy-start.9 = (f32[2]{0:T(128)S(1)}, f32[2]{0:T(128)}, u32[]{:S(2)}) copy-start(f32[2]{0:T(128)} %fusion.43) | copy-start | bytes 28
  303.4 1.1 copy-start.7
where the time goes:
time: 318 us; the launch traced here: 314 us
  other arithmetic  160 us (50%)
  starting transfers between devices  54.5 us (17%)
  local copies, waits for them, and re-layouts  41.7 us (13%)
  waiting for transfers between devices  40.7 us (13%)
  blocking collectives  9.19 us (3%)
  loops' own time  3.85 us (1%)
    reduce_sum x82, other arithmetic, apply_transpose(): return jnp.sum(blocks * vector[..., :, None, :], axis=-3)  92 us
    reduce_sum x40, other arithmetic, apply_block(): return jnp.sum(blocks * vector[..., None, :, :], axis=-2)  52.1 us
    ppermute x12, waiting for transfers between devices, from_behind(): lax.ppermute(value, axis, [(source, source + steps) for source in range(f...  40 us
    ppermute x12, starting transfers between devices, from_behind(): lax.ppermute(value, axis, [(source, source + steps) for source in range(f...  32.4 us
    mul x20, local copies, waits for them, and re-layouts, apply_transpose(): return jnp.sum(blocks * vector[..., :, None, :], axis=-3)  19.2 us
    ppermute x4, starting transfers between devices, extended(): before = lax.ppermute(last, axis, up)  16.9 us
    mul x16, local copies, waits for them, and re-layouts, apply_block(): return jnp.sum(blocks * vector[..., None, :, :], axis=-2)  14.8 us
    psum x1, blocking collectives, on_device(): mesh_sens = lax.psum(local_sens, 'cond')  9.19 us
  transfers between devices with their start and end apart: 20, of which 13 were waited for; matrix products, arithmetic and copies ran while one was open for 24% of the time, Pallas kernels for 0%

commit v1 on v0

--- a/solution.py
+++ b/solution.py
@@ -1,6 +1,8 @@
 import jax
 import jax.numpy as jnp
 from jax import lax
+from jax.experimental import pallas as pl
+from jax.experimental.pallas import tpu as pltpu
 from jax.sharding import PartitionSpec as P
 
 NZ = 32
@@ -26,41 +28,115 @@
     return lax.ppermute(value, axis, [(source, source + steps) for source in range(first, last)])
 
 
-def apply_block(blocks, vector):
-    return jnp.sum(blocks * vector[..., None, :, :], axis=-2)
-
-
-def apply_transpose(blocks, vector):
-    return jnp.sum(blocks * vector[..., :, None, :], axis=-3)
-
-
-def upper_sweep(rhs, near, far, incoming):
-
-    def step(carry, item):
-        last, before = carry
-        value, near_cell, far_cell = item
-        now = value - apply_block(near_cell, last) - apply_block(far_cell, before)
-        return ((now, last), now)
-
-    carry, values = lax.scan(step, (incoming[0], incoming[1]), (rhs, near, far))
-    return (values, jnp.stack([carry[0], carry[1]]))
-
-
-def lower_sweep(rhs, inverse, near, far, incoming):
-
-    def step(carry, item):
-        pending, partial_value = carry
-        value, inverse_cell, near_cell, far_cell = item
-        now = apply_transpose(inverse_cell, value - pending)
-        return (
-            (partial_value + apply_transpose(near_cell, now), apply_transpose(far_cell, now)),
-            now,
-        )
-
-    carry, values = lax.scan(
-        step, (incoming[0], incoming[1]), (rhs, inverse, near, far), reverse=True
-    )
-    return (values, jnp.stack([carry[0], carry[1]]))
+def _vmem_specs(n):
+    return [pl.BlockSpec(memory_space=pltpu.VMEM) for _ in range(n)]
+
+
+def _rows_times(blocks_ref, index, vec):
+    total = None
+    for a in range(vec.shape[0]):
+        term = blocks_ref[index + (a,)] * vec[a : a + 1, :]
+        total = term if total is None else total + term
+    return total
+
+
+def upper_pallas(rhs, near_t, far_t, incoming, want_values):
+    count, conds, nv = near_t.shape[0], near_t.shape[1], near_t.shape[2]
+    width = incoming.shape[1]
+    has_rhs = rhs is not None
+
+    def kernel(*refs):
+        if has_rhs:
+            rhs_ref, nt_ref, ft_ref, inc_ref = refs[:4]
+            outs = refs[4:]
+        else:
+            nt_ref, ft_ref, inc_ref = refs[:3]
+            outs = refs[3:]
+        if want_values:
+            val_ref, carry_ref = outs
+        else:
+            (carry_ref,) = outs
+        carry_ref[...] = inc_ref[...]
+
+        def step(i, unused):
+            for k in range(width):
+                for c in range(conds):
+                    last = carry_ref[0, k, c]
+                    before = carry_ref[1, k, c]
+                    acc = _rows_times(nt_ref, (i, c), last) + _rows_times(ft_ref, (i, c), before)
+                    if has_rhs:
+                        now = rhs_ref[i, c] - acc
+                    else:
+                        now = -acc
+                    carry_ref[1, k, c] = last
+                    carry_ref[0, k, c] = now
+                    if want_values:
+                        val_ref[i, c] = now
+            return unused
+
+        lax.fori_loop(0, count, step, 0)
+
+    shape = incoming.shape
+    out_shape = [jax.ShapeDtypeStruct(shape, jnp.float32)]
+    if want_values:
+        out_shape = [jax.ShapeDtypeStruct(rhs.shape, jnp.float32)] + out_shape
+    args = ([rhs] if has_rhs else []) + [near_t, far_t, incoming]
+    return pl.pallas_call(
+        kernel,
+        out_shape=tuple(out_shape),
+        in_specs=_vmem_specs(len(args)),
+        out_specs=tuple(_vmem_specs(len(out_shape))),
+    )(*args)
+
+
+def lower_pallas(rhs, inverse, near, far, incoming, want_values):
+    count, conds, nv = inverse.shape[0], inverse.shape[1], inverse.shape[2]
+    width = incoming.shape[1]
+    has_rhs = rhs is not None
+
+    def kernel(*refs):
+        if has_rhs:
+            rhs_ref, d_ref, b_ref, a_ref, inc_ref = refs[:5]
+            outs = refs[5:]
+        else:
+            d_ref, b_ref, a_ref, inc_ref = refs[:4]
+            outs = refs[4:]
+        if want_values:
+            val_ref, carry_ref = outs
+        else:
+            (carry_ref,) = outs
+        carry_ref[...] = inc_ref[...]
+
+        def step(t, unused):
+            i = count - 1 - t
+            for k in range(width):
+                for c in range(conds):
+                    pending = carry_ref[0, k, c]
+                    partial_value = carry_ref[1, k, c]
+                    if has_rhs:
+                        r = rhs_ref[i, c] - pending
+                    else:
+                        r = -pending
+                    now = _rows_times(d_ref, (i, c), r)
+                    carry_ref[0, k, c] = partial_value + _rows_times(b_ref, (i, c), now)
+                    carry_ref[1, k, c] = _rows_times(a_ref, (i, c), now)
+                    if want_values:
+                        val_ref[i, c] = now
+            return unused
+
+        lax.fori_loop(0, count, step, 0)
+
+    shape = incoming.shape
+    out_shape = [jax.ShapeDtypeStruct(shape, jnp.float32)]
+    if want_values:
+        out_shape = [jax.ShapeDtypeStruct(rhs.shape, jnp.float32)] + out_shape
+    args = ([rhs] if has_rhs else []) + [inverse, near, far, incoming]
+    return pl.pallas_call(
+        kernel,
+        out_shape=tuple(out_shape),
+        in_specs=_vmem_specs(len(args)),
+        out_specs=tuple(_vmem_specs(len(out_shape))),
+    )(*args)
 
 
 def unit_carries(shape):
@@ -105,7 +181,14 @@
 ):
     keep = (1.0 - wall_mask.astype(jnp.float32))[:, None, None, :]
     carry_shape = psi_old.shape[1:]
-    zeros = jnp.zeros((2,) + carry_shape, jnp.float32)
+    zeros = jnp.zeros((2, 1) + carry_shape, jnp.float32)
+    units = unit_carries(carry_shape)
+    near_t = jnp.swapaxes(near_upper, 2, 3)
+    far_t = jnp.swapaxes(far_upper, 2, 3)
+    (response,) = upper_pallas(None, near_t, far_t, units, False)
+    matrix = as_matrix(response)
+    (response,) = lower_pallas(None, inverse_diag, near_lower, far_lower, units, False)
+    reverse_matrix = as_matrix(response)
     psi = psi_old
     for step in range(ITERS):
         stream_pad = extended(psi, (("gx", 0),), 1)
@@ -118,25 +201,19 @@
         zres = jnp.einsum(
             "icvjq,cvqk->icvjk", grid, z_inverse, precision=lax.Precision.HIGHEST
         ).reshape(rhs.shape)
-        yres = apply_transpose(y_inverse, zres)
-        blank = jnp.zeros((yres.shape[0], 1) + carry_shape, jnp.float32)
-        units = unit_carries(carry_shape)
-        values, offset = upper_sweep(yres, near_upper, far_upper, zeros)
-        values, response = upper_sweep(blank, near_upper, far_upper, units)
-        matrix = as_matrix(response)
-        vector = as_vector(offset)
+        yres = jnp.sum(y_inverse * zres[..., :, None, :], axis=-3)
+        _, offset = upper_pallas(yres, near_t, far_t, zeros, True)
+        vector = as_vector(offset[:, 0])
 
         def upper_reversal(turn, incoming):
             return from_behind(carry_through(incoming, matrix, vector), "gx", 1)
 
         entering = lax.fori_loop(0, lax.axis_size("gx") - 1, upper_reversal, jnp.zeros_like(vector))
-        upper, leaving = upper_sweep(
-            yres, near_upper, far_upper, from_vector(entering, carry_shape[1])
-        )
-        values, offset = lower_sweep(upper, inverse_diag, near_lower, far_lower, zeros)
-        values, response = lower_sweep(blank, inverse_diag, near_lower, far_lower, units)
-        reverse_matrix = as_matrix(response)
-        vector_back = as_vector(offset)
+        upper, _ = upper_pallas(
+            yres, near_t, far_t, from_vector(entering, carry_shape[1])[:, None], True
+        )
+        _, offset = lower_pallas(upper, inverse_diag, near_lower, far_lower, zeros, True)
+        vector_back = as_vector(offset[:, 0])
 
         def lower_turn(turn, incoming):
             return from_behind(carry_through(incoming, reverse_matrix, vector_back), "gx", -1)
@@ -144,8 +221,13 @@
         entering = lax.fori_loop(
             0, lax.axis_size("gx") - 1, lower_turn, jnp.zeros_like(vector_back)
         )
-        lower, leaving = lower_sweep(
-            upper, inverse_diag, near_lower, far_lower, from_vector(entering, carry_shape[1])
+        lower, _ = lower_pallas(
+            upper,
+            inverse_diag,
+            near_lower,
+            far_lower,
+            from_vector(entering, carry_shape[1])[:, None],
+            True,
         )
         psi = (psi + 0.05 * lower) * keep
     onehot = (cond_index[:, None] == jnp.arange(weight_table.shape[0])[None, :]).astype(jnp.float32)

time: 318 us -> 191 us (0.60)
  other arithmetic: 160 us -> 8.34 us
  Pallas kernels: 0 us -> 42.5 us
  local copies, waits for them, and re-layouts: 41.7 us -> 28.1 us
  loops' own time: 3.85 us -> 0.32 us
    reduce_sum x122 -> x2, other arithmetic: 144 us -> 1.16 us  [on_device(): yres = jnp.sum(y_inverse * zres[..., :, None, :], axis=-3)]
    pallas_call x0 -> x10, Pallas kernels: none -> 42.5 us  [the longest x5 23 us: lower_pallas(): pl.pallas_call(kernel, out_shape=tuple(out_shape), in_specs=_vmem_specs(l...]
    mul x36 -> x4, local copies, waits for them, and re-layouts: 34 us -> 3.14 us  [on_device(): yres = jnp.sum(y_inverse * zres[..., :, None, :], axis=-3)]
    transpose x0 -> x5, local copies, waits for them, and re-layouts: none -> 7.52 us  [the longest x1 4 us: on_device(): far_t = jnp.swapaxes(far_upper, 2, 3)]
    unnamed x24 -> x26, local copies, waits for them, and re-layouts: 0.64 us -> 6.36 us
    sub x80 -> x0, other arithmetic: 4.04 us -> none  [the longest x40 2.42 us: step(): now = value - apply_block(near_cell, last) - apply_block(far_cell, before)]
    another operation x10 -> x0, loops' own time: 3.53 us -> none  [the longest x5 2.09 us: lower_sweep(): lax.scan(step, (incoming[0], incoming[1]), (rhs, inverse, near, far), rev...]
  transfers between devices with their start and end apart: 20 -> 20, of which waited for: 13 -> 13; matrix products, arithmetic and copies ran while one was open for 24% -> 7% of each run, Pallas kernels for 0% -> 8%
where the time goes in v1:
time: 191 us; the launch traced here: 190 us
  starting transfers between devices  54.7 us (29%)
  Pallas kernels  42.5 us (22%)
  waiting for transfers between devices  41 us (21%)
  local copies, waits for them, and re-layouts  28.1 us (15%)
  blocking collectives  9.19 us (5%)
  other arithmetic  8.34 us (4%)
  matrix products  4.7 us (2%)
    ppermute x12, waiting for transfers between devices, from_behind(): lax.ppermute(value, axis, [(source, source + steps) for source in range(f...  39.7 us
    ppermute x12, starting transfers between devices, from_behind(): lax.ppermute(value, axis, [(source, source + steps) for source in range(f...  33.2 us
    pallas_call x5, Pallas kernels, lower_pallas(): pl.pallas_call(kernel, out_shape=tuple(out_shape), in_specs=_vmem_specs(l...  23 us
    pallas_call x5, Pallas kernels, upper_pallas(): pl.pallas_call(kernel, out_shape=tuple(out_shape), in_specs=_vmem_specs(l...  19.5 us
    ppermute x4, starting transfers between devices, extended(): before = lax.ppermute(last, axis, up)  16.4 us
    psum x1, blocking collectives, on_device(): mesh_sens = lax.psum(local_sens, 'cond')  9.19 us
    unnamed x26, local copies, waits for them, and re-layouts  6.36 us
    ppermute x4, starting transfers between devices, extended(): after = lax.ppermute(first, axis, down)  5.16 us
  transfers between devices with their start and end apart: 20, of which 13 were waited for; matrix products, arithmetic and copies ran while one was open for 7% of the time, Pallas kernels for 8%

profile of v1, /device:TPU:0, one launch (start us, length us, event | category | flops | bytes accessed | tf_op | source)
XLA Modules:
  0.0 189.9 jit_solution(4398059664275504274)
XLA Ops:
  0.6 1.0 copy.172
  1.8 1.3 collective-permute-start.6
  3.0 3.0 %collective-permute-start.7 = (f32[8,2,6,32]{3,2,1,0:T(8,128)S(1)}, f32[8,2,6,32]{3,2,1,0:T(8,128)S(1)}, u32[]{:S(2)}, u32[]{:S(2)}) collective-permute-start(f32[8,2,6,32]{3,2,1,0:T(8,128)S(1)} %get-tuple-element.159), channel_id=1, source_target_pairs={{0,1},{1,2},{2,3},{4,5},{5,6},{6,7},{8,9},{9,10},{10,11},{12,13},{... | collective-permute-start | bytes 36872 | tf_op jit(solution)/shard_map/ppermute | solution.py:19
  6.1 1.3 collective-permute-start.4
  7.4 5.6 %collective-permute-start.5 = (f32[1,2,6,512]{3,2,1,0:T(8,128)S(1)}, f32[1,2,6,512]{3,2,1,0:T(8,128)S(1)}, u32[]{:S(2)}, u32[]{:S(2)}) collective-permute-start(f32[1,2,6,512]{3,2,1,0:T(8,128)S(1)} %get-tuple-element.157), channel_id=1, source_target_pairs={{0,4},{4,8},{8,12},{1,5},{5,9},{9,13},{2,6},{6,10},{10,14},{3,7},{... | collective-permute-start | bytes 73736 | tf_op jit(solution)/shard_map/ppermute | solution.py:19
  13.7 4.0 %copy_bitcast_fusion = (f32[8,2,6,6,512]{4,3,2,1,0:T(8,128)}, f32[8,2,6,6,512]{4,3,2,1,0:T(8,128)}) fusion(f32[8,2,6,6,512]{4,1,3,2,0:T(2,128)} %param.24, f32[8,2,6,6,512]{4,1,3,2,0:T(2,128)} %param.23), kind=kLoop, calls=%fused_computation.8 | loop fusion | bytes 4718592 | tf_op jit(solution)/shard_map/transpose | solution.py:187
  17.7 1.1 broadcast_in_dim.28.refs_2_.refs_3_
  18.8 7.1 %shard_map.140 = f32[2,12,2,6,512]{4,3,2,1,0:T(8,128)} custom-call(f32[8,2,6,6,512]{4,3,2,1,0:T(8,128)} %get-tuple-element.161.refs_0_.refs_1_, f32[8,2,6,6,512]{4,3,2,1,0:T(8,128)} %get-tuple-element.160.refs_1_.refs_2_, f32[2,12,2,6,512]{4,3,2,1,0:T(8,128)} %broadcast_in_dim.28.refs_2_.refs_3_), custom_call_target="tpu_custom_call" | custom-call | tf_op jit(solution)/shard_map/pallas_call | solution.py:84
  25.9 1.7 copy.155
  27.6 1.4 copy.169.refs_0_.refs_1_
  29.1 1.4 copy.170.refs_1_.refs_2_
  30.5 1.4 copy.171.refs_2_.refs_3_
  32.0 8.4 %shard_map.143 = f32[2,12,2,6,512]{4,3,2,1,0:T(8,128)} custom-call(f32[8,2,6,6,512]{4,3,2,1,0:T(8,128)} %copy.169.refs_0_.refs_1_, f32[8,2,6,6,512]{4,3,2,1,0:T(8,128)} %copy.170.refs_1_.refs_2_, f32[8,2,6,6,512]{4,3,2,1,0:T(8,128)} %copy.171.refs_2_.refs_3_, f32[2,12,2,6,512]{4,3,2,1,0:T(8,128)} %broadcast_in_dim.28.refs_2_.refs_3_), custom_call_target="tpu_custom_call" | custom-call | tf_op jit(solution)/shard_map/pallas_call | solution.py:134
  40.4 1.6 copy.163
  42.7 1.8 convolution_bitcast_fusion.1
  44.5 1.4 mul.70
  48.0 3.1 %shard_map.141 = (f32[8,2,6,512]{3,2,1,0:T(8,128)}, f32[2,1,2,6,512]{4,3,2,1,0:T(8,128)}) custom-call(f32[8,2,6,512]{3,2,1,0:T(8,128)} %copy.159.refs_0_, f32[8,2,6,6,512]{4,3,2,1,0:T(8,128)} %get-tuple-element.161.refs_0_.refs_1_, f32[8,2,6,6,512]{4,3,2,1,0:T(8,128)} %get-tuple-element.160.refs_1_.refs_2_, f32[2,1,2,6,512]{4,3,2,1,0:T(8,128)} %broadcast_in_dim.29.refs_3_.refs_4_), custom_call_target="tpu_custom_call" | custom-call | tf_op jit(solution)/shard_map/pallas_call | solution.py:84
  51.1 0.9 copy.157
  52.0 18.6 %while.40 = (s32[]{:T(128)}, f32[12,2,512]{2,1,0:T(2,128)S(1)}, f32[12,12,2,512]{3,2,1,0:T(2,128)S(1)}, f32[12,2,512]{2,1,0:T(2,128)S(1)}, s32[]{:T(128)}) while((s32[]{:T(128)}, f32[12,2,512]{2,1,0:T(2,128)S(1)}, f32[12,12,2,512]{3,2,1,0:T(2,128)S(1)}, f32[12,2,512]{2,1,0:T(2,128)S(1)}, s32[]{:T(128)}) %tuple.89), condition=%wide.region_2.0_spmd, body=%wide.region_1.0_spmd.sunk | while | flops 294914 | bytes 1032293 | solution.py:211
  52.4 3.9 %collective-permute-start = (f32[12,2,512]{2,1,0:T(2,128)S(1)}, f32[12,2,512]{2,1,0:T(2,128)S(1)}, u32[]{:S(2)}, u32[]{:S(2)}) collective-permute-start(f32[12,2,512]{2,1,0:T(2,128)S(1)} %bitcast_add_fusion.8), channel_id=1, source_target_pairs={{0,4},{4,8},{8,12},{1,5},{5,9},{9,13},{2,6},{6,10},{10,14},{3,7},{... | collective-permute-start | bytes 147464 | tf_op jit(solution)/shard_map/while/body/eval_jaxpr/ppermute | solution.py:28
  56.3 1.7 collective-permute-done
  58.3 4.4 %collective-permute-start = (f32[12,2,512]{2,1,0:T(2,128)S(1)}, f32[12,2,512]{2,1,0:T(2,128)S(1)}, u32[]{:S(2)}, u32[]{:S(2)}) collective-permute-start(f32[12,2,512]{2,1,0:T(2,128)S(1)} %bitcast_add_fusion.8), channel_id=1, source_target_pairs={{0,4},{4,8},{8,12},{1,5},{5,9},{9,13},{2,6},{6,10},{10,14},{3,7},{... | collective-permute-start | bytes 147464 | tf_op jit(solution)/shard_map/while/body/eval_jaxpr/ppermute | solution.py:28
  62.7 1.7 collective-permute-done
  64.7 4.2 %collective-permute-start = (f32[12,2,512]{2,1,0:T(2,128)S(1)}, f32[12,2,512]{2,1,0:T(2,128)S(1)}, u32[]{:S(2)}, u32[]{:S(2)}) collective-permute-start(f32[12,2,512]{2,1,0:T(2,128)S(1)} %bitcast_add_fusion.8), channel_id=1, source_target_pairs={{0,4},{4,8},{8,12},{1,5},{5,9},{9,13},{2,6},{6,10},{10,14},{3,7},{... | collective-permute-start | bytes 147464 | tf_op jit(solution)/shard_map/while/body/eval_jaxpr/ppermute | solution.py:28
  69.0 1.7 collective-permute-done
  71.3 3.1 %shard_map.142 = (f32[8,2,6,512]{3,2,1,0:T(8,128)}, f32[2,1,2,6,512]{4,3,2,1,0:T(8,128)}) custom-call(f32[8,2,6,512]{3,2,1,0:T(8,128)} %copy.159.refs_0_, f32[8,2,6,6,512]{4,3,2,1,0:T(8,128)} %get-tuple-element.161.refs_0_.refs_1_, f32[8,2,6,6,512]{4,3,2,1,0:T(8,128)} %get-tuple-element.160.refs_1_.refs_2_, f32[2,1,2,6,512]{4,3,2,1,0:T(8,128)} %bitcast.147), custom_call_target="tpu_custom_call" | custom-call | tf_op jit(solution)/shard_map/pallas_call | solution.py:84
  74.4 3.7 %shard_map.144 = (f32[8,2,6,512]{3,2,1,0:T(8,128)}, f32[2,1,2,6,512]{4,3,2,1,0:T(8,128)}) custom-call(f32[8,2,6,512]{3,2,1,0:T(8,128)} %get-tuple-element.100.refs_0_, f32[8,2,6,6,512]{4,3,2,1,0:T(8,128)} %copy.169.refs_0_.refs_1_, f32[8,2,6,6,512]{4,3,2,1,0:T(8,128)} %copy.170.refs_1_.refs_2_, f32[8,2,6,6,512]{4,3,2,1,0:T(8,128)} %copy.171.refs_2_.refs_3_, ...), custom_call_target="tpu_custom_call" | custom-call | tf_op jit(solution)/shard_map/pallas_call | solution.py:134
  79.0 19.3 %while.41 = (s32[]{:T(128)}, f32[12,2,512]{2,1,0:T(2,128)S(1)}, f32[12,12,2,512]{3,2,1,0:T(2,128)S(1)}, f32[12,2,512]{2,1,0:T(2,128)S(1)}, s32[]{:T(128)}) while((s32[]{:T(128)}, f32[12,2,512]{2,1,0:T(2,128)S(1)}, f32[12,12,2,512]{3,2,1,0:T(2,128)S(1)}, f32[12,2,512]{2,1,0:T(2,128)S(1)}, s32[]{:T(128)}) %tuple.90), condition=%wide.region_4.0_spmd, body=%wide.region_3.0_spmd.sunk | while | flops 294914 | bytes 1032293 | solution.py:221
  79.3 1.3 collective-permute-start.1
  80.6 5.0 %collective-permute-done.1 = f32[12,2,512]{2,1,0:T(2,128)S(1)} collective-permute-done((f32[12,2,512]{2,1,0:T(2,128)S(1)}, f32[12,2,512]{2,1,0:T(2,128)S(1)}, u32[]{:S(2)}, u32[]{:S(2)}) %collective-permute-start.1) | collective-permute-done | bytes 49184 | tf_op jit(solution)/shard_map/while/body/eval_jaxpr/ppermute | solution.py:28
  85.9 1.3 collective-permute-start.1
  87.2 4.7 %collective-permute-done.1 = f32[12,2,512]{2,1,0:T(2,128)S(1)} collective-permute-done((f32[12,2,512]{2,1,0:T(2,128)S(1)}, f32[12,2,512]{2,1,0:T(2,128)S(1)}, u32[]{:S(2)}, u32[]{:S(2)}) %collective-permute-start.1) | collective-permute-done | bytes 49184 | tf_op jit(solution)/shard_map/while/body/eval_jaxpr/ppermute | solution.py:28
  92.2 1.3 collective-permute-start.1
  93.5 4.8 %collective-permute-done.1 = f32[12,2,512]{2,1,0:T(2,128)S(1)} collective-permute-done((f32[12,2,512]{2,1,0:T(2,128)S(1)}, f32[12,2,512]{2,1,0:T(2,128)S(1)}, u32[]{:S(2)}, u32[]{:S(2)}) %collective-permute-start.1) | collective-permute-done | bytes 49184 | tf_op jit(solution)/shard_map/while/body/eval_jaxpr/ppermute | solution.py:28
  98.9 3.7 %shard_map.145 = (f32[8,2,6,512]{3,2,1,0:T(8,128)}, f32[2,1,2,6,512]{4,3,2,1,0:T(8,128)}) custom-call(f32[8,2,6,512]{3,2,1,0:T(8,128)} %get-tuple-element.100.refs_0_, f32[8,2,6,6,512]{4,3,2,1,0:T(8,128)} %copy.169.refs_0_.refs_1_, f32[8,2,6,6,512]{4,3,2,1,0:T(8,128)} %copy.170.refs_1_.refs_2_, f32[8,2,6,6,512]{4,3,2,1,0:T(8,128)} %copy.171.refs_2_.refs_3_, ...), custom_call_target="tpu_custom_call" | custom-call | tf_op jit(solution)/shard_map/pallas_call | solution.py:134
  102.6 1.0 add_multiply_fusion.1
  103.7 1.3 collective-permute-start.10
  105.0 3.0 %collective-permute-start.11 = (f32[8,2,6,32]{3,2,1,0:T(8,128)S(1)}, f32[8,2,6,32]{3,2,1,0:T(8,128)S(1)}, u32[]{:S(2)}, u32[]{:S(2)}) collective-permute-start(f32[8,2,6,32]{3,2,1,0:T(8,128)S(1)} %get-tuple-element.155), channel_id=1, source_target_pairs={{0,1},{1,2},{2,3},{4,5},{5,6},{6,7},{8,9},{9,10},{10,11},{12,13},{... | collective-permute-start | bytes 36872 | tf_op jit(solution)/shard_map/ppermute | solution.py:19
  108.0 1.3 collective-permute-start.8
  109.3 4.7 %collective-permute-start.9 = (f32[1,2,6,512]{3,2,1,0:T(8,128)S(1)}, f32[1,2,6,512]{3,2,1,0:T(8,128)S(1)}, u32[]{:S(2)}, u32[]{:S(2)}) collective-permute-start(f32[1,2,6,512]{3,2,1,0:T(8,128)S(1)} %get-tuple-element.153), channel_id=1, source_target_pairs={{0,4},{4,8},{8,12},{1,5},{5,9},{9,13},{2,6},{6,10},{10,14},{3,7},{... | collective-permute-start | bytes 73736 | tf_op jit(solution)/shard_map/ppermute | solution.py:19
  114.3 1.4 collective-permute-done.9
  116.0 1.2 reshape.65
  117.2 2.9 %convolution_bitcast_fusion = f32[8,2,6,16,32]{4,3,0,2,1:T(8,128)} fusion(f32[8,2,6,16,32]{4,3,0,2,1:T(8,128)} %reshape.65, f32[2,6,32,32]{3,2,1,0:T(8,128)S(1)} %copy-done), kind=kOutput, calls=%fused_computation.10 | convolution fusion | flops 18874368 | bytes 442368 | tf_op jit(solution)/shard_map/icvjq,cvqk->icvjk/dot_general | solution.py:201
  120.1 1.4 mul.78
  123.1 3.1 %shard_map.146 = (f32[8,2,6,512]{3,2,1,0:T(8,128)}, f32[2,1,2,6,512]{4,3,2,1,0:T(8,128)}) custom-call(f32[8,2,6,512]{3,2,1,0:T(8,128)} %copy.179.refs_0_, f32[8,2,6,6,512]{4,3,2,1,0:T(8,128)} %get-tuple-element.161.refs_0_.refs_1_, f32[8,2,6,6,512]{4,3,2,1,0:T(8,128)} %get-tuple-element.160.refs_1_.refs_2_, f32[2,1,2,6,512]{4,3,2,1,0:T(8,128)} %broadcast_in_dim.29.refs_3_.refs_4_), custom_call_target="tpu_custom_call" | custom-call | tf_op jit(solution)/shard_map/pallas_call | solution.py:84
  127.1 19.0 %while.42 = (s32[]{:T(128)}, f32[12,2,512]{2,1,0:T(2,128)S(1)}, f32[12,12,2,512]{3,2,1,0:T(2,128)S(1)}, f32[12,2,512]{2,1,0:T(2,128)S(1)}, s32[]{:T(128)}) while((s32[]{:T(128)}, f32[12,2,512]{2,1,0:T(2,128)S(1)}, f32[12,12,2,512]{3,2,1,0:T(2,128)S(1)}, f32[12,2,512]{2,1,0:T(2,128)S(1)}, s32[]{:T(128)}) %tuple.88), condition=%wide.region_7.0_spmd, body=%wide.region_6.0_spmd.sunk | while | flops 294914 | bytes 1032293 | solution.py:211
  127.4 4.4 %collective-permute-start.2 = (f32[12,2,512]{2,1,0:T(2,128)S(1)}, f32[12,2,512]{2,1,0:T(2,128)S(1)}, u32[]{:S(2)}, u32[]{:S(2)}) collective-permute-start(f32[12,2,512]{2,1,0:T(2,128)S(1)} %bitcast_add_fusion.10), channel_id=1, source_target_pairs={{0,4},{4,8},{8,12},{1,5},{5,9},{9,13},{2,6},{6,10},{10,14},{3,7},{... | collective-permute-start | bytes 147464 | tf_op jit(solution)/shard_map/while/body/eval_jaxpr/ppermute | solution.py:28
  131.8 1.7 collective-permute-done.2
  133.8 4.2 %collective-permute-start.2 = (f32[12,2,512]{2,1,0:T(2,128)S(1)}, f32[12,2,512]{2,1,0:T(2,128)S(1)}, u32[]{:S(2)}, u32[]{:S(2)}) collective-permute-start(f32[12,2,512]{2,1,0:T(2,128)S(1)} %bitcast_add_fusion.10), channel_id=1, source_target_pairs={{0,4},{4,8},{8,12},{1,5},{5,9},{9,13},{2,6},{6,10},{10,14},{3,7},{... | collective-permute-start | bytes 147464 | tf_op jit(solution)/shard_map/while/body/eval_jaxpr/ppermute | solution.py:28
  138.1 1.7 collective-permute-done.2
  140.1 4.2 %collective-permute-start.2 = (f32[12,2,512]{2,1,0:T(2,128)S(1)}, f32[12,2,512]{2,1,0:T(2,128)S(1)}, u32[]{:S(2)}, u32[]{:S(2)}) collective-permute-start(f32[12,2,512]{2,1,0:T(2,128)S(1)} %bitcast_add_fusion.10), channel_id=1, source_target_pairs={{0,4},{4,8},{8,12},{1,5},{5,9},{9,13},{2,6},{6,10},{10,14},{3,7},{... | collective-permute-start | bytes 147464 | tf_op jit(solution)/shard_map/while/body/eval_jaxpr/ppermute | solution.py:28
  144.3 1.7 collective-permute-done.2
  146.7 3.1 %shard_map.147 = (f32[8,2,6,512]{3,2,1,0:T(8,128)}, f32[2,1,2,6,512]{4,3,2,1,0:T(8,128)}) custom-call(f32[8,2,6,512]{3,2,1,0:T(8,128)} %copy.179.refs_0_, f32[8,2,6,6,512]{4,3,2,1,0:T(8,128)} %get-tuple-element.161.refs_0_.refs_1_, f32[8,2,6,6,512]{4,3,2,1,0:T(8,128)} %get-tuple-element.160.refs_1_.refs_2_, f32[2,1,2,6,512]{4,3,2,1,0:T(8,128)} %bitcast.146), custom_call_target="tpu_custom_call" | custom-call | tf_op jit(solution)/shard_map/pallas_call | solution.py:84
  149.8 3.6 %shard_map.148 = (f32[8,2,6,512]{3,2,1,0:T(8,128)}, f32[2,1,2,6,512]{4,3,2,1,0:T(8,128)}) custom-call(f32[8,2,6,512]{3,2,1,0:T(8,128)} %get-tuple-element.106.refs_0_, f32[8,2,6,6,512]{4,3,2,1,0:T(8,128)} %copy.169.refs_0_.refs_1_, f32[8,2,6,6,512]{4,3,2,1,0:T(8,128)} %copy.170.refs_1_.refs_2_, f32[8,2,6,6,512]{4,3,2,1,0:T(8,128)} %copy.171.refs_2_.refs_3_, ...), custom_call_target="tpu_custom_call" | custom-call | tf_op jit(solution)/shard_map/pallas_call | solution.py:134
  154.3 19.6 %while.43 = (s32[]{:T(128)}, f32[12,2,512]{2,1,0:T(2,128)S(1)}, f32[12,12,2,512]{3,2,1,0:T(2,128)S(1)}, f32[12,2,512]{2,1,0:T(2,128)S(1)}, s32[]{:T(128)}) while((s32[]{:T(128)}, f32[12,2,512]{2,1,0:T(2,128)S(1)}, f32[12,12,2,512]{3,2,1,0:T(2,128)S(1)}, f32[12,2,512]{2,1,0:T(2,128)S(1)}, s32[]{:T(128)}) %tuple.87), condition=%wide.region_9.0_spmd, body=%wide.region_8.0_spmd.sunk | while | flops 294914 | bytes 1032293 | solution.py:221
  154.6 1.3 collective-permute-start.3
  155.9 5.0 %collective-permute-done.3 = f32[12,2,512]{2,1,0:T(2,128)S(1)} collective-permute-done((f32[12,2,512]{2,1,0:T(2,128)S(1)}, f32[12,2,512]{2,1,0:T(2,128)S(1)}, u32[]{:S(2)}, u32[]{:S(2)}) %collective-permute-start.3) | collective-permute-done | bytes 49184 | tf_op jit(solution)/shard_map/while/body/eval_jaxpr/ppermute | solution.py:28
  161.2 1.3 collective-permute-start.3
  162.5 5.1 %collective-permute-done.3 = f32[12,2,512]{2,1,0:T(2,128)S(1)} collective-permute-done((f32[12,2,512]{2,1,0:T(2,128)S(1)}, f32[12,2,512]{2,1,0:T(2,128)S(1)}, u32[]{:S(2)}, u32[]{:S(2)}) %collective-permute-start.3) | collective-permute-done | bytes 49184 | tf_op jit(solution)/shard_map/while/body/eval_jaxpr/ppermute | solution.py:28
  168.0 1.3 collective-permute-start.3
  169.3 4.7 %collective-permute-done.3 = f32[12,2,512]{2,1,0:T(2,128)S(1)} collective-permute-done((f32[12,2,512]{2,1,0:T(2,128)S(1)}, f32[12,2,512]{2,1,0:T(2,128)S(1)}, u32[]{:S(2)}, u32[]{:S(2)}) %collective-permute-start.3) | collective-permute-done | bytes 49184 | tf_op jit(solution)/shard_map/while/body/eval_jaxpr/ppermute | solution.py:28
  174.6 3.6 %shard_map.149 = (f32[8,2,6,512]{3,2,1,0:T(8,128)}, f32[2,1,2,6,512]{4,3,2,1,0:T(8,128)}) custom-call(f32[8,2,6,512]{3,2,1,0:T(8,128)} %get-tuple-element.106.refs_0_, f32[8,2,6,6,512]{4,3,2,1,0:T(8,128)} %copy.169.refs_0_.refs_1_, f32[8,2,6,6,512]{4,3,2,1,0:T(8,128)} %copy.170.refs_1_.refs_2_, f32[8,2,6,6,512]{4,3,2,1,0:T(8,128)} %copy.171.refs_2_.refs_3_, ...), custom_call_target="tpu_custom_call" | custom-call | tf_op jit(solution)/shard_map/pallas_call | solution.py:134
  178.2 1.1 multiply_bitcast_fusion
  179.9 9.2 %psum.7 = f32[8,3,512]{2,0,1:T(8,128)} all-reduce(f32[8,3,512]{2,0,1:T(8,128)S(1)} %bitcast.148), channel_id=1, replica_groups=mesh['cond'=2,'gx'=4,'gy'=4] {'cond'}, use_global_device_ids=true, to_apply=%region_11.0 | all-reduce | flops 12288 | bytes 98304 | tf_op jit(solution)/shard_map/psum | solution.py:241
  (86 shorter events, 15.6 us)
Async XLA Ops:
  0.6 42.0 %copy-start = (f32[2,6,32,32]{3,2,1,0:T(8,128)S(1)}, f32[2,6,32,32]{3,2,1,0:T(8,128)}, u32[]{:S(2)}) copy-start(f32[2,6,32,32]{3,2,1,0:T(8,128)} %param.29) | copy-start | bytes 147460
  1.8 40.3 %collective-permute-start.6 = (f32[8,2,6,32]{3,2,1,0:T(8,128)S(1)}, f32[8,2,6,32]{3,2,1,0:T(8,128)S(1)}, u32[]{:S(2)}, u32[]{:S(2)}) collective-permute-start(f32[8,2,6,32]{3,2,1,0:T(8,128)S(1)} %get-tuple-element.158), channel_id=1, source_target_pairs={{1,0},{2,1},{3,2},{5,4},{6,5},{7,6},{9,8},{10,9},{11,10},{13,12},{... | collective-permute-start | bytes 36872 | tf_op jit(solution)/shard_map/ppermute | solution.py:20
  3.0 39.0 %collective-permute-start.7 = (f32[8,2,6,32]{3,2,1,0:T(8,128)S(1)}, f32[8,2,6,32]{3,2,1,0:T(8,128)S(1)}, u32[]{:S(2)}, u32[]{:S(2)}) collective-permute-start(f32[8,2,6,32]{3,2,1,0:T(8,128)S(1)} %get-tuple-element.159), channel_id=1, source_target_pairs={{0,1},{1,2},{2,3},{4,5},{5,6},{6,7},{8,9},{9,10},{10,11},{12,13},{... | collective-permute-start | bytes 36872 | tf_op jit(solution)/shard_map/ppermute | solution.py:19
  6.1 36.0 %collective-permute-start.4 = (f32[1,2,6,512]{3,2,1,0:T(8,128)S(1)}, f32[1,2,6,512]{3,2,1,0:T(8,128)S(1)}, u32[]{:S(2)}, u32[]{:S(2)}) collective-permute-start(f32[1,2,6,512]{3,2,1,0:T(8,128)S(1)} %get-tuple-element.156), channel_id=1, source_target_pairs={{4,0},{8,4},{12,8},{5,1},{9,5},{13,9},{6,2},{10,6},{14,10},{7,3},{... | collective-permute-start | bytes 73736 | tf_op jit(solution)/shard_map/ppermute | solution.py:20
  7.4 34.7 %collective-permute-start.5 = (f32[1,2,6,512]{3,2,1,0:T(8,128)S(1)}, f32[1,2,6,512]{3,2,1,0:T(8,128)S(1)}, u32[]{:S(2)}, u32[]{:S(2)}) collective-permute-start(f32[1,2,6,512]{3,2,1,0:T(8,128)S(1)} %get-tuple-element.157), channel_id=1, source_target_pairs={{0,4},{4,8},{8,12},{1,5},{5,9},{9,13},{2,6},{6,10},{10,14},{3,7},{... | collective-permute-start | bytes 73736 | tf_op jit(solution)/shard_map/ppermute | solution.py:19
  25.9 1.7 copy-start.2
  27.6 1.5 copy-start.3
  29.1 1.4 copy-start.4
  40.4 1.7 copy-start.5
  42.7 3.4 %copy-start.1 = (f32[8,2,6,6,512]{4,1,3,2,0:T(2,128)S(1)}, f32[8,2,6,6,512]{4,1,3,2,0:T(2,128)}, u32[]{:S(2)}) copy-start(f32[8,2,6,6,512]{4,1,3,2,0:T(2,128)} %param.28) | copy-start | bytes 3538948
  52.4 5.7 %collective-permute-start = (f32[12,2,512]{2,1,0:T(2,128)S(1)}, f32[12,2,512]{2,1,0:T(2,128)S(1)}, u32[]{:S(2)}, u32[]{:S(2)}) collective-permute-start(f32[12,2,512]{2,1,0:T(2,128)S(1)} %bitcast_add_fusion.8), channel_id=1, source_target_pairs={{0,4},{4,8},{8,12},{1,5},{5,9},{9,13},{2,6},{6,10},{10,14},{3,7},{... | collective-permute-start | bytes 147464 | tf_op jit(solution)/shard_map/while/body/eval_jaxpr/ppermute | solution.py:28
  58.3 6.1 %collective-permute-start = (f32[12,2,512]{2,1,0:T(2,128)S(1)}, f32[12,2,512]{2,1,0:T(2,128)S(1)}, u32[]{:S(2)}, u32[]{:S(2)}) collective-permute-start(f32[12,2,512]{2,1,0:T(2,128)S(1)} %bitcast_add_fusion.8), channel_id=1, source_target_pairs={{0,4},{4,8},{8,12},{1,5},{5,9},{9,13},{2,6},{6,10},{10,14},{3,7},{... | collective-permute-start | bytes 147464 | tf_op jit(solution)/shard_map/while/body/eval_jaxpr/ppermute | solution.py:28
  64.7 6.0 %collective-permute-start = (f32[12,2,512]{2,1,0:T(2,128)S(1)}, f32[12,2,512]{2,1,0:T(2,128)S(1)}, u32[]{:S(2)}, u32[]{:S(2)}) collective-permute-start(f32[12,2,512]{2,1,0:T(2,128)S(1)} %bitcast_add_fusion.8), channel_id=1, source_target_pairs={{0,4},{4,8},{8,12},{1,5},{5,9},{9,13},{2,6},{6,10},{10,14},{3,7},{... | collective-permute-start | bytes 147464 | tf_op jit(solution)/shard_map/while/body/eval_jaxpr/ppermute | solution.py:28
  79.3 6.3 %collective-permute-start.1 = (f32[12,2,512]{2,1,0:T(2,128)S(1)}, f32[12,2,512]{2,1,0:T(2,128)S(1)}, u32[]{:S(2)}, u32[]{:S(2)}) collective-permute-start(f32[12,2,512]{2,1,0:T(2,128)S(1)} %bitcast_add_fusion.9), channel_id=1, source_target_pairs={{4,0},{8,4},{12,8},{5,1},{9,5},{13,9},{6,2},{10,6},{14,10},{7,3},{... | collective-permute-start | bytes 147464 | tf_op jit(solution)/shard_map/while/body/eval_jaxpr/ppermute | solution.py:28
  85.9 6.0 %collective-permute-start.1 = (f32[12,2,512]{2,1,0:T(2,128)S(1)}, f32[12,2,512]{2,1,0:T(2,128)S(1)}, u32[]{:S(2)}, u32[]{:S(2)}) collective-permute-start(f32[12,2,512]{2,1,0:T(2,128)S(1)} %bitcast_add_fusion.9), channel_id=1, source_target_pairs={{4,0},{8,4},{12,8},{5,1},{9,5},{13,9},{6,2},{10,6},{14,10},{7,3},{... | collective-permute-start | bytes 147464 | tf_op jit(solution)/shard_map/while/body/eval_jaxpr/ppermute | solution.py:28
  92.2 6.1 %collective-permute-start.1 = (f32[12,2,512]{2,1,0:T(2,128)S(1)}, f32[12,2,512]{2,1,0:T(2,128)S(1)}, u32[]{:S(2)}, u32[]{:S(2)}) collective-permute-start(f32[12,2,512]{2,1,0:T(2,128)S(1)} %bitcast_add_fusion.9), channel_id=1, source_target_pairs={{4,0},{8,4},{12,8},{5,1},{9,5},{13,9},{6,2},{10,6},{14,10},{7,3},{... | collective-permute-start | bytes 147464 | tf_op jit(solution)/shard_map/while/body/eval_jaxpr/ppermute | solution.py:28
  98.9 3.7 %copy-start.6 = (f32[8,2,6,512]{3,1,2,0:T(2,128)S(1)}, f32[8,2,6,512]{3,1,2,0:T(2,128)}, u32[]{:S(2)}) copy-start(f32[8,2,6,512]{3,1,2,0:T(2,128)} %param.21) | copy-start | bytes 589828
  98.9 15.2 %copy-start.8 = (f32[8]{0:T(128)S(1)}, f32[8]{0:T(128)}, u32[]{:S(2)}) copy-start(f32[8]{0:T(128)} %param.33) | copy-start | bytes 100
  98.9 15.2 %copy-start.9 = (s32[2]{0:T(128)S(1)}, s32[2]{0:T(128)}, u32[]{:S(2)}) copy-start(s32[2]{0:T(128)} %param.32) | copy-start | bytes 28
  103.7 10.6 %collective-permute-start.10 = (f32[8,2,6,32]{3,2,1,0:T(8,128)S(1)}, f32[8,2,6,32]{3,2,1,0:T(8,128)S(1)}, u32[]{:S(2)}, u32[]{:S(2)}) collective-permute-start(f32[8,2,6,32]{3,2,1,0:T(8,128)S(1)} %get-tuple-element.154), channel_id=1, source_target_pairs={{1,0},{2,1},{3,2},{5,4},{6,5},{7,6},{9,8},{10,9},{11,10},{13,12},{... | collective-permute-start | bytes 36872 | tf_op jit(solution)/shard_map/ppermute | solution.py:20
  105.0 9.3 %collective-permute-start.11 = (f32[8,2,6,32]{3,2,1,0:T(8,128)S(1)}, f32[8,2,6,32]{3,2,1,0:T(8,128)S(1)}, u32[]{:S(2)}, u32[]{:S(2)}) collective-permute-start(f32[8,2,6,32]{3,2,1,0:T(8,128)S(1)} %get-tuple-element.155), channel_id=1, source_target_pairs={{0,1},{1,2},{2,3},{4,5},{5,6},{6,7},{8,9},{9,10},{10,11},{12,13},{... | collective-permute-start | bytes 36872 | tf_op jit(solution)/shard_map/ppermute | solution.py:19
  108.0 6.3 %collective-permute-start.8 = (f32[1,2,6,512]{3,2,1,0:T(8,128)S(1)}, f32[1,2,6,512]{3,2,1,0:T(8,128)S(1)}, u32[]{:S(2)}, u32[]{:S(2)}) collective-permute-start(f32[1,2,6,512]{3,2,1,0:T(8,128)S(1)} %get-tuple-element.152), channel_id=1, source_target_pairs={{4,0},{8,4},{12,8},{5,1},{9,5},{13,9},{6,2},{10,6},{14,10},{7,3},{... | collective-permute-start | bytes 73736 | tf_op jit(solution)/shard_map/ppermute | solution.py:20
  109.3 6.3 %collective-permute-start.9 = (f32[1,2,6,512]{3,2,1,0:T(8,128)S(1)}, f32[1,2,6,512]{3,2,1,0:T(8,128)S(1)}, u32[]{:S(2)}, u32[]{:S(2)}) collective-permute-start(f32[1,2,6,512]{3,2,1,0:T(8,128)S(1)} %get-tuple-element.153), channel_id=1, source_target_pairs={{0,4},{4,8},{8,12},{1,5},{5,9},{9,13},{2,6},{6,10},{10,14},{3,7},{... | collective-permute-start | bytes 73736 | tf_op jit(solution)/shard_map/ppermute | solution.py:19
  127.4 6.1 %collective-permute-start.2 = (f32[12,2,512]{2,1,0:T(2,128)S(1)}, f32[12,2,512]{2,1,0:T(2,128)S(1)}, u32[]{:S(2)}, u32[]{:S(2)}) collective-permute-start(f32[12,2,512]{2,1,0:T(2,128)S(1)} %bitcast_add_fusion.10), channel_id=1, source_target_pairs={{0,4},{4,8},{8,12},{1,5},{5,9},{9,13},{2,6},{6,10},{10,14},{3,7},{... | collective-permute-start | bytes 147464 | tf_op jit(solution)/shard_map/while/body/eval_jaxpr/ppermute | solution.py:28
  133.8 6.0 %collective-permute-start.2 = (f32[12,2,512]{2,1,0:T(2,128)S(1)}, f32[12,2,512]{2,1,0:T(2,128)S(1)}, u32[]{:S(2)}, u32[]{:S(2)}) collective-permute-start(f32[12,2,512]{2,1,0:T(2,128)S(1)} %bitcast_add_fusion.10), channel_id=1, source_target_pairs={{0,4},{4,8},{8,12},{1,5},{5,9},{9,13},{2,6},{6,10},{10,14},{3,7},{... | collective-permute-start | bytes 147464 | tf_op jit(solution)/shard_map/while/body/eval_jaxpr/ppermute | solution.py:28
  140.1 6.0 %collective-permute-start.2 = (f32[12,2,512]{2,1,0:T(2,128)S(1)}, f32[12,2,512]{2,1,0:T(2,128)S(1)}, u32[]{:S(2)}, u32[]{:S(2)}) collective-permute-start(f32[12,2,512]{2,1,0:T(2,128)S(1)} %bitcast_add_fusion.10), channel_id=1, source_target_pairs={{0,4},{4,8},{8,12},{1,5},{5,9},{9,13},{2,6},{6,10},{10,14},{3,7},{... | collective-permute-start | bytes 147464 | tf_op jit(solution)/shard_map/while/body/eval_jaxpr/ppermute | solution.py:28
  154.6 6.3 %collective-permute-start.3 = (f32[12,2,512]{2,1,0:T(2,128)S(1)}, f32[12,2,512]{2,1,0:T(2,128)S(1)}, u32[]{:S(2)}, u32[]{:S(2)}) collective-permute-start(f32[12,2,512]{2,1,0:T(2,128)S(1)} %bitcast_add_fusion.11), channel_id=1, source_target_pairs={{4,0},{8,4},{12,8},{5,1},{9,5},{13,9},{6,2},{10,6},{14,10},{7,3},{... | collective-permute-start | bytes 147464 | tf_op jit(solution)/shard_map/while/body/eval_jaxpr/ppermute | solution.py:28
  161.2 6.5 %collective-permute-start.3 = (f32[12,2,512]{2,1,0:T(2,128)S(1)}, f32[12,2,512]{2,1,0:T(2,128)S(1)}, u32[]{:S(2)}, u32[]{:S(2)}) collective-permute-start(f32[12,2,512]{2,1,0:T(2,128)S(1)} %bitcast_add_fusion.11), channel_id=1, source_target_pairs={{4,0},{8,4},{12,8},{5,1},{9,5},{13,9},{6,2},{10,6},{14,10},{7,3},{... | collective-permute-start | bytes 147464 | tf_op jit(solution)/shard_map/while/body/eval_jaxpr/ppermute | solution.py:28
  168.0 6.0 %collective-permute-start.3 = (f32[12,2,512]{2,1,0:T(2,128)S(1)}, f32[12,2,512]{2,1,0:T(2,128)S(1)}, u32[]{:S(2)}, u32[]{:S(2)}) collective-permute-start(f32[12,2,512]{2,1,0:T(2,128)S(1)} %bitcast_add_fusion.11), channel_id=1, source_target_pairs={{4,0},{8,4},{12,8},{5,1},{9,5},{13,9},{6,2},{10,6},{14,10},{7,3},{... | collective-permute-start | bytes 147464 | tf_op jit(solution)/shard_map/while/body/eval_jaxpr/ppermute | solution.py:28
  178.2 1.3 copy-start.7

commit v2 on v1

--- a/solution.py
+++ b/solution.py
@@ -162,6 +162,37 @@
 
 def carry_through(vector, matrix, offset):
     return jnp.einsum("kcl,kmcl->mcl", vector, matrix, precision=lax.Precision.HIGHEST) + offset
+
+
+def compose(first, then):
+    return jnp.sum(first[:, :, None] * then[None], axis=1)
+
+
+def chain_products(matrix, steps):
+    count = lax.axis_size("gx")
+    products = []
+    reach = matrix
+    for s in range(1, count - 1):
+        arrived = from_behind(reach, "gx", steps)
+        products.append(arrived)
+        if s < count - 2:
+            reach = compose(arrived, matrix)
+    return products
+
+
+def gathered_carry(vector, products, steps):
+    count = lax.axis_size("gx")
+    here = lax.axis_index("gx")
+    offsets = lax.all_gather(vector, "gx")
+    total = jnp.zeros_like(vector)
+    for s in range(count - 1):
+        source = here - steps * (s + 1)
+        valid = jnp.logical_and(source >= 0, source < count)
+        term = lax.dynamic_index_in_dim(offsets, jnp.clip(source, 0, count - 1), 0, keepdims=False)
+        if s > 0:
+            term = jnp.sum(term[:, None] * products[s - 1], axis=0)
+        total = total + jnp.where(valid, term, 0.0)
+    return total
 
 
 def on_device(
@@ -189,6 +220,8 @@
     matrix = as_matrix(response)
     (response,) = lower_pallas(None, inverse_diag, near_lower, far_lower, units, False)
     reverse_matrix = as_matrix(response)
+    upper_products = chain_products(matrix, 1)
+    lower_products = chain_products(reverse_matrix, -1)
     psi = psi_old
     for step in range(ITERS):
         stream_pad = extended(psi, (("gx", 0),), 1)
@@ -203,24 +236,12 @@
         ).reshape(rhs.shape)
         yres = jnp.sum(y_inverse * zres[..., :, None, :], axis=-3)
         _, offset = upper_pallas(yres, near_t, far_t, zeros, True)
-        vector = as_vector(offset[:, 0])
-
-        def upper_reversal(turn, incoming):
-            return from_behind(carry_through(incoming, matrix, vector), "gx", 1)
-
-        entering = lax.fori_loop(0, lax.axis_size("gx") - 1, upper_reversal, jnp.zeros_like(vector))
+        entering = gathered_carry(as_vector(offset[:, 0]), upper_products, 1)
         upper, _ = upper_pallas(
             yres, near_t, far_t, from_vector(entering, carry_shape[1])[:, None], True
         )
         _, offset = lower_pallas(upper, inverse_diag, near_lower, far_lower, zeros, True)
-        vector_back = as_vector(offset[:, 0])
-
-        def lower_turn(turn, incoming):
-            return from_behind(carry_through(incoming, reverse_matrix, vector_back), "gx", -1)
-
-        entering = lax.fori_loop(
-            0, lax.axis_size("gx") - 1, lower_turn, jnp.zeros_like(vector_back)
-        )
+        entering = gathered_carry(as_vector(offset[:, 0]), lower_products, -1)
         lower, _ = lower_pallas(
             upper,
             inverse_diag,

time: 191 us -> 201 us (1.052)
  blocking collectives: 9.19 us -> 66.9 us
  waiting for transfers between devices: 41 us -> 4.94 us
  starting transfers between devices: 54.7 us -> 29.6 us
  other arithmetic: 8.34 us -> 19.2 us
  local copies, waits for them, and re-layouts: 28.1 us -> 31.2 us
    all_gather x0 -> x4, blocking collectives: none -> 57.7 us  [gathered_carry(): offsets = lax.all_gather(vector, 'gx')]
    ppermute x12 -> x4, waiting for transfers between devices: 39.7 us -> 3.57 us  [from_behind(): lax.ppermute(value, axis, [(source, source + steps) for source in range(f...]
    ppermute x12 -> x4, starting transfers between devices: 33.2 us -> 8.26 us  [from_behind(): lax.ppermute(value, axis, [(source, source + steps) for source in range(f...]
    reduce_sum x0 -> x10, other arithmetic: none -> 11.8 us  [the longest x2 9.76 us: compose(): return jnp.sum(first[:, :, None] * then[None], axis=1)]
    dot_general x12 -> x0, other arithmetic: 3.02 us -> none  [carry_through(): jnp.einsum('kcl,kmcl->mcl', vector, matrix, precision=lax.Precision.HIGHEST)]
    broadcast_in_dim x0 -> x4, other arithmetic: none -> 2.65 us  [on_device(): from_vector(entering, carry_shape[1])[:, None]]
    reshape x4 -> x0, local copies, waits for them, and re-layouts: 2.55 us -> none  [from_vector(): vector.reshape(2, count, vector.shape[1], vector.shape[2])]
    unnamed x26 -> x32, local copies, waits for them, and re-layouts: 6.36 us -> 7.2 us
  transfers between devices with their start and end apart: 20 -> 12, of which waited for: 13 -> 2; matrix products, arithmetic and copies ran while one was open for 7% -> 17% of each run, Pallas kernels for 8% -> 13%
where the time goes in v2:
time: 201 us; the launch traced here: 200 us
  blocking collectives  66.9 us (33%)
  Pallas kernels  42.3 us (21%)
  local copies, waits for them, and re-layouts  31.2 us (16%)
  starting transfers between devices  29.6 us (15%)
  other arithmetic  19.2 us (10%)
  waiting for transfers between devices  4.94 us (2%)
  matrix products  4.53 us (2%)
    all_gather x4, blocking collectives, gathered_carry(): offsets = lax.all_gather(vector, 'gx')  57.7 us
    pallas_call x5, Pallas kernels, lower_pallas(): pl.pallas_call(kernel, out_shape=tuple(out_shape), in_specs=_vmem_specs(l...  22.9 us
    pallas_call x5, Pallas kernels, upper_pallas(): pl.pallas_call(kernel, out_shape=tuple(out_shape), in_specs=_vmem_specs(l...  19.5 us
    ppermute x4, starting transfers between devices, extended(): before = lax.ppermute(last, axis, up)  16.2 us
    reduce_sum x2, other arithmetic, compose(): return jnp.sum(first[:, :, None] * then[None], axis=1)  9.76 us
    psum x1, blocking collectives, on_device(): mesh_sens = lax.psum(local_sens, 'cond')  9.19 us
    ppermute x4, starting transfers between devices, from_behind(): lax.ppermute(value, axis, [(source, source + steps) for source in range(f...  8.26 us
    unnamed x32, local copies, waits for them, and re-layouts  7.2 us
  transfers between devices with their start and end apart: 12, of which 2 were waited for; matrix products, arithmetic and copies ran while one was open for 17% of the time, Pallas kernels for 13%

profile of v2, /device:TPU:0, one launch (start us, length us, event | category | flops | bytes accessed | tf_op | source)
XLA Modules:
  0.0 199.9 jit_solution(4407830636772119424)
XLA Ops:
  0.6 1.0 copy.192
  1.8 1.3 collective-permute-start.2
  3.0 3.0 %collective-permute-start.3 = (f32[8,2,6,32]{3,2,1,0:T(8,128)S(1)}, f32[8,2,6,32]{3,2,1,0:T(8,128)S(1)}, u32[]{:S(2)}, u32[]{:S(2)}) collective-permute-start(f32[8,2,6,32]{3,2,1,0:T(8,128)S(1)} %get-tuple-element.35), channel_id=1, source_target_pairs={{0,1},{1,2},{2,3},{4,5},{5,6},{6,7},{8,9},{9,10},{10,11},{12,13},{... | collective-permute-start | bytes 36872 | tf_op jit(solution)/shard_map/ppermute | solution.py:19
  6.1 1.3 collective-permute-start
  7.4 5.6 %collective-permute-start.1 = (f32[1,2,6,512]{3,2,1,0:T(8,128)S(1)}, f32[1,2,6,512]{3,2,1,0:T(8,128)S(1)}, u32[]{:S(2)}, u32[]{:S(2)}) collective-permute-start(f32[1,2,6,512]{3,2,1,0:T(8,128)S(1)} %get-tuple-element.33), channel_id=1, source_target_pairs={{0,4},{4,8},{8,12},{1,5},{5,9},{9,13},{2,6},{6,10},{10,14},{3,7},{... | collective-permute-start | bytes 73736 | tf_op jit(solution)/shard_map/ppermute | solution.py:19
  13.0 4.0 %copy_bitcast_fusion = (f32[8,2,6,6,512]{4,3,2,1,0:T(8,128)}, f32[8,2,6,6,512]{4,3,2,1,0:T(8,128)}) fusion(f32[8,2,6,6,512]{4,1,3,2,0:T(2,128)} %param.16, f32[8,2,6,6,512]{4,1,3,2,0:T(2,128)} %param.15), kind=kLoop, calls=%fused_computation.2 | loop fusion | bytes 4718592 | tf_op jit(solution)/shard_map/transpose | solution.py:218
  17.1 1.1 broadcast_in_dim.57.refs_2_.refs_3_
  18.1 7.1 %shard_map.141 = f32[2,12,2,6,512]{4,3,2,1,0:T(8,128)} custom-call(f32[8,2,6,6,512]{4,3,2,1,0:T(8,128)} %get-tuple-element.49.refs_1_.refs_0_, f32[8,2,6,6,512]{4,3,2,1,0:T(8,128)} %get-tuple-element.48.refs_2_.refs_1_, f32[2,12,2,6,512]{4,3,2,1,0:T(8,128)} %broadcast_in_dim.57.refs_2_.refs_3_), custom_call_target="tpu_custom_call" | custom-call | tf_op jit(solution)/shard_map/pallas_call | solution.py:84
  25.2 2.6 %copy.173 = f32[12,2,6,2,512]{4,3,2,1,0:T(2,128)} copy(f32[12,2,6,2,512]{4,2,3,0,1:T(8,128)} %bitcast.105) | data formatting | bytes 1179648 | tf_op jit(solution)/shard_map/transpose | solution.py:150
  27.7 3.9 %collective-permute-start.4 = (f32[12,12,2,512]{3,2,1,0:T(2,128)}, f32[12,12,2,512]{3,2,1,0:T(2,128)S(1)}, u32[]{:S(2)}, u32[]{:S(2)}) collective-permute-start(f32[12,12,2,512]{3,2,1,0:T(2,128)} %bitcast.13), channel_id=1, source_target_pairs={{0,4},{4,8},{8,12},{1,5},{5,9},{9,13},{2,6},{6,10},{10,14},{3,7},{... | collective-permute-start | bytes 1769480 | tf_op jit(solution)/shard_map/ppermute | solution.py:28
  31.8 1.4 copy.189.refs_1_.refs_0_
  33.2 1.4 copy.190.refs_2_.refs_1_
  34.6 1.4 copy.191.refs_3_.refs_2_
  36.1 8.3 %shard_map.144 = f32[2,12,2,6,512]{4,3,2,1,0:T(8,128)} custom-call(f32[8,2,6,6,512]{4,3,2,1,0:T(8,128)} %copy.189.refs_1_.refs_0_, f32[8,2,6,6,512]{4,3,2,1,0:T(8,128)} %copy.190.refs_2_.refs_1_, f32[8,2,6,6,512]{4,3,2,1,0:T(8,128)} %copy.191.refs_3_.refs_2_, f32[2,12,2,6,512]{4,3,2,1,0:T(8,128)} %broadcast_in_dim.57.refs_2_.refs_3_), custom_call_target="tpu_custom_call" | custom-call | tf_op jit(solution)/shard_map/pallas_call | solution.py:134
  44.4 2.5 %copy.185 = f32[12,2,6,2,512]{4,3,2,1,0:T(2,128)} copy(f32[12,2,6,2,512]{4,2,3,0,1:T(8,128)} %bitcast.104) | data formatting | bytes 1179648 | tf_op jit(solution)/shard_map/transpose | solution.py:150
  46.9 1.3 collective-permute-start.6
  48.8 1.7 convolution_bitcast_fusion.1
  50.5 1.4 mul.176
  52.1 0.6 multiply_reduce_fusion.3
  52.7 0.8 copy.177.refs_0_
  53.5 0.6 broadcast_in_dim.55.refs_3_.refs_4_
  54.1 3.1 %shard_map.140 = (f32[8,2,6,512]{3,2,1,0:T(8,128)}, f32[2,1,2,6,512]{4,3,2,1,0:T(8,128)}) custom-call(f32[8,2,6,512]{3,2,1,0:T(8,128)} %copy.177.refs_0_, f32[8,2,6,6,512]{4,3,2,1,0:T(8,128)} %get-tuple-element.49.refs_1_.refs_0_, f32[8,2,6,6,512]{4,3,2,1,0:T(8,128)} %get-tuple-element.48.refs_2_.refs_1_, f32[2,1,2,6,512]{4,3,2,1,0:T(8,128)} %broadcast_in_dim.55.refs_3_.refs_4_), custom_call_target="tpu_custom_call" | custom-call | tf_op jit(solution)/shard_map/pallas_call | solution.py:84
  57.2 0.9 copy.172
  58.1 15.2 %all_gather.12 = f32[4,12,2,512]{3,2,1,0:T(2,128)S(1)} all-gather(f32[1,12,2,512]{3,2,1,0:T(2,128)S(1)} %bitcast.111), channel_id=1, replica_groups=mesh['cond'=2,'gx'=4,'gy'=4] {'gx'}, dimensions={0}, use_global_device_ids=true | all-gather | bytes 245760 | tf_op jit(solution)/shard_map/all_gather | solution.py:186
  73.4 4.5 %multiply_reduce_fusion.1 = f32[12,12,2,512]{3,2,1,0:T(2,128)S(1)} fusion(f32[12,12,2,512]{3,2,1,0:T(2,128)} %bitcast.13, f32[12,12,2,512]{3,2,1,0:T(2,128)S(1)} %collective-permute-done.4), kind=kLoop, calls=%fused_computation.1 | loop fusion | flops 3391488 | bytes 1769472 | tf_op jit(solution)/shard_map/reduce_sum | solution.py:168
  77.8 1.8 collective-permute-start.5
  79.6 5.3 %multiply_reduce_fusion = f32[12,12,2,512]{3,2,1,0:T(2,128)} fusion(f32[12,12,2,512]{3,2,1,0:T(2,128)} %bitcast.25, f32[12,12,2,512]{3,2,1,0:T(2,128)S(1)} %collective-permute-done.6), kind=kLoop, calls=%fused_computation | loop fusion | flops 3391488 | bytes 1769472 | tf_op jit(solution)/shard_map/reduce_sum | solution.py:168
  84.9 1.3 collective-permute-start.7
  86.5 3.6 %collective-permute-done.5 = f32[12,12,2,512]{3,2,1,0:T(2,128)S(1)} collective-permute-done((f32[12,12,2,512]{3,2,1,0:T(2,128)S(1)}, f32[12,12,2,512]{3,2,1,0:T(2,128)S(1)}, u32[]{:S(2)}, u32[]{:S(2)}) %collective-permute-start.5) | collective-permute-done | bytes 589856 | tf_op jit(solution)/shard_map/ppermute | solution.py:28
  90.1 0.9 copy-done.2
  91.2 0.7 fusion.15.refs_3_
  91.9 3.1 %shard_map.142 = (f32[8,2,6,512]{3,2,1,0:T(8,128)}, f32[2,1,2,6,512]{4,3,2,1,0:T(8,128)}) custom-call(f32[8,2,6,512]{3,2,1,0:T(8,128)} %copy.177.refs_0_, f32[8,2,6,6,512]{4,3,2,1,0:T(8,128)} %get-tuple-element.49.refs_1_.refs_0_, f32[8,2,6,6,512]{4,3,2,1,0:T(8,128)} %get-tuple-element.48.refs_2_.refs_1_, f32[2,1,2,6,512]{4,3,2,1,0:T(8,128)} %fusion.15.refs_3_), custom_call_target="tpu_custom_call" | custom-call | tf_op jit(solution)/shard_map/pallas_call | solution.py:84
  95.0 3.6 %shard_map.143 = (f32[8,2,6,512]{3,2,1,0:T(8,128)}, f32[2,1,2,6,512]{4,3,2,1,0:T(8,128)}) custom-call(f32[8,2,6,512]{3,2,1,0:T(8,128)} %get-tuple-element.11.refs_0_, f32[8,2,6,6,512]{4,3,2,1,0:T(8,128)} %copy.189.refs_1_.refs_0_, f32[8,2,6,6,512]{4,3,2,1,0:T(8,128)} %copy.190.refs_2_.refs_1_, f32[8,2,6,6,512]{4,3,2,1,0:T(8,128)} %copy.191.refs_3_.refs_2_, ...), custom_call_target="tpu_custom_call" | custom-call | tf_op jit(solution)/shard_map/pallas_call | solution.py:134
  98.6 0.9 copy.181
  99.5 14.6 %all_gather.13 = f32[4,12,2,512]{3,2,1,0:T(2,128)S(1)} all-gather(f32[1,12,2,512]{3,2,1,0:T(2,128)S(1)} %bitcast.112), channel_id=1, replica_groups=mesh['cond'=2,'gx'=4,'gy'=4] {'gx'}, dimensions={0}, use_global_device_ids=true | all-gather | bytes 245760 | tf_op jit(solution)/shard_map/all_gather | solution.py:186
  114.8 0.7 fusion.14.refs_4_
  115.4 3.7 %shard_map.145 = (f32[8,2,6,512]{3,2,1,0:T(8,128)}, f32[2,1,2,6,512]{4,3,2,1,0:T(8,128)}) custom-call(f32[8,2,6,512]{3,2,1,0:T(8,128)} %get-tuple-element.11.refs_0_, f32[8,2,6,6,512]{4,3,2,1,0:T(8,128)} %copy.189.refs_1_.refs_0_, f32[8,2,6,6,512]{4,3,2,1,0:T(8,128)} %copy.190.refs_2_.refs_1_, f32[8,2,6,6,512]{4,3,2,1,0:T(8,128)} %copy.191.refs_3_.refs_2_, ...), custom_call_target="tpu_custom_call" | custom-call | tf_op jit(solution)/shard_map/pallas_call | solution.py:134
  119.1 1.1 add_multiply_fusion.1
  120.3 1.3 collective-permute-start.10
  121.6 3.0 %collective-permute-start.11 = (f32[8,2,6,32]{3,2,1,0:T(8,128)S(1)}, f32[8,2,6,32]{3,2,1,0:T(8,128)S(1)}, u32[]{:S(2)}, u32[]{:S(2)}) collective-permute-start(f32[8,2,6,32]{3,2,1,0:T(8,128)S(1)} %get-tuple-element.31), channel_id=1, source_target_pairs={{0,1},{1,2},{2,3},{4,5},{5,6},{6,7},{8,9},{9,10},{10,11},{12,13},{... | collective-permute-start | bytes 36872 | tf_op jit(solution)/shard_map/ppermute | solution.py:19
  124.7 1.3 collective-permute-start.8
  126.0 4.5 %collective-permute-start.9 = (f32[1,2,6,512]{3,2,1,0:T(8,128)S(1)}, f32[1,2,6,512]{3,2,1,0:T(8,128)S(1)}, u32[]{:S(2)}, u32[]{:S(2)}) collective-permute-start(f32[1,2,6,512]{3,2,1,0:T(8,128)S(1)} %get-tuple-element.29), channel_id=1, source_target_pairs={{0,4},{4,8},{8,12},{1,5},{5,9},{9,13},{2,6},{6,10},{10,14},{3,7},{... | collective-permute-start | bytes 73736 | tf_op jit(solution)/shard_map/ppermute | solution.py:19
  130.8 1.4 collective-permute-done.9
  132.3 0.8 copy.194
  133.1 2.1 %reshape.109 = f32[8,2,6,16,32]{4,3,0,2,1:T(8,128)} reshape(f32[8,2,6,512]{3,0,2,1:T(8,128)} %copy.194) | data formatting | bytes 393216 | tf_op jit(solution)/shard_map/reshape | solution.py:233
  135.2 2.8 %convolution_bitcast_fusion = f32[8,2,6,16,32]{4,3,0,2,1:T(8,128)} fusion(f32[8,2,6,16,32]{4,3,0,2,1:T(8,128)} %reshape.109, f32[2,6,32,32]{3,2,1,0:T(8,128)S(1)} %copy-done), kind=kOutput, calls=%fused_computation.4 | convolution fusion | flops 18874368 | bytes 442368 | tf_op jit(solution)/shard_map/icvjq,cvqk->icvjk/dot_general | solution.py:234
  138.0 2.1 %mul.202 = f32[8,2,6,512]{3,0,2,1:T(8,128)} reshape(f32[8,2,6,16,32]{4,3,0,2,1:T(8,128)} %convolution_bitcast_fusion) | data formatting | bytes 393216 | tf_op jit(solution)/shard_map/mul | solution.py:237
  140.1 1.1 copy.195
  141.2 0.6 multiply_reduce_fusion.2
  141.8 0.8 copy.201.refs_0_
  142.6 3.1 %shard_map.146 = (f32[8,2,6,512]{3,2,1,0:T(8,128)}, f32[2,1,2,6,512]{4,3,2,1,0:T(8,128)}) custom-call(f32[8,2,6,512]{3,2,1,0:T(8,128)} %copy.201.refs_0_, f32[8,2,6,6,512]{4,3,2,1,0:T(8,128)} %get-tuple-element.49.refs_1_.refs_0_, f32[8,2,6,6,512]{4,3,2,1,0:T(8,128)} %get-tuple-element.48.refs_2_.refs_1_, f32[2,1,2,6,512]{4,3,2,1,0:T(8,128)} %broadcast_in_dim.55.refs_3_.refs_4_), custom_call_target="tpu_custom_call" | custom-call | tf_op jit(solution)/shard_map/pallas_call | solution.py:84
  145.7 0.9 copy.197
  146.6 14.1 %all_gather.14 = f32[4,12,2,512]{3,2,1,0:T(2,128)S(1)} all-gather(f32[1,12,2,512]{3,2,1,0:T(2,128)S(1)} %bitcast.113), channel_id=1, replica_groups=mesh['cond'=2,'gx'=4,'gy'=4] {'gx'}, dimensions={0}, use_global_device_ids=true | all-gather | bytes 245760 | tf_op jit(solution)/shard_map/all_gather | solution.py:186
  161.3 0.7 fusion.13.refs_3_
  162.0 3.1 %shard_map.147 = (f32[8,2,6,512]{3,2,1,0:T(8,128)}, f32[2,1,2,6,512]{4,3,2,1,0:T(8,128)}) custom-call(f32[8,2,6,512]{3,2,1,0:T(8,128)} %copy.201.refs_0_, f32[8,2,6,6,512]{4,3,2,1,0:T(8,128)} %get-tuple-element.49.refs_1_.refs_0_, f32[8,2,6,6,512]{4,3,2,1,0:T(8,128)} %get-tuple-element.48.refs_2_.refs_1_, f32[2,1,2,6,512]{4,3,2,1,0:T(8,128)} %fusion.13.refs_3_), custom_call_target="tpu_custom_call" | custom-call | tf_op jit(solution)/shard_map/pallas_call | solution.py:84
  165.0 3.6 %shard_map.148 = (f32[8,2,6,512]{3,2,1,0:T(8,128)}, f32[2,1,2,6,512]{4,3,2,1,0:T(8,128)}) custom-call(f32[8,2,6,512]{3,2,1,0:T(8,128)} %get-tuple-element.15.refs_0_, f32[8,2,6,6,512]{4,3,2,1,0:T(8,128)} %copy.189.refs_1_.refs_0_, f32[8,2,6,6,512]{4,3,2,1,0:T(8,128)} %copy.190.refs_2_.refs_1_, f32[8,2,6,6,512]{4,3,2,1,0:T(8,128)} %copy.191.refs_3_.refs_2_, ...), custom_call_target="tpu_custom_call" | custom-call | tf_op jit(solution)/shard_map/pallas_call | solution.py:134
  168.7 0.9 copy.205
  169.6 13.8 %all_gather.15 = f32[4,12,2,512]{3,2,1,0:T(2,128)S(1)} all-gather(f32[1,12,2,512]{3,2,1,0:T(2,128)S(1)} %bitcast.114), channel_id=1, replica_groups=mesh['cond'=2,'gx'=4,'gy'=4] {'gx'}, dimensions={0}, use_global_device_ids=true | all-gather | bytes 245760 | tf_op jit(solution)/shard_map/all_gather | solution.py:186
  184.0 0.7 fusion.12.refs_4_
  184.6 3.6 %shard_map.149 = (f32[8,2,6,512]{3,2,1,0:T(8,128)}, f32[2,1,2,6,512]{4,3,2,1,0:T(8,128)}) custom-call(f32[8,2,6,512]{3,2,1,0:T(8,128)} %get-tuple-element.15.refs_0_, f32[8,2,6,6,512]{4,3,2,1,0:T(8,128)} %copy.189.refs_1_.refs_0_, f32[8,2,6,6,512]{4,3,2,1,0:T(8,128)} %copy.190.refs_2_.refs_1_, f32[8,2,6,6,512]{4,3,2,1,0:T(8,128)} %copy.191.refs_3_.refs_2_, ...), custom_call_target="tpu_custom_call" | custom-call | tf_op jit(solution)/shard_map/pallas_call | solution.py:134
  188.3 1.1 multiply_bitcast_fusion
  189.5 0.3 multiply_reduce_fusion.4
  189.9 9.2 %psum.7 = f32[8,3,512]{2,0,1:T(8,128)} all-reduce(f32[8,3,512]{2,0,1:T(8,128)S(1)} %bitcast.106), channel_id=1, replica_groups=mesh['cond'=2,'gx'=4,'gy'=4] {'cond'}, use_global_device_ids=true, to_apply=%region_13.14 | all-reduce | flops 12288 | bytes 98304 | tf_op jit(solution)/shard_map/psum | solution.py:262
  199.1 0.8 copy.212
  (70 shorter events, 3.9 us)
Async XLA Ops:
  0.6 48.2 %copy-start = (f32[2,6,32,32]{3,2,1,0:T(8,128)S(1)}, f32[2,6,32,32]{3,2,1,0:T(8,128)}, u32[]{:S(2)}) copy-start(f32[2,6,32,32]{3,2,1,0:T(8,128)} %param.21) | copy-start | bytes 147460
  1.8 45.1 %collective-permute-start.2 = (f32[8,2,6,32]{3,2,1,0:T(8,128)S(1)}, f32[8,2,6,32]{3,2,1,0:T(8,128)S(1)}, u32[]{:S(2)}, u32[]{:S(2)}) collective-permute-start(f32[8,2,6,32]{3,2,1,0:T(8,128)S(1)} %get-tuple-element.34), channel_id=1, source_target_pairs={{1,0},{2,1},{3,2},{5,4},{6,5},{7,6},{9,8},{10,9},{11,10},{13,12},{... | collective-permute-start | bytes 36872 | tf_op jit(solution)/shard_map/ppermute | solution.py:20
  3.0 45.1 %collective-permute-start.3 = (f32[8,2,6,32]{3,2,1,0:T(8,128)S(1)}, f32[8,2,6,32]{3,2,1,0:T(8,128)S(1)}, u32[]{:S(2)}, u32[]{:S(2)}) collective-permute-start(f32[8,2,6,32]{3,2,1,0:T(8,128)S(1)} %get-tuple-element.35), channel_id=1, source_target_pairs={{0,1},{1,2},{2,3},{4,5},{5,6},{6,7},{8,9},{9,10},{10,11},{12,13},{... | collective-permute-start | bytes 36872 | tf_op jit(solution)/shard_map/ppermute | solution.py:19
  6.1 42.1 %collective-permute-start = (f32[1,2,6,512]{3,2,1,0:T(8,128)S(1)}, f32[1,2,6,512]{3,2,1,0:T(8,128)S(1)}, u32[]{:S(2)}, u32[]{:S(2)}) collective-permute-start(f32[1,2,6,512]{3,2,1,0:T(8,128)S(1)} %get-tuple-element.32), channel_id=1, source_target_pairs={{4,0},{8,4},{12,8},{5,1},{9,5},{13,9},{6,2},{10,6},{14,10},{7,3},{... | collective-permute-start | bytes 73736 | tf_op jit(solution)/shard_map/ppermute | solution.py:20
  7.4 40.8 %collective-permute-start.1 = (f32[1,2,6,512]{3,2,1,0:T(8,128)S(1)}, f32[1,2,6,512]{3,2,1,0:T(8,128)S(1)}, u32[]{:S(2)}, u32[]{:S(2)}) collective-permute-start(f32[1,2,6,512]{3,2,1,0:T(8,128)S(1)} %get-tuple-element.33), channel_id=1, source_target_pairs={{0,4},{4,8},{8,12},{1,5},{5,9},{9,13},{2,6},{6,10},{10,14},{3,7},{... | collective-permute-start | bytes 73736 | tf_op jit(solution)/shard_map/ppermute | solution.py:19
  25.2 6.5 %copy-start.10 = (s32[8,512]{1,0:T(8,128)S(1)}, s32[8,512]{1,0:T(8,128)}, u32[]{:S(2)}) copy-start(s32[8,512]{1,0:T(8,128)} %param.23) | copy-start | bytes 49156
  25.2 6.6 %copy-start.4 = (f32[8,2,6,6,512]{4,1,3,2,0:T(2,128)S(1)}, f32[8,2,6,6,512]{4,1,3,2,0:T(2,128)}, u32[]{:S(2)}) copy-start(f32[8,2,6,6,512]{4,1,3,2,0:T(2,128)} %param.17) | copy-start | bytes 3538948
  27.7 45.6 %collective-permute-start.4 = (f32[12,12,2,512]{3,2,1,0:T(2,128)}, f32[12,12,2,512]{3,2,1,0:T(2,128)S(1)}, u32[]{:S(2)}, u32[]{:S(2)}) collective-permute-start(f32[12,12,2,512]{3,2,1,0:T(2,128)} %bitcast.13), channel_id=1, source_target_pairs={{0,4},{4,8},{8,12},{1,5},{5,9},{9,13},{2,6},{6,10},{10,14},{3,7},{... | collective-permute-start | bytes 1769480 | tf_op jit(solution)/shard_map/ppermute | solution.py:28
  31.8 1.4 copy-start.5
  33.2 1.4 copy-start.6
  44.4 3.8 %copy-start.7 = (f32[8,2,6,512]{3,1,2,0:T(2,128)S(1)}, f32[8,2,6,512]{3,1,2,0:T(2,128)}, u32[]{:S(2)}) copy-start(f32[8,2,6,512]{3,1,2,0:T(2,128)} %param.14) | copy-start | bytes 589828
  46.9 32.7 %collective-permute-start.6 = (f32[12,12,2,512]{3,2,1,0:T(2,128)}, f32[12,12,2,512]{3,2,1,0:T(2,128)S(1)}, u32[]{:S(2)}, u32[]{:S(2)}) collective-permute-start(f32[12,12,2,512]{3,2,1,0:T(2,128)} %bitcast.25), channel_id=1, source_target_pairs={{4,0},{8,4},{12,8},{5,1},{9,5},{13,9},{6,2},{10,6},{14,10},{7,3},{... | collective-permute-start | bytes 1769480 | tf_op jit(solution)/shard_map/ppermute | solution.py:28
  48.8 3.3 %copy-start.1 = (f32[8,2,6,6,512]{4,1,3,2,0:T(2,128)S(1)}, f32[8,2,6,6,512]{4,1,3,2,0:T(2,128)}, u32[]{:S(2)}) copy-start(f32[8,2,6,6,512]{4,1,3,2,0:T(2,128)} %param.20) | copy-start | bytes 3538948
  77.8 12.2 %collective-permute-start.5 = (f32[12,12,2,512]{3,2,1,0:T(2,128)S(1)}, f32[12,12,2,512]{3,2,1,0:T(2,128)S(1)}, u32[]{:S(2)}, u32[]{:S(2)}) collective-permute-start(f32[12,12,2,512]{3,2,1,0:T(2,128)S(1)} %multiply_reduce_fusion.1), channel_id=1, source_target_pairs={{0,4},{4,8},{8,12},{1,5},{5,9},{9,13},{2,6},{6,10},{10,14},{3,7},{... | collective-permute-start | bytes 1769480 | tf_op jit(solution)/shard_map/ppermute | solution.py:28
  84.9 29.6 %collective-permute-start.7 = (f32[12,12,2,512]{3,2,1,0:T(2,128)}, f32[12,12,2,512]{3,2,1,0:T(2,128)S(1)}, u32[]{:S(2)}, u32[]{:S(2)}) collective-permute-start(f32[12,12,2,512]{3,2,1,0:T(2,128)} %multiply_reduce_fusion), channel_id=1, source_target_pairs={{4,0},{8,4},{12,8},{5,1},{9,5},{13,9},{6,2},{10,6},{14,10},{7,3},{... | collective-permute-start | bytes 1769480 | tf_op jit(solution)/shard_map/ppermute | solution.py:28
  90.1 0.9 copy-start.2
  115.4 15.1 %copy-start.11 = (f32[8]{0:T(128)S(1)}, f32[8]{0:T(128)}, u32[]{:S(2)}) copy-start(f32[8]{0:T(128)} %param.25) | copy-start | bytes 100
  115.4 15.1 %copy-start.12 = (s32[2]{0:T(128)S(1)}, s32[2]{0:T(128)}, u32[]{:S(2)}) copy-start(s32[2]{0:T(128)} %param.24) | copy-start | bytes 28
  119.1 13.0 %copy-start.8 = (f32[8,2,6,512]{3,1,2,0:T(2,128)S(1)}, f32[8,2,6,512]{3,1,2,0:T(2,128)}, u32[]{:S(2)}) copy-start(f32[8,2,6,512]{3,1,2,0:T(2,128)} %param.14) | copy-start | bytes 589828
  120.3 10.4 %collective-permute-start.10 = (f32[8,2,6,32]{3,2,1,0:T(8,128)S(1)}, f32[8,2,6,32]{3,2,1,0:T(8,128)S(1)}, u32[]{:S(2)}, u32[]{:S(2)}) collective-permute-start(f32[8,2,6,32]{3,2,1,0:T(8,128)S(1)} %get-tuple-element.30), channel_id=1, source_target_pairs={{1,0},{2,1},{3,2},{5,4},{6,5},{7,6},{9,8},{10,9},{11,10},{13,12},{... | collective-permute-start | bytes 36872 | tf_op jit(solution)/shard_map/ppermute | solution.py:20
  121.6 9.1 %collective-permute-start.11 = (f32[8,2,6,32]{3,2,1,0:T(8,128)S(1)}, f32[8,2,6,32]{3,2,1,0:T(8,128)S(1)}, u32[]{:S(2)}, u32[]{:S(2)}) collective-permute-start(f32[8,2,6,32]{3,2,1,0:T(8,128)S(1)} %get-tuple-element.31), channel_id=1, source_target_pairs={{0,1},{1,2},{2,3},{4,5},{5,6},{6,7},{8,9},{9,10},{10,11},{12,13},{... | collective-permute-start | bytes 36872 | tf_op jit(solution)/shard_map/ppermute | solution.py:19
  124.7 6.1 %collective-permute-start.8 = (f32[1,2,6,512]{3,2,1,0:T(8,128)S(1)}, f32[1,2,6,512]{3,2,1,0:T(8,128)S(1)}, u32[]{:S(2)}, u32[]{:S(2)}) collective-permute-start(f32[1,2,6,512]{3,2,1,0:T(8,128)S(1)} %get-tuple-element.28), channel_id=1, source_target_pairs={{4,0},{8,4},{12,8},{5,1},{9,5},{13,9},{6,2},{10,6},{14,10},{7,3},{... | collective-permute-start | bytes 73736 | tf_op jit(solution)/shard_map/ppermute | solution.py:20
  126.0 6.1 %collective-permute-start.9 = (f32[1,2,6,512]{3,2,1,0:T(8,128)S(1)}, f32[1,2,6,512]{3,2,1,0:T(8,128)S(1)}, u32[]{:S(2)}, u32[]{:S(2)}) collective-permute-start(f32[1,2,6,512]{3,2,1,0:T(8,128)S(1)} %get-tuple-element.29), channel_id=1, source_target_pairs={{0,4},{4,8},{8,12},{1,5},{5,9},{9,13},{2,6},{6,10},{10,14},{3,7},{... | collective-permute-start | bytes 73736 | tf_op jit(solution)/shard_map/ppermute | solution.py:19
  145.7 15.3 %copy-start.3 = (f32[12,12,2,512]{3,2,1,0:T(2,128)S(1)}, f32[12,12,2,512]{3,2,1,0:T(2,128)}, u32[]{:S(2)}) copy-start(f32[12,12,2,512]{3,2,1,0:T(2,128)} %copy-done.2) | copy-start | bytes 1769476
  188.3 1.3 copy-start.9

commit v3 on v1

--- a/solution.py
+++ b/solution.py
@@ -162,6 +162,23 @@
 
 def carry_through(vector, matrix, offset):
     return jnp.einsum("kcl,kmcl->mcl", vector, matrix, precision=lax.Precision.HIGHEST) + offset
+
+
+def shifted_operators(matrix, steps):
+    count = lax.axis_size("gx")
+    return [from_behind(matrix, "gx", steps * s) for s in range(1, count - 1)]
+
+
+def gathered_carry(vector, operators, steps):
+    count = lax.axis_size("gx")
+    if count == 1:
+        return jnp.zeros_like(vector)
+    total = from_behind(vector, "gx", steps * (count - 1))
+    for s in range(count - 2, 0, -1):
+        total = jnp.sum(total[:, None] * operators[s - 1], axis=0) + from_behind(
+            vector, "gx", steps * s
+        )
+    return total
 
 
 def on_device(
@@ -189,6 +206,8 @@
     matrix = as_matrix(response)
     (response,) = lower_pallas(None, inverse_diag, near_lower, far_lower, units, False)
     reverse_matrix = as_matrix(response)
+    upper_products = shifted_operators(matrix, 1)
+    lower_products = shifted_operators(reverse_matrix, -1)
     psi = psi_old
     for step in range(ITERS):
         stream_pad = extended(psi, (("gx", 0),), 1)
@@ -203,24 +222,12 @@
         ).reshape(rhs.shape)
         yres = jnp.sum(y_inverse * zres[..., :, None, :], axis=-3)
         _, offset = upper_pallas(yres, near_t, far_t, zeros, True)
-        vector = as_vector(offset[:, 0])
-
-        def upper_reversal(turn, incoming):
-            return from_behind(carry_through(incoming, matrix, vector), "gx", 1)
-
-        entering = lax.fori_loop(0, lax.axis_size("gx") - 1, upper_reversal, jnp.zeros_like(vector))
+        entering = gathered_carry(as_vector(offset[:, 0]), upper_products, 1)
         upper, _ = upper_pallas(
             yres, near_t, far_t, from_vector(entering, carry_shape[1])[:, None], True
         )
         _, offset = lower_pallas(upper, inverse_diag, near_lower, far_lower, zeros, True)
-        vector_back = as_vector(offset[:, 0])
-
-        def lower_turn(turn, incoming):
-            return from_behind(carry_through(incoming, reverse_matrix, vector_back), "gx", -1)
-
-        entering = lax.fori_loop(
-            0, lax.axis_size("gx") - 1, lower_turn, jnp.zeros_like(vector_back)
-        )
+        entering = gathered_carry(as_vector(offset[:, 0]), lower_products, -1)
         lower, _ = lower_pallas(
             upper,
             inverse_diag,

time: 191 us -> 173 us (0.906)
  waiting for transfers between devices: 41 us -> 26 us
  matrix products: 4.7 us -> 1.6 us
    ppermute x12 -> x16, waiting for transfers between devices: 39.7 us -> 25.3 us  [from_behind(): lax.ppermute(value, axis, [(source, source + steps) for source in range(f...]
    reduce_sum x0 -> x8, other arithmetic: none -> 4.19 us  [gathered_carry(): jnp.sum(total[:, None] * operators[s - 1], axis=0)]
    dot_general x2, matrix products: 4.7 us -> 1.6 us  [on_device(): jnp.einsum('icvjq,cvqk->icvjk', grid, z_inverse, precision=lax.Precision....]
    dot_general x12 -> x0, other arithmetic: 3.02 us -> none  [carry_through(): jnp.einsum('kcl,kmcl->mcl', vector, matrix, precision=lax.Precision.HIGHEST)]
    mul x4, local copies, waits for them, and re-layouts: 3.14 us -> 0.96 us  [on_device(): yres = jnp.sum(y_inverse * zres[..., :, None, :], axis=-3)]
    ppermute x12 -> x16, starting transfers between devices: 33.2 us -> 34 us  [from_behind(): lax.ppermute(value, axis, [(source, source + steps) for source in range(f...]
    unnamed x26 -> x42, local copies, waits for them, and re-layouts: 6.36 us -> 6.39 us
  transfers between devices with their start and end apart: 20 -> 24, of which waited for: 13 -> 8; matrix products, arithmetic and copies ran while one was open for 7% -> 15% of each run, Pallas kernels for 8% -> 15%
where the time goes in v3:
time: 173 us; the launch traced here: 172 us
  starting transfers between devices  55.5 us (32%)
  Pallas kernels  42.7 us (25%)
  local copies, waits for them, and re-layouts  26.5 us (15%)
  waiting for transfers between devices  26 us (15%)
  blocking collectives  9.19 us (5%)
  other arithmetic  8.72 us (5%)
    ppermute x16, starting transfers between devices, from_behind(): lax.ppermute(value, axis, [(source, source + steps) for source in range(f...  34 us
    ppermute x16, waiting for transfers between devices, from_behind(): lax.ppermute(value, axis, [(source, source + steps) for source in range(f...  25.3 us
    pallas_call x5, Pallas kernels, lower_pallas(): pl.pallas_call(kernel, out_shape=tuple(out_shape), in_specs=_vmem_specs(l...  23.1 us
    pallas_call x5, Pallas kernels, upper_pallas(): pl.pallas_call(kernel, out_shape=tuple(out_shape), in_specs=_vmem_specs(l...  19.6 us
    ppermute x4, starting transfers between devices, extended(): before = lax.ppermute(last, axis, up)  16.4 us
    psum x1, blocking collectives, on_device(): mesh_sens = lax.psum(local_sens, 'cond')  9.19 us
    unnamed x42, local copies, waits for them, and re-layouts  6.39 us
    ppermute x4, starting transfers between devices, extended(): after = lax.ppermute(first, axis, down)  5.15 us
  transfers between devices with their start and end apart: 24, of which 8 were waited for; matrix products, arithmetic and copies ran while one was open for 15% of the time, Pallas kernels for 15%

profile of v3, /device:TPU:0, one launch (start us, length us, event | category | flops | bytes accessed | tf_op | source)
XLA Modules:
  0.0 171.5 jit_solution(15528192496722780296)
XLA Ops:
  0.6 1.0 copy.172
  1.8 1.3 collective-permute-start.2
  3.0 3.0 %collective-permute-start.3 = (f32[8,2,6,32]{3,2,1,0:T(8,128)S(1)}, f32[8,2,6,32]{3,2,1,0:T(8,128)S(1)}, u32[]{:S(2)}, u32[]{:S(2)}) collective-permute-start(f32[8,2,6,32]{3,2,1,0:T(8,128)S(1)} %get-tuple-element.35), channel_id=1, source_target_pairs={{0,1},{1,2},{2,3},{4,5},{5,6},{6,7},{8,9},{9,10},{10,11},{12,13},{... | collective-permute-start | bytes 36872 | tf_op jit(solution)/shard_map/ppermute | solution.py:19
  6.1 1.3 collective-permute-start
  7.4 5.6 %collective-permute-start.1 = (f32[1,2,6,512]{3,2,1,0:T(8,128)S(1)}, f32[1,2,6,512]{3,2,1,0:T(8,128)S(1)}, u32[]{:S(2)}, u32[]{:S(2)}) collective-permute-start(f32[1,2,6,512]{3,2,1,0:T(8,128)S(1)} %get-tuple-element.33), channel_id=1, source_target_pairs={{0,4},{4,8},{8,12},{1,5},{5,9},{9,13},{2,6},{6,10},{10,14},{3,7},{... | collective-permute-start | bytes 73736 | tf_op jit(solution)/shard_map/ppermute | solution.py:19
  13.0 4.0 %copy_bitcast_fusion = (f32[8,2,6,6,512]{4,3,2,1,0:T(8,128)}, f32[8,2,6,6,512]{4,3,2,1,0:T(8,128)}) fusion(f32[8,2,6,6,512]{4,1,3,2,0:T(2,128)} %param.16, f32[8,2,6,6,512]{4,1,3,2,0:T(2,128)} %param.15), kind=kLoop, calls=%fused_computation | loop fusion | bytes 4718592 | tf_op jit(solution)/shard_map/transpose | solution.py:204
  17.0 1.1 broadcast_in_dim.15.refs_2_.refs_3_
  18.1 7.1 %shard_map.141 = f32[2,12,2,6,512]{4,3,2,1,0:T(8,128)} custom-call(f32[8,2,6,6,512]{4,3,2,1,0:T(8,128)} %get-tuple-element.37.refs_1_.refs_0_, f32[8,2,6,6,512]{4,3,2,1,0:T(8,128)} %get-tuple-element.36.refs_2_.refs_1_, f32[2,12,2,6,512]{4,3,2,1,0:T(8,128)} %broadcast_in_dim.15.refs_2_.refs_3_), custom_call_target="tpu_custom_call" | custom-call | tf_op jit(solution)/shard_map/pallas_call | solution.py:84
  25.2 2.5 %copy.157 = f32[12,2,6,2,512]{4,3,2,1,0:T(2,128)} copy(f32[12,2,6,2,512]{4,2,3,0,1:T(8,128)} %bitcast.85) | data formatting | bytes 1179648 | tf_op jit(solution)/shard_map/transpose | solution.py:150
  27.6 5.7 %collective-permute-start.5 = (f32[12,12,2,512]{3,2,1,0:T(2,128)}, f32[12,12,2,512]{3,2,1,0:T(2,128)}, u32[]{:S(2)}, u32[]{:S(2)}) collective-permute-start(f32[12,12,2,512]{3,2,1,0:T(2,128)} %bitcast.11), channel_id=1, source_target_pairs={{0,8},{4,12},{1,9},{5,13},{2,10},{6,14},{3,11},{7,15},{16,24},{20,... | collective-permute-start | bytes 1769480 | tf_op jit(solution)/shard_map/ppermute | solution.py:28
  33.4 1.3 collective-permute-start.7
  35.4 0.8 convolution_bitcast_fusion.1
  37.2 0.7 copy.159.refs_0_
  38.0 0.6 broadcast_in_dim.14.refs_3_.refs_4_
  38.6 3.2 %shard_map.140 = (f32[8,2,6,512]{3,2,1,0:T(8,128)}, f32[2,1,2,6,512]{4,3,2,1,0:T(8,128)}) custom-call(f32[8,2,6,512]{3,2,1,0:T(8,128)} %copy.159.refs_0_, f32[8,2,6,6,512]{4,3,2,1,0:T(8,128)} %get-tuple-element.37.refs_1_.refs_0_, f32[8,2,6,6,512]{4,3,2,1,0:T(8,128)} %get-tuple-element.36.refs_2_.refs_1_, f32[2,1,2,6,512]{4,3,2,1,0:T(8,128)} %broadcast_in_dim.14.refs_3_.refs_4_), custom_call_target="tpu_custom_call" | custom-call | tf_op jit(solution)/shard_map/pallas_call | solution.py:84
  41.8 0.9 copy.156
  42.7 1.4 collective-permute-start.4
  44.1 1.5 copy.169.refs_1_.refs_0_
  45.6 1.4 copy.170.refs_2_.refs_1_
  47.0 1.4 copy.171.refs_3_.refs_2_
  48.5 8.4 %shard_map.144 = f32[2,12,2,6,512]{4,3,2,1,0:T(8,128)} custom-call(f32[8,2,6,6,512]{4,3,2,1,0:T(8,128)} %copy.169.refs_1_.refs_0_, f32[8,2,6,6,512]{4,3,2,1,0:T(8,128)} %copy.170.refs_2_.refs_1_, f32[8,2,6,6,512]{4,3,2,1,0:T(8,128)} %copy.171.refs_3_.refs_2_, f32[2,12,2,6,512]{4,3,2,1,0:T(8,128)} %broadcast_in_dim.15.refs_2_.refs_3_), custom_call_target="tpu_custom_call" | custom-call | tf_op jit(solution)/shard_map/pallas_call | solution.py:134
  56.9 2.4 %copy.167 = f32[12,2,6,2,512]{4,3,2,1,0:T(2,128)} copy(f32[12,2,6,2,512]{4,2,3,0,1:T(8,128)} %bitcast.84) | data formatting | bytes 1179648 | tf_op jit(solution)/shard_map/transpose | solution.py:150
  59.3 1.3 collective-permute-start.10
  60.6 1.3 collective-permute-start.12
  61.9 6.1 %collective-permute-start.6 = (f32[12,2,512]{2,1,0:T(2,128)S(1)}, f32[12,2,512]{2,1,0:T(2,128)S(1)}, u32[]{:S(2)}, u32[]{:S(2)}) collective-permute-start(f32[12,2,512]{2,1,0:T(2,128)S(1)} %bitcast.100), channel_id=1, source_target_pairs={{0,8},{4,12},{1,9},{5,13},{2,10},{6,14},{3,11},{7,15},{16,24},{20,... | collective-permute-start | bytes 147464 | tf_op jit(solution)/shard_map/ppermute | solution.py:28
  68.0 4.0 %collective-permute-start.8 = (f32[12,2,512]{2,1,0:T(2,128)S(1)}, f32[12,2,512]{2,1,0:T(2,128)S(1)}, u32[]{:S(2)}, u32[]{:S(2)}) collective-permute-start(f32[12,2,512]{2,1,0:T(2,128)S(1)} %bitcast.101), channel_id=1, source_target_pairs={{0,4},{4,8},{8,12},{1,5},{5,9},{9,13},{2,6},{6,10},{10,14},{3,7},{... | collective-permute-start | bytes 147464 | tf_op jit(solution)/shard_map/ppermute | solution.py:28
  72.0 1.3 multiply_reduce_fusion.10
  74.4 3.1 %shard_map.142 = (f32[8,2,6,512]{3,2,1,0:T(8,128)}, f32[2,1,2,6,512]{4,3,2,1,0:T(8,128)}) custom-call(f32[8,2,6,512]{3,2,1,0:T(8,128)} %copy.159.refs_0_, f32[8,2,6,6,512]{4,3,2,1,0:T(8,128)} %get-tuple-element.37.refs_1_.refs_0_, f32[8,2,6,6,512]{4,3,2,1,0:T(8,128)} %get-tuple-element.36.refs_2_.refs_1_, f32[2,1,2,6,512]{4,3,2,1,0:T(8,128)} %bitcast.89), custom_call_target="tpu_custom_call" | custom-call | tf_op jit(solution)/shard_map/pallas_call | solution.py:84
  77.5 3.7 %shard_map.143 = (f32[8,2,6,512]{3,2,1,0:T(8,128)}, f32[2,1,2,6,512]{4,3,2,1,0:T(8,128)}) custom-call(f32[8,2,6,512]{3,2,1,0:T(8,128)} %get-tuple-element.11.refs_0_, f32[8,2,6,6,512]{4,3,2,1,0:T(8,128)} %copy.169.refs_1_.refs_0_, f32[8,2,6,6,512]{4,3,2,1,0:T(8,128)} %copy.170.refs_2_.refs_1_, f32[8,2,6,6,512]{4,3,2,1,0:T(8,128)} %copy.171.refs_3_.refs_2_, ...), custom_call_target="tpu_custom_call" | custom-call | tf_op jit(solution)/shard_map/pallas_call | solution.py:134
  81.1 0.9 copy.163
  82.0 1.3 collective-permute-start.9
  83.3 1.3 collective-permute-start.11
  84.6 1.3 collective-permute-start.13
  85.9 4.1 %collective-permute-done.10 = f32[12,12,2,512]{3,2,1,0:T(2,128)S(1)} collective-permute-done((f32[12,12,2,512]{3,2,1,0:T(2,128)}, f32[12,12,2,512]{3,2,1,0:T(2,128)S(1)}, u32[]{:S(2)}, u32[]{:S(2)}) %collective-permute-start.10) | collective-permute-done | bytes 589856 | tf_op jit(solution)/shard_map/ppermute | solution.py:28
  90.0 1.1 collective-permute-done.9
  91.4 14.1 %collective-permute-done.11 = f32[12,2,512]{2,1,0:T(2,128)S(1)} collective-permute-done((f32[12,2,512]{2,1,0:T(2,128)S(1)}, f32[12,2,512]{2,1,0:T(2,128)S(1)}, u32[]{:S(2)}, u32[]{:S(2)}) %collective-permute-start.11) | collective-permute-done | bytes 49184 | tf_op jit(solution)/shard_map/ppermute | solution.py:28
  106.4 3.7 %shard_map.145 = (f32[8,2,6,512]{3,2,1,0:T(8,128)}, f32[2,1,2,6,512]{4,3,2,1,0:T(8,128)}) custom-call(f32[8,2,6,512]{3,2,1,0:T(8,128)} %get-tuple-element.11.refs_0_, f32[8,2,6,6,512]{4,3,2,1,0:T(8,128)} %copy.169.refs_1_.refs_0_, f32[8,2,6,6,512]{4,3,2,1,0:T(8,128)} %copy.170.refs_2_.refs_1_, f32[8,2,6,6,512]{4,3,2,1,0:T(8,128)} %copy.171.refs_3_.refs_2_, ...), custom_call_target="tpu_custom_call" | custom-call | tf_op jit(solution)/shard_map/pallas_call | solution.py:134
  110.1 1.1 add_multiply_fusion.1
  111.2 1.3 collective-permute-start.14
  112.5 4.5 %collective-permute-start.15 = (f32[1,2,6,512]{3,2,1,0:T(8,128)S(1)}, f32[1,2,6,512]{3,2,1,0:T(8,128)S(1)}, u32[]{:S(2)}, u32[]{:S(2)}) collective-permute-start(f32[1,2,6,512]{3,2,1,0:T(8,128)S(1)} %get-tuple-element.29), channel_id=1, source_target_pairs={{0,4},{4,8},{8,12},{1,5},{5,9},{9,13},{2,6},{6,10},{10,14},{3,7},{... | collective-permute-start | bytes 73736 | tf_op jit(solution)/shard_map/ppermute | solution.py:19
  117.1 1.3 collective-permute-start.16
  118.4 3.2 %collective-permute-start.17 = (f32[8,2,6,32]{3,2,1,0:T(8,128)S(1)}, f32[8,2,6,32]{3,2,1,0:T(8,128)S(1)}, u32[]{:S(2)}, u32[]{:S(2)}) collective-permute-start(f32[8,2,6,32]{3,2,1,0:T(8,128)S(1)} %get-tuple-element.31), channel_id=1, source_target_pairs={{0,1},{1,2},{2,3},{4,5},{5,6},{6,7},{8,9},{9,10},{10,11},{12,13},{... | collective-permute-start | bytes 36872 | tf_op jit(solution)/shard_map/ppermute | solution.py:19
  121.7 0.7 collective-permute-done.17
  122.9 0.8 convolution_bitcast_fusion
  124.8 0.8 copy.179.refs_0_
  125.6 3.1 %shard_map.146 = (f32[8,2,6,512]{3,2,1,0:T(8,128)}, f32[2,1,2,6,512]{4,3,2,1,0:T(8,128)}) custom-call(f32[8,2,6,512]{3,2,1,0:T(8,128)} %copy.179.refs_0_, f32[8,2,6,6,512]{4,3,2,1,0:T(8,128)} %get-tuple-element.37.refs_1_.refs_0_, f32[8,2,6,6,512]{4,3,2,1,0:T(8,128)} %get-tuple-element.36.refs_2_.refs_1_, f32[2,1,2,6,512]{4,3,2,1,0:T(8,128)} %broadcast_in_dim.14.refs_3_.refs_4_), custom_call_target="tpu_custom_call" | custom-call | tf_op jit(solution)/shard_map/pallas_call | solution.py:84
  128.7 0.9 copy.177
  129.6 1.3 collective-permute-start.18
  130.9 2.0 %collective-permute-start.19 = (f32[12,2,512]{2,1,0:T(2,128)S(1)}, f32[12,2,512]{2,1,0:T(2,128)S(1)}, u32[]{:S(2)}, u32[]{:S(2)}) collective-permute-start(f32[12,2,512]{2,1,0:T(2,128)S(1)} %bitcast.109), channel_id=1, source_target_pairs={{0,8},{4,12},{1,9},{5,13},{2,10},{6,14},{3,11},{7,15},{16,24},{20,... | collective-permute-start | bytes 147464 | tf_op jit(solution)/shard_map/ppermute | solution.py:28
  132.9 1.8 %collective-permute-start.20 = (f32[12,2,512]{2,1,0:T(2,128)S(1)}, f32[12,2,512]{2,1,0:T(2,128)S(1)}, u32[]{:S(2)}, u32[]{:S(2)}) collective-permute-start(f32[12,2,512]{2,1,0:T(2,128)S(1)} %bitcast.110), channel_id=1, source_target_pairs={{0,4},{4,8},{8,12},{1,5},{5,9},{9,13},{2,6},{6,10},{10,14},{3,7},{... | collective-permute-start | bytes 147464 | tf_op jit(solution)/shard_map/ppermute | solution.py:28
  134.8 1.3 multiply_reduce_fusion.6
  137.4 3.1 %shard_map.147 = (f32[8,2,6,512]{3,2,1,0:T(8,128)}, f32[2,1,2,6,512]{4,3,2,1,0:T(8,128)}) custom-call(f32[8,2,6,512]{3,2,1,0:T(8,128)} %copy.179.refs_0_, f32[8,2,6,6,512]{4,3,2,1,0:T(8,128)} %get-tuple-element.37.refs_1_.refs_0_, f32[8,2,6,6,512]{4,3,2,1,0:T(8,128)} %get-tuple-element.36.refs_2_.refs_1_, f32[2,1,2,6,512]{4,3,2,1,0:T(8,128)} %bitcast.88), custom_call_target="tpu_custom_call" | custom-call | tf_op jit(solution)/shard_map/pallas_call | solution.py:84
  140.5 3.7 %shard_map.148 = (f32[8,2,6,512]{3,2,1,0:T(8,128)}, f32[2,1,2,6,512]{4,3,2,1,0:T(8,128)}) custom-call(f32[8,2,6,512]{3,2,1,0:T(8,128)} %get-tuple-element.15.refs_0_, f32[8,2,6,6,512]{4,3,2,1,0:T(8,128)} %copy.169.refs_1_.refs_0_, f32[8,2,6,6,512]{4,3,2,1,0:T(8,128)} %copy.170.refs_2_.refs_1_, f32[8,2,6,6,512]{4,3,2,1,0:T(8,128)} %copy.171.refs_3_.refs_2_, ...), custom_call_target="tpu_custom_call" | custom-call | tf_op jit(solution)/shard_map/pallas_call | solution.py:134
  144.2 0.9 copy.183
  145.1 1.3 collective-permute-start.21
  146.6 1.3 collective-permute-start.22
  147.9 1.3 collective-permute-start.23
  149.2 3.9 %collective-permute-done.21 = f32[12,2,512]{2,1,0:T(2,128)S(1)} collective-permute-done((f32[12,2,512]{2,1,0:T(2,128)S(1)}, f32[12,2,512]{2,1,0:T(2,128)S(1)}, u32[]{:S(2)}, u32[]{:S(2)}) %collective-permute-start.21) | collective-permute-done | bytes 49184 | tf_op jit(solution)/shard_map/ppermute | solution.py:28
  153.4 1.8 %collective-permute-done.22 = f32[12,2,512]{2,1,0:T(2,128)S(1)} collective-permute-done((f32[12,2,512]{2,1,0:T(2,128)S(1)}, f32[12,2,512]{2,1,0:T(2,128)S(1)}, u32[]{:S(2)}, u32[]{:S(2)}) %collective-permute-start.22) | collective-permute-done | bytes 49184 | tf_op jit(solution)/shard_map/ppermute | solution.py:28
  155.6 0.6 copy.214
  156.2 3.6 %shard_map.149 = (f32[8,2,6,512]{3,2,1,0:T(8,128)}, f32[2,1,2,6,512]{4,3,2,1,0:T(8,128)}) custom-call(f32[8,2,6,512]{3,2,1,0:T(8,128)} %get-tuple-element.15.refs_0_, f32[8,2,6,6,512]{4,3,2,1,0:T(8,128)} %copy.169.refs_1_.refs_0_, f32[8,2,6,6,512]{4,3,2,1,0:T(8,128)} %copy.170.refs_2_.refs_1_, f32[8,2,6,6,512]{4,3,2,1,0:T(8,128)} %copy.171.refs_3_.refs_2_, ...), custom_call_target="tpu_custom_call" | custom-call | tf_op jit(solution)/shard_map/pallas_call | solution.py:134
  159.9 1.1 multiply_bitcast_fusion
  161.5 9.2 %psum.7 = f32[8,3,512]{2,0,1:T(8,128)} all-reduce(f32[8,3,512]{2,0,1:T(8,128)S(1)} %bitcast.90), channel_id=1, replica_groups=mesh['cond'=2,'gx'=4,'gy'=4] {'cond'}, use_global_device_ids=true, to_apply=%region_11.0 | all-reduce | flops 12288 | bytes 98304 | tf_op jit(solution)/shard_map/psum | solution.py:248
  170.7 0.8 copy.188
  (94 shorter events, 8.2 us)
Async XLA Ops:
  0.6 34.7 %copy-start = (f32[2,6,32,32]{3,2,1,0:T(8,128)S(1)}, f32[2,6,32,32]{3,2,1,0:T(8,128)}, u32[]{:S(2)}) copy-start(f32[2,6,32,32]{3,2,1,0:T(8,128)} %param.21) | copy-start | bytes 147460
  1.8 31.6 %collective-permute-start.2 = (f32[8,2,6,32]{3,2,1,0:T(8,128)S(1)}, f32[8,2,6,32]{3,2,1,0:T(8,128)S(1)}, u32[]{:S(2)}, u32[]{:S(2)}) collective-permute-start(f32[8,2,6,32]{3,2,1,0:T(8,128)S(1)} %get-tuple-element.34), channel_id=1, source_target_pairs={{1,0},{2,1},{3,2},{5,4},{6,5},{7,6},{9,8},{10,9},{11,10},{13,12},{... | collective-permute-start | bytes 36872 | tf_op jit(solution)/shard_map/ppermute | solution.py:20
  3.0 31.7 %collective-permute-start.3 = (f32[8,2,6,32]{3,2,1,0:T(8,128)S(1)}, f32[8,2,6,32]{3,2,1,0:T(8,128)S(1)}, u32[]{:S(2)}, u32[]{:S(2)}) collective-permute-start(f32[8,2,6,32]{3,2,1,0:T(8,128)S(1)} %get-tuple-element.35), channel_id=1, source_target_pairs={{0,1},{1,2},{2,3},{4,5},{5,6},{6,7},{8,9},{9,10},{10,11},{12,13},{... | collective-permute-start | bytes 36872 | tf_op jit(solution)/shard_map/ppermute | solution.py:19
  6.1 28.6 %collective-permute-start = (f32[1,2,6,512]{3,2,1,0:T(8,128)S(1)}, f32[1,2,6,512]{3,2,1,0:T(8,128)S(1)}, u32[]{:S(2)}, u32[]{:S(2)}) collective-permute-start(f32[1,2,6,512]{3,2,1,0:T(8,128)S(1)} %get-tuple-element.32), channel_id=1, source_target_pairs={{4,0},{8,4},{12,8},{5,1},{9,5},{13,9},{6,2},{10,6},{14,10},{7,3},{... | collective-permute-start | bytes 73736 | tf_op jit(solution)/shard_map/ppermute | solution.py:20
  7.4 27.3 %collective-permute-start.1 = (f32[1,2,6,512]{3,2,1,0:T(8,128)S(1)}, f32[1,2,6,512]{3,2,1,0:T(8,128)S(1)}, u32[]{:S(2)}, u32[]{:S(2)}) collective-permute-start(f32[1,2,6,512]{3,2,1,0:T(8,128)S(1)} %get-tuple-element.33), channel_id=1, source_target_pairs={{0,4},{4,8},{8,12},{1,5},{5,9},{9,13},{2,6},{6,10},{10,14},{3,7},{... | collective-permute-start | bytes 73736 | tf_op jit(solution)/shard_map/ppermute | solution.py:19
  25.2 9.6 %copy-start.11 = (f32[8,2,6,512]{3,1,2,0:T(2,128)S(1)}, f32[8,2,6,512]{3,1,2,0:T(2,128)}, u32[]{:S(2)}) copy-start(f32[8,2,6,512]{3,1,2,0:T(2,128)} %param.14) | copy-start | bytes 589828
  27.6 40.4 %collective-permute-start.5 = (f32[12,12,2,512]{3,2,1,0:T(2,128)}, f32[12,12,2,512]{3,2,1,0:T(2,128)}, u32[]{:S(2)}, u32[]{:S(2)}) collective-permute-start(f32[12,12,2,512]{3,2,1,0:T(2,128)} %bitcast.11), channel_id=1, source_target_pairs={{0,8},{4,12},{1,9},{5,13},{2,10},{6,14},{3,11},{7,15},{16,24},{20,... | collective-permute-start | bytes 1769480 | tf_op jit(solution)/shard_map/ppermute | solution.py:28
  33.4 40.0 %collective-permute-start.7 = (f32[12,12,2,512]{3,2,1,0:T(2,128)}, f32[12,12,2,512]{3,2,1,0:T(2,128)S(1)}, u32[]{:S(2)}, u32[]{:S(2)}) collective-permute-start(f32[12,12,2,512]{3,2,1,0:T(2,128)} %bitcast.11), channel_id=1, source_target_pairs={{0,4},{4,8},{8,12},{1,5},{5,9},{9,13},{2,6},{6,10},{10,14},{3,7},{... | collective-permute-start | bytes 1769480 | tf_op jit(solution)/shard_map/ppermute | solution.py:28
  35.3 1.3 copy-start.1
  38.6 5.5 %copy-start.8 = (f32[8,2,6,6,512]{4,1,3,2,0:T(2,128)S(1)}, f32[8,2,6,6,512]{4,1,3,2,0:T(2,128)}, u32[]{:S(2)}) copy-start(f32[8,2,6,6,512]{4,1,3,2,0:T(2,128)} %param.17) | copy-start | bytes 3538948
  42.7 2.9 %copy-start.9 = (f32[8,2,6,6,512]{4,1,3,2,0:T(2,128)S(1)}, f32[8,2,6,6,512]{4,1,3,2,0:T(2,128)}, u32[]{:S(2)}) copy-start(f32[8,2,6,6,512]{4,1,3,2,0:T(2,128)} %param.18) | copy-start | bytes 3538948
  42.7 19.2 %collective-permute-start.4 = (f32[12,2,512]{2,1,0:T(2,128)S(1)}, f32[12,2,512]{2,1,0:T(2,128)S(1)}, u32[]{:S(2)}, u32[]{:S(2)}) collective-permute-start(f32[12,2,512]{2,1,0:T(2,128)S(1)} %bitcast.99), channel_id=1, source_target_pairs={{0,12},{1,13},{2,14},{3,15},{16,28},{17,29},{18,30},{19,31}} | collective-permute-start | bytes 147464 | tf_op jit(solution)/shard_map/ppermute | solution.py:28
  45.6 1.4 copy-start.10
  59.3 30.7 %collective-permute-start.10 = (f32[12,12,2,512]{3,2,1,0:T(2,128)}, f32[12,12,2,512]{3,2,1,0:T(2,128)S(1)}, u32[]{:S(2)}, u32[]{:S(2)}) collective-permute-start(f32[12,12,2,512]{3,2,1,0:T(2,128)} %bitcast.19), channel_id=1, source_target_pairs={{8,0},{12,4},{9,1},{13,5},{10,2},{14,6},{11,3},{15,7},{24,16},{28,... | collective-permute-start | bytes 1769480 | tf_op jit(solution)/shard_map/ppermute | solution.py:28
  60.6 44.9 %collective-permute-start.12 = (f32[12,12,2,512]{3,2,1,0:T(2,128)}, f32[12,12,2,512]{3,2,1,0:T(2,128)S(1)}, u32[]{:S(2)}, u32[]{:S(2)}) collective-permute-start(f32[12,12,2,512]{3,2,1,0:T(2,128)} %bitcast.19), channel_id=1, source_target_pairs={{4,0},{8,4},{12,8},{5,1},{9,5},{13,9},{6,2},{10,6},{14,10},{7,3},{... | collective-permute-start | bytes 1769480 | tf_op jit(solution)/shard_map/ppermute | solution.py:28
  61.9 11.4 %collective-permute-start.6 = (f32[12,2,512]{2,1,0:T(2,128)S(1)}, f32[12,2,512]{2,1,0:T(2,128)S(1)}, u32[]{:S(2)}, u32[]{:S(2)}) collective-permute-start(f32[12,2,512]{2,1,0:T(2,128)S(1)} %bitcast.100), channel_id=1, source_target_pairs={{0,8},{4,12},{1,9},{5,13},{2,10},{6,14},{3,11},{7,15},{16,24},{20,... | collective-permute-start | bytes 147464 | tf_op jit(solution)/shard_map/ppermute | solution.py:28
  68.0 5.7 %collective-permute-start.8 = (f32[12,2,512]{2,1,0:T(2,128)S(1)}, f32[12,2,512]{2,1,0:T(2,128)S(1)}, u32[]{:S(2)}, u32[]{:S(2)}) collective-permute-start(f32[12,2,512]{2,1,0:T(2,128)S(1)} %bitcast.101), channel_id=1, source_target_pairs={{0,4},{4,8},{8,12},{1,5},{5,9},{9,13},{2,6},{6,10},{10,14},{3,7},{... | collective-permute-start | bytes 147464 | tf_op jit(solution)/shard_map/ppermute | solution.py:28
  73.4 4.1 %copy-start.2 = (f32[12,12,2,512]{3,2,1,0:T(2,128)}, f32[12,12,2,512]{3,2,1,0:T(2,128)S(1)}, u32[]{:S(2)}) copy-start(f32[12,12,2,512]{3,2,1,0:T(2,128)S(1)} %collective-permute-done.7) | copy-start | bytes 1769476
  77.5 5.8 %copy-start.15 = (s32[8,512]{1,0:T(8,128)S(1)}, s32[8,512]{1,0:T(8,128)}, u32[]{:S(2)}) copy-start(s32[8,512]{1,0:T(8,128)} %param.23) | copy-start | bytes 49156
  82.0 9.1 %collective-permute-start.9 = (f32[12,2,512]{2,1,0:T(2,128)S(1)}, f32[12,2,512]{2,1,0:T(2,128)S(1)}, u32[]{:S(2)}, u32[]{:S(2)}) collective-permute-start(f32[12,2,512]{2,1,0:T(2,128)S(1)} %bitcast.102), channel_id=1, source_target_pairs={{12,0},{13,1},{14,2},{15,3},{28,16},{29,17},{30,18},{31,19}} | collective-permute-start | bytes 147464 | tf_op jit(solution)/shard_map/ppermute | solution.py:28
  83.3 22.1 %collective-permute-start.11 = (f32[12,2,512]{2,1,0:T(2,128)S(1)}, f32[12,2,512]{2,1,0:T(2,128)S(1)}, u32[]{:S(2)}, u32[]{:S(2)}) collective-permute-start(f32[12,2,512]{2,1,0:T(2,128)S(1)} %bitcast.103), channel_id=1, source_target_pairs={{8,0},{12,4},{9,1},{13,5},{10,2},{14,6},{11,3},{15,7},{24,16},{28,... | collective-permute-start | bytes 147464 | tf_op jit(solution)/shard_map/ppermute | solution.py:28
  84.6 21.1 %collective-permute-start.13 = (f32[12,2,512]{2,1,0:T(2,128)S(1)}, f32[12,2,512]{2,1,0:T(2,128)S(1)}, u32[]{:S(2)}, u32[]{:S(2)}) collective-permute-start(f32[12,2,512]{2,1,0:T(2,128)S(1)} %bitcast.104), channel_id=1, source_target_pairs={{4,0},{8,4},{12,8},{5,1},{9,5},{13,9},{6,2},{10,6},{14,10},{7,3},{... | collective-permute-start | bytes 147464 | tf_op jit(solution)/shard_map/ppermute | solution.py:28
  90.0 20.1 %copy-start.6 = (f32[12,12,2,512]{3,2,1,0:T(2,128)}, f32[12,12,2,512]{3,2,1,0:T(2,128)S(1)}, u32[]{:S(2)}) copy-start(f32[12,12,2,512]{3,2,1,0:T(2,128)S(1)} %collective-permute-done.10) | copy-start | bytes 1769476
  105.5 4.6 %copy-start.4 = (f32[12,12,2,512]{3,2,1,0:T(2,128)}, f32[12,12,2,512]{3,2,1,0:T(2,128)S(1)}, u32[]{:S(2)}) copy-start(f32[12,12,2,512]{3,2,1,0:T(2,128)S(1)} %collective-permute-done.12) | copy-start | bytes 1769476
  106.4 3.7 %copy-start.13 = (f32[8,2,6,512]{3,1,2,0:T(2,128)S(1)}, f32[8,2,6,512]{3,1,2,0:T(2,128)}, u32[]{:S(2)}) copy-start(f32[8,2,6,512]{3,1,2,0:T(2,128)} %param.13) | copy-start | bytes 589828
  110.1 12.3 %copy-start.12 = (f32[8,2,6,512]{3,1,2,0:T(2,128)S(1)}, f32[8,2,6,512]{3,1,2,0:T(2,128)}, u32[]{:S(2)}) copy-start(f32[8,2,6,512]{3,1,2,0:T(2,128)} %param.14) | copy-start | bytes 589828
  111.2 11.2 %collective-permute-start.14 = (f32[1,2,6,512]{3,2,1,0:T(8,128)S(1)}, f32[1,2,6,512]{3,2,1,0:T(8,128)S(1)}, u32[]{:S(2)}, u32[]{:S(2)}) collective-permute-start(f32[1,2,6,512]{3,2,1,0:T(8,128)S(1)} %get-tuple-element.28), channel_id=1, source_target_pairs={{4,0},{8,4},{12,8},{5,1},{9,5},{13,9},{6,2},{10,6},{14,10},{7,3},{... | collective-permute-start | bytes 73736 | tf_op jit(solution)/shard_map/ppermute | solution.py:20
  112.5 9.9 %collective-permute-start.15 = (f32[1,2,6,512]{3,2,1,0:T(8,128)S(1)}, f32[1,2,6,512]{3,2,1,0:T(8,128)S(1)}, u32[]{:S(2)}, u32[]{:S(2)}) collective-permute-start(f32[1,2,6,512]{3,2,1,0:T(8,128)S(1)} %get-tuple-element.29), channel_id=1, source_target_pairs={{0,4},{4,8},{8,12},{1,5},{5,9},{9,13},{2,6},{6,10},{10,14},{3,7},{... | collective-permute-start | bytes 73736 | tf_op jit(solution)/shard_map/ppermute | solution.py:19
  117.1 4.5 %collective-permute-start.16 = (f32[8,2,6,32]{3,2,1,0:T(8,128)S(1)}, f32[8,2,6,32]{3,2,1,0:T(8,128)S(1)}, u32[]{:S(2)}, u32[]{:S(2)}) collective-permute-start(f32[8,2,6,32]{3,2,1,0:T(8,128)S(1)} %get-tuple-element.30), channel_id=1, source_target_pairs={{1,0},{2,1},{3,2},{5,4},{6,5},{7,6},{9,8},{10,9},{11,10},{13,12},{... | collective-permute-start | bytes 36872 | tf_op jit(solution)/shard_map/ppermute | solution.py:20
  118.4 3.9 %collective-permute-start.17 = (f32[8,2,6,32]{3,2,1,0:T(8,128)S(1)}, f32[8,2,6,32]{3,2,1,0:T(8,128)S(1)}, u32[]{:S(2)}, u32[]{:S(2)}) collective-permute-start(f32[8,2,6,32]{3,2,1,0:T(8,128)S(1)} %get-tuple-element.31), channel_id=1, source_target_pairs={{0,1},{1,2},{2,3},{4,5},{5,6},{6,7},{8,9},{9,10},{10,11},{12,13},{... | collective-permute-start | bytes 36872 | tf_op jit(solution)/shard_map/ppermute | solution.py:19
  128.7 7.5 %copy-start.3 = (f32[12,12,2,512]{3,2,1,0:T(2,128)S(1)}, f32[12,12,2,512]{3,2,1,0:T(2,128)}, u32[]{:S(2)}) copy-start(f32[12,12,2,512]{3,2,1,0:T(2,128)} %copy-done.2) | copy-start | bytes 1769476
  129.6 5.1 %collective-permute-start.18 = (f32[12,2,512]{2,1,0:T(2,128)S(1)}, f32[12,2,512]{2,1,0:T(2,128)S(1)}, u32[]{:S(2)}, u32[]{:S(2)}) collective-permute-start(f32[12,2,512]{2,1,0:T(2,128)S(1)} %bitcast.108), channel_id=1, source_target_pairs={{0,12},{1,13},{2,14},{3,15},{16,28},{17,29},{18,30},{19,31}} | collective-permute-start | bytes 147464 | tf_op jit(solution)/shard_map/ppermute | solution.py:28
  130.9 5.2 %collective-permute-start.19 = (f32[12,2,512]{2,1,0:T(2,128)S(1)}, f32[12,2,512]{2,1,0:T(2,128)S(1)}, u32[]{:S(2)}, u32[]{:S(2)}) collective-permute-start(f32[12,2,512]{2,1,0:T(2,128)S(1)} %bitcast.109), channel_id=1, source_target_pairs={{0,8},{4,12},{1,9},{5,13},{2,10},{6,14},{3,11},{7,15},{16,24},{20,... | collective-permute-start | bytes 147464 | tf_op jit(solution)/shard_map/ppermute | solution.py:28
  132.9 3.8 %collective-permute-start.20 = (f32[12,2,512]{2,1,0:T(2,128)S(1)}, f32[12,2,512]{2,1,0:T(2,128)S(1)}, u32[]{:S(2)}, u32[]{:S(2)}) collective-permute-start(f32[12,2,512]{2,1,0:T(2,128)S(1)} %bitcast.110), channel_id=1, source_target_pairs={{0,4},{4,8},{8,12},{1,5},{5,9},{9,13},{2,6},{6,10},{10,14},{3,7},{... | collective-permute-start | bytes 147464 | tf_op jit(solution)/shard_map/ppermute | solution.py:28
  140.5 6.0 %copy-start.16 = (f32[8]{0:T(128)S(1)}, f32[8]{0:T(128)}, u32[]{:S(2)}) copy-start(f32[8]{0:T(128)} %param.25) | copy-start | bytes 100
  140.5 6.0 %copy-start.17 = (s32[2]{0:T(128)S(1)}, s32[2]{0:T(128)}, u32[]{:S(2)}) copy-start(s32[2]{0:T(128)} %param.24) | copy-start | bytes 28
  140.5 12.7 %copy-start.7 = (f32[12,12,2,512]{3,2,1,0:T(2,128)S(1)}, f32[12,12,2,512]{3,2,1,0:T(2,128)}, u32[]{:S(2)}) copy-start(f32[12,12,2,512]{3,2,1,0:T(2,128)} %copy-done.6) | copy-start | bytes 1769476
  144.2 11.1 %copy-start.5 = (f32[12,12,2,512]{3,2,1,0:T(2,128)S(1)}, f32[12,12,2,512]{3,2,1,0:T(2,128)}, u32[]{:S(2)}) copy-start(f32[12,12,2,512]{3,2,1,0:T(2,128)} %copy-done.4) | copy-start | bytes 1769476
  145.1 8.0 %collective-permute-start.21 = (f32[12,2,512]{2,1,0:T(2,128)S(1)}, f32[12,2,512]{2,1,0:T(2,128)S(1)}, u32[]{:S(2)}, u32[]{:S(2)}) collective-permute-start(f32[12,2,512]{2,1,0:T(2,128)S(1)} %bitcast.105), channel_id=1, source_target_pairs={{12,0},{13,1},{14,2},{15,3},{28,16},{29,17},{30,18},{31,19}} | collective-permute-start | bytes 147464 | tf_op jit(solution)/shard_map/ppermute | solution.py:28
  146.6 8.6 %collective-permute-start.22 = (f32[12,2,512]{2,1,0:T(2,128)S(1)}, f32[12,2,512]{2,1,0:T(2,128)S(1)}, u32[]{:S(2)}, u32[]{:S(2)}) collective-permute-start(f32[12,2,512]{2,1,0:T(2,128)S(1)} %bitcast.106), channel_id=1, source_target_pairs={{8,0},{12,4},{9,1},{13,5},{10,2},{14,6},{11,3},{15,7},{24,16},{28,... | collective-permute-start | bytes 147464 | tf_op jit(solution)/shard_map/ppermute | solution.py:28
  147.9 7.6 %collective-permute-start.23 = (f32[12,2,512]{2,1,0:T(2,128)S(1)}, f32[12,2,512]{2,1,0:T(2,128)S(1)}, u32[]{:S(2)}, u32[]{:S(2)}) collective-permute-start(f32[12,2,512]{2,1,0:T(2,128)S(1)} %bitcast.107), channel_id=1, source_target_pairs={{4,0},{8,4},{12,8},{5,1},{9,5},{13,9},{6,2},{10,6},{14,10},{7,3},{... | collective-permute-start | bytes 147464 | tf_op jit(solution)/shard_map/ppermute | solution.py:28
  159.9 1.3 copy-start.14

commit v4 on v3

--- a/solution.py
+++ b/solution.py
@@ -40,23 +40,37 @@
     return total
 
 
+def _init_carry(carry_ref, inc_ref):
+    if inc_ref is not None:
+        carry_ref[...] = inc_ref[...]
+        return
+    slots, width, conds, nv, lanes = carry_ref.shape
+    rows = lax.broadcasted_iota(jnp.int32, (nv, lanes), 0)
+    for slot in range(slots):
+        for k in range(width):
+            unit = (rows == k - slot * nv).astype(jnp.float32)
+            for c in range(conds):
+                carry_ref[slot, k, c] = unit
+
+
 def upper_pallas(rhs, near_t, far_t, incoming, want_values):
     count, conds, nv = near_t.shape[0], near_t.shape[1], near_t.shape[2]
-    width = incoming.shape[1]
+    has_inc = not isinstance(incoming, tuple)
+    shape = incoming.shape if has_inc else incoming
+    width = shape[1]
     has_rhs = rhs is not None
 
     def kernel(*refs):
-        if has_rhs:
-            rhs_ref, nt_ref, ft_ref, inc_ref = refs[:4]
-            outs = refs[4:]
-        else:
-            nt_ref, ft_ref, inc_ref = refs[:3]
-            outs = refs[3:]
+        refs = list(refs)
+        rhs_ref = refs.pop(0) if has_rhs else None
+        nt_ref, ft_ref = refs.pop(0), refs.pop(0)
+        inc_ref = refs.pop(0) if has_inc else None
+        outs = refs
         if want_values:
             val_ref, carry_ref = outs
         else:
             (carry_ref,) = outs
-        carry_ref[...] = inc_ref[...]
+        _init_carry(carry_ref, inc_ref)
 
         def step(i, unused):
             for k in range(width):
@@ -76,11 +90,10 @@
 
         lax.fori_loop(0, count, step, 0)
 
-    shape = incoming.shape
     out_shape = [jax.ShapeDtypeStruct(shape, jnp.float32)]
     if want_values:
         out_shape = [jax.ShapeDtypeStruct(rhs.shape, jnp.float32)] + out_shape
-    args = ([rhs] if has_rhs else []) + [near_t, far_t, incoming]
+    args = ([rhs] if has_rhs else []) + [near_t, far_t] + ([incoming] if has_inc else [])
     return pl.pallas_call(
         kernel,
         out_shape=tuple(out_shape),
@@ -91,21 +104,22 @@
 
 def lower_pallas(rhs, inverse, near, far, incoming, want_values):
     count, conds, nv = inverse.shape[0], inverse.shape[1], inverse.shape[2]
-    width = incoming.shape[1]
+    has_inc = not isinstance(incoming, tuple)
+    shape = incoming.shape if has_inc else incoming
+    width = shape[1]
     has_rhs = rhs is not None
 
     def kernel(*refs):
-        if has_rhs:
-            rhs_ref, d_ref, b_ref, a_ref, inc_ref = refs[:5]
-            outs = refs[5:]
-        else:
-            d_ref, b_ref, a_ref, inc_ref = refs[:4]
-            outs = refs[4:]
+        refs = list(refs)
+        rhs_ref = refs.pop(0) if has_rhs else None
+        d_ref, b_ref, a_ref = refs.pop(0), refs.pop(0), refs.pop(0)
+        inc_ref = refs.pop(0) if has_inc else None
+        outs = refs
         if want_values:
             val_ref, carry_ref = outs
         else:
             (carry_ref,) = outs
-        carry_ref[...] = inc_ref[...]
+        _init_carry(carry_ref, inc_ref)
 
         def step(t, unused):
             i = count - 1 - t
@@ -126,11 +140,10 @@
 
         lax.fori_loop(0, count, step, 0)
 
-    shape = incoming.shape
     out_shape = [jax.ShapeDtypeStruct(shape, jnp.float32)]
     if want_values:
         out_shape = [jax.ShapeDtypeStruct(rhs.shape, jnp.float32)] + out_shape
-    args = ([rhs] if has_rhs else []) + [inverse, near, far, incoming]
+    args = ([rhs] if has_rhs else []) + [inverse, near, far] + ([incoming] if has_inc else [])
     return pl.pallas_call(
         kernel,
         out_shape=tuple(out_shape),
@@ -139,29 +152,11 @@
     )(*args)
 
 
-def unit_carries(shape):
-    width = 2 * shape[1]
-    table = jnp.eye(width, dtype=jnp.float32).reshape(width, 2, shape[1]).transpose(1, 0, 2)
-    return jnp.broadcast_to(table[:, :, None, :, None], (2, width, shape[0], shape[1], shape[2]))
-
-
-def as_matrix(response):
-    width = response.shape[1]
-    return jnp.transpose(response, (1, 0, 3, 2, 4)).reshape(
-        width, width, response.shape[2], response.shape[4]
-    )
-
-
-def as_vector(carry):
-    return jnp.transpose(carry, (0, 2, 1, 3)).reshape(-1, carry.shape[1], carry.shape[3])
-
-
-def from_vector(vector, count):
-    return vector.reshape(2, count, vector.shape[1], vector.shape[2]).transpose(0, 2, 1, 3)
-
-
-def carry_through(vector, matrix, offset):
-    return jnp.einsum("kcl,kmcl->mcl", vector, matrix, precision=lax.Precision.HIGHEST) + offset
+def carry_through(vector, response):
+    slots, width, conds, nv, lanes = response.shape
+    split = response.reshape(slots, slots, nv, conds, nv, lanes)
+    inputs = jnp.transpose(vector, (0, 2, 1, 3))[None, :, :, :, None, :]
+    return jnp.sum(jnp.sum(split * inputs, axis=2), axis=1)
 
 
 def shifted_operators(matrix, steps):
@@ -175,7 +170,7 @@
         return jnp.zeros_like(vector)
     total = from_behind(vector, "gx", steps * (count - 1))
     for s in range(count - 2, 0, -1):
-        total = jnp.sum(total[:, None] * operators[s - 1], axis=0) + from_behind(
+        total = carry_through(total, operators[s - 1]) + from_behind(
             vector, "gx", steps * s
         )
     return total
@@ -199,13 +194,13 @@
     keep = (1.0 - wall_mask.astype(jnp.float32))[:, None, None, :]
     carry_shape = psi_old.shape[1:]
     zeros = jnp.zeros((2, 1) + carry_shape, jnp.float32)
-    units = unit_carries(carry_shape)
+    units = (2, 2 * carry_shape[1]) + carry_shape
     near_t = jnp.swapaxes(near_upper, 2, 3)
     far_t = jnp.swapaxes(far_upper, 2, 3)
     (response,) = upper_pallas(None, near_t, far_t, units, False)
-    matrix = as_matrix(response)
+    matrix = response
     (response,) = lower_pallas(None, inverse_diag, near_lower, far_lower, units, False)
-    reverse_matrix = as_matrix(response)
+    reverse_matrix = response
     upper_products = shifted_operators(matrix, 1)
     lower_products = shifted_operators(reverse_matrix, -1)
     psi = psi_old
@@ -222,20 +217,11 @@
         ).reshape(rhs.shape)
         yres = jnp.sum(y_inverse * zres[..., :, None, :], axis=-3)
         _, offset = upper_pallas(yres, near_t, far_t, zeros, True)
-        entering = gathered_carry(as_vector(offset[:, 0]), upper_products, 1)
-        upper, _ = upper_pallas(
-            yres, near_t, far_t, from_vector(entering, carry_shape[1])[:, None], True
-        )
+        entering = gathered_carry(offset[:, 0], upper_products, 1)
+        upper, _ = upper_pallas(yres, near_t, far_t, entering[:, None], True)
         _, offset = lower_pallas(upper, inverse_diag, near_lower, far_lower, zeros, True)
-        entering = gathered_carry(as_vector(offset[:, 0]), lower_products, -1)
-        lower, _ = lower_pallas(
-            upper,
-            inverse_diag,
-            near_lower,
-            far_lower,
-            from_vector(entering, carry_shape[1])[:, None],
-            True,
-        )
+        entering = gathered_carry(offset[:, 0], lower_products, -1)
+        lower, _ = lower_pallas(upper, inverse_diag, near_lower, far_lower, entering[:, None], True)
         psi = (psi + 0.05 * lower) * keep
     onehot = (cond_index[:, None] == jnp.arange(weight_table.shape[0])[None, :]).astype(jnp.float32)
     weights = jnp.sum(onehot * weight_table[None, :], axis=1)
@@ -245,7 +231,10 @@
         sens_terms,
         precision=lax.Precision.HIGHEST,
     )
-    mesh_sens = lax.psum(local_sens, "cond")
+    if lax.axis_size("cond") == 2:
+        mesh_sens = local_sens + lax.ppermute(local_sens, "cond", [(0, 1), (1, 0)])
+    else:
+        mesh_sens = lax.psum(local_sens, "cond")
     return (psi, mesh_sens)
 
 

time: 173 us -> 166 us (0.960)
  blocking collectives: 9.19 us -> 0 us
  local copies, waits for them, and re-layouts: 26.5 us -> 19.6 us
  waiting for transfers between devices: 26 us -> 31.1 us
  other arithmetic: 8.72 us -> 11.7 us
  starting transfers between devices: 55.5 us -> 57.6 us
    psum x1 -> x0, blocking collectives: 9.19 us -> none  [on_device(): mesh_sens = lax.psum(local_sens, 'cond')]
    transpose x6 -> x8, local copies, waits for them, and re-layouts: 8.54 us -> 0.32 us  [carry_through(): inputs = jnp.transpose(vector, (0, 2, 1, 3))[None, :, :, :, None, :]]
    pallas_call x0 -> x2, local copies, waits for them, and re-layouts: none -> 4.91 us  [the longest x1 2.47 us: upper_pallas(): pl.pallas_call(kernel, out_shape=tuple(out_shape), in_specs=_vmem_specs(l...]
    ppermute x16, waiting for transfers between devices: 25.3 us -> 28.7 us  [from_behind(): lax.ppermute(value, axis, [(source, source + steps) for source in range(f...]
    broadcast_in_dim x0 -> x4, other arithmetic: none -> 2.57 us  [the longest x2 1.29 us: on_device(): upper, _ = upper_pallas(yres, near_t, far_t, entering[:, None], True)]
    reshape x4 -> x0, local copies, waits for them, and re-layouts: 2.54 us -> none  [from_vector(): vector.reshape(2, count, vector.shape[1], vector.shape[2])]
    ppermute x0 -> x1, waiting for transfers between devices: none -> 1.77 us  [on_device(): mesh_sens = local_sens + lax.ppermute(local_sens, 'cond', [(0, 1), (1, 0)])]
    unnamed x42 -> x44, local copies, waits for them, and re-layouts: 6.39 us -> 6.39 us
  transfers between devices with their start and end apart: 24 -> 25, of which waited for: 8 -> 8; matrix products, arithmetic and copies ran while one was open for 15% -> 14% of each run, Pallas kernels for 15% -> 15%
where the time goes in v4:
time: 166 us; the launch traced here: 165 us
  starting transfers between devices  57.6 us (35%)
  Pallas kernels  42.3 us (25%)
  waiting for transfers between devices  31.1 us (19%)
  local copies, waits for them, and re-layouts  19.6 us (12%)
  other arithmetic  11.7 us (7%)
    ppermute x16, starting transfers between devices, from_behind(): lax.ppermute(value, axis, [(source, source + steps) for source in range(f...  34.6 us
    ppermute x16, waiting for transfers between devices, from_behind(): lax.ppermute(value, axis, [(source, source + steps) for source in range(f...  28.7 us
    pallas_call x5, Pallas kernels, lower_pallas(): pl.pallas_call(kernel, out_shape=tuple(out_shape), in_specs=_vmem_specs(l...  22.9 us
    pallas_call x5, Pallas kernels, upper_pallas(): pl.pallas_call(kernel, out_shape=tuple(out_shape), in_specs=_vmem_specs(l...  19.4 us
    ppermute x4, starting transfers between devices, extended(): before = lax.ppermute(last, axis, up)  16.4 us
    unnamed x44, local copies, waits for them, and re-layouts  6.39 us
    ppermute x4, starting transfers between devices, extended(): after = lax.ppermute(first, axis, down)  5.15 us
    reduce_sum x8, other arithmetic, carry_through(): return jnp.sum(jnp.sum(split * inputs, axis=2), axis=1)  4.17 us
  transfers between devices with their start and end apart: 25, of which 8 were waited for; matrix products, arithmetic and copies ran while one was open for 14% of the time, Pallas kernels for 15%

profile of v4, /device:TPU:0, one launch (start us, length us, event | category | flops | bytes accessed | tf_op | source)
XLA Modules:
  0.0 165.4 jit_solution(15200500027253273544)
XLA Ops:
  0.6 1.0 copy.236
  1.8 1.3 collective-permute-start.2
  3.0 3.0 %collective-permute-start.3 = (f32[8,2,6,32]{3,2,1,0:T(8,128)S(1)}, f32[8,2,6,32]{3,2,1,0:T(8,128)S(1)}, u32[]{:S(2)}, u32[]{:S(2)}) collective-permute-start(f32[8,2,6,32]{3,2,1,0:T(8,128)S(1)} %get-tuple-element.37), channel_id=1, source_target_pairs={{0,1},{1,2},{2,3},{4,5},{5,6},{6,7},{8,9},{9,10},{10,11},{12,13},{... | collective-permute-start | bytes 36872 | tf_op jit(solution)/shard_map/ppermute | solution.py:19
  6.1 1.3 collective-permute-start
  7.4 5.6 %collective-permute-start.1 = (f32[1,2,6,512]{3,2,1,0:T(8,128)S(1)}, f32[1,2,6,512]{3,2,1,0:T(8,128)S(1)}, u32[]{:S(2)}, u32[]{:S(2)}) collective-permute-start(f32[1,2,6,512]{3,2,1,0:T(8,128)S(1)} %get-tuple-element.35), channel_id=1, source_target_pairs={{0,4},{4,8},{8,12},{1,5},{5,9},{9,13},{2,6},{6,10},{10,14},{3,7},{... | collective-permute-start | bytes 73736 | tf_op jit(solution)/shard_map/ppermute | solution.py:19
  13.0 4.0 %copy_bitcast_fusion = (f32[8,2,6,6,512]{4,3,2,1,0:T(8,128)}, f32[8,2,6,6,512]{4,3,2,1,0:T(8,128)}) fusion(f32[8,2,6,6,512]{4,1,3,2,0:T(2,128)} %param.16, f32[8,2,6,6,512]{4,1,3,2,0:T(2,128)} %param.15), kind=kLoop, calls=%fused_computation | loop fusion | bytes 4718592 | tf_op jit(solution)/shard_map/transpose | solution.py:199
  17.0 6.9 %shard_map.140 = f32[2,12,2,6,512]{4,3,2,1,0:T(8,128)} custom-call(f32[8,2,6,6,512]{4,3,2,1,0:T(8,128)} %get-tuple-element.39.refs_0_.refs_1_, f32[8,2,6,6,512]{4,3,2,1,0:T(8,128)} %get-tuple-element.38.refs_1_.refs_2_), custom_call_target="tpu_custom_call" | custom-call | tf_op jit(solution)/shard_map/pallas_call | solution.py:97
  23.9 2.5 %copy.213 = f32[2,12,2,6,512]{4,2,3,1,0:T(2,128)} copy(f32[2,12,2,6,512]{4,3,2,1,0:T(8,128)} %shard_map.140) | data formatting | bytes 1179648 | tf_op jit(solution)/shard_map/pallas_call | solution.py:97
  26.4 5.8 %collective-permute-start.5 = (f32[2,12,2,6,512]{4,2,3,1,0:T(2,128)}, f32[2,12,2,6,512]{4,2,3,1,0:T(2,128)}, u32[]{:S(2)}, u32[]{:S(2)}) collective-permute-start(f32[2,12,2,6,512]{4,2,3,1,0:T(2,128)} %copy.213), channel_id=1, source_target_pairs={{0,8},{4,12},{1,9},{5,13},{2,10},{6,14},{3,11},{7,15},{16,24},{20,... | collective-permute-start | bytes 1769480 | tf_op jit(solution)/shard_map/ppermute | solution.py:28
  32.2 1.3 collective-permute-start.4
  34.1 0.8 convolution_bitcast_fusion.1
  36.0 0.8 copy.220.refs_0_
  36.8 0.6 broadcast_in_dim.10.refs_3_.refs_4_
  37.4 3.2 %shard_map.141 = (f32[8,2,6,512]{3,2,1,0:T(8,128)}, f32[2,1,2,6,512]{4,3,2,1,0:T(8,128)}) custom-call(f32[8,2,6,512]{3,2,1,0:T(8,128)} %copy.220.refs_0_, f32[8,2,6,6,512]{4,3,2,1,0:T(8,128)} %get-tuple-element.39.refs_0_.refs_1_, f32[8,2,6,6,512]{4,3,2,1,0:T(8,128)} %get-tuple-element.38.refs_1_.refs_2_, f32[2,1,2,6,512]{4,3,2,1,0:T(8,128)} %broadcast_in_dim.10.refs_3_.refs_4_), custom_call_target="tpu_custom_call" | custom-call | tf_op jit(solution)/shard_map/pallas_call | solution.py:97
  40.6 1.4 collective-permute-start.6
  42.0 1.4 copy.233.refs_0_.refs_1_
  43.5 1.4 copy.234.refs_1_.refs_2_
  44.9 1.4 copy.235.refs_2_.refs_3_
  46.3 8.2 %shard_map.143 = f32[2,12,2,6,512]{4,3,2,1,0:T(8,128)} custom-call(f32[8,2,6,6,512]{4,3,2,1,0:T(8,128)} %copy.233.refs_0_.refs_1_, f32[8,2,6,6,512]{4,3,2,1,0:T(8,128)} %copy.234.refs_1_.refs_2_, f32[8,2,6,6,512]{4,3,2,1,0:T(8,128)} %copy.235.refs_2_.refs_3_), custom_call_target="tpu_custom_call" | custom-call | tf_op jit(solution)/shard_map/pallas_call | solution.py:147
  54.5 2.4 %copy.224 = f32[2,12,2,6,512]{4,2,3,1,0:T(2,128)} copy(f32[2,12,2,6,512]{4,3,2,1,0:T(8,128)} %shard_map.143) | data formatting | bytes 1179648 | tf_op jit(solution)/shard_map/pallas_call | solution.py:147
  57.0 1.3 collective-permute-start.10
  58.3 1.3 collective-permute-start.9
  59.6 6.1 %collective-permute-start.7 = (f32[2,2,6,512]{3,2,1,0:T(8,128)S(1)}, f32[2,2,6,512]{3,2,1,0:T(8,128)S(1)}, u32[]{:S(2)}, u32[]{:S(2)}) collective-permute-start(f32[2,2,6,512]{3,2,1,0:T(8,128)S(1)} %bitcast.88), channel_id=1, source_target_pairs={{0,8},{4,12},{1,9},{5,13},{2,10},{6,14},{3,11},{7,15},{16,24},{20,... | collective-permute-start | bytes 147464 | tf_op jit(solution)/shard_map/ppermute | solution.py:28
  65.8 4.0 %collective-permute-start.8 = (f32[2,2,6,512]{3,2,1,0:T(8,128)S(1)}, f32[2,2,6,512]{3,2,1,0:T(8,128)S(1)}, u32[]{:S(2)}, u32[]{:S(2)}) collective-permute-start(f32[2,2,6,512]{3,2,1,0:T(8,128)S(1)} %bitcast.89), channel_id=1, source_target_pairs={{0,4},{4,8},{8,12},{1,5},{5,9},{9,13},{2,6},{6,10},{10,14},{3,7},{... | collective-permute-start | bytes 147464 | tf_op jit(solution)/shard_map/ppermute | solution.py:28
  69.7 1.3 multiply_reduce_fusion.10
  71.6 0.6 fusion.18.refs_3_
  72.3 3.1 %shard_map.142 = (f32[8,2,6,512]{3,2,1,0:T(8,128)}, f32[2,1,2,6,512]{4,3,2,1,0:T(8,128)}) custom-call(f32[8,2,6,512]{3,2,1,0:T(8,128)} %copy.220.refs_0_, f32[8,2,6,6,512]{4,3,2,1,0:T(8,128)} %get-tuple-element.39.refs_0_.refs_1_, f32[8,2,6,6,512]{4,3,2,1,0:T(8,128)} %get-tuple-element.38.refs_1_.refs_2_, f32[2,1,2,6,512]{4,3,2,1,0:T(8,128)} %fusion.18.refs_3_), custom_call_target="tpu_custom_call" | custom-call | tf_op jit(solution)/shard_map/pallas_call | solution.py:97
  75.4 3.7 %shard_map.144 = (f32[8,2,6,512]{3,2,1,0:T(8,128)}, f32[2,1,2,6,512]{4,3,2,1,0:T(8,128)}) custom-call(f32[8,2,6,512]{3,2,1,0:T(8,128)} %get-tuple-element.11.refs_0_, f32[8,2,6,6,512]{4,3,2,1,0:T(8,128)} %copy.233.refs_0_.refs_1_, f32[8,2,6,6,512]{4,3,2,1,0:T(8,128)} %copy.234.refs_1_.refs_2_, f32[8,2,6,6,512]{4,3,2,1,0:T(8,128)} %copy.235.refs_2_.refs_3_, ...), custom_call_target="tpu_custom_call" | custom-call | tf_op jit(solution)/shard_map/pallas_call | solution.py:147
  79.0 1.3 collective-permute-start.11
  80.3 1.3 collective-permute-start.12
  81.6 1.3 collective-permute-start.13
  82.9 6.0 %collective-permute-done.11 = f32[2,2,6,512]{3,2,1,0:T(8,128)S(1)} collective-permute-done((f32[2,2,6,512]{3,2,1,0:T(8,128)}, f32[2,2,6,512]{3,2,1,0:T(8,128)S(1)}, u32[]{:S(2)}, u32[]{:S(2)}) %collective-permute-start.11) | collective-permute-done | bytes 49184 | tf_op jit(solution)/shard_map/ppermute | solution.py:28
  89.2 14.9 %collective-permute-done.12 = f32[2,2,6,512]{3,2,1,0:T(8,128)S(1)} collective-permute-done((f32[2,2,6,512]{3,2,1,0:T(8,128)}, f32[2,2,6,512]{3,2,1,0:T(8,128)S(1)}, u32[]{:S(2)}, u32[]{:S(2)}) %collective-permute-start.12) | collective-permute-done | bytes 49184 | tf_op jit(solution)/shard_map/ppermute | solution.py:28
  104.5 0.6 fusion.16.refs_4_
  105.2 3.7 %shard_map.145 = (f32[8,2,6,512]{3,2,1,0:T(8,128)}, f32[2,1,2,6,512]{4,3,2,1,0:T(8,128)}) custom-call(f32[8,2,6,512]{3,2,1,0:T(8,128)} %get-tuple-element.11.refs_0_, f32[8,2,6,6,512]{4,3,2,1,0:T(8,128)} %copy.233.refs_0_.refs_1_, f32[8,2,6,6,512]{4,3,2,1,0:T(8,128)} %copy.234.refs_1_.refs_2_, f32[8,2,6,6,512]{4,3,2,1,0:T(8,128)} %copy.235.refs_2_.refs_3_, ...), custom_call_target="tpu_custom_call" | custom-call | tf_op jit(solution)/shard_map/pallas_call | solution.py:147
  108.9 1.1 add_multiply_fusion.1
  109.9 1.3 collective-permute-start.14
  111.2 4.5 %collective-permute-start.15 = (f32[1,2,6,512]{3,2,1,0:T(8,128)S(1)}, f32[1,2,6,512]{3,2,1,0:T(8,128)S(1)}, u32[]{:S(2)}, u32[]{:S(2)}) collective-permute-start(f32[1,2,6,512]{3,2,1,0:T(8,128)S(1)} %get-tuple-element.31), channel_id=1, source_target_pairs={{0,4},{4,8},{8,12},{1,5},{5,9},{9,13},{2,6},{6,10},{10,14},{3,7},{... | collective-permute-start | bytes 73736 | tf_op jit(solution)/shard_map/ppermute | solution.py:19
  115.9 1.3 collective-permute-start.16
  117.2 3.2 %collective-permute-start.17 = (f32[8,2,6,32]{3,2,1,0:T(8,128)S(1)}, f32[8,2,6,32]{3,2,1,0:T(8,128)S(1)}, u32[]{:S(2)}, u32[]{:S(2)}) collective-permute-start(f32[8,2,6,32]{3,2,1,0:T(8,128)S(1)} %get-tuple-element.33), channel_id=1, source_target_pairs={{0,1},{1,2},{2,3},{4,5},{5,6},{6,7},{8,9},{9,10},{10,11},{12,13},{... | collective-permute-start | bytes 36872 | tf_op jit(solution)/shard_map/ppermute | solution.py:19
  120.4 0.7 collective-permute-done.17
  121.7 0.8 convolution_bitcast_fusion
  123.6 0.8 copy.245.refs_0_
  124.4 3.1 %shard_map.146 = (f32[8,2,6,512]{3,2,1,0:T(8,128)}, f32[2,1,2,6,512]{4,3,2,1,0:T(8,128)}) custom-call(f32[8,2,6,512]{3,2,1,0:T(8,128)} %copy.245.refs_0_, f32[8,2,6,6,512]{4,3,2,1,0:T(8,128)} %get-tuple-element.39.refs_0_.refs_1_, f32[8,2,6,6,512]{4,3,2,1,0:T(8,128)} %get-tuple-element.38.refs_1_.refs_2_, f32[2,1,2,6,512]{4,3,2,1,0:T(8,128)} %broadcast_in_dim.10.refs_3_.refs_4_), custom_call_target="tpu_custom_call" | custom-call | tf_op jit(solution)/shard_map/pallas_call | solution.py:97
  127.5 1.5 collective-permute-start.18
  129.0 2.2 %collective-permute-start.19 = (f32[2,2,6,512]{3,2,1,0:T(8,128)}, f32[2,2,6,512]{3,2,1,0:T(8,128)S(1)}, u32[]{:S(2)}, u32[]{:S(2)}) collective-permute-start(f32[2,2,6,512]{3,2,1,0:T(8,128)} %bitcast.97), channel_id=1, source_target_pairs={{0,8},{4,12},{1,9},{5,13},{2,10},{6,14},{3,11},{7,15},{16,24},{20,... | collective-permute-start | bytes 147464 | tf_op jit(solution)/shard_map/ppermute | solution.py:28
  131.2 1.8 %collective-permute-start.20 = (f32[2,2,6,512]{3,2,1,0:T(8,128)}, f32[2,2,6,512]{3,2,1,0:T(8,128)S(1)}, u32[]{:S(2)}, u32[]{:S(2)}) collective-permute-start(f32[2,2,6,512]{3,2,1,0:T(8,128)} %bitcast.98), channel_id=1, source_target_pairs={{0,4},{4,8},{8,12},{1,5},{5,9},{9,13},{2,6},{6,10},{10,14},{3,7},{... | collective-permute-start | bytes 147464 | tf_op jit(solution)/shard_map/ppermute | solution.py:28
  133.1 1.3 multiply_reduce_fusion.6
  134.8 0.9 collective-permute-done.20
  135.6 0.6 fusion.14.refs_3_
  136.3 3.1 %shard_map.147 = (f32[8,2,6,512]{3,2,1,0:T(8,128)}, f32[2,1,2,6,512]{4,3,2,1,0:T(8,128)}) custom-call(f32[8,2,6,512]{3,2,1,0:T(8,128)} %copy.245.refs_0_, f32[8,2,6,6,512]{4,3,2,1,0:T(8,128)} %get-tuple-element.39.refs_0_.refs_1_, f32[8,2,6,6,512]{4,3,2,1,0:T(8,128)} %get-tuple-element.38.refs_1_.refs_2_, f32[2,1,2,6,512]{4,3,2,1,0:T(8,128)} %fusion.14.refs_3_), custom_call_target="tpu_custom_call" | custom-call | tf_op jit(solution)/shard_map/pallas_call | solution.py:97
  139.4 3.7 %shard_map.148 = (f32[8,2,6,512]{3,2,1,0:T(8,128)}, f32[2,1,2,6,512]{4,3,2,1,0:T(8,128)}) custom-call(f32[8,2,6,512]{3,2,1,0:T(8,128)} %get-tuple-element.15.refs_0_, f32[8,2,6,6,512]{4,3,2,1,0:T(8,128)} %copy.233.refs_0_.refs_1_, f32[8,2,6,6,512]{4,3,2,1,0:T(8,128)} %copy.234.refs_1_.refs_2_, f32[8,2,6,6,512]{4,3,2,1,0:T(8,128)} %copy.235.refs_2_.refs_3_, ...), custom_call_target="tpu_custom_call" | custom-call | tf_op jit(solution)/shard_map/pallas_call | solution.py:147
  143.1 1.4 collective-permute-start.21
  144.8 1.3 collective-permute-start.22
  146.1 1.3 collective-permute-start.23
  147.4 4.2 %collective-permute-done.21 = f32[2,2,6,512]{3,2,1,0:T(8,128)S(1)} collective-permute-done((f32[2,2,6,512]{3,2,1,0:T(8,128)}, f32[2,2,6,512]{3,2,1,0:T(8,128)S(1)}, u32[]{:S(2)}, u32[]{:S(2)}) %collective-permute-start.21) | collective-permute-done | bytes 49184 | tf_op jit(solution)/shard_map/ppermute | solution.py:28
  151.9 2.4 %collective-permute-done.22 = f32[2,2,6,512]{3,2,1,0:T(8,128)S(1)} collective-permute-done((f32[2,2,6,512]{3,2,1,0:T(8,128)}, f32[2,2,6,512]{3,2,1,0:T(8,128)S(1)}, u32[]{:S(2)}, u32[]{:S(2)}) %collective-permute-start.22) | collective-permute-done | bytes 49184 | tf_op jit(solution)/shard_map/ppermute | solution.py:28
  154.7 0.6 fusion.12.refs_4_
  155.3 3.6 %shard_map.149 = (f32[8,2,6,512]{3,2,1,0:T(8,128)}, f32[2,1,2,6,512]{4,3,2,1,0:T(8,128)}) custom-call(f32[8,2,6,512]{3,2,1,0:T(8,128)} %get-tuple-element.15.refs_0_, f32[8,2,6,6,512]{4,3,2,1,0:T(8,128)} %copy.233.refs_0_.refs_1_, f32[8,2,6,6,512]{4,3,2,1,0:T(8,128)} %copy.234.refs_1_.refs_2_, f32[8,2,6,6,512]{4,3,2,1,0:T(8,128)} %copy.235.refs_2_.refs_3_, ...), custom_call_target="tpu_custom_call" | custom-call | tf_op jit(solution)/shard_map/pallas_call | solution.py:147
  159.0 1.1 multiply_bitcast_fusion
  160.6 1.6 collective-permute-start.24
  162.2 0.8 copy.256
  163.0 1.8 %collective-permute-done.24 = f32[8,3,512]{2,0,1:T(8,128)S(1)} collective-permute-done((f32[8,3,512]{2,0,1:T(8,128)S(1)}, f32[8,3,512]{2,0,1:T(8,128)S(1)}, u32[]{:S(2)}, u32[]{:S(2)}) %collective-permute-start.24) | collective-permute-done | bytes 49184 | tf_op jit(solution)/shard_map/ppermute | solution.py:235
  164.8 0.6 fusion.27
  (95 shorter events, 6.3 us)
Async XLA Ops:
  0.6 33.5 %copy-start = (f32[2,6,32,32]{3,2,1,0:T(8,128)S(1)}, f32[2,6,32,32]{3,2,1,0:T(8,128)}, u32[]{:S(2)}) copy-start(f32[2,6,32,32]{3,2,1,0:T(8,128)} %param.21) | copy-start | bytes 147460
  1.8 30.4 %collective-permute-start.2 = (f32[8,2,6,32]{3,2,1,0:T(8,128)S(1)}, f32[8,2,6,32]{3,2,1,0:T(8,128)S(1)}, u32[]{:S(2)}, u32[]{:S(2)}) collective-permute-start(f32[8,2,6,32]{3,2,1,0:T(8,128)S(1)} %get-tuple-element.36), channel_id=1, source_target_pairs={{1,0},{2,1},{3,2},{5,4},{6,5},{7,6},{9,8},{10,9},{11,10},{13,12},{... | collective-permute-start | bytes 36872 | tf_op jit(solution)/shard_map/ppermute | solution.py:20
  3.0 30.4 %collective-permute-start.3 = (f32[8,2,6,32]{3,2,1,0:T(8,128)S(1)}, f32[8,2,6,32]{3,2,1,0:T(8,128)S(1)}, u32[]{:S(2)}, u32[]{:S(2)}) collective-permute-start(f32[8,2,6,32]{3,2,1,0:T(8,128)S(1)} %get-tuple-element.37), channel_id=1, source_target_pairs={{0,1},{1,2},{2,3},{4,5},{5,6},{6,7},{8,9},{9,10},{10,11},{12,13},{... | collective-permute-start | bytes 36872 | tf_op jit(solution)/shard_map/ppermute | solution.py:19
  6.1 27.4 %collective-permute-start = (f32[1,2,6,512]{3,2,1,0:T(8,128)S(1)}, f32[1,2,6,512]{3,2,1,0:T(8,128)S(1)}, u32[]{:S(2)}, u32[]{:S(2)}) collective-permute-start(f32[1,2,6,512]{3,2,1,0:T(8,128)S(1)} %get-tuple-element.34), channel_id=1, source_target_pairs={{4,0},{8,4},{12,8},{5,1},{9,5},{13,9},{6,2},{10,6},{14,10},{7,3},{... | collective-permute-start | bytes 73736 | tf_op jit(solution)/shard_map/ppermute | solution.py:20
  7.4 26.1 %collective-permute-start.1 = (f32[1,2,6,512]{3,2,1,0:T(8,128)S(1)}, f32[1,2,6,512]{3,2,1,0:T(8,128)S(1)}, u32[]{:S(2)}, u32[]{:S(2)}) collective-permute-start(f32[1,2,6,512]{3,2,1,0:T(8,128)S(1)} %get-tuple-element.35), channel_id=1, source_target_pairs={{0,4},{4,8},{8,12},{1,5},{5,9},{9,13},{2,6},{6,10},{10,14},{3,7},{... | collective-permute-start | bytes 73736 | tf_op jit(solution)/shard_map/ppermute | solution.py:19
  23.9 9.6 %copy-start.11 = (f32[8,2,6,512]{3,1,2,0:T(2,128)S(1)}, f32[8,2,6,512]{3,1,2,0:T(2,128)}, u32[]{:S(2)}) copy-start(f32[8,2,6,512]{3,1,2,0:T(2,128)} %param.14) | copy-start | bytes 589828
  26.4 39.4 %collective-permute-start.5 = (f32[2,12,2,6,512]{4,2,3,1,0:T(2,128)}, f32[2,12,2,6,512]{4,2,3,1,0:T(2,128)}, u32[]{:S(2)}, u32[]{:S(2)}) collective-permute-start(f32[2,12,2,6,512]{4,2,3,1,0:T(2,128)} %copy.213), channel_id=1, source_target_pairs={{0,8},{4,12},{1,9},{5,13},{2,10},{6,14},{3,11},{7,15},{16,24},{20,... | collective-permute-start | bytes 1769480 | tf_op jit(solution)/shard_map/ppermute | solution.py:28
  32.2 39.0 %collective-permute-start.4 = (f32[2,12,2,6,512]{4,2,3,1,0:T(2,128)}, f32[2,12,2,6,512]{4,2,3,1,0:T(2,128)S(1)}, u32[]{:S(2)}, u32[]{:S(2)}) collective-permute-start(f32[2,12,2,6,512]{4,2,3,1,0:T(2,128)} %copy.213), channel_id=1, source_target_pairs={{0,4},{4,8},{8,12},{1,5},{5,9},{9,13},{2,6},{6,10},{10,14},{3,7},{... | collective-permute-start | bytes 1769480 | tf_op jit(solution)/shard_map/ppermute | solution.py:28
  34.1 1.3 copy-start.1
  37.4 4.6 %copy-start.8 = (f32[8,2,6,6,512]{4,1,3,2,0:T(2,128)S(1)}, f32[8,2,6,6,512]{4,1,3,2,0:T(2,128)}, u32[]{:S(2)}) copy-start(f32[8,2,6,6,512]{4,1,3,2,0:T(2,128)} %param.17) | copy-start | bytes 3538948
  40.6 2.9 %copy-start.9 = (f32[8,2,6,6,512]{4,1,3,2,0:T(2,128)S(1)}, f32[8,2,6,6,512]{4,1,3,2,0:T(2,128)}, u32[]{:S(2)}) copy-start(f32[8,2,6,6,512]{4,1,3,2,0:T(2,128)} %param.18) | copy-start | bytes 3538948
  40.6 19.0 %collective-permute-start.6 = (f32[2,2,6,512]{3,2,1,0:T(8,128)}, f32[2,2,6,512]{3,2,1,0:T(8,128)S(1)}, u32[]{:S(2)}, u32[]{:S(2)}) collective-permute-start(f32[2,2,6,512]{3,2,1,0:T(8,128)} %bitcast.87), channel_id=1, source_target_pairs={{0,12},{1,13},{2,14},{3,15},{16,28},{17,29},{18,30},{19,31}} | collective-permute-start | bytes 147464 | tf_op jit(solution)/shard_map/ppermute | solution.py:28
  43.5 1.4 copy-start.10
  54.5 5.0 %copy-start.16 = (f32[2,1,2,6,512]{4,3,2,1,0:T(8,128)S(1)}, f32[2,1,2,6,512]{4,3,2,1,0:T(8,128)}, u32[]{:S(2)}) copy-start(f32[2,1,2,6,512]{4,3,2,1,0:T(8,128)} %get-tuple-element.10) | copy-start | bytes 147460
  57.0 32.0 %collective-permute-start.10 = (f32[2,12,2,6,512]{4,2,3,1,0:T(2,128)}, f32[2,12,2,6,512]{4,2,3,1,0:T(2,128)S(1)}, u32[]{:S(2)}, u32[]{:S(2)}) collective-permute-start(f32[2,12,2,6,512]{4,2,3,1,0:T(2,128)} %copy.224), channel_id=1, source_target_pairs={{8,0},{12,4},{9,1},{13,5},{10,2},{14,6},{11,3},{15,7},{24,16},{28,... | collective-permute-start | bytes 1769480 | tf_op jit(solution)/shard_map/ppermute | solution.py:28
  58.3 46.0 %collective-permute-start.9 = (f32[2,12,2,6,512]{4,2,3,1,0:T(2,128)}, f32[2,12,2,6,512]{4,2,3,1,0:T(2,128)S(1)}, u32[]{:S(2)}, u32[]{:S(2)}) collective-permute-start(f32[2,12,2,6,512]{4,2,3,1,0:T(2,128)} %copy.224), channel_id=1, source_target_pairs={{4,0},{8,4},{12,8},{5,1},{9,5},{13,9},{6,2},{10,6},{14,10},{7,3},{... | collective-permute-start | bytes 1769480 | tf_op jit(solution)/shard_map/ppermute | solution.py:28
  59.6 11.5 %collective-permute-start.7 = (f32[2,2,6,512]{3,2,1,0:T(8,128)S(1)}, f32[2,2,6,512]{3,2,1,0:T(8,128)S(1)}, u32[]{:S(2)}, u32[]{:S(2)}) collective-permute-start(f32[2,2,6,512]{3,2,1,0:T(8,128)S(1)} %bitcast.88), channel_id=1, source_target_pairs={{0,8},{4,12},{1,9},{5,13},{2,10},{6,14},{3,11},{7,15},{16,24},{20,... | collective-permute-start | bytes 147464 | tf_op jit(solution)/shard_map/ppermute | solution.py:28
  65.8 5.8 %collective-permute-start.8 = (f32[2,2,6,512]{3,2,1,0:T(8,128)S(1)}, f32[2,2,6,512]{3,2,1,0:T(8,128)S(1)}, u32[]{:S(2)}, u32[]{:S(2)}) collective-permute-start(f32[2,2,6,512]{3,2,1,0:T(8,128)S(1)} %bitcast.89), channel_id=1, source_target_pairs={{0,4},{4,8},{8,12},{1,5},{5,9},{9,13},{2,6},{6,10},{10,14},{3,7},{... | collective-permute-start | bytes 147464 | tf_op jit(solution)/shard_map/ppermute | solution.py:28
  71.2 4.2 %copy-start.2 = (f32[2,12,2,6,512]{4,2,3,1,0:T(2,128)}, f32[2,12,2,6,512]{4,2,3,1,0:T(2,128)S(1)}, u32[]{:S(2)}) copy-start(f32[2,12,2,6,512]{4,2,3,1,0:T(2,128)S(1)} %collective-permute-done.4) | copy-start | bytes 1769476
  75.4 5.0 %copy-start.15 = (s32[8,512]{1,0:T(8,128)S(1)}, s32[8,512]{1,0:T(8,128)}, u32[]{:S(2)}) copy-start(s32[8,512]{1,0:T(8,128)} %param.23) | copy-start | bytes 49156
  79.0 9.9 %collective-permute-start.11 = (f32[2,2,6,512]{3,2,1,0:T(8,128)}, f32[2,2,6,512]{3,2,1,0:T(8,128)S(1)}, u32[]{:S(2)}, u32[]{:S(2)}) collective-permute-start(f32[2,2,6,512]{3,2,1,0:T(8,128)} %bitcast.90), channel_id=1, source_target_pairs={{12,0},{13,1},{14,2},{15,3},{28,16},{29,17},{30,18},{31,19}} | collective-permute-start | bytes 147464 | tf_op jit(solution)/shard_map/ppermute | solution.py:28
  80.3 23.8 %collective-permute-start.12 = (f32[2,2,6,512]{3,2,1,0:T(8,128)}, f32[2,2,6,512]{3,2,1,0:T(8,128)S(1)}, u32[]{:S(2)}, u32[]{:S(2)}) collective-permute-start(f32[2,2,6,512]{3,2,1,0:T(8,128)} %bitcast.91), channel_id=1, source_target_pairs={{8,0},{12,4},{9,1},{13,5},{10,2},{14,6},{11,3},{15,7},{24,16},{28,... | collective-permute-start | bytes 147464 | tf_op jit(solution)/shard_map/ppermute | solution.py:28
  81.6 22.9 %collective-permute-start.13 = (f32[2,2,6,512]{3,2,1,0:T(8,128)}, f32[2,2,6,512]{3,2,1,0:T(8,128)S(1)}, u32[]{:S(2)}, u32[]{:S(2)}) collective-permute-start(f32[2,2,6,512]{3,2,1,0:T(8,128)} %bitcast.92), channel_id=1, source_target_pairs={{4,0},{8,4},{12,8},{5,1},{9,5},{13,9},{6,2},{10,6},{14,10},{7,3},{... | collective-permute-start | bytes 147464 | tf_op jit(solution)/shard_map/ppermute | solution.py:28
  89.0 19.9 %copy-start.6 = (f32[2,12,2,6,512]{4,2,3,1,0:T(2,128)}, f32[2,12,2,6,512]{4,2,3,1,0:T(2,128)S(1)}, u32[]{:S(2)}) copy-start(f32[2,12,2,6,512]{4,2,3,1,0:T(2,128)S(1)} %collective-permute-done.10) | copy-start | bytes 1769476
  104.2 4.6 %copy-start.4 = (f32[2,12,2,6,512]{4,2,3,1,0:T(2,128)}, f32[2,12,2,6,512]{4,2,3,1,0:T(2,128)S(1)}, u32[]{:S(2)}) copy-start(f32[2,12,2,6,512]{4,2,3,1,0:T(2,128)S(1)} %collective-permute-done.9) | copy-start | bytes 1769476
  105.2 3.7 %copy-start.13 = (f32[8,2,6,512]{3,1,2,0:T(2,128)S(1)}, f32[8,2,6,512]{3,1,2,0:T(2,128)}, u32[]{:S(2)}) copy-start(f32[8,2,6,512]{3,1,2,0:T(2,128)} %param.13) | copy-start | bytes 589828
  108.8 12.3 %copy-start.12 = (f32[8,2,6,512]{3,1,2,0:T(2,128)S(1)}, f32[8,2,6,512]{3,1,2,0:T(2,128)}, u32[]{:S(2)}) copy-start(f32[8,2,6,512]{3,1,2,0:T(2,128)} %param.14) | copy-start | bytes 589828
  109.9 11.2 %collective-permute-start.14 = (f32[1,2,6,512]{3,2,1,0:T(8,128)S(1)}, f32[1,2,6,512]{3,2,1,0:T(8,128)S(1)}, u32[]{:S(2)}, u32[]{:S(2)}) collective-permute-start(f32[1,2,6,512]{3,2,1,0:T(8,128)S(1)} %get-tuple-element.30), channel_id=1, source_target_pairs={{4,0},{8,4},{12,8},{5,1},{9,5},{13,9},{6,2},{10,6},{14,10},{7,3},{... | collective-permute-start | bytes 73736 | tf_op jit(solution)/shard_map/ppermute | solution.py:20
  111.2 9.9 %collective-permute-start.15 = (f32[1,2,6,512]{3,2,1,0:T(8,128)S(1)}, f32[1,2,6,512]{3,2,1,0:T(8,128)S(1)}, u32[]{:S(2)}, u32[]{:S(2)}) collective-permute-start(f32[1,2,6,512]{3,2,1,0:T(8,128)S(1)} %get-tuple-element.31), channel_id=1, source_target_pairs={{0,4},{4,8},{8,12},{1,5},{5,9},{9,13},{2,6},{6,10},{10,14},{3,7},{... | collective-permute-start | bytes 73736 | tf_op jit(solution)/shard_map/ppermute | solution.py:19
  115.9 4.5 %collective-permute-start.16 = (f32[8,2,6,32]{3,2,1,0:T(8,128)S(1)}, f32[8,2,6,32]{3,2,1,0:T(8,128)S(1)}, u32[]{:S(2)}, u32[]{:S(2)}) collective-permute-start(f32[8,2,6,32]{3,2,1,0:T(8,128)S(1)} %get-tuple-element.32), channel_id=1, source_target_pairs={{1,0},{2,1},{3,2},{5,4},{6,5},{7,6},{9,8},{10,9},{11,10},{13,12},{... | collective-permute-start | bytes 36872 | tf_op jit(solution)/shard_map/ppermute | solution.py:20
  117.2 3.9 %collective-permute-start.17 = (f32[8,2,6,32]{3,2,1,0:T(8,128)S(1)}, f32[8,2,6,32]{3,2,1,0:T(8,128)S(1)}, u32[]{:S(2)}, u32[]{:S(2)}) collective-permute-start(f32[8,2,6,32]{3,2,1,0:T(8,128)S(1)} %get-tuple-element.33), channel_id=1, source_target_pairs={{0,1},{1,2},{2,3},{4,5},{5,6},{6,7},{8,9},{9,10},{10,11},{12,13},{... | collective-permute-start | bytes 36872 | tf_op jit(solution)/shard_map/ppermute | solution.py:19
  127.5 7.0 %copy-start.3 = (f32[2,12,2,6,512]{4,2,3,1,0:T(2,128)S(1)}, f32[2,12,2,6,512]{4,2,3,1,0:T(2,128)}, u32[]{:S(2)}) copy-start(f32[2,12,2,6,512]{4,2,3,1,0:T(2,128)} %copy-done.2) | copy-start | bytes 1769476
  127.5 5.6 %collective-permute-start.18 = (f32[2,2,6,512]{3,2,1,0:T(8,128)}, f32[2,2,6,512]{3,2,1,0:T(8,128)S(1)}, u32[]{:S(2)}, u32[]{:S(2)}) collective-permute-start(f32[2,2,6,512]{3,2,1,0:T(8,128)} %bitcast.96), channel_id=1, source_target_pairs={{0,12},{1,13},{2,14},{3,15},{16,28},{17,29},{18,30},{19,31}} | collective-permute-start | bytes 147464 | tf_op jit(solution)/shard_map/ppermute | solution.py:28
  129.0 5.5 %collective-permute-start.19 = (f32[2,2,6,512]{3,2,1,0:T(8,128)}, f32[2,2,6,512]{3,2,1,0:T(8,128)S(1)}, u32[]{:S(2)}, u32[]{:S(2)}) collective-permute-start(f32[2,2,6,512]{3,2,1,0:T(8,128)} %bitcast.97), channel_id=1, source_target_pairs={{0,8},{4,12},{1,9},{5,13},{2,10},{6,14},{3,11},{7,15},{16,24},{20,... | collective-permute-start | bytes 147464 | tf_op jit(solution)/shard_map/ppermute | solution.py:28
  131.2 4.4 %collective-permute-start.20 = (f32[2,2,6,512]{3,2,1,0:T(8,128)}, f32[2,2,6,512]{3,2,1,0:T(8,128)S(1)}, u32[]{:S(2)}, u32[]{:S(2)}) collective-permute-start(f32[2,2,6,512]{3,2,1,0:T(8,128)} %bitcast.98), channel_id=1, source_target_pairs={{0,4},{4,8},{8,12},{1,5},{5,9},{9,13},{2,6},{6,10},{10,14},{3,7},{... | collective-permute-start | bytes 147464 | tf_op jit(solution)/shard_map/ppermute | solution.py:28
  139.4 5.2 %copy-start.17 = (f32[8]{0:T(128)S(1)}, f32[8]{0:T(128)}, u32[]{:S(2)}) copy-start(f32[8]{0:T(128)} %param.25) | copy-start | bytes 100
  139.4 5.2 %copy-start.18 = (s32[2]{0:T(128)S(1)}, s32[2]{0:T(128)}, u32[]{:S(2)}) copy-start(s32[2]{0:T(128)} %param.24) | copy-start | bytes 28
  139.4 12.3 %copy-start.7 = (f32[2,12,2,6,512]{4,2,3,1,0:T(2,128)S(1)}, f32[2,12,2,6,512]{4,2,3,1,0:T(2,128)}, u32[]{:S(2)}) copy-start(f32[2,12,2,6,512]{4,2,3,1,0:T(2,128)} %copy-done.6) | copy-start | bytes 1769476
  143.1 11.3 %copy-start.5 = (f32[2,12,2,6,512]{4,2,3,1,0:T(2,128)S(1)}, f32[2,12,2,6,512]{4,2,3,1,0:T(2,128)}, u32[]{:S(2)}) copy-start(f32[2,12,2,6,512]{4,2,3,1,0:T(2,128)} %copy-done.4) | copy-start | bytes 1769476
  143.1 8.5 %collective-permute-start.21 = (f32[2,2,6,512]{3,2,1,0:T(8,128)}, f32[2,2,6,512]{3,2,1,0:T(8,128)S(1)}, u32[]{:S(2)}, u32[]{:S(2)}) collective-permute-start(f32[2,2,6,512]{3,2,1,0:T(8,128)} %bitcast.93), channel_id=1, source_target_pairs={{12,0},{13,1},{14,2},{15,3},{28,16},{29,17},{30,18},{31,19}} | collective-permute-start | bytes 147464 | tf_op jit(solution)/shard_map/ppermute | solution.py:28
  144.8 9.6 %collective-permute-start.22 = (f32[2,2,6,512]{3,2,1,0:T(8,128)}, f32[2,2,6,512]{3,2,1,0:T(8,128)S(1)}, u32[]{:S(2)}, u32[]{:S(2)}) collective-permute-start(f32[2,2,6,512]{3,2,1,0:T(8,128)} %bitcast.94), channel_id=1, source_target_pairs={{8,0},{12,4},{9,1},{13,5},{10,2},{14,6},{11,3},{15,7},{24,16},{28,... | collective-permute-start | bytes 147464 | tf_op jit(solution)/shard_map/ppermute | solution.py:28
  146.1 8.6 %collective-permute-start.23 = (f32[2,2,6,512]{3,2,1,0:T(8,128)}, f32[2,2,6,512]{3,2,1,0:T(8,128)S(1)}, u32[]{:S(2)}, u32[]{:S(2)}) collective-permute-start(f32[2,2,6,512]{3,2,1,0:T(8,128)} %bitcast.95), channel_id=1, source_target_pairs={{4,0},{8,4},{12,8},{5,1},{9,5},{13,9},{6,2},{10,6},{14,10},{7,3},{... | collective-permute-start | bytes 147464 | tf_op jit(solution)/shard_map/ppermute | solution.py:28
  159.0 1.3 copy-start.14
  160.6 4.2 %collective-permute-start.24 = (f32[8,3,512]{2,0,1:T(8,128)S(1)}, f32[8,3,512]{2,0,1:T(8,128)S(1)}, u32[]{:S(2)}, u32[]{:S(2)}) collective-permute-start(f32[8,3,512]{2,0,1:T(8,128)S(1)} %bitcast.86), channel_id=1, source_target_pairs={{0,16},{16,0},{1,17},{17,1},{2,18},{18,2},{3,19},{19,3},{4,20},{20... | collective-permute-start | bytes 147464 | tf_op jit(solution)/shard_map/ppermute | solution.py:235

commit v5 on v4

--- a/solution.py
+++ b/solution.py
@@ -216,6 +216,8 @@
             "icvjq,cvqk->icvjk", grid, z_inverse, precision=lax.Precision.HIGHEST
         ).reshape(rhs.shape)
         yres = jnp.sum(y_inverse * zres[..., :, None, :], axis=-3)
+        if step == 0:
+            yres, _ = lax.optimization_barrier((yres, reverse_matrix))
         _, offset = upper_pallas(yres, near_t, far_t, zeros, True)
         entering = gathered_carry(offset[:, 0], upper_products, 1)
         upper, _ = upper_pallas(yres, near_t, far_t, entering[:, None], True)

time: 166 us -> 167 us (level)
    unnamed x44 -> x46, local copies, waits for them, and re-layouts: 6.39 us -> 6.39 us
  transfers between devices with their start and end apart: 25 -> 25, of which waited for: 8 -> 10; matrix products, arithmetic and copies ran while one was open for 14% -> 14% of each run, Pallas kernels for 15% -> 15%
where the time goes in v5:
time: 167 us; the launch traced here: 166 us
  starting transfers between devices  57.2 us (34%)
  Pallas kernels  42.3 us (25%)
  waiting for transfers between devices  31.8 us (19%)
  local copies, waits for them, and re-layouts  19.8 us (12%)
  other arithmetic  12.5 us (7%)
    ppermute x16, starting transfers between devices, from_behind(): lax.ppermute(value, axis, [(source, source + steps) for source in range(f...  33.5 us
    ppermute x16, waiting for transfers between devices, from_behind(): lax.ppermute(value, axis, [(source, source + steps) for source in range(f...  29.3 us
    pallas_call x5, Pallas kernels, lower_pallas(): pl.pallas_call(kernel, out_shape=tuple(out_shape), in_specs=_vmem_specs(l...  22.8 us
    pallas_call x5, Pallas kernels, upper_pallas(): pl.pallas_call(kernel, out_shape=tuple(out_shape), in_specs=_vmem_specs(l...  19.4 us
    ppermute x4, starting transfers between devices, extended(): before = lax.ppermute(last, axis, up)  17 us
    unnamed x46, local copies, waits for them, and re-layouts  6.39 us
    ppermute x4, starting transfers between devices, extended(): after = lax.ppermute(first, axis, down)  5.14 us
    reduce_sum x8, other arithmetic, carry_through(): return jnp.sum(jnp.sum(split * inputs, axis=2), axis=1)  4.17 us
  transfers between devices with their start and end apart: 25, of which 10 were waited for; matrix products, arithmetic and copies ran while one was open for 14% of the time, Pallas kernels for 15%

profile of v5, /device:TPU:0, one launch (start us, length us, event | category | flops | bytes accessed | tf_op | source)
XLA Modules:
  0.0 166.4 jit_solution(14359898351010124149)
XLA Ops:
  0.6 1.0 copy.236
  1.7 0.7 fusion.24
  2.4 1.3 collective-permute-start.2
  3.7 3.0 %collective-permute-start.3 = (f32[8,2,6,32]{3,2,1,0:T(8,128)}, f32[8,2,6,32]{3,2,1,0:T(8,128)S(1)}, u32[]{:S(2)}, u32[]{:S(2)}) collective-permute-start(f32[8,2,6,32]{3,2,1,0:T(8,128)} %get-tuple-element.39), channel_id=1, source_target_pairs={{0,1},{1,2},{2,3},{4,5},{5,6},{6,7},{8,9},{9,10},{10,11},{12,13},{... | collective-permute-start | bytes 36872 | tf_op jit(solution)/shard_map/ppermute | solution.py:19
  7.3 1.3 collective-permute-start
  8.6 6.2 %collective-permute-start.1 = (f32[1,2,6,512]{3,2,1,0:T(8,128)}, f32[1,2,6,512]{3,2,1,0:T(8,128)}, u32[]{:S(2)}, u32[]{:S(2)}) collective-permute-start(f32[1,2,6,512]{3,2,1,0:T(8,128)} %get-tuple-element.37), channel_id=1, source_target_pairs={{0,4},{4,8},{8,12},{1,5},{5,9},{9,13},{2,6},{6,10},{10,14},{3,7},{... | collective-permute-start | bytes 73736 | tf_op jit(solution)/shard_map/ppermute | solution.py:19
  14.8 4.0 %copy_bitcast_fusion = (f32[8,2,6,6,512]{4,3,2,1,0:T(8,128)}, f32[8,2,6,6,512]{4,3,2,1,0:T(8,128)}) fusion(f32[8,2,6,6,512]{4,1,3,2,0:T(2,128)} %param.16, f32[8,2,6,6,512]{4,1,3,2,0:T(2,128)} %param.15), kind=kLoop, calls=%fused_computation | loop fusion | bytes 4718592 | tf_op jit(solution)/shard_map/transpose | solution.py:199
  18.8 6.9 %shard_map.141 = f32[2,12,2,6,512]{4,3,2,1,0:T(8,128)} custom-call(f32[8,2,6,6,512]{4,3,2,1,0:T(8,128)} %get-tuple-element.41.refs_0_.refs_1_, f32[8,2,6,6,512]{4,3,2,1,0:T(8,128)} %get-tuple-element.40.refs_1_.refs_2_), custom_call_target="tpu_custom_call" | custom-call | tf_op jit(solution)/shard_map/pallas_call | solution.py:97
  25.7 2.6 %copy.216 = f32[2,12,2,6,512]{4,2,3,1,0:T(2,128)} copy(f32[2,12,2,6,512]{4,3,2,1,0:T(8,128)} %shard_map.141) | data formatting | bytes 1179648 | tf_op jit(solution)/shard_map/pallas_call | solution.py:97
  28.3 5.1 %collective-permute-start.5 = (f32[2,12,2,6,512]{4,2,3,1,0:T(2,128)}, f32[2,12,2,6,512]{4,2,3,1,0:T(2,128)S(1)}, u32[]{:S(2)}, u32[]{:S(2)}) collective-permute-start(f32[2,12,2,6,512]{4,2,3,1,0:T(2,128)} %copy.216), channel_id=1, source_target_pairs={{0,8},{4,12},{1,9},{5,13},{2,10},{6,14},{3,11},{7,15},{16,24},{20,... | collective-permute-start | bytes 1769480 | tf_op jit(solution)/shard_map/ppermute | solution.py:28
  33.4 1.4 copy.211.refs_0_.refs_1_
  34.8 1.4 copy.212.refs_1_.refs_2_
  36.2 1.4 copy.213.refs_2_.refs_3_
  37.7 8.2 %shard_map.140 = f32[2,12,2,6,512]{4,3,2,1,0:T(8,128)} custom-call(f32[8,2,6,6,512]{4,3,2,1,0:T(8,128)} %copy.211.refs_0_.refs_1_, f32[8,2,6,6,512]{4,3,2,1,0:T(8,128)} %copy.212.refs_1_.refs_2_, f32[8,2,6,6,512]{4,3,2,1,0:T(8,128)} %copy.213.refs_2_.refs_3_), custom_call_target="tpu_custom_call" | custom-call | tf_op jit(solution)/shard_map/pallas_call | solution.py:147
  45.8 2.2 %collective-permute-start.4 = (f32[2,12,2,6,512]{4,2,3,1,0:T(2,128)}, f32[2,12,2,6,512]{4,2,3,1,0:T(2,128)}, u32[]{:S(2)}, u32[]{:S(2)}) collective-permute-start(f32[2,12,2,6,512]{4,2,3,1,0:T(2,128)} %copy.216), channel_id=1, source_target_pairs={{0,4},{4,8},{8,12},{1,5},{5,9},{9,13},{2,6},{6,10},{10,14},{3,7},{... | collective-permute-start | bytes 1769480 | tf_op jit(solution)/shard_map/ppermute | solution.py:28
  48.0 1.0 fusion
  49.4 0.8 convolution_bitcast_fusion.1
  51.3 0.7 copy.223.refs_0_
  52.7 3.2 %shard_map.142 = (f32[8,2,6,512]{3,2,1,0:T(8,128)}, f32[2,1,2,6,512]{4,3,2,1,0:T(8,128)}) custom-call(f32[8,2,6,512]{3,2,1,0:T(8,128)} %copy.223.refs_0_, f32[8,2,6,6,512]{4,3,2,1,0:T(8,128)} %get-tuple-element.41.refs_0_.refs_1_, f32[8,2,6,6,512]{4,3,2,1,0:T(8,128)} %get-tuple-element.40.refs_1_.refs_2_, f32[2,1,2,6,512]{4,3,2,1,0:T(8,128)} %broadcast_in_dim.10.refs_3_.refs_4_), custom_call_target="tpu_custom_call" | custom-call | tf_op jit(solution)/shard_map/pallas_call | solution.py:97
  55.9 1.4 collective-permute-start.6
  57.3 1.3 copy.224
  58.6 1.3 collective-permute-start.10
  59.9 1.3 collective-permute-start.9
  61.2 1.1 collective-permute-done.6
  62.2 5.1 %collective-permute-start.7 = (f32[2,2,6,512]{3,2,1,0:T(8,128)S(1)}, f32[2,2,6,512]{3,2,1,0:T(8,128)S(1)}, u32[]{:S(2)}, u32[]{:S(2)}) collective-permute-start(f32[2,2,6,512]{3,2,1,0:T(8,128)S(1)} %bitcast.88), channel_id=1, source_target_pairs={{0,8},{4,12},{1,9},{5,13},{2,10},{6,14},{3,11},{7,15},{16,24},{20,... | collective-permute-start | bytes 147464 | tf_op jit(solution)/shard_map/ppermute | solution.py:28
  67.4 4.0 %collective-permute-start.8 = (f32[2,2,6,512]{3,2,1,0:T(8,128)S(1)}, f32[2,2,6,512]{3,2,1,0:T(8,128)S(1)}, u32[]{:S(2)}, u32[]{:S(2)}) collective-permute-start(f32[2,2,6,512]{3,2,1,0:T(8,128)S(1)} %bitcast.89), channel_id=1, source_target_pairs={{0,4},{4,8},{8,12},{1,5},{5,9},{9,13},{2,6},{6,10},{10,14},{3,7},{... | collective-permute-start | bytes 147464 | tf_op jit(solution)/shard_map/ppermute | solution.py:28
  71.7 1.3 multiply_reduce_fusion.9
  73.8 3.1 %shard_map.143 = (f32[8,2,6,512]{3,2,1,0:T(8,128)}, f32[2,1,2,6,512]{4,3,2,1,0:T(8,128)}) custom-call(f32[8,2,6,512]{3,2,1,0:T(8,128)} %copy.223.refs_0_, f32[8,2,6,6,512]{4,3,2,1,0:T(8,128)} %get-tuple-element.41.refs_0_.refs_1_, f32[8,2,6,6,512]{4,3,2,1,0:T(8,128)} %get-tuple-element.40.refs_1_.refs_2_, f32[2,1,2,6,512]{4,3,2,1,0:T(8,128)} %fusion.18.refs_3_), custom_call_target="tpu_custom_call" | custom-call | tf_op jit(solution)/shard_map/pallas_call | solution.py:97
  76.9 3.7 %shard_map.144 = (f32[8,2,6,512]{3,2,1,0:T(8,128)}, f32[2,1,2,6,512]{4,3,2,1,0:T(8,128)}) custom-call(f32[8,2,6,512]{3,2,1,0:T(8,128)} %get-tuple-element.13.refs_0_, f32[8,2,6,6,512]{4,3,2,1,0:T(8,128)} %copy.211.refs_0_.refs_1_, f32[8,2,6,6,512]{4,3,2,1,0:T(8,128)} %copy.212.refs_1_.refs_2_, f32[8,2,6,6,512]{4,3,2,1,0:T(8,128)} %copy.213.refs_2_.refs_3_, ...), custom_call_target="tpu_custom_call" | custom-call | tf_op jit(solution)/shard_map/pallas_call | solution.py:147
  80.6 1.3 collective-permute-start.11
  81.9 1.3 collective-permute-start.12
  83.2 1.3 collective-permute-start.13
  84.5 7.2 %collective-permute-done.11 = f32[2,2,6,512]{3,2,1,0:T(8,128)S(1)} collective-permute-done((f32[2,2,6,512]{3,2,1,0:T(8,128)}, f32[2,2,6,512]{3,2,1,0:T(8,128)S(1)}, u32[]{:S(2)}, u32[]{:S(2)}) %collective-permute-start.11) | collective-permute-done | bytes 49184 | tf_op jit(solution)/shard_map/ppermute | solution.py:28
  92.0 13.2 %collective-permute-done.12 = f32[2,2,6,512]{3,2,1,0:T(8,128)S(1)} collective-permute-done((f32[2,2,6,512]{3,2,1,0:T(8,128)}, f32[2,2,6,512]{3,2,1,0:T(8,128)S(1)}, u32[]{:S(2)}, u32[]{:S(2)}) %collective-permute-start.12) | collective-permute-done | bytes 49184 | tf_op jit(solution)/shard_map/ppermute | solution.py:28
  105.5 0.6 fusion.16.refs_4_
  106.2 3.7 %shard_map.145 = (f32[8,2,6,512]{3,2,1,0:T(8,128)}, f32[2,1,2,6,512]{4,3,2,1,0:T(8,128)}) custom-call(f32[8,2,6,512]{3,2,1,0:T(8,128)} %get-tuple-element.13.refs_0_, f32[8,2,6,6,512]{4,3,2,1,0:T(8,128)} %copy.211.refs_0_.refs_1_, f32[8,2,6,6,512]{4,3,2,1,0:T(8,128)} %copy.212.refs_1_.refs_2_, f32[8,2,6,6,512]{4,3,2,1,0:T(8,128)} %copy.213.refs_2_.refs_3_, ...), custom_call_target="tpu_custom_call" | custom-call | tf_op jit(solution)/shard_map/pallas_call | solution.py:147
  109.8 1.1 add_multiply_fusion.1
  110.9 1.3 collective-permute-start.14
  112.2 4.5 %collective-permute-start.15 = (f32[1,2,6,512]{3,2,1,0:T(8,128)S(1)}, f32[1,2,6,512]{3,2,1,0:T(8,128)S(1)}, u32[]{:S(2)}, u32[]{:S(2)}) collective-permute-start(f32[1,2,6,512]{3,2,1,0:T(8,128)S(1)} %get-tuple-element.33), channel_id=1, source_target_pairs={{0,4},{4,8},{8,12},{1,5},{5,9},{9,13},{2,6},{6,10},{10,14},{3,7},{... | collective-permute-start | bytes 73736 | tf_op jit(solution)/shard_map/ppermute | solution.py:19
  116.9 1.3 collective-permute-start.16
  118.2 3.2 %collective-permute-start.17 = (f32[8,2,6,32]{3,2,1,0:T(8,128)S(1)}, f32[8,2,6,32]{3,2,1,0:T(8,128)S(1)}, u32[]{:S(2)}, u32[]{:S(2)}) collective-permute-start(f32[8,2,6,32]{3,2,1,0:T(8,128)S(1)} %get-tuple-element.35), channel_id=1, source_target_pairs={{0,1},{1,2},{2,3},{4,5},{5,6},{6,7},{8,9},{9,10},{10,11},{12,13},{... | collective-permute-start | bytes 36872 | tf_op jit(solution)/shard_map/ppermute | solution.py:19
  121.4 0.7 collective-permute-done.17
  122.7 0.8 convolution_bitcast_fusion
  124.6 0.8 copy.245.refs_0_
  125.3 3.1 %shard_map.146 = (f32[8,2,6,512]{3,2,1,0:T(8,128)}, f32[2,1,2,6,512]{4,3,2,1,0:T(8,128)}) custom-call(f32[8,2,6,512]{3,2,1,0:T(8,128)} %copy.245.refs_0_, f32[8,2,6,6,512]{4,3,2,1,0:T(8,128)} %get-tuple-element.41.refs_0_.refs_1_, f32[8,2,6,6,512]{4,3,2,1,0:T(8,128)} %get-tuple-element.40.refs_1_.refs_2_, f32[2,1,2,6,512]{4,3,2,1,0:T(8,128)} %broadcast_in_dim.10.refs_3_.refs_4_), custom_call_target="tpu_custom_call" | custom-call | tf_op jit(solution)/shard_map/pallas_call | solution.py:97
  128.5 1.4 collective-permute-start.18
  129.8 2.2 %collective-permute-start.19 = (f32[2,2,6,512]{3,2,1,0:T(8,128)}, f32[2,2,6,512]{3,2,1,0:T(8,128)S(1)}, u32[]{:S(2)}, u32[]{:S(2)}) collective-permute-start(f32[2,2,6,512]{3,2,1,0:T(8,128)} %bitcast.97), channel_id=1, source_target_pairs={{0,8},{4,12},{1,9},{5,13},{2,10},{6,14},{3,11},{7,15},{16,24},{20,... | collective-permute-start | bytes 147464 | tf_op jit(solution)/shard_map/ppermute | solution.py:28
  132.1 1.8 %collective-permute-start.20 = (f32[2,2,6,512]{3,2,1,0:T(8,128)}, f32[2,2,6,512]{3,2,1,0:T(8,128)S(1)}, u32[]{:S(2)}, u32[]{:S(2)}) collective-permute-start(f32[2,2,6,512]{3,2,1,0:T(8,128)} %bitcast.98), channel_id=1, source_target_pairs={{0,4},{4,8},{8,12},{1,5},{5,9},{9,13},{2,6},{6,10},{10,14},{3,7},{... | collective-permute-start | bytes 147464 | tf_op jit(solution)/shard_map/ppermute | solution.py:28
  134.4 1.3 multiply_reduce_fusion.5
  135.8 0.7 collective-permute-done.20
  137.1 3.1 %shard_map.147 = (f32[8,2,6,512]{3,2,1,0:T(8,128)}, f32[2,1,2,6,512]{4,3,2,1,0:T(8,128)}) custom-call(f32[8,2,6,512]{3,2,1,0:T(8,128)} %copy.245.refs_0_, f32[8,2,6,6,512]{4,3,2,1,0:T(8,128)} %get-tuple-element.41.refs_0_.refs_1_, f32[8,2,6,6,512]{4,3,2,1,0:T(8,128)} %get-tuple-element.40.refs_1_.refs_2_, f32[2,1,2,6,512]{4,3,2,1,0:T(8,128)} %fusion.14.refs_3_), custom_call_target="tpu_custom_call" | custom-call | tf_op jit(solution)/shard_map/pallas_call | solution.py:97
  140.3 3.7 %shard_map.148 = (f32[8,2,6,512]{3,2,1,0:T(8,128)}, f32[2,1,2,6,512]{4,3,2,1,0:T(8,128)}) custom-call(f32[8,2,6,512]{3,2,1,0:T(8,128)} %get-tuple-element.17.refs_0_, f32[8,2,6,6,512]{4,3,2,1,0:T(8,128)} %copy.211.refs_0_.refs_1_, f32[8,2,6,6,512]{4,3,2,1,0:T(8,128)} %copy.212.refs_1_.refs_2_, f32[8,2,6,6,512]{4,3,2,1,0:T(8,128)} %copy.213.refs_2_.refs_3_, ...), custom_call_target="tpu_custom_call" | custom-call | tf_op jit(solution)/shard_map/pallas_call | solution.py:147
  144.0 1.4 collective-permute-start.21
  145.6 1.3 collective-permute-start.22
  146.9 1.3 collective-permute-start.23
  148.2 4.4 %collective-permute-done.21 = f32[2,2,6,512]{3,2,1,0:T(8,128)S(1)} collective-permute-done((f32[2,2,6,512]{3,2,1,0:T(8,128)}, f32[2,2,6,512]{3,2,1,0:T(8,128)S(1)}, u32[]{:S(2)}, u32[]{:S(2)}) %collective-permute-start.21) | collective-permute-done | bytes 49184 | tf_op jit(solution)/shard_map/ppermute | solution.py:28
  152.9 2.4 %collective-permute-done.22 = f32[2,2,6,512]{3,2,1,0:T(8,128)S(1)} collective-permute-done((f32[2,2,6,512]{3,2,1,0:T(8,128)}, f32[2,2,6,512]{3,2,1,0:T(8,128)S(1)}, u32[]{:S(2)}, u32[]{:S(2)}) %collective-permute-start.22) | collective-permute-done | bytes 49184 | tf_op jit(solution)/shard_map/ppermute | solution.py:28
  155.7 0.6 fusion.12.refs_4_
  156.3 3.6 %shard_map.149 = (f32[8,2,6,512]{3,2,1,0:T(8,128)}, f32[2,1,2,6,512]{4,3,2,1,0:T(8,128)}) custom-call(f32[8,2,6,512]{3,2,1,0:T(8,128)} %get-tuple-element.17.refs_0_, f32[8,2,6,6,512]{4,3,2,1,0:T(8,128)} %copy.211.refs_0_.refs_1_, f32[8,2,6,6,512]{4,3,2,1,0:T(8,128)} %copy.212.refs_1_.refs_2_, f32[8,2,6,6,512]{4,3,2,1,0:T(8,128)} %copy.213.refs_2_.refs_3_, ...), custom_call_target="tpu_custom_call" | custom-call | tf_op jit(solution)/shard_map/pallas_call | solution.py:147
  159.9 1.1 multiply_bitcast_fusion
  161.6 1.6 collective-permute-start.24
  163.1 0.8 copy.256
  164.0 1.8 %collective-permute-done.24 = f32[8,3,512]{2,0,1:T(8,128)S(1)} collective-permute-done((f32[8,3,512]{2,0,1:T(8,128)S(1)}, f32[8,3,512]{2,0,1:T(8,128)S(1)}, u32[]{:S(2)}, u32[]{:S(2)}) %collective-permute-start.24) | collective-permute-done | bytes 49184 | tf_op jit(solution)/shard_map/ppermute | solution.py:237
  165.7 0.6 fusion.27
  (97 shorter events, 8.7 us)
Async XLA Ops:
  0.6 48.8 %copy-start = (f32[2,6,32,32]{3,2,1,0:T(8,128)S(1)}, f32[2,6,32,32]{3,2,1,0:T(8,128)}, u32[]{:S(2)}) copy-start(f32[2,6,32,32]{3,2,1,0:T(8,128)} %param.21) | copy-start | bytes 147460
  2.4 43.5 %collective-permute-start.2 = (f32[8,2,6,32]{3,2,1,0:T(8,128)}, f32[8,2,6,32]{3,2,1,0:T(8,128)S(1)}, u32[]{:S(2)}, u32[]{:S(2)}) collective-permute-start(f32[8,2,6,32]{3,2,1,0:T(8,128)} %get-tuple-element.38), channel_id=1, source_target_pairs={{1,0},{2,1},{3,2},{5,4},{6,5},{7,6},{9,8},{10,9},{11,10},{13,12},{... | collective-permute-start | bytes 36872 | tf_op jit(solution)/shard_map/ppermute | solution.py:20
  3.7 44.4 %collective-permute-start.3 = (f32[8,2,6,32]{3,2,1,0:T(8,128)}, f32[8,2,6,32]{3,2,1,0:T(8,128)S(1)}, u32[]{:S(2)}, u32[]{:S(2)}) collective-permute-start(f32[8,2,6,32]{3,2,1,0:T(8,128)} %get-tuple-element.39), channel_id=1, source_target_pairs={{0,1},{1,2},{2,3},{4,5},{5,6},{6,7},{8,9},{9,10},{10,11},{12,13},{... | collective-permute-start | bytes 36872 | tf_op jit(solution)/shard_map/ppermute | solution.py:19
  7.3 40.7 %collective-permute-start = (f32[1,2,6,512]{3,2,1,0:T(8,128)}, f32[1,2,6,512]{3,2,1,0:T(8,128)}, u32[]{:S(2)}, u32[]{:S(2)}) collective-permute-start(f32[1,2,6,512]{3,2,1,0:T(8,128)} %get-tuple-element.36), channel_id=1, source_target_pairs={{4,0},{8,4},{12,8},{5,1},{9,5},{13,9},{6,2},{10,6},{14,10},{7,3},{... | collective-permute-start | bytes 73736 | tf_op jit(solution)/shard_map/ppermute | solution.py:20
  8.6 39.4 %collective-permute-start.1 = (f32[1,2,6,512]{3,2,1,0:T(8,128)}, f32[1,2,6,512]{3,2,1,0:T(8,128)}, u32[]{:S(2)}, u32[]{:S(2)}) collective-permute-start(f32[1,2,6,512]{3,2,1,0:T(8,128)} %get-tuple-element.37), channel_id=1, source_target_pairs={{0,4},{4,8},{8,12},{1,5},{5,9},{9,13},{2,6},{6,10},{10,14},{3,7},{... | collective-permute-start | bytes 73736 | tf_op jit(solution)/shard_map/ppermute | solution.py:19
  25.7 7.7 %copy-start.9 = (f32[8,2,6,6,512]{4,1,3,2,0:T(2,128)S(1)}, f32[8,2,6,6,512]{4,1,3,2,0:T(2,128)}, u32[]{:S(2)}) copy-start(f32[8,2,6,6,512]{4,1,3,2,0:T(2,128)} %param.17) | copy-start | bytes 3538948
  28.3 6.5 %copy-start.10 = (f32[8,2,6,6,512]{4,1,3,2,0:T(2,128)S(1)}, f32[8,2,6,6,512]{4,1,3,2,0:T(2,128)}, u32[]{:S(2)}) copy-start(f32[8,2,6,6,512]{4,1,3,2,0:T(2,128)} %param.18) | copy-start | bytes 3538948
  28.3 39.1 %collective-permute-start.5 = (f32[2,12,2,6,512]{4,2,3,1,0:T(2,128)}, f32[2,12,2,6,512]{4,2,3,1,0:T(2,128)S(1)}, u32[]{:S(2)}, u32[]{:S(2)}) collective-permute-start(f32[2,12,2,6,512]{4,2,3,1,0:T(2,128)} %copy.216), channel_id=1, source_target_pairs={{0,8},{4,12},{1,9},{5,13},{2,10},{6,14},{3,11},{7,15},{16,24},{20,... | collective-permute-start | bytes 1769480 | tf_op jit(solution)/shard_map/ppermute | solution.py:28
  34.8 1.4 copy-start.11
  37.7 10.4 %copy-start.12 = (f32[8,2,6,512]{3,1,2,0:T(2,128)S(1)}, f32[8,2,6,512]{3,1,2,0:T(2,128)}, u32[]{:S(2)}) copy-start(f32[8,2,6,512]{3,1,2,0:T(2,128)} %param.14) | copy-start | bytes 589828
  45.8 25.8 %collective-permute-start.4 = (f32[2,12,2,6,512]{4,2,3,1,0:T(2,128)}, f32[2,12,2,6,512]{4,2,3,1,0:T(2,128)}, u32[]{:S(2)}, u32[]{:S(2)}) collective-permute-start(f32[2,12,2,6,512]{4,2,3,1,0:T(2,128)} %copy.216), channel_id=1, source_target_pairs={{0,4},{4,8},{8,12},{1,5},{5,9},{9,13},{2,6},{6,10},{10,14},{3,7},{... | collective-permute-start | bytes 1769480 | tf_op jit(solution)/shard_map/ppermute | solution.py:28
  49.4 1.3 copy-start.1
  52.7 4.6 %copy-start.2 = (f32[2,12,2,6,512]{4,3,2,1,0:T(8,128)S(1)}, f32[2,12,2,6,512]{4,3,2,1,0:T(8,128)}, u32[]{:S(2)}) copy-start(f32[2,12,2,6,512]{4,3,2,1,0:T(8,128)} %shard_map.140) | copy-start | bytes 1769476
  55.9 6.4 %copy-start.17 = (f32[2,1,2,6,512]{4,3,2,1,0:T(8,128)S(1)}, f32[2,1,2,6,512]{4,3,2,1,0:T(8,128)}, u32[]{:S(2)}) copy-start(f32[2,1,2,6,512]{4,3,2,1,0:T(8,128)} %get-tuple-element.12) | copy-start | bytes 147460
  55.9 6.3 %collective-permute-start.6 = (f32[2,2,6,512]{3,2,1,0:T(8,128)}, f32[2,2,6,512]{3,2,1,0:T(8,128)S(1)}, u32[]{:S(2)}, u32[]{:S(2)}) collective-permute-start(f32[2,2,6,512]{3,2,1,0:T(8,128)} %bitcast.87), channel_id=1, source_target_pairs={{0,12},{1,13},{2,14},{3,15},{16,28},{17,29},{18,30},{19,31}} | collective-permute-start | bytes 147464 | tf_op jit(solution)/shard_map/ppermute | solution.py:28
  58.6 33.2 %collective-permute-start.10 = (f32[2,12,2,6,512]{4,2,3,1,0:T(2,128)}, f32[2,12,2,6,512]{4,2,3,1,0:T(2,128)S(1)}, u32[]{:S(2)}, u32[]{:S(2)}) collective-permute-start(f32[2,12,2,6,512]{4,2,3,1,0:T(2,128)} %copy.224), channel_id=1, source_target_pairs={{8,0},{12,4},{9,1},{13,5},{10,2},{14,6},{11,3},{15,7},{24,16},{28,... | collective-permute-start | bytes 1769480 | tf_op jit(solution)/shard_map/ppermute | solution.py:28
  59.9 45.4 %collective-permute-start.9 = (f32[2,12,2,6,512]{4,2,3,1,0:T(2,128)}, f32[2,12,2,6,512]{4,2,3,1,0:T(2,128)S(1)}, u32[]{:S(2)}, u32[]{:S(2)}) collective-permute-start(f32[2,12,2,6,512]{4,2,3,1,0:T(2,128)} %copy.224), channel_id=1, source_target_pairs={{4,0},{8,4},{12,8},{5,1},{9,5},{13,9},{6,2},{10,6},{14,10},{7,3},{... | collective-permute-start | bytes 1769480 | tf_op jit(solution)/shard_map/ppermute | solution.py:28
  62.2 9.4 %collective-permute-start.7 = (f32[2,2,6,512]{3,2,1,0:T(8,128)S(1)}, f32[2,2,6,512]{3,2,1,0:T(8,128)S(1)}, u32[]{:S(2)}, u32[]{:S(2)}) collective-permute-start(f32[2,2,6,512]{3,2,1,0:T(8,128)S(1)} %bitcast.88), channel_id=1, source_target_pairs={{0,8},{4,12},{1,9},{5,13},{2,10},{6,14},{3,11},{7,15},{16,24},{20,... | collective-permute-start | bytes 147464 | tf_op jit(solution)/shard_map/ppermute | solution.py:28
  67.3 9.6 %copy-start.3 = (f32[2,12,2,6,512]{4,2,3,1,0:T(2,128)}, f32[2,12,2,6,512]{4,2,3,1,0:T(2,128)S(1)}, u32[]{:S(2)}) copy-start(f32[2,12,2,6,512]{4,2,3,1,0:T(2,128)S(1)} %collective-permute-done.5) | copy-start | bytes 1769476
  67.4 5.8 %collective-permute-start.8 = (f32[2,2,6,512]{3,2,1,0:T(8,128)S(1)}, f32[2,2,6,512]{3,2,1,0:T(8,128)S(1)}, u32[]{:S(2)}, u32[]{:S(2)}) collective-permute-start(f32[2,2,6,512]{3,2,1,0:T(8,128)S(1)} %bitcast.89), channel_id=1, source_target_pairs={{0,4},{4,8},{8,12},{1,5},{5,9},{9,13},{2,6},{6,10},{10,14},{3,7},{... | collective-permute-start | bytes 147464 | tf_op jit(solution)/shard_map/ppermute | solution.py:28
  76.9 5.0 %copy-start.16 = (s32[8,512]{1,0:T(8,128)S(1)}, s32[8,512]{1,0:T(8,128)}, u32[]{:S(2)}) copy-start(s32[8,512]{1,0:T(8,128)} %param.23) | copy-start | bytes 49156
  80.6 11.1 %collective-permute-start.11 = (f32[2,2,6,512]{3,2,1,0:T(8,128)}, f32[2,2,6,512]{3,2,1,0:T(8,128)S(1)}, u32[]{:S(2)}, u32[]{:S(2)}) collective-permute-start(f32[2,2,6,512]{3,2,1,0:T(8,128)} %bitcast.90), channel_id=1, source_target_pairs={{12,0},{13,1},{14,2},{15,3},{28,16},{29,17},{30,18},{31,19}} | collective-permute-start | bytes 147464 | tf_op jit(solution)/shard_map/ppermute | solution.py:28
  81.9 23.3 %collective-permute-start.12 = (f32[2,2,6,512]{3,2,1,0:T(8,128)}, f32[2,2,6,512]{3,2,1,0:T(8,128)S(1)}, u32[]{:S(2)}, u32[]{:S(2)}) collective-permute-start(f32[2,2,6,512]{3,2,1,0:T(8,128)} %bitcast.91), channel_id=1, source_target_pairs={{8,0},{12,4},{9,1},{13,5},{10,2},{14,6},{11,3},{15,7},{24,16},{28,... | collective-permute-start | bytes 147464 | tf_op jit(solution)/shard_map/ppermute | solution.py:28
  83.2 22.3 %collective-permute-start.13 = (f32[2,2,6,512]{3,2,1,0:T(8,128)}, f32[2,2,6,512]{3,2,1,0:T(8,128)S(1)}, u32[]{:S(2)}, u32[]{:S(2)}) collective-permute-start(f32[2,2,6,512]{3,2,1,0:T(8,128)} %bitcast.92), channel_id=1, source_target_pairs={{4,0},{8,4},{12,8},{5,1},{9,5},{13,9},{6,2},{10,6},{14,10},{7,3},{... | collective-permute-start | bytes 147464 | tf_op jit(solution)/shard_map/ppermute | solution.py:28
  91.7 18.1 %copy-start.7 = (f32[2,12,2,6,512]{4,2,3,1,0:T(2,128)}, f32[2,12,2,6,512]{4,2,3,1,0:T(2,128)S(1)}, u32[]{:S(2)}) copy-start(f32[2,12,2,6,512]{4,2,3,1,0:T(2,128)S(1)} %collective-permute-done.10) | copy-start | bytes 1769476
  105.2 4.6 %copy-start.5 = (f32[2,12,2,6,512]{4,2,3,1,0:T(2,128)}, f32[2,12,2,6,512]{4,2,3,1,0:T(2,128)S(1)}, u32[]{:S(2)}) copy-start(f32[2,12,2,6,512]{4,2,3,1,0:T(2,128)S(1)} %collective-permute-done.9) | copy-start | bytes 1769476
  106.2 3.7 %copy-start.14 = (f32[8,2,6,512]{3,1,2,0:T(2,128)S(1)}, f32[8,2,6,512]{3,1,2,0:T(2,128)}, u32[]{:S(2)}) copy-start(f32[8,2,6,512]{3,1,2,0:T(2,128)} %param.13) | copy-start | bytes 589828
  109.8 12.3 %copy-start.13 = (f32[8,2,6,512]{3,1,2,0:T(2,128)S(1)}, f32[8,2,6,512]{3,1,2,0:T(2,128)}, u32[]{:S(2)}) copy-start(f32[8,2,6,512]{3,1,2,0:T(2,128)} %param.14) | copy-start | bytes 589828
  110.9 11.2 %collective-permute-start.14 = (f32[1,2,6,512]{3,2,1,0:T(8,128)S(1)}, f32[1,2,6,512]{3,2,1,0:T(8,128)S(1)}, u32[]{:S(2)}, u32[]{:S(2)}) collective-permute-start(f32[1,2,6,512]{3,2,1,0:T(8,128)S(1)} %get-tuple-element.32), channel_id=1, source_target_pairs={{4,0},{8,4},{12,8},{5,1},{9,5},{13,9},{6,2},{10,6},{14,10},{7,3},{... | collective-permute-start | bytes 73736 | tf_op jit(solution)/shard_map/ppermute | solution.py:20
  112.2 9.9 %collective-permute-start.15 = (f32[1,2,6,512]{3,2,1,0:T(8,128)S(1)}, f32[1,2,6,512]{3,2,1,0:T(8,128)S(1)}, u32[]{:S(2)}, u32[]{:S(2)}) collective-permute-start(f32[1,2,6,512]{3,2,1,0:T(8,128)S(1)} %get-tuple-element.33), channel_id=1, source_target_pairs={{0,4},{4,8},{8,12},{1,5},{5,9},{9,13},{2,6},{6,10},{10,14},{3,7},{... | collective-permute-start | bytes 73736 | tf_op jit(solution)/shard_map/ppermute | solution.py:19
  116.9 4.5 %collective-permute-start.16 = (f32[8,2,6,32]{3,2,1,0:T(8,128)S(1)}, f32[8,2,6,32]{3,2,1,0:T(8,128)S(1)}, u32[]{:S(2)}, u32[]{:S(2)}) collective-permute-start(f32[8,2,6,32]{3,2,1,0:T(8,128)S(1)} %get-tuple-element.34), channel_id=1, source_target_pairs={{1,0},{2,1},{3,2},{5,4},{6,5},{7,6},{9,8},{10,9},{11,10},{13,12},{... | collective-permute-start | bytes 36872 | tf_op jit(solution)/shard_map/ppermute | solution.py:20
  118.2 3.9 %collective-permute-start.17 = (f32[8,2,6,32]{3,2,1,0:T(8,128)S(1)}, f32[8,2,6,32]{3,2,1,0:T(8,128)S(1)}, u32[]{:S(2)}, u32[]{:S(2)}) collective-permute-start(f32[8,2,6,32]{3,2,1,0:T(8,128)S(1)} %get-tuple-element.35), channel_id=1, source_target_pairs={{0,1},{1,2},{2,3},{4,5},{5,6},{6,7},{8,9},{9,10},{10,11},{12,13},{... | collective-permute-start | bytes 36872 | tf_op jit(solution)/shard_map/ppermute | solution.py:19
  125.3 8.6 %copy-start.4 = (f32[2,12,2,6,512]{4,2,3,1,0:T(2,128)S(1)}, f32[2,12,2,6,512]{4,2,3,1,0:T(2,128)}, u32[]{:S(2)}) copy-start(f32[2,12,2,6,512]{4,2,3,1,0:T(2,128)} %copy-done.3) | copy-start | bytes 1769476
  128.5 5.4 %collective-permute-start.18 = (f32[2,2,6,512]{3,2,1,0:T(8,128)}, f32[2,2,6,512]{3,2,1,0:T(8,128)S(1)}, u32[]{:S(2)}, u32[]{:S(2)}) collective-permute-start(f32[2,2,6,512]{3,2,1,0:T(8,128)} %bitcast.96), channel_id=1, source_target_pairs={{0,12},{1,13},{2,14},{3,15},{16,28},{17,29},{18,30},{19,31}} | collective-permute-start | bytes 147464 | tf_op jit(solution)/shard_map/ppermute | solution.py:28
  129.8 4.5 %collective-permute-start.19 = (f32[2,2,6,512]{3,2,1,0:T(8,128)}, f32[2,2,6,512]{3,2,1,0:T(8,128)S(1)}, u32[]{:S(2)}, u32[]{:S(2)}) collective-permute-start(f32[2,2,6,512]{3,2,1,0:T(8,128)} %bitcast.97), channel_id=1, source_target_pairs={{0,8},{4,12},{1,9},{5,13},{2,10},{6,14},{3,11},{7,15},{16,24},{20,... | collective-permute-start | bytes 147464 | tf_op jit(solution)/shard_map/ppermute | solution.py:28
  132.1 4.4 %collective-permute-start.20 = (f32[2,2,6,512]{3,2,1,0:T(8,128)}, f32[2,2,6,512]{3,2,1,0:T(8,128)S(1)}, u32[]{:S(2)}, u32[]{:S(2)}) collective-permute-start(f32[2,2,6,512]{3,2,1,0:T(8,128)} %bitcast.98), channel_id=1, source_target_pairs={{0,4},{4,8},{8,12},{1,5},{5,9},{9,13},{2,6},{6,10},{10,14},{3,7},{... | collective-permute-start | bytes 147464 | tf_op jit(solution)/shard_map/ppermute | solution.py:28
  140.3 5.2 %copy-start.18 = (f32[8]{0:T(128)S(1)}, f32[8]{0:T(128)}, u32[]{:S(2)}) copy-start(f32[8]{0:T(128)} %param.25) | copy-start | bytes 100
  140.3 5.2 %copy-start.19 = (s32[2]{0:T(128)S(1)}, s32[2]{0:T(128)}, u32[]{:S(2)}) copy-start(s32[2]{0:T(128)} %param.24) | copy-start | bytes 28
  140.3 12.4 %copy-start.8 = (f32[2,12,2,6,512]{4,2,3,1,0:T(2,128)S(1)}, f32[2,12,2,6,512]{4,2,3,1,0:T(2,128)}, u32[]{:S(2)}) copy-start(f32[2,12,2,6,512]{4,2,3,1,0:T(2,128)} %copy-done.7) | copy-start | bytes 1769476
  144.0 11.4 %copy-start.6 = (f32[2,12,2,6,512]{4,2,3,1,0:T(2,128)S(1)}, f32[2,12,2,6,512]{4,2,3,1,0:T(2,128)}, u32[]{:S(2)}) copy-start(f32[2,12,2,6,512]{4,2,3,1,0:T(2,128)} %copy-done.5) | copy-start | bytes 1769476
  144.0 8.6 %collective-permute-start.21 = (f32[2,2,6,512]{3,2,1,0:T(8,128)}, f32[2,2,6,512]{3,2,1,0:T(8,128)S(1)}, u32[]{:S(2)}, u32[]{:S(2)}) collective-permute-start(f32[2,2,6,512]{3,2,1,0:T(8,128)} %bitcast.93), channel_id=1, source_target_pairs={{12,0},{13,1},{14,2},{15,3},{28,16},{29,17},{30,18},{31,19}} | collective-permute-start | bytes 147464 | tf_op jit(solution)/shard_map/ppermute | solution.py:28
  145.6 9.7 %collective-permute-start.22 = (f32[2,2,6,512]{3,2,1,0:T(8,128)}, f32[2,2,6,512]{3,2,1,0:T(8,128)S(1)}, u32[]{:S(2)}, u32[]{:S(2)}) collective-permute-start(f32[2,2,6,512]{3,2,1,0:T(8,128)} %bitcast.94), channel_id=1, source_target_pairs={{8,0},{12,4},{9,1},{13,5},{10,2},{14,6},{11,3},{15,7},{24,16},{28,... | collective-permute-start | bytes 147464 | tf_op jit(solution)/shard_map/ppermute | solution.py:28
  146.9 8.7 %collective-permute-start.23 = (f32[2,2,6,512]{3,2,1,0:T(8,128)}, f32[2,2,6,512]{3,2,1,0:T(8,128)S(1)}, u32[]{:S(2)}, u32[]{:S(2)}) collective-permute-start(f32[2,2,6,512]{3,2,1,0:T(8,128)} %bitcast.95), channel_id=1, source_target_pairs={{4,0},{8,4},{12,8},{5,1},{9,5},{13,9},{6,2},{10,6},{14,10},{7,3},{... | collective-permute-start | bytes 147464 | tf_op jit(solution)/shard_map/ppermute | solution.py:28
  159.9 1.3 copy-start.15
  161.6 4.2 %collective-permute-start.24 = (f32[8,3,512]{2,0,1:T(8,128)S(1)}, f32[8,3,512]{2,0,1:T(8,128)S(1)}, u32[]{:S(2)}, u32[]{:S(2)}) collective-permute-start(f32[8,3,512]{2,0,1:T(8,128)S(1)} %bitcast.86), channel_id=1, source_target_pairs={{0,16},{16,0},{1,17},{17,1},{2,18},{18,2},{3,19},{19,3},{4,20},{20... | collective-permute-start | bytes 147464 | tf_op jit(solution)/shard_map/ppermute | solution.py:237

commit v6 on v5

--- a/solution.py
+++ b/solution.py
@@ -33,11 +33,18 @@
 
 
 def _rows_times(blocks_ref, index, vec):
+    i, c = index
+    nv = vec.shape[0]
     total = None
-    for a in range(vec.shape[0]):
-        term = blocks_ref[index + (a,)] * vec[a : a + 1, :]
+    for a in range(nv):
+        rows = blocks_ref[i, pl.ds((c * nv + a) * nv, nv), :]
+        term = rows * vec[a : a + 1, :]
         total = term if total is None else total + term
     return total
+
+
+def dense(blocks):
+    return blocks.reshape(blocks.shape[0], -1, blocks.shape[-1])
 
 
 def _init_carry(carry_ref, inc_ref):
@@ -55,6 +62,7 @@
 
 def upper_pallas(rhs, near_t, far_t, incoming, want_values):
     count, conds, nv = near_t.shape[0], near_t.shape[1], near_t.shape[2]
+    near_t, far_t = dense(near_t), dense(far_t)
     has_inc = not isinstance(incoming, tuple)
     shape = incoming.shape if has_inc else incoming
     width = shape[1]
@@ -104,6 +112,7 @@
 
 def lower_pallas(rhs, inverse, near, far, incoming, want_values):
     count, conds, nv = inverse.shape[0], inverse.shape[1], inverse.shape[2]
+    inverse, near, far = dense(inverse), dense(near), dense(far)
     has_inc = not isinstance(incoming, tuple)
     shape = incoming.shape if has_inc else incoming
     width = shape[1]

time: 167 us -> 176 us (1.054)
  Pallas kernels: 42.3 us -> 48 us
  local copies, waits for them, and re-layouts: 19.8 us -> 23.5 us
    reshape x0 -> x5, local copies, waits for them, and re-layouts: none -> 8.61 us  [dense(): return blocks.reshape(blocks.shape[0], -1, blocks.shape[-1])]
    pallas_call x5, Pallas kernels: 22.8 us -> 26.9 us  [lower_pallas(): pl.pallas_call(kernel, out_shape=tuple(out_shape), in_specs=_vmem_specs(l...]
    transpose x1 -> x0, local copies, waits for them, and re-layouts: 4.01 us -> none  [on_device(): far_t = jnp.swapaxes(far_upper, 2, 3)]
    unnamed x46 -> x50, local copies, waits for them, and re-layouts: 6.39 us -> 6.81 us
  transfers between devices with their start and end apart: 25 -> 25, of which waited for: 10 -> 10; matrix products, arithmetic and copies ran while one was open for 14% -> 16% of each run, Pallas kernels for 15% -> 18%
where the time goes in v6:
time: 176 us; the launch traced here: 175 us
  starting transfers between devices  55.9 us (32%)
  Pallas kernels  48 us (27%)
  waiting for transfers between devices  33.2 us (19%)
  local copies, waits for them, and re-layouts  23.5 us (13%)
  other arithmetic  11.7 us (7%)
    ppermute x16, starting transfers between devices, from_behind(): lax.ppermute(value, axis, [(source, source + steps) for source in range(f...  33 us
    ppermute x16, waiting for transfers between devices, from_behind(): lax.ppermute(value, axis, [(source, source + steps) for source in range(f...  30.5 us
    pallas_call x5, Pallas kernels, lower_pallas(): pl.pallas_call(kernel, out_shape=tuple(out_shape), in_specs=_vmem_specs(l...  26.9 us
    pallas_call x5, Pallas kernels, upper_pallas(): pl.pallas_call(kernel, out_shape=tuple(out_shape), in_specs=_vmem_specs(l...  21.1 us
    ppermute x4, starting transfers between devices, extended(): before = lax.ppermute(last, axis, up)  16.2 us
    reshape x5, local copies, waits for them, and re-layouts, dense(): return blocks.reshape(blocks.shape[0], -1, blocks.shape[-1])  8.61 us
    unnamed x50, local copies, waits for them, and re-layouts  6.81 us
    ppermute x4, starting transfers between devices, extended(): after = lax.ppermute(first, axis, down)  5.15 us
  transfers between devices with their start and end apart: 25, of which 10 were waited for; matrix products, arithmetic and copies ran while one was open for 16% of the time, Pallas kernels for 18%

profile of v6, /device:TPU:0, one launch (start us, length us, event | category | flops | bytes accessed | tf_op | source)
XLA Modules:
  0.0 175.2 jit_solution(655859253116136980)
XLA Ops:
  0.6 1.0 copy.272
  1.7 1.3 collective-permute-start
  3.0 5.6 %collective-permute-start.1 = (f32[1,2,6,512]{3,2,1,0:T(8,128)S(1)}, f32[1,2,6,512]{3,2,1,0:T(8,128)S(1)}, u32[]{:S(2)}, u32[]{:S(2)}) collective-permute-start(f32[1,2,6,512]{3,2,1,0:T(8,128)S(1)} %get-tuple-element.37), channel_id=1, source_target_pairs={{0,4},{4,8},{8,12},{1,5},{5,9},{9,13},{2,6},{6,10},{10,14},{3,7},{... | collective-permute-start | bytes 73736 | tf_op jit(solution)/shard_map/ppermute | solution.py:19
  8.7 1.3 collective-permute-start.2
  10.0 3.0 %collective-permute-start.3 = (f32[8,2,6,32]{3,2,1,0:T(8,128)S(1)}, f32[8,2,6,32]{3,2,1,0:T(8,128)S(1)}, u32[]{:S(2)}, u32[]{:S(2)}) collective-permute-start(f32[8,2,6,32]{3,2,1,0:T(8,128)S(1)} %get-tuple-element.39), channel_id=1, source_target_pairs={{0,1},{1,2},{2,3},{4,5},{5,6},{6,7},{8,9},{9,10},{10,11},{12,13},{... | collective-permute-start | bytes 36872 | tf_op jit(solution)/shard_map/ppermute | solution.py:19
  13.0 2.0 %copy.244 = f32[8,2,6,6,512]{4,0,2,3,1:T(8,128)S(1)} copy(f32[8,2,6,6,512]{4,1,3,2,0:T(2,128)} %param.15) | data formatting | bytes 2359296 | tf_op args[2]
  15.0 1.7 copy.258.refs_0_.refs_1_
  16.7 0.7 copy.245
  17.4 1.7 copy.259.refs_1_.refs_2_
  19.1 8.8 %shard_map.141 = f32[2,12,2,6,512]{4,3,2,1,0:T(8,128)} custom-call(f32[8,72,512]{2,1,0:T(8,128)} %copy.258.refs_0_.refs_1_, f32[8,72,512]{2,1,0:T(8,128)} %copy.259.refs_1_.refs_2_), custom_call_target="tpu_custom_call" | custom-call | tf_op jit(solution)/shard_map/pallas_call | solution.py:105
  27.9 2.5 %copy.248 = f32[2,12,2,6,512]{4,2,3,1,0:T(2,128)} copy(f32[2,12,2,6,512]{4,3,2,1,0:T(8,128)} %shard_map.141) | data formatting | bytes 1179648 | tf_op jit(solution)/shard_map/pallas_call | solution.py:105
  30.4 5.0 %collective-permute-start.5 = (f32[2,12,2,6,512]{4,2,3,1,0:T(2,128)}, f32[2,12,2,6,512]{4,2,3,1,0:T(2,128)S(1)}, u32[]{:S(2)}, u32[]{:S(2)}) collective-permute-start(f32[2,12,2,6,512]{4,2,3,1,0:T(2,128)} %copy.248), channel_id=1, source_target_pairs={{0,8},{4,12},{1,9},{5,13},{2,10},{6,14},{3,11},{7,15},{16,24},{20,... | collective-permute-start | bytes 1769480 | tf_op jit(solution)/shard_map/ppermute | solution.py:28
  35.4 0.7 copy.238
  36.1 1.7 copy.241.refs_0_.refs_1_
  37.8 0.7 copy.239
  38.5 1.7 copy.242.refs_1_.refs_2_
  40.9 1.7 copy.243.refs_2_.refs_3_
  42.6 12.2 %shard_map.140 = f32[2,12,2,6,512]{4,3,2,1,0:T(8,128)} custom-call(f32[8,72,512]{2,1,0:T(8,128)} %copy.241.refs_0_.refs_1_, f32[8,72,512]{2,1,0:T(8,128)} %copy.242.refs_1_.refs_2_, f32[8,72,512]{2,1,0:T(8,128)} %copy.243.refs_2_.refs_3_), custom_call_target="tpu_custom_call" | custom-call | tf_op jit(solution)/shard_map/pallas_call | solution.py:156
  54.8 2.1 %collective-permute-start.4 = (f32[2,12,2,6,512]{4,2,3,1,0:T(2,128)}, f32[2,12,2,6,512]{4,2,3,1,0:T(2,128)}, u32[]{:S(2)}, u32[]{:S(2)}) collective-permute-start(f32[2,12,2,6,512]{4,2,3,1,0:T(2,128)} %copy.248), channel_id=1, source_target_pairs={{0,4},{4,8},{8,12},{1,5},{5,9},{9,13},{2,6},{6,10},{10,14},{3,7},{... | collective-permute-start | bytes 1769480 | tf_op jit(solution)/shard_map/ppermute | solution.py:28
  57.6 0.8 convolution_bitcast_fusion.1
  59.4 0.8 copy.257.refs_0_
  60.8 3.2 %shard_map.142 = (f32[8,2,6,512]{3,2,1,0:T(8,128)}, f32[2,1,2,6,512]{4,3,2,1,0:T(8,128)}) custom-call(f32[8,2,6,512]{3,2,1,0:T(8,128)} %copy.257.refs_0_, f32[8,72,512]{2,1,0:T(8,128)} %copy.258.refs_0_.refs_1_, f32[8,72,512]{2,1,0:T(8,128)} %copy.259.refs_1_.refs_2_, f32[2,1,2,6,512]{4,3,2,1,0:T(8,128)} %broadcast_in_dim.10.refs_3_.refs_4_), custom_call_target="tpu_custom_call" | custom-call | tf_op jit(solution)/shard_map/pallas_call | solution.py:105
  64.0 1.4 collective-permute-start.6
  65.4 1.3 copy.260
  66.7 1.3 collective-permute-start.10
  68.0 1.3 collective-permute-start.9
  69.3 2.1 %collective-permute-done.6 = f32[2,2,6,512]{3,2,1,0:T(8,128)S(1)} collective-permute-done((f32[2,2,6,512]{3,2,1,0:T(8,128)}, f32[2,2,6,512]{3,2,1,0:T(8,128)S(1)}, u32[]{:S(2)}, u32[]{:S(2)}) %collective-permute-start.6) | collective-permute-done | bytes 49184 | tf_op jit(solution)/shard_map/ppermute | solution.py:28
  71.4 4.0 %collective-permute-start.7 = (f32[2,2,6,512]{3,2,1,0:T(8,128)S(1)}, f32[2,2,6,512]{3,2,1,0:T(8,128)S(1)}, u32[]{:S(2)}, u32[]{:S(2)}) collective-permute-start(f32[2,2,6,512]{3,2,1,0:T(8,128)S(1)} %bitcast.98), channel_id=1, source_target_pairs={{0,8},{4,12},{1,9},{5,13},{2,10},{6,14},{3,11},{7,15},{16,24},{20,... | collective-permute-start | bytes 147464 | tf_op jit(solution)/shard_map/ppermute | solution.py:28
  75.5 4.6 %collective-permute-start.8 = (f32[2,2,6,512]{3,2,1,0:T(8,128)S(1)}, f32[2,2,6,512]{3,2,1,0:T(8,128)S(1)}, u32[]{:S(2)}, u32[]{:S(2)}) collective-permute-start(f32[2,2,6,512]{3,2,1,0:T(8,128)S(1)} %bitcast.99), channel_id=1, source_target_pairs={{0,4},{4,8},{8,12},{1,5},{5,9},{9,13},{2,6},{6,10},{10,14},{3,7},{... | collective-permute-start | bytes 147464 | tf_op jit(solution)/shard_map/ppermute | solution.py:28
  80.5 1.3 multiply_reduce_fusion.9
  82.6 3.0 %shard_map.143 = (f32[8,2,6,512]{3,2,1,0:T(8,128)}, f32[2,1,2,6,512]{4,3,2,1,0:T(8,128)}) custom-call(f32[8,2,6,512]{3,2,1,0:T(8,128)} %copy.257.refs_0_, f32[8,72,512]{2,1,0:T(8,128)} %copy.258.refs_0_.refs_1_, f32[8,72,512]{2,1,0:T(8,128)} %copy.259.refs_1_.refs_2_, f32[2,1,2,6,512]{4,3,2,1,0:T(8,128)} %fusion.18.refs_3_), custom_call_target="tpu_custom_call" | custom-call | tf_op jit(solution)/shard_map/pallas_call | solution.py:105
  85.7 3.7 %shard_map.144 = (f32[8,2,6,512]{3,2,1,0:T(8,128)}, f32[2,1,2,6,512]{4,3,2,1,0:T(8,128)}) custom-call(f32[8,2,6,512]{3,2,1,0:T(8,128)} %get-tuple-element.13.refs_0_, f32[8,72,512]{2,1,0:T(8,128)} %copy.241.refs_0_.refs_1_, f32[8,72,512]{2,1,0:T(8,128)} %copy.242.refs_1_.refs_2_, f32[8,72,512]{2,1,0:T(8,128)} %copy.243.refs_2_.refs_3_, ...), custom_call_target="tpu_custom_call" | custom-call | tf_op jit(solution)/shard_map/pallas_call | solution.py:156
  89.3 1.3 collective-permute-start.11
  90.6 1.3 collective-permute-start.12
  91.9 1.3 collective-permute-start.13
  93.2 5.6 %collective-permute-done.11 = f32[2,2,6,512]{3,2,1,0:T(8,128)S(1)} collective-permute-done((f32[2,2,6,512]{3,2,1,0:T(8,128)}, f32[2,2,6,512]{3,2,1,0:T(8,128)S(1)}, u32[]{:S(2)}, u32[]{:S(2)}) %collective-permute-start.11) | collective-permute-done | bytes 49184 | tf_op jit(solution)/shard_map/ppermute | solution.py:28
  99.1 14.9 %collective-permute-done.12 = f32[2,2,6,512]{3,2,1,0:T(8,128)S(1)} collective-permute-done((f32[2,2,6,512]{3,2,1,0:T(8,128)}, f32[2,2,6,512]{3,2,1,0:T(8,128)S(1)}, u32[]{:S(2)}, u32[]{:S(2)}) %collective-permute-start.12) | collective-permute-done | bytes 49184 | tf_op jit(solution)/shard_map/ppermute | solution.py:28
  115.1 3.7 %shard_map.145 = (f32[8,2,6,512]{3,2,1,0:T(8,128)}, f32[2,1,2,6,512]{4,3,2,1,0:T(8,128)}) custom-call(f32[8,2,6,512]{3,2,1,0:T(8,128)} %get-tuple-element.13.refs_0_, f32[8,72,512]{2,1,0:T(8,128)} %copy.241.refs_0_.refs_1_, f32[8,72,512]{2,1,0:T(8,128)} %copy.242.refs_1_.refs_2_, f32[8,72,512]{2,1,0:T(8,128)} %copy.243.refs_2_.refs_3_, ...), custom_call_target="tpu_custom_call" | custom-call | tf_op jit(solution)/shard_map/pallas_call | solution.py:156
  118.8 1.1 add_multiply_fusion.1
  119.9 1.3 collective-permute-start.14
  121.2 4.5 %collective-permute-start.15 = (f32[1,2,6,512]{3,2,1,0:T(8,128)S(1)}, f32[1,2,6,512]{3,2,1,0:T(8,128)S(1)}, u32[]{:S(2)}, u32[]{:S(2)}) collective-permute-start(f32[1,2,6,512]{3,2,1,0:T(8,128)S(1)} %get-tuple-element.33), channel_id=1, source_target_pairs={{0,4},{4,8},{8,12},{1,5},{5,9},{9,13},{2,6},{6,10},{10,14},{3,7},{... | collective-permute-start | bytes 73736 | tf_op jit(solution)/shard_map/ppermute | solution.py:19
  125.8 1.3 collective-permute-start.16
  127.1 3.0 %collective-permute-start.17 = (f32[8,2,6,32]{3,2,1,0:T(8,128)S(1)}, f32[8,2,6,32]{3,2,1,0:T(8,128)S(1)}, u32[]{:S(2)}, u32[]{:S(2)}) collective-permute-start(f32[8,2,6,32]{3,2,1,0:T(8,128)S(1)} %get-tuple-element.35), channel_id=1, source_target_pairs={{0,1},{1,2},{2,3},{4,5},{5,6},{6,7},{8,9},{9,10},{10,11},{12,13},{... | collective-permute-start | bytes 36872 | tf_op jit(solution)/shard_map/ppermute | solution.py:19
  130.1 0.9 collective-permute-done.17
  131.6 0.8 convolution_bitcast_fusion
  133.5 0.8 copy.283.refs_0_
  134.3 3.1 %shard_map.146 = (f32[8,2,6,512]{3,2,1,0:T(8,128)}, f32[2,1,2,6,512]{4,3,2,1,0:T(8,128)}) custom-call(f32[8,2,6,512]{3,2,1,0:T(8,128)} %copy.283.refs_0_, f32[8,72,512]{2,1,0:T(8,128)} %copy.258.refs_0_.refs_1_, f32[8,72,512]{2,1,0:T(8,128)} %copy.259.refs_1_.refs_2_, f32[2,1,2,6,512]{4,3,2,1,0:T(8,128)} %broadcast_in_dim.10.refs_3_.refs_4_), custom_call_target="tpu_custom_call" | custom-call | tf_op jit(solution)/shard_map/pallas_call | solution.py:105
  137.4 1.4 collective-permute-start.18
  138.8 2.2 %collective-permute-start.19 = (f32[2,2,6,512]{3,2,1,0:T(8,128)}, f32[2,2,6,512]{3,2,1,0:T(8,128)S(1)}, u32[]{:S(2)}, u32[]{:S(2)}) collective-permute-start(f32[2,2,6,512]{3,2,1,0:T(8,128)} %bitcast.107), channel_id=1, source_target_pairs={{0,8},{4,12},{1,9},{5,13},{2,10},{6,14},{3,11},{7,15},{16,24},{20,... | collective-permute-start | bytes 147464 | tf_op jit(solution)/shard_map/ppermute | solution.py:28
  141.0 1.8 %collective-permute-start.20 = (f32[2,2,6,512]{3,2,1,0:T(8,128)}, f32[2,2,6,512]{3,2,1,0:T(8,128)S(1)}, u32[]{:S(2)}, u32[]{:S(2)}) collective-permute-start(f32[2,2,6,512]{3,2,1,0:T(8,128)} %bitcast.108), channel_id=1, source_target_pairs={{0,4},{4,8},{8,12},{1,5},{5,9},{9,13},{2,6},{6,10},{10,14},{3,7},{... | collective-permute-start | bytes 147464 | tf_op jit(solution)/shard_map/ppermute | solution.py:28
  143.4 1.3 multiply_reduce_fusion.5
  144.7 0.7 collective-permute-done.20
  146.1 3.1 %shard_map.147 = (f32[8,2,6,512]{3,2,1,0:T(8,128)}, f32[2,1,2,6,512]{4,3,2,1,0:T(8,128)}) custom-call(f32[8,2,6,512]{3,2,1,0:T(8,128)} %copy.283.refs_0_, f32[8,72,512]{2,1,0:T(8,128)} %copy.258.refs_0_.refs_1_, f32[8,72,512]{2,1,0:T(8,128)} %copy.259.refs_1_.refs_2_, f32[2,1,2,6,512]{4,3,2,1,0:T(8,128)} %fusion.14.refs_3_), custom_call_target="tpu_custom_call" | custom-call | tf_op jit(solution)/shard_map/pallas_call | solution.py:105
  149.1 3.7 %shard_map.148 = (f32[8,2,6,512]{3,2,1,0:T(8,128)}, f32[2,1,2,6,512]{4,3,2,1,0:T(8,128)}) custom-call(f32[8,2,6,512]{3,2,1,0:T(8,128)} %get-tuple-element.17.refs_0_, f32[8,72,512]{2,1,0:T(8,128)} %copy.241.refs_0_.refs_1_, f32[8,72,512]{2,1,0:T(8,128)} %copy.242.refs_1_.refs_2_, f32[8,72,512]{2,1,0:T(8,128)} %copy.243.refs_2_.refs_3_, ...), custom_call_target="tpu_custom_call" | custom-call | tf_op jit(solution)/shard_map/pallas_call | solution.py:156
  152.8 1.4 collective-permute-start.21
  154.4 1.3 collective-permute-start.22
  155.7 1.3 collective-permute-start.23
  157.0 4.5 %collective-permute-done.21 = f32[2,2,6,512]{3,2,1,0:T(8,128)S(1)} collective-permute-done((f32[2,2,6,512]{3,2,1,0:T(8,128)}, f32[2,2,6,512]{3,2,1,0:T(8,128)S(1)}, u32[]{:S(2)}, u32[]{:S(2)}) %collective-permute-start.21) | collective-permute-done | bytes 49184 | tf_op jit(solution)/shard_map/ppermute | solution.py:28
  161.8 2.4 %collective-permute-done.22 = f32[2,2,6,512]{3,2,1,0:T(8,128)S(1)} collective-permute-done((f32[2,2,6,512]{3,2,1,0:T(8,128)}, f32[2,2,6,512]{3,2,1,0:T(8,128)S(1)}, u32[]{:S(2)}, u32[]{:S(2)}) %collective-permute-start.22) | collective-permute-done | bytes 49184 | tf_op jit(solution)/shard_map/ppermute | solution.py:28
  165.2 3.6 %shard_map.149 = (f32[8,2,6,512]{3,2,1,0:T(8,128)}, f32[2,1,2,6,512]{4,3,2,1,0:T(8,128)}) custom-call(f32[8,2,6,512]{3,2,1,0:T(8,128)} %get-tuple-element.17.refs_0_, f32[8,72,512]{2,1,0:T(8,128)} %copy.241.refs_0_.refs_1_, f32[8,72,512]{2,1,0:T(8,128)} %copy.242.refs_1_.refs_2_, f32[8,72,512]{2,1,0:T(8,128)} %copy.243.refs_2_.refs_3_, ...), custom_call_target="tpu_custom_call" | custom-call | tf_op jit(solution)/shard_map/pallas_call | solution.py:156
  168.8 1.1 multiply_bitcast_fusion
  170.4 1.6 collective-permute-start.24
  172.0 0.8 copy.296
  172.8 1.8 %collective-permute-done.24 = f32[8,3,512]{2,0,1:T(8,128)S(1)} collective-permute-done((f32[8,3,512]{2,0,1:T(8,128)S(1)}, f32[8,3,512]{2,0,1:T(8,128)S(1)}, u32[]{:S(2)}, u32[]{:S(2)}) %collective-permute-start.24) | collective-permute-done | bytes 49184 | tf_op jit(solution)/shard_map/ppermute | solution.py:246
  (105 shorter events, 10.9 us)
Async XLA Ops:
  0.6 56.9 %copy-start = (f32[2,6,32,32]{3,2,1,0:T(8,128)S(1)}, f32[2,6,32,32]{3,2,1,0:T(8,128)}, u32[]{:S(2)}) copy-start(f32[2,6,32,32]{3,2,1,0:T(8,128)} %param.21) | copy-start | bytes 147460
  1.7 55.3 %collective-permute-start = (f32[1,2,6,512]{3,2,1,0:T(8,128)S(1)}, f32[1,2,6,512]{3,2,1,0:T(8,128)S(1)}, u32[]{:S(2)}, u32[]{:S(2)}) collective-permute-start(f32[1,2,6,512]{3,2,1,0:T(8,128)S(1)} %get-tuple-element.36), channel_id=1, source_target_pairs={{4,0},{8,4},{12,8},{5,1},{9,5},{13,9},{6,2},{10,6},{14,10},{7,3},{... | collective-permute-start | bytes 73736 | tf_op jit(solution)/shard_map/ppermute | solution.py:20
  3.0 54.0 %collective-permute-start.1 = (f32[1,2,6,512]{3,2,1,0:T(8,128)S(1)}, f32[1,2,6,512]{3,2,1,0:T(8,128)S(1)}, u32[]{:S(2)}, u32[]{:S(2)}) collective-permute-start(f32[1,2,6,512]{3,2,1,0:T(8,128)S(1)} %get-tuple-element.37), channel_id=1, source_target_pairs={{0,4},{4,8},{8,12},{1,5},{5,9},{9,13},{2,6},{6,10},{10,14},{3,7},{... | collective-permute-start | bytes 73736 | tf_op jit(solution)/shard_map/ppermute | solution.py:19
  8.7 46.2 %collective-permute-start.2 = (f32[8,2,6,32]{3,2,1,0:T(8,128)S(1)}, f32[8,2,6,32]{3,2,1,0:T(8,128)S(1)}, u32[]{:S(2)}, u32[]{:S(2)}) collective-permute-start(f32[8,2,6,32]{3,2,1,0:T(8,128)S(1)} %get-tuple-element.38), channel_id=1, source_target_pairs={{1,0},{2,1},{3,2},{5,4},{6,5},{7,6},{9,8},{10,9},{11,10},{13,12},{... | collective-permute-start | bytes 36872 | tf_op jit(solution)/shard_map/ppermute | solution.py:20
  10.0 47.0 %collective-permute-start.3 = (f32[8,2,6,32]{3,2,1,0:T(8,128)S(1)}, f32[8,2,6,32]{3,2,1,0:T(8,128)S(1)}, u32[]{:S(2)}, u32[]{:S(2)}) collective-permute-start(f32[8,2,6,32]{3,2,1,0:T(8,128)S(1)} %get-tuple-element.39), channel_id=1, source_target_pairs={{0,1},{1,2},{2,3},{4,5},{5,6},{6,7},{8,9},{9,10},{10,11},{12,13},{... | collective-permute-start | bytes 36872 | tf_op jit(solution)/shard_map/ppermute | solution.py:19
  15.0 1.7 copy-start.9
  27.9 7.5 %copy-start.10 = (f32[8,2,6,6,512]{4,1,3,2,0:T(2,128)S(1)}, f32[8,2,6,6,512]{4,1,3,2,0:T(2,128)}, u32[]{:S(2)}) copy-start(f32[8,2,6,6,512]{4,1,3,2,0:T(2,128)} %param.17) | copy-start | bytes 3538948
  30.4 45.1 %collective-permute-start.5 = (f32[2,12,2,6,512]{4,2,3,1,0:T(2,128)}, f32[2,12,2,6,512]{4,2,3,1,0:T(2,128)S(1)}, u32[]{:S(2)}, u32[]{:S(2)}) collective-permute-start(f32[2,12,2,6,512]{4,2,3,1,0:T(2,128)} %copy.248), channel_id=1, source_target_pairs={{0,8},{4,12},{1,9},{5,13},{2,10},{6,14},{3,11},{7,15},{16,24},{20,... | collective-permute-start | bytes 1769480 | tf_op jit(solution)/shard_map/ppermute | solution.py:28
  36.1 1.7 copy-start.11
  38.5 1.7 copy-start.12
  42.6 14.3 %copy-start.13 = (f32[8,2,6,512]{3,1,2,0:T(2,128)S(1)}, f32[8,2,6,512]{3,1,2,0:T(2,128)}, u32[]{:S(2)}) copy-start(f32[8,2,6,512]{3,1,2,0:T(2,128)} %param.14) | copy-start | bytes 589828
  54.8 25.6 %collective-permute-start.4 = (f32[2,12,2,6,512]{4,2,3,1,0:T(2,128)}, f32[2,12,2,6,512]{4,2,3,1,0:T(2,128)}, u32[]{:S(2)}, u32[]{:S(2)}) collective-permute-start(f32[2,12,2,6,512]{4,2,3,1,0:T(2,128)} %copy.248), channel_id=1, source_target_pairs={{0,4},{4,8},{8,12},{1,5},{5,9},{9,13},{2,6},{6,10},{10,14},{3,7},{... | collective-permute-start | bytes 1769480 | tf_op jit(solution)/shard_map/ppermute | solution.py:28
  57.5 1.3 copy-start.1
  60.8 4.6 %copy-start.2 = (f32[2,12,2,6,512]{4,3,2,1,0:T(8,128)S(1)}, f32[2,12,2,6,512]{4,3,2,1,0:T(8,128)}, u32[]{:S(2)}) copy-start(f32[2,12,2,6,512]{4,3,2,1,0:T(8,128)} %shard_map.140) | copy-start | bytes 1769476
  64.0 7.4 %copy-start.18 = (f32[2,1,2,6,512]{4,3,2,1,0:T(8,128)S(1)}, f32[2,1,2,6,512]{4,3,2,1,0:T(8,128)}, u32[]{:S(2)}) copy-start(f32[2,1,2,6,512]{4,3,2,1,0:T(8,128)} %get-tuple-element.12) | copy-start | bytes 147460
  64.0 7.4 %collective-permute-start.6 = (f32[2,2,6,512]{3,2,1,0:T(8,128)}, f32[2,2,6,512]{3,2,1,0:T(8,128)S(1)}, u32[]{:S(2)}, u32[]{:S(2)}) collective-permute-start(f32[2,2,6,512]{3,2,1,0:T(8,128)} %bitcast.97), channel_id=1, source_target_pairs={{0,12},{1,13},{2,14},{3,15},{16,28},{17,29},{18,30},{19,31}} | collective-permute-start | bytes 147464 | tf_op jit(solution)/shard_map/ppermute | solution.py:28
  66.7 32.2 %collective-permute-start.10 = (f32[2,12,2,6,512]{4,2,3,1,0:T(2,128)}, f32[2,12,2,6,512]{4,2,3,1,0:T(2,128)S(1)}, u32[]{:S(2)}, u32[]{:S(2)}) collective-permute-start(f32[2,12,2,6,512]{4,2,3,1,0:T(2,128)} %copy.260), channel_id=1, source_target_pairs={{8,0},{12,4},{9,1},{13,5},{10,2},{14,6},{11,3},{15,7},{24,16},{28,... | collective-permute-start | bytes 1769480 | tf_op jit(solution)/shard_map/ppermute | solution.py:28
  68.0 46.1 %collective-permute-start.9 = (f32[2,12,2,6,512]{4,2,3,1,0:T(2,128)}, f32[2,12,2,6,512]{4,2,3,1,0:T(2,128)S(1)}, u32[]{:S(2)}, u32[]{:S(2)}) collective-permute-start(f32[2,12,2,6,512]{4,2,3,1,0:T(2,128)} %copy.260), channel_id=1, source_target_pairs={{4,0},{8,4},{12,8},{5,1},{9,5},{13,9},{6,2},{10,6},{14,10},{7,3},{... | collective-permute-start | bytes 1769480 | tf_op jit(solution)/shard_map/ppermute | solution.py:28
  71.4 8.9 %collective-permute-start.7 = (f32[2,2,6,512]{3,2,1,0:T(8,128)S(1)}, f32[2,2,6,512]{3,2,1,0:T(8,128)S(1)}, u32[]{:S(2)}, u32[]{:S(2)}) collective-permute-start(f32[2,2,6,512]{3,2,1,0:T(8,128)S(1)} %bitcast.98), channel_id=1, source_target_pairs={{0,8},{4,12},{1,9},{5,13},{2,10},{6,14},{3,11},{7,15},{16,24},{20,... | collective-permute-start | bytes 147464 | tf_op jit(solution)/shard_map/ppermute | solution.py:28
  75.5 10.2 %copy-start.3 = (f32[2,12,2,6,512]{4,2,3,1,0:T(2,128)}, f32[2,12,2,6,512]{4,2,3,1,0:T(2,128)S(1)}, u32[]{:S(2)}) copy-start(f32[2,12,2,6,512]{4,2,3,1,0:T(2,128)S(1)} %collective-permute-done.5) | copy-start | bytes 1769476
  75.5 6.5 %collective-permute-start.8 = (f32[2,2,6,512]{3,2,1,0:T(8,128)S(1)}, f32[2,2,6,512]{3,2,1,0:T(8,128)S(1)}, u32[]{:S(2)}, u32[]{:S(2)}) collective-permute-start(f32[2,2,6,512]{3,2,1,0:T(8,128)S(1)} %bitcast.99), channel_id=1, source_target_pairs={{0,4},{4,8},{8,12},{1,5},{5,9},{9,13},{2,6},{6,10},{10,14},{3,7},{... | collective-permute-start | bytes 147464 | tf_op jit(solution)/shard_map/ppermute | solution.py:28
  85.7 4.9 %copy-start.17 = (s32[8,512]{1,0:T(8,128)S(1)}, s32[8,512]{1,0:T(8,128)}, u32[]{:S(2)}) copy-start(s32[8,512]{1,0:T(8,128)} %param.23) | copy-start | bytes 49156
  89.3 9.5 %collective-permute-start.11 = (f32[2,2,6,512]{3,2,1,0:T(8,128)}, f32[2,2,6,512]{3,2,1,0:T(8,128)S(1)}, u32[]{:S(2)}, u32[]{:S(2)}) collective-permute-start(f32[2,2,6,512]{3,2,1,0:T(8,128)} %bitcast.100), channel_id=1, source_target_pairs={{12,0},{13,1},{14,2},{15,3},{28,16},{29,17},{30,18},{31,19}} | collective-permute-start | bytes 147464 | tf_op jit(solution)/shard_map/ppermute | solution.py:28
  90.6 23.4 %collective-permute-start.12 = (f32[2,2,6,512]{3,2,1,0:T(8,128)}, f32[2,2,6,512]{3,2,1,0:T(8,128)S(1)}, u32[]{:S(2)}, u32[]{:S(2)}) collective-permute-start(f32[2,2,6,512]{3,2,1,0:T(8,128)} %bitcast.101), channel_id=1, source_target_pairs={{8,0},{12,4},{9,1},{13,5},{10,2},{14,6},{11,3},{15,7},{24,16},{28,... | collective-permute-start | bytes 147464 | tf_op jit(solution)/shard_map/ppermute | solution.py:28
  91.9 22.5 %collective-permute-start.13 = (f32[2,2,6,512]{3,2,1,0:T(8,128)}, f32[2,2,6,512]{3,2,1,0:T(8,128)S(1)}, u32[]{:S(2)}, u32[]{:S(2)}) collective-permute-start(f32[2,2,6,512]{3,2,1,0:T(8,128)} %bitcast.102), channel_id=1, source_target_pairs={{4,0},{8,4},{12,8},{5,1},{9,5},{13,9},{6,2},{10,6},{14,10},{7,3},{... | collective-permute-start | bytes 147464 | tf_op jit(solution)/shard_map/ppermute | solution.py:28
  98.9 19.9 %copy-start.7 = (f32[2,12,2,6,512]{4,2,3,1,0:T(2,128)}, f32[2,12,2,6,512]{4,2,3,1,0:T(2,128)S(1)}, u32[]{:S(2)}) copy-start(f32[2,12,2,6,512]{4,2,3,1,0:T(2,128)S(1)} %collective-permute-done.10) | copy-start | bytes 1769476
  114.1 4.6 %copy-start.5 = (f32[2,12,2,6,512]{4,2,3,1,0:T(2,128)}, f32[2,12,2,6,512]{4,2,3,1,0:T(2,128)S(1)}, u32[]{:S(2)}) copy-start(f32[2,12,2,6,512]{4,2,3,1,0:T(2,128)S(1)} %collective-permute-done.9) | copy-start | bytes 1769476
  115.1 3.7 %copy-start.15 = (f32[8,2,6,512]{3,1,2,0:T(2,128)S(1)}, f32[8,2,6,512]{3,1,2,0:T(2,128)}, u32[]{:S(2)}) copy-start(f32[8,2,6,512]{3,1,2,0:T(2,128)} %param.13) | copy-start | bytes 589828
  118.8 12.3 %copy-start.14 = (f32[8,2,6,512]{3,1,2,0:T(2,128)S(1)}, f32[8,2,6,512]{3,1,2,0:T(2,128)}, u32[]{:S(2)}) copy-start(f32[8,2,6,512]{3,1,2,0:T(2,128)} %param.14) | copy-start | bytes 589828
  119.9 11.2 %collective-permute-start.14 = (f32[1,2,6,512]{3,2,1,0:T(8,128)S(1)}, f32[1,2,6,512]{3,2,1,0:T(8,128)S(1)}, u32[]{:S(2)}, u32[]{:S(2)}) collective-permute-start(f32[1,2,6,512]{3,2,1,0:T(8,128)S(1)} %get-tuple-element.32), channel_id=1, source_target_pairs={{4,0},{8,4},{12,8},{5,1},{9,5},{13,9},{6,2},{10,6},{14,10},{7,3},{... | collective-permute-start | bytes 73736 | tf_op jit(solution)/shard_map/ppermute | solution.py:20
  121.2 9.9 %collective-permute-start.15 = (f32[1,2,6,512]{3,2,1,0:T(8,128)S(1)}, f32[1,2,6,512]{3,2,1,0:T(8,128)S(1)}, u32[]{:S(2)}, u32[]{:S(2)}) collective-permute-start(f32[1,2,6,512]{3,2,1,0:T(8,128)S(1)} %get-tuple-element.33), channel_id=1, source_target_pairs={{0,4},{4,8},{8,12},{1,5},{5,9},{9,13},{2,6},{6,10},{10,14},{3,7},{... | collective-permute-start | bytes 73736 | tf_op jit(solution)/shard_map/ppermute | solution.py:19
  125.8 4.3 %collective-permute-start.16 = (f32[8,2,6,32]{3,2,1,0:T(8,128)S(1)}, f32[8,2,6,32]{3,2,1,0:T(8,128)S(1)}, u32[]{:S(2)}, u32[]{:S(2)}) collective-permute-start(f32[8,2,6,32]{3,2,1,0:T(8,128)S(1)} %get-tuple-element.34), channel_id=1, source_target_pairs={{1,0},{2,1},{3,2},{5,4},{6,5},{7,6},{9,8},{10,9},{11,10},{13,12},{... | collective-permute-start | bytes 36872 | tf_op jit(solution)/shard_map/ppermute | solution.py:20
  127.1 3.9 %collective-permute-start.17 = (f32[8,2,6,32]{3,2,1,0:T(8,128)S(1)}, f32[8,2,6,32]{3,2,1,0:T(8,128)S(1)}, u32[]{:S(2)}, u32[]{:S(2)}) collective-permute-start(f32[8,2,6,32]{3,2,1,0:T(8,128)S(1)} %get-tuple-element.35), channel_id=1, source_target_pairs={{0,1},{1,2},{2,3},{4,5},{5,6},{6,7},{8,9},{9,10},{10,11},{12,13},{... | collective-permute-start | bytes 36872 | tf_op jit(solution)/shard_map/ppermute | solution.py:19
  134.3 8.7 %copy-start.4 = (f32[2,12,2,6,512]{4,2,3,1,0:T(2,128)S(1)}, f32[2,12,2,6,512]{4,2,3,1,0:T(2,128)}, u32[]{:S(2)}) copy-start(f32[2,12,2,6,512]{4,2,3,1,0:T(2,128)} %copy-done.3) | copy-start | bytes 1769476
  137.4 5.5 %collective-permute-start.18 = (f32[2,2,6,512]{3,2,1,0:T(8,128)}, f32[2,2,6,512]{3,2,1,0:T(8,128)S(1)}, u32[]{:S(2)}, u32[]{:S(2)}) collective-permute-start(f32[2,2,6,512]{3,2,1,0:T(8,128)} %bitcast.106), channel_id=1, source_target_pairs={{0,12},{1,13},{2,14},{3,15},{16,28},{17,29},{18,30},{19,31}} | collective-permute-start | bytes 147464 | tf_op jit(solution)/shard_map/ppermute | solution.py:28
  138.8 4.5 %collective-permute-start.19 = (f32[2,2,6,512]{3,2,1,0:T(8,128)}, f32[2,2,6,512]{3,2,1,0:T(8,128)S(1)}, u32[]{:S(2)}, u32[]{:S(2)}) collective-permute-start(f32[2,2,6,512]{3,2,1,0:T(8,128)} %bitcast.107), channel_id=1, source_target_pairs={{0,8},{4,12},{1,9},{5,13},{2,10},{6,14},{3,11},{7,15},{16,24},{20,... | collective-permute-start | bytes 147464 | tf_op jit(solution)/shard_map/ppermute | solution.py:28
  141.0 4.4 %collective-permute-start.20 = (f32[2,2,6,512]{3,2,1,0:T(8,128)}, f32[2,2,6,512]{3,2,1,0:T(8,128)S(1)}, u32[]{:S(2)}, u32[]{:S(2)}) collective-permute-start(f32[2,2,6,512]{3,2,1,0:T(8,128)} %bitcast.108), channel_id=1, source_target_pairs={{0,4},{4,8},{8,12},{1,5},{5,9},{9,13},{2,6},{6,10},{10,14},{3,7},{... | collective-permute-start | bytes 147464 | tf_op jit(solution)/shard_map/ppermute | solution.py:28
  149.1 5.1 %copy-start.19 = (f32[8]{0:T(128)S(1)}, f32[8]{0:T(128)}, u32[]{:S(2)}) copy-start(f32[8]{0:T(128)} %param.25) | copy-start | bytes 100
  149.1 5.1 %copy-start.20 = (s32[2]{0:T(128)S(1)}, s32[2]{0:T(128)}, u32[]{:S(2)}) copy-start(s32[2]{0:T(128)} %param.24) | copy-start | bytes 28
  149.1 12.4 %copy-start.8 = (f32[2,12,2,6,512]{4,2,3,1,0:T(2,128)S(1)}, f32[2,12,2,6,512]{4,2,3,1,0:T(2,128)}, u32[]{:S(2)}) copy-start(f32[2,12,2,6,512]{4,2,3,1,0:T(2,128)} %copy-done.7) | copy-start | bytes 1769476
  152.8 11.4 %copy-start.6 = (f32[2,12,2,6,512]{4,2,3,1,0:T(2,128)S(1)}, f32[2,12,2,6,512]{4,2,3,1,0:T(2,128)}, u32[]{:S(2)}) copy-start(f32[2,12,2,6,512]{4,2,3,1,0:T(2,128)} %copy-done.5) | copy-start | bytes 1769476
  152.8 8.7 %collective-permute-start.21 = (f32[2,2,6,512]{3,2,1,0:T(8,128)}, f32[2,2,6,512]{3,2,1,0:T(8,128)S(1)}, u32[]{:S(2)}, u32[]{:S(2)}) collective-permute-start(f32[2,2,6,512]{3,2,1,0:T(8,128)} %bitcast.103), channel_id=1, source_target_pairs={{12,0},{13,1},{14,2},{15,3},{28,16},{29,17},{30,18},{31,19}} | collective-permute-start | bytes 147464 | tf_op jit(solution)/shard_map/ppermute | solution.py:28
  154.4 9.7 %collective-permute-start.22 = (f32[2,2,6,512]{3,2,1,0:T(8,128)}, f32[2,2,6,512]{3,2,1,0:T(8,128)S(1)}, u32[]{:S(2)}, u32[]{:S(2)}) collective-permute-start(f32[2,2,6,512]{3,2,1,0:T(8,128)} %bitcast.104), channel_id=1, source_target_pairs={{8,0},{12,4},{9,1},{13,5},{10,2},{14,6},{11,3},{15,7},{24,16},{28,... | collective-permute-start | bytes 147464 | tf_op jit(solution)/shard_map/ppermute | solution.py:28
  155.7 8.8 %collective-permute-start.23 = (f32[2,2,6,512]{3,2,1,0:T(8,128)}, f32[2,2,6,512]{3,2,1,0:T(8,128)S(1)}, u32[]{:S(2)}, u32[]{:S(2)}) collective-permute-start(f32[2,2,6,512]{3,2,1,0:T(8,128)} %bitcast.105), channel_id=1, source_target_pairs={{4,0},{8,4},{12,8},{5,1},{9,5},{13,9},{6,2},{10,6},{14,10},{7,3},{... | collective-permute-start | bytes 147464 | tf_op jit(solution)/shard_map/ppermute | solution.py:28
  168.8 1.3 copy-start.16
  170.4 4.2 %collective-permute-start.24 = (f32[8,3,512]{2,0,1:T(8,128)S(1)}, f32[8,3,512]{2,0,1:T(8,128)S(1)}, u32[]{:S(2)}, u32[]{:S(2)}) collective-permute-start(f32[8,3,512]{2,0,1:T(8,128)S(1)} %bitcast.96), channel_id=1, source_target_pairs={{0,16},{16,0},{1,17},{17,1},{2,18},{18,2},{3,19},{19,3},{4,20},{20... | collective-permute-start | bytes 147464 | tf_op jit(solution)/shard_map/ppermute | solution.py:246

commit v7 on v4

--- a/solution.py
+++ b/solution.py
@@ -33,11 +33,13 @@
 
 
 def _rows_times(blocks_ref, index, vec):
-    total = None
-    for a in range(vec.shape[0]):
-        term = blocks_ref[index + (a,)] * vec[a : a + 1, :]
-        total = term if total is None else total + term
-    return total
+    terms = [blocks_ref[index + (a,)] * vec[a : a + 1, :] for a in range(vec.shape[0])]
+    while len(terms) > 1:
+        paired = [terms[j] + terms[j + 1] for j in range(0, len(terms) - 1, 2)]
+        if len(terms) % 2:
+            paired.append(terms[-1])
+        terms = paired
+    return terms[0]
 
 
 def _init_carry(carry_ref, inc_ref):
@@ -70,6 +72,23 @@
             val_ref, carry_ref = outs
         else:
             (carry_ref,) = outs
+        if width == 1:
+            lasts = [inc_ref[0, 0, c] for c in range(conds)]
+            befores = [inc_ref[1, 0, c] for c in range(conds)]
+            for i in range(count):
+                for c in range(conds):
+                    acc = _rows_times(nt_ref, (i, c), lasts[c]) + _rows_times(
+                        ft_ref, (i, c), befores[c]
+                    )
+                    now = rhs_ref[i, c] - acc
+                    befores[c] = lasts[c]
+                    lasts[c] = now
+                    if want_values:
+                        val_ref[i, c] = now
+            for c in range(conds):
+                carry_ref[0, 0, c] = lasts[c]
+                carry_ref[1, 0, c] = befores[c]
+            return
         _init_carry(carry_ref, inc_ref)
 
         def step(i, unused):
@@ -119,6 +138,20 @@
             val_ref, carry_ref = outs
         else:
             (carry_ref,) = outs
+        if width == 1:
+            pendings = [inc_ref[0, 0, c] for c in range(conds)]
+            partials = [inc_ref[1, 0, c] for c in range(conds)]
+            for i in range(count - 1, -1, -1):
+                for c in range(conds):
+                    now = _rows_times(d_ref, (i, c), rhs_ref[i, c] - pendings[c])
+                    pendings[c] = partials[c] + _rows_times(b_ref, (i, c), now)
+                    partials[c] = _rows_times(a_ref, (i, c), now)
+                    if want_values:
+                        val_ref[i, c] = now
+            for c in range(conds):
+                carry_ref[0, 0, c] = pendings[c]
+                carry_ref[1, 0, c] = partials[c]
+            return
         _init_carry(carry_ref, inc_ref)
 
         def step(t, unused):

time: 166 us -> 166 us (level)
  no operation moved by 1% of the time
where the time goes in v7:
time: 166 us; the launch traced here: 165 us
  starting transfers between devices  57.6 us (35%)
  Pallas kernels  41.7 us (25%)
  waiting for transfers between devices  31.3 us (19%)
  local copies, waits for them, and re-layouts  19.6 us (12%)
  other arithmetic  11.7 us (7%)
    ppermute x16, starting transfers between devices, from_behind(): lax.ppermute(value, axis, [(source, source + steps) for source in range(f...  34.6 us
    ppermute x16, waiting for transfers between devices, from_behind(): lax.ppermute(value, axis, [(source, source + steps) for source in range(f...  28.8 us
    pallas_call x5, Pallas kernels, lower_pallas(): pl.pallas_call(kernel, out_shape=tuple(out_shape), in_specs=_vmem_specs(l...  22.7 us
    pallas_call x5, Pallas kernels, upper_pallas(): pl.pallas_call(kernel, out_shape=tuple(out_shape), in_specs=_vmem_specs(l...  19 us
    ppermute x4, starting transfers between devices, extended(): before = lax.ppermute(last, axis, up)  16.4 us
    unnamed x44, local copies, waits for them, and re-layouts  6.39 us
    ppermute x4, starting transfers between devices, extended(): after = lax.ppermute(first, axis, down)  5.15 us
    reduce_sum x8, other arithmetic, carry_through(): return jnp.sum(jnp.sum(split * inputs, axis=2), axis=1)  4.17 us
  transfers between devices with their start and end apart: 25, of which 8 were waited for; matrix products, arithmetic and copies ran while one was open for 14% of the time, Pallas kernels for 15%

profile of v7, /device:TPU:0, one launch (start us, length us, event | category | flops | bytes accessed | tf_op | source)
XLA Modules:
  0.0 164.9 jit_solution(16037657518866343714)
XLA Ops:
  0.6 1.0 copy.236
  1.8 1.3 collective-permute-start.2
  3.0 3.0 %collective-permute-start.3 = (f32[8,2,6,32]{3,2,1,0:T(8,128)S(1)}, f32[8,2,6,32]{3,2,1,0:T(8,128)S(1)}, u32[]{:S(2)}, u32[]{:S(2)}) collective-permute-start(f32[8,2,6,32]{3,2,1,0:T(8,128)S(1)} %get-tuple-element.37), channel_id=1, source_target_pairs={{0,1},{1,2},{2,3},{4,5},{5,6},{6,7},{8,9},{9,10},{10,11},{12,13},{... | collective-permute-start | bytes 36872 | tf_op jit(solution)/shard_map/ppermute | solution.py:19
  6.1 1.3 collective-permute-start
  7.4 5.6 %collective-permute-start.1 = (f32[1,2,6,512]{3,2,1,0:T(8,128)S(1)}, f32[1,2,6,512]{3,2,1,0:T(8,128)S(1)}, u32[]{:S(2)}, u32[]{:S(2)}) collective-permute-start(f32[1,2,6,512]{3,2,1,0:T(8,128)S(1)} %get-tuple-element.35), channel_id=1, source_target_pairs={{0,4},{4,8},{8,12},{1,5},{5,9},{9,13},{2,6},{6,10},{10,14},{3,7},{... | collective-permute-start | bytes 73736 | tf_op jit(solution)/shard_map/ppermute | solution.py:19
  13.0 4.0 %copy_bitcast_fusion = (f32[8,2,6,6,512]{4,3,2,1,0:T(8,128)}, f32[8,2,6,6,512]{4,3,2,1,0:T(8,128)}) fusion(f32[8,2,6,6,512]{4,1,3,2,0:T(2,128)} %param.16, f32[8,2,6,6,512]{4,1,3,2,0:T(2,128)} %param.15), kind=kLoop, calls=%fused_computation | loop fusion | bytes 4718592 | tf_op jit(solution)/shard_map/transpose | solution.py:232
  17.0 6.8 %shard_map.140 = f32[2,12,2,6,512]{4,3,2,1,0:T(8,128)} custom-call(f32[8,2,6,6,512]{4,3,2,1,0:T(8,128)} %get-tuple-element.39.refs_0_.refs_1_, f32[8,2,6,6,512]{4,3,2,1,0:T(8,128)} %get-tuple-element.38.refs_1_.refs_2_), custom_call_target="tpu_custom_call" | custom-call | tf_op jit(solution)/shard_map/pallas_call | solution.py:116
  23.9 2.5 %copy.213 = f32[2,12,2,6,512]{4,2,3,1,0:T(2,128)} copy(f32[2,12,2,6,512]{4,3,2,1,0:T(8,128)} %shard_map.140) | data formatting | bytes 1179648 | tf_op jit(solution)/shard_map/pallas_call | solution.py:116
  26.3 5.8 %collective-permute-start.5 = (f32[2,12,2,6,512]{4,2,3,1,0:T(2,128)}, f32[2,12,2,6,512]{4,2,3,1,0:T(2,128)}, u32[]{:S(2)}, u32[]{:S(2)}) collective-permute-start(f32[2,12,2,6,512]{4,2,3,1,0:T(2,128)} %copy.213), channel_id=1, source_target_pairs={{0,8},{4,12},{1,9},{5,13},{2,10},{6,14},{3,11},{7,15},{16,24},{20,... | collective-permute-start | bytes 1769480 | tf_op jit(solution)/shard_map/ppermute | solution.py:28
  32.1 1.3 collective-permute-start.4
  34.1 0.8 convolution_bitcast_fusion.1
  36.0 0.8 copy.220.refs_0_
  36.7 0.6 broadcast_in_dim.10.refs_3_.refs_4_
  37.4 3.1 %shard_map.141 = (f32[8,2,6,512]{3,2,1,0:T(8,128)}, f32[2,1,2,6,512]{4,3,2,1,0:T(8,128)}) custom-call(f32[8,2,6,512]{3,2,1,0:T(8,128)} %copy.220.refs_0_, f32[8,2,6,6,512]{4,3,2,1,0:T(8,128)} %get-tuple-element.39.refs_0_.refs_1_, f32[8,2,6,6,512]{4,3,2,1,0:T(8,128)} %get-tuple-element.38.refs_1_.refs_2_, f32[2,1,2,6,512]{4,3,2,1,0:T(8,128)} %broadcast_in_dim.10.refs_3_.refs_4_), custom_call_target="tpu_custom_call" | custom-call | tf_op jit(solution)/shard_map/pallas_call | solution.py:116
  40.5 1.4 collective-permute-start.6
  41.9 1.4 copy.233.refs_0_.refs_1_
  43.4 1.4 copy.234.refs_1_.refs_2_
  44.8 1.4 copy.235.refs_2_.refs_3_
  46.2 8.3 %shard_map.143 = f32[2,12,2,6,512]{4,3,2,1,0:T(8,128)} custom-call(f32[8,2,6,6,512]{4,3,2,1,0:T(8,128)} %copy.233.refs_0_.refs_1_, f32[8,2,6,6,512]{4,3,2,1,0:T(8,128)} %copy.234.refs_1_.refs_2_, f32[8,2,6,6,512]{4,3,2,1,0:T(8,128)} %copy.235.refs_2_.refs_3_), custom_call_target="tpu_custom_call" | custom-call | tf_op jit(solution)/shard_map/pallas_call | solution.py:180
  54.5 2.4 %copy.224 = f32[2,12,2,6,512]{4,2,3,1,0:T(2,128)} copy(f32[2,12,2,6,512]{4,3,2,1,0:T(8,128)} %shard_map.143) | data formatting | bytes 1179648 | tf_op jit(solution)/shard_map/pallas_call | solution.py:180
  56.9 1.3 collective-permute-start.10
  58.2 1.3 collective-permute-start.9
  59.5 6.1 %collective-permute-start.7 = (f32[2,2,6,512]{3,2,1,0:T(8,128)S(1)}, f32[2,2,6,512]{3,2,1,0:T(8,128)S(1)}, u32[]{:S(2)}, u32[]{:S(2)}) collective-permute-start(f32[2,2,6,512]{3,2,1,0:T(8,128)S(1)} %bitcast.88), channel_id=1, source_target_pairs={{0,8},{4,12},{1,9},{5,13},{2,10},{6,14},{3,11},{7,15},{16,24},{20,... | collective-permute-start | bytes 147464 | tf_op jit(solution)/shard_map/ppermute | solution.py:28
  65.7 4.0 %collective-permute-start.8 = (f32[2,2,6,512]{3,2,1,0:T(8,128)S(1)}, f32[2,2,6,512]{3,2,1,0:T(8,128)S(1)}, u32[]{:S(2)}, u32[]{:S(2)}) collective-permute-start(f32[2,2,6,512]{3,2,1,0:T(8,128)S(1)} %bitcast.89), channel_id=1, source_target_pairs={{0,4},{4,8},{8,12},{1,5},{5,9},{9,13},{2,6},{6,10},{10,14},{3,7},{... | collective-permute-start | bytes 147464 | tf_op jit(solution)/shard_map/ppermute | solution.py:28
  69.7 1.3 multiply_reduce_fusion.10
  71.6 0.6 fusion.18.refs_3_
  72.2 3.0 %shard_map.142 = (f32[8,2,6,512]{3,2,1,0:T(8,128)}, f32[2,1,2,6,512]{4,3,2,1,0:T(8,128)}) custom-call(f32[8,2,6,512]{3,2,1,0:T(8,128)} %copy.220.refs_0_, f32[8,2,6,6,512]{4,3,2,1,0:T(8,128)} %get-tuple-element.39.refs_0_.refs_1_, f32[8,2,6,6,512]{4,3,2,1,0:T(8,128)} %get-tuple-element.38.refs_1_.refs_2_, f32[2,1,2,6,512]{4,3,2,1,0:T(8,128)} %fusion.18.refs_3_), custom_call_target="tpu_custom_call" | custom-call | tf_op jit(solution)/shard_map/pallas_call | solution.py:116
  75.2 3.6 %shard_map.144 = (f32[8,2,6,512]{3,2,1,0:T(8,128)}, f32[2,1,2,6,512]{4,3,2,1,0:T(8,128)}) custom-call(f32[8,2,6,512]{3,2,1,0:T(8,128)} %get-tuple-element.11.refs_0_, f32[8,2,6,6,512]{4,3,2,1,0:T(8,128)} %copy.233.refs_0_.refs_1_, f32[8,2,6,6,512]{4,3,2,1,0:T(8,128)} %copy.234.refs_1_.refs_2_, f32[8,2,6,6,512]{4,3,2,1,0:T(8,128)} %copy.235.refs_2_.refs_3_, ...), custom_call_target="tpu_custom_call" | custom-call | tf_op jit(solution)/shard_map/pallas_call | solution.py:180
  78.8 1.3 collective-permute-start.11
  80.1 1.3 collective-permute-start.12
  81.4 1.3 collective-permute-start.13
  82.7 6.3 %collective-permute-done.11 = f32[2,2,6,512]{3,2,1,0:T(8,128)S(1)} collective-permute-done((f32[2,2,6,512]{3,2,1,0:T(8,128)}, f32[2,2,6,512]{3,2,1,0:T(8,128)S(1)}, u32[]{:S(2)}, u32[]{:S(2)}) %collective-permute-start.11) | collective-permute-done | bytes 49184 | tf_op jit(solution)/shard_map/ppermute | solution.py:28
  89.3 14.8 %collective-permute-done.12 = f32[2,2,6,512]{3,2,1,0:T(8,128)S(1)} collective-permute-done((f32[2,2,6,512]{3,2,1,0:T(8,128)}, f32[2,2,6,512]{3,2,1,0:T(8,128)S(1)}, u32[]{:S(2)}, u32[]{:S(2)}) %collective-permute-start.12) | collective-permute-done | bytes 49184 | tf_op jit(solution)/shard_map/ppermute | solution.py:28
  104.5 0.6 fusion.16.refs_4_
  105.1 3.6 %shard_map.145 = (f32[8,2,6,512]{3,2,1,0:T(8,128)}, f32[2,1,2,6,512]{4,3,2,1,0:T(8,128)}) custom-call(f32[8,2,6,512]{3,2,1,0:T(8,128)} %get-tuple-element.11.refs_0_, f32[8,2,6,6,512]{4,3,2,1,0:T(8,128)} %copy.233.refs_0_.refs_1_, f32[8,2,6,6,512]{4,3,2,1,0:T(8,128)} %copy.234.refs_1_.refs_2_, f32[8,2,6,6,512]{4,3,2,1,0:T(8,128)} %copy.235.refs_2_.refs_3_, ...), custom_call_target="tpu_custom_call" | custom-call | tf_op jit(solution)/shard_map/pallas_call | solution.py:180
  108.7 1.1 add_multiply_fusion.1
  109.8 1.3 collective-permute-start.14
  111.1 4.5 %collective-permute-start.15 = (f32[1,2,6,512]{3,2,1,0:T(8,128)S(1)}, f32[1,2,6,512]{3,2,1,0:T(8,128)S(1)}, u32[]{:S(2)}, u32[]{:S(2)}) collective-permute-start(f32[1,2,6,512]{3,2,1,0:T(8,128)S(1)} %get-tuple-element.31), channel_id=1, source_target_pairs={{0,4},{4,8},{8,12},{1,5},{5,9},{9,13},{2,6},{6,10},{10,14},{3,7},{... | collective-permute-start | bytes 73736 | tf_op jit(solution)/shard_map/ppermute | solution.py:19
  115.7 1.3 collective-permute-start.16
  117.0 3.2 %collective-permute-start.17 = (f32[8,2,6,32]{3,2,1,0:T(8,128)S(1)}, f32[8,2,6,32]{3,2,1,0:T(8,128)S(1)}, u32[]{:S(2)}, u32[]{:S(2)}) collective-permute-start(f32[8,2,6,32]{3,2,1,0:T(8,128)S(1)} %get-tuple-element.33), channel_id=1, source_target_pairs={{0,1},{1,2},{2,3},{4,5},{5,6},{6,7},{8,9},{9,10},{10,11},{12,13},{... | collective-permute-start | bytes 36872 | tf_op jit(solution)/shard_map/ppermute | solution.py:19
  120.3 0.7 collective-permute-done.17
  121.6 0.8 convolution_bitcast_fusion
  123.5 0.8 copy.245.refs_0_
  124.2 3.0 %shard_map.146 = (f32[8,2,6,512]{3,2,1,0:T(8,128)}, f32[2,1,2,6,512]{4,3,2,1,0:T(8,128)}) custom-call(f32[8,2,6,512]{3,2,1,0:T(8,128)} %copy.245.refs_0_, f32[8,2,6,6,512]{4,3,2,1,0:T(8,128)} %get-tuple-element.39.refs_0_.refs_1_, f32[8,2,6,6,512]{4,3,2,1,0:T(8,128)} %get-tuple-element.38.refs_1_.refs_2_, f32[2,1,2,6,512]{4,3,2,1,0:T(8,128)} %broadcast_in_dim.10.refs_3_.refs_4_), custom_call_target="tpu_custom_call" | custom-call | tf_op jit(solution)/shard_map/pallas_call | solution.py:116
  127.2 1.5 collective-permute-start.18
  128.7 2.2 %collective-permute-start.19 = (f32[2,2,6,512]{3,2,1,0:T(8,128)}, f32[2,2,6,512]{3,2,1,0:T(8,128)S(1)}, u32[]{:S(2)}, u32[]{:S(2)}) collective-permute-start(f32[2,2,6,512]{3,2,1,0:T(8,128)} %bitcast.97), channel_id=1, source_target_pairs={{0,8},{4,12},{1,9},{5,13},{2,10},{6,14},{3,11},{7,15},{16,24},{20,... | collective-permute-start | bytes 147464 | tf_op jit(solution)/shard_map/ppermute | solution.py:28
  130.9 1.8 %collective-permute-start.20 = (f32[2,2,6,512]{3,2,1,0:T(8,128)}, f32[2,2,6,512]{3,2,1,0:T(8,128)S(1)}, u32[]{:S(2)}, u32[]{:S(2)}) collective-permute-start(f32[2,2,6,512]{3,2,1,0:T(8,128)} %bitcast.98), channel_id=1, source_target_pairs={{0,4},{4,8},{8,12},{1,5},{5,9},{9,13},{2,6},{6,10},{10,14},{3,7},{... | collective-permute-start | bytes 147464 | tf_op jit(solution)/shard_map/ppermute | solution.py:28
  132.9 1.3 multiply_reduce_fusion.6
  134.5 0.9 collective-permute-done.20
  135.4 0.6 fusion.14.refs_3_
  136.0 3.0 %shard_map.147 = (f32[8,2,6,512]{3,2,1,0:T(8,128)}, f32[2,1,2,6,512]{4,3,2,1,0:T(8,128)}) custom-call(f32[8,2,6,512]{3,2,1,0:T(8,128)} %copy.245.refs_0_, f32[8,2,6,6,512]{4,3,2,1,0:T(8,128)} %get-tuple-element.39.refs_0_.refs_1_, f32[8,2,6,6,512]{4,3,2,1,0:T(8,128)} %get-tuple-element.38.refs_1_.refs_2_, f32[2,1,2,6,512]{4,3,2,1,0:T(8,128)} %fusion.14.refs_3_), custom_call_target="tpu_custom_call" | custom-call | tf_op jit(solution)/shard_map/pallas_call | solution.py:116
  139.1 3.7 %shard_map.148 = (f32[8,2,6,512]{3,2,1,0:T(8,128)}, f32[2,1,2,6,512]{4,3,2,1,0:T(8,128)}) custom-call(f32[8,2,6,512]{3,2,1,0:T(8,128)} %get-tuple-element.15.refs_0_, f32[8,2,6,6,512]{4,3,2,1,0:T(8,128)} %copy.233.refs_0_.refs_1_, f32[8,2,6,6,512]{4,3,2,1,0:T(8,128)} %copy.234.refs_1_.refs_2_, f32[8,2,6,6,512]{4,3,2,1,0:T(8,128)} %copy.235.refs_2_.refs_3_, ...), custom_call_target="tpu_custom_call" | custom-call | tf_op jit(solution)/shard_map/pallas_call | solution.py:180
  142.7 1.4 collective-permute-start.21
  144.4 1.3 collective-permute-start.22
  145.7 1.3 collective-permute-start.23
  147.0 4.2 %collective-permute-done.21 = f32[2,2,6,512]{3,2,1,0:T(8,128)S(1)} collective-permute-done((f32[2,2,6,512]{3,2,1,0:T(8,128)}, f32[2,2,6,512]{3,2,1,0:T(8,128)S(1)}, u32[]{:S(2)}, u32[]{:S(2)}) %collective-permute-start.21) | collective-permute-done | bytes 49184 | tf_op jit(solution)/shard_map/ppermute | solution.py:28
  151.5 2.4 %collective-permute-done.22 = f32[2,2,6,512]{3,2,1,0:T(8,128)S(1)} collective-permute-done((f32[2,2,6,512]{3,2,1,0:T(8,128)}, f32[2,2,6,512]{3,2,1,0:T(8,128)S(1)}, u32[]{:S(2)}, u32[]{:S(2)}) %collective-permute-start.22) | collective-permute-done | bytes 49184 | tf_op jit(solution)/shard_map/ppermute | solution.py:28
  154.3 0.6 fusion.12.refs_4_
  154.9 3.6 %shard_map.149 = (f32[8,2,6,512]{3,2,1,0:T(8,128)}, f32[2,1,2,6,512]{4,3,2,1,0:T(8,128)}) custom-call(f32[8,2,6,512]{3,2,1,0:T(8,128)} %get-tuple-element.15.refs_0_, f32[8,2,6,6,512]{4,3,2,1,0:T(8,128)} %copy.233.refs_0_.refs_1_, f32[8,2,6,6,512]{4,3,2,1,0:T(8,128)} %copy.234.refs_1_.refs_2_, f32[8,2,6,6,512]{4,3,2,1,0:T(8,128)} %copy.235.refs_2_.refs_3_, ...), custom_call_target="tpu_custom_call" | custom-call | tf_op jit(solution)/shard_map/pallas_call | solution.py:180
  158.5 1.1 multiply_bitcast_fusion
  160.1 1.6 collective-permute-start.24
  161.7 0.8 copy.256
  162.5 1.8 %collective-permute-done.24 = f32[8,3,512]{2,0,1:T(8,128)S(1)} collective-permute-done((f32[8,3,512]{2,0,1:T(8,128)S(1)}, f32[8,3,512]{2,0,1:T(8,128)S(1)}, u32[]{:S(2)}, u32[]{:S(2)}) %collective-permute-start.24) | collective-permute-done | bytes 49184 | tf_op jit(solution)/shard_map/ppermute | solution.py:268
  164.3 0.6 fusion.27
  (95 shorter events, 6.3 us)
Async XLA Ops:
  0.6 33.5 %copy-start = (f32[2,6,32,32]{3,2,1,0:T(8,128)S(1)}, f32[2,6,32,32]{3,2,1,0:T(8,128)}, u32[]{:S(2)}) copy-start(f32[2,6,32,32]{3,2,1,0:T(8,128)} %param.21) | copy-start | bytes 147460
  1.8 30.4 %collective-permute-start.2 = (f32[8,2,6,32]{3,2,1,0:T(8,128)S(1)}, f32[8,2,6,32]{3,2,1,0:T(8,128)S(1)}, u32[]{:S(2)}, u32[]{:S(2)}) collective-permute-start(f32[8,2,6,32]{3,2,1,0:T(8,128)S(1)} %get-tuple-element.36), channel_id=1, source_target_pairs={{1,0},{2,1},{3,2},{5,4},{6,5},{7,6},{9,8},{10,9},{11,10},{13,12},{... | collective-permute-start | bytes 36872 | tf_op jit(solution)/shard_map/ppermute | solution.py:20
  3.0 30.4 %collective-permute-start.3 = (f32[8,2,6,32]{3,2,1,0:T(8,128)S(1)}, f32[8,2,6,32]{3,2,1,0:T(8,128)S(1)}, u32[]{:S(2)}, u32[]{:S(2)}) collective-permute-start(f32[8,2,6,32]{3,2,1,0:T(8,128)S(1)} %get-tuple-element.37), channel_id=1, source_target_pairs={{0,1},{1,2},{2,3},{4,5},{5,6},{6,7},{8,9},{9,10},{10,11},{12,13},{... | collective-permute-start | bytes 36872 | tf_op jit(solution)/shard_map/ppermute | solution.py:19
  6.1 27.4 %collective-permute-start = (f32[1,2,6,512]{3,2,1,0:T(8,128)S(1)}, f32[1,2,6,512]{3,2,1,0:T(8,128)S(1)}, u32[]{:S(2)}, u32[]{:S(2)}) collective-permute-start(f32[1,2,6,512]{3,2,1,0:T(8,128)S(1)} %get-tuple-element.34), channel_id=1, source_target_pairs={{4,0},{8,4},{12,8},{5,1},{9,5},{13,9},{6,2},{10,6},{14,10},{7,3},{... | collective-permute-start | bytes 73736 | tf_op jit(solution)/shard_map/ppermute | solution.py:20
  7.4 26.1 %collective-permute-start.1 = (f32[1,2,6,512]{3,2,1,0:T(8,128)S(1)}, f32[1,2,6,512]{3,2,1,0:T(8,128)S(1)}, u32[]{:S(2)}, u32[]{:S(2)}) collective-permute-start(f32[1,2,6,512]{3,2,1,0:T(8,128)S(1)} %get-tuple-element.35), channel_id=1, source_target_pairs={{0,4},{4,8},{8,12},{1,5},{5,9},{9,13},{2,6},{6,10},{10,14},{3,7},{... | collective-permute-start | bytes 73736 | tf_op jit(solution)/shard_map/ppermute | solution.py:19
  23.9 9.6 %copy-start.11 = (f32[8,2,6,512]{3,1,2,0:T(2,128)S(1)}, f32[8,2,6,512]{3,1,2,0:T(2,128)}, u32[]{:S(2)}) copy-start(f32[8,2,6,512]{3,1,2,0:T(2,128)} %param.14) | copy-start | bytes 589828
  26.3 39.4 %collective-permute-start.5 = (f32[2,12,2,6,512]{4,2,3,1,0:T(2,128)}, f32[2,12,2,6,512]{4,2,3,1,0:T(2,128)}, u32[]{:S(2)}, u32[]{:S(2)}) collective-permute-start(f32[2,12,2,6,512]{4,2,3,1,0:T(2,128)} %copy.213), channel_id=1, source_target_pairs={{0,8},{4,12},{1,9},{5,13},{2,10},{6,14},{3,11},{7,15},{16,24},{20,... | collective-permute-start | bytes 1769480 | tf_op jit(solution)/shard_map/ppermute | solution.py:28
  32.1 39.0 %collective-permute-start.4 = (f32[2,12,2,6,512]{4,2,3,1,0:T(2,128)}, f32[2,12,2,6,512]{4,2,3,1,0:T(2,128)S(1)}, u32[]{:S(2)}, u32[]{:S(2)}) collective-permute-start(f32[2,12,2,6,512]{4,2,3,1,0:T(2,128)} %copy.213), channel_id=1, source_target_pairs={{0,4},{4,8},{8,12},{1,5},{5,9},{9,13},{2,6},{6,10},{10,14},{3,7},{... | collective-permute-start | bytes 1769480 | tf_op jit(solution)/shard_map/ppermute | solution.py:28
  34.1 1.3 copy-start.1
  37.4 4.5 %copy-start.8 = (f32[8,2,6,6,512]{4,1,3,2,0:T(2,128)S(1)}, f32[8,2,6,6,512]{4,1,3,2,0:T(2,128)}, u32[]{:S(2)}) copy-start(f32[8,2,6,6,512]{4,1,3,2,0:T(2,128)} %param.17) | copy-start | bytes 3538948
  40.5 2.9 %copy-start.9 = (f32[8,2,6,6,512]{4,1,3,2,0:T(2,128)S(1)}, f32[8,2,6,6,512]{4,1,3,2,0:T(2,128)}, u32[]{:S(2)}) copy-start(f32[8,2,6,6,512]{4,1,3,2,0:T(2,128)} %param.18) | copy-start | bytes 3538948
  40.5 19.0 %collective-permute-start.6 = (f32[2,2,6,512]{3,2,1,0:T(8,128)}, f32[2,2,6,512]{3,2,1,0:T(8,128)S(1)}, u32[]{:S(2)}, u32[]{:S(2)}) collective-permute-start(f32[2,2,6,512]{3,2,1,0:T(8,128)} %bitcast.87), channel_id=1, source_target_pairs={{0,12},{1,13},{2,14},{3,15},{16,28},{17,29},{18,30},{19,31}} | collective-permute-start | bytes 147464 | tf_op jit(solution)/shard_map/ppermute | solution.py:28
  43.4 1.4 copy-start.10
  54.5 5.0 %copy-start.16 = (f32[2,1,2,6,512]{4,3,2,1,0:T(8,128)S(1)}, f32[2,1,2,6,512]{4,3,2,1,0:T(8,128)}, u32[]{:S(2)}) copy-start(f32[2,1,2,6,512]{4,3,2,1,0:T(8,128)} %get-tuple-element.10) | copy-start | bytes 147460
  56.9 32.1 %collective-permute-start.10 = (f32[2,12,2,6,512]{4,2,3,1,0:T(2,128)}, f32[2,12,2,6,512]{4,2,3,1,0:T(2,128)S(1)}, u32[]{:S(2)}, u32[]{:S(2)}) collective-permute-start(f32[2,12,2,6,512]{4,2,3,1,0:T(2,128)} %copy.224), channel_id=1, source_target_pairs={{8,0},{12,4},{9,1},{13,5},{10,2},{14,6},{11,3},{15,7},{24,16},{28,... | collective-permute-start | bytes 1769480 | tf_op jit(solution)/shard_map/ppermute | solution.py:28
  58.2 46.0 %collective-permute-start.9 = (f32[2,12,2,6,512]{4,2,3,1,0:T(2,128)}, f32[2,12,2,6,512]{4,2,3,1,0:T(2,128)S(1)}, u32[]{:S(2)}, u32[]{:S(2)}) collective-permute-start(f32[2,12,2,6,512]{4,2,3,1,0:T(2,128)} %copy.224), channel_id=1, source_target_pairs={{4,0},{8,4},{12,8},{5,1},{9,5},{13,9},{6,2},{10,6},{14,10},{7,3},{... | collective-permute-start | bytes 1769480 | tf_op jit(solution)/shard_map/ppermute | solution.py:28
  59.5 11.5 %collective-permute-start.7 = (f32[2,2,6,512]{3,2,1,0:T(8,128)S(1)}, f32[2,2,6,512]{3,2,1,0:T(8,128)S(1)}, u32[]{:S(2)}, u32[]{:S(2)}) collective-permute-start(f32[2,2,6,512]{3,2,1,0:T(8,128)S(1)} %bitcast.88), channel_id=1, source_target_pairs={{0,8},{4,12},{1,9},{5,13},{2,10},{6,14},{3,11},{7,15},{16,24},{20,... | collective-permute-start | bytes 147464 | tf_op jit(solution)/shard_map/ppermute | solution.py:28
  65.7 5.8 %collective-permute-start.8 = (f32[2,2,6,512]{3,2,1,0:T(8,128)S(1)}, f32[2,2,6,512]{3,2,1,0:T(8,128)S(1)}, u32[]{:S(2)}, u32[]{:S(2)}) collective-permute-start(f32[2,2,6,512]{3,2,1,0:T(8,128)S(1)} %bitcast.89), channel_id=1, source_target_pairs={{0,4},{4,8},{8,12},{1,5},{5,9},{9,13},{2,6},{6,10},{10,14},{3,7},{... | collective-permute-start | bytes 147464 | tf_op jit(solution)/shard_map/ppermute | solution.py:28
  71.1 4.1 %copy-start.2 = (f32[2,12,2,6,512]{4,2,3,1,0:T(2,128)}, f32[2,12,2,6,512]{4,2,3,1,0:T(2,128)S(1)}, u32[]{:S(2)}) copy-start(f32[2,12,2,6,512]{4,2,3,1,0:T(2,128)S(1)} %collective-permute-done.4) | copy-start | bytes 1769476
  75.2 4.9 %copy-start.15 = (s32[8,512]{1,0:T(8,128)S(1)}, s32[8,512]{1,0:T(8,128)}, u32[]{:S(2)}) copy-start(s32[8,512]{1,0:T(8,128)} %param.23) | copy-start | bytes 49156
  78.8 10.2 %collective-permute-start.11 = (f32[2,2,6,512]{3,2,1,0:T(8,128)}, f32[2,2,6,512]{3,2,1,0:T(8,128)S(1)}, u32[]{:S(2)}, u32[]{:S(2)}) collective-permute-start(f32[2,2,6,512]{3,2,1,0:T(8,128)} %bitcast.90), channel_id=1, source_target_pairs={{12,0},{13,1},{14,2},{15,3},{28,16},{29,17},{30,18},{31,19}} | collective-permute-start | bytes 147464 | tf_op jit(solution)/shard_map/ppermute | solution.py:28
  80.1 24.0 %collective-permute-start.12 = (f32[2,2,6,512]{3,2,1,0:T(8,128)}, f32[2,2,6,512]{3,2,1,0:T(8,128)S(1)}, u32[]{:S(2)}, u32[]{:S(2)}) collective-permute-start(f32[2,2,6,512]{3,2,1,0:T(8,128)} %bitcast.91), channel_id=1, source_target_pairs={{8,0},{12,4},{9,1},{13,5},{10,2},{14,6},{11,3},{15,7},{24,16},{28,... | collective-permute-start | bytes 147464 | tf_op jit(solution)/shard_map/ppermute | solution.py:28
  81.4 23.0 %collective-permute-start.13 = (f32[2,2,6,512]{3,2,1,0:T(8,128)}, f32[2,2,6,512]{3,2,1,0:T(8,128)S(1)}, u32[]{:S(2)}, u32[]{:S(2)}) collective-permute-start(f32[2,2,6,512]{3,2,1,0:T(8,128)} %bitcast.92), channel_id=1, source_target_pairs={{4,0},{8,4},{12,8},{5,1},{9,5},{13,9},{6,2},{10,6},{14,10},{7,3},{... | collective-permute-start | bytes 147464 | tf_op jit(solution)/shard_map/ppermute | solution.py:28
  89.0 19.7 %copy-start.6 = (f32[2,12,2,6,512]{4,2,3,1,0:T(2,128)}, f32[2,12,2,6,512]{4,2,3,1,0:T(2,128)S(1)}, u32[]{:S(2)}) copy-start(f32[2,12,2,6,512]{4,2,3,1,0:T(2,128)S(1)} %collective-permute-done.10) | copy-start | bytes 1769476
  104.2 4.5 %copy-start.4 = (f32[2,12,2,6,512]{4,2,3,1,0:T(2,128)}, f32[2,12,2,6,512]{4,2,3,1,0:T(2,128)S(1)}, u32[]{:S(2)}) copy-start(f32[2,12,2,6,512]{4,2,3,1,0:T(2,128)S(1)} %collective-permute-done.9) | copy-start | bytes 1769476
  105.1 3.6 %copy-start.13 = (f32[8,2,6,512]{3,1,2,0:T(2,128)S(1)}, f32[8,2,6,512]{3,1,2,0:T(2,128)}, u32[]{:S(2)}) copy-start(f32[8,2,6,512]{3,1,2,0:T(2,128)} %param.13) | copy-start | bytes 589828
  108.7 12.3 %copy-start.12 = (f32[8,2,6,512]{3,1,2,0:T(2,128)S(1)}, f32[8,2,6,512]{3,1,2,0:T(2,128)}, u32[]{:S(2)}) copy-start(f32[8,2,6,512]{3,1,2,0:T(2,128)} %param.14) | copy-start | bytes 589828
  109.8 11.2 %collective-permute-start.14 = (f32[1,2,6,512]{3,2,1,0:T(8,128)S(1)}, f32[1,2,6,512]{3,2,1,0:T(8,128)S(1)}, u32[]{:S(2)}, u32[]{:S(2)}) collective-permute-start(f32[1,2,6,512]{3,2,1,0:T(8,128)S(1)} %get-tuple-element.30), channel_id=1, source_target_pairs={{4,0},{8,4},{12,8},{5,1},{9,5},{13,9},{6,2},{10,6},{14,10},{7,3},{... | collective-permute-start | bytes 73736 | tf_op jit(solution)/shard_map/ppermute | solution.py:20
  111.1 9.9 %collective-permute-start.15 = (f32[1,2,6,512]{3,2,1,0:T(8,128)S(1)}, f32[1,2,6,512]{3,2,1,0:T(8,128)S(1)}, u32[]{:S(2)}, u32[]{:S(2)}) collective-permute-start(f32[1,2,6,512]{3,2,1,0:T(8,128)S(1)} %get-tuple-element.31), channel_id=1, source_target_pairs={{0,4},{4,8},{8,12},{1,5},{5,9},{9,13},{2,6},{6,10},{10,14},{3,7},{... | collective-permute-start | bytes 73736 | tf_op jit(solution)/shard_map/ppermute | solution.py:19
  115.7 4.5 %collective-permute-start.16 = (f32[8,2,6,32]{3,2,1,0:T(8,128)S(1)}, f32[8,2,6,32]{3,2,1,0:T(8,128)S(1)}, u32[]{:S(2)}, u32[]{:S(2)}) collective-permute-start(f32[8,2,6,32]{3,2,1,0:T(8,128)S(1)} %get-tuple-element.32), channel_id=1, source_target_pairs={{1,0},{2,1},{3,2},{5,4},{6,5},{7,6},{9,8},{10,9},{11,10},{13,12},{... | collective-permute-start | bytes 36872 | tf_op jit(solution)/shard_map/ppermute | solution.py:20
  117.0 3.9 %collective-permute-start.17 = (f32[8,2,6,32]{3,2,1,0:T(8,128)S(1)}, f32[8,2,6,32]{3,2,1,0:T(8,128)S(1)}, u32[]{:S(2)}, u32[]{:S(2)}) collective-permute-start(f32[8,2,6,32]{3,2,1,0:T(8,128)S(1)} %get-tuple-element.33), channel_id=1, source_target_pairs={{0,1},{1,2},{2,3},{4,5},{5,6},{6,7},{8,9},{9,10},{10,11},{12,13},{... | collective-permute-start | bytes 36872 | tf_op jit(solution)/shard_map/ppermute | solution.py:19
  127.2 7.0 %copy-start.3 = (f32[2,12,2,6,512]{4,2,3,1,0:T(2,128)S(1)}, f32[2,12,2,6,512]{4,2,3,1,0:T(2,128)}, u32[]{:S(2)}) copy-start(f32[2,12,2,6,512]{4,2,3,1,0:T(2,128)} %copy-done.2) | copy-start | bytes 1769476
  127.2 5.6 %collective-permute-start.18 = (f32[2,2,6,512]{3,2,1,0:T(8,128)}, f32[2,2,6,512]{3,2,1,0:T(8,128)S(1)}, u32[]{:S(2)}, u32[]{:S(2)}) collective-permute-start(f32[2,2,6,512]{3,2,1,0:T(8,128)} %bitcast.96), channel_id=1, source_target_pairs={{0,12},{1,13},{2,14},{3,15},{16,28},{17,29},{18,30},{19,31}} | collective-permute-start | bytes 147464 | tf_op jit(solution)/shard_map/ppermute | solution.py:28
  128.7 5.5 %collective-permute-start.19 = (f32[2,2,6,512]{3,2,1,0:T(8,128)}, f32[2,2,6,512]{3,2,1,0:T(8,128)S(1)}, u32[]{:S(2)}, u32[]{:S(2)}) collective-permute-start(f32[2,2,6,512]{3,2,1,0:T(8,128)} %bitcast.97), channel_id=1, source_target_pairs={{0,8},{4,12},{1,9},{5,13},{2,10},{6,14},{3,11},{7,15},{16,24},{20,... | collective-permute-start | bytes 147464 | tf_op jit(solution)/shard_map/ppermute | solution.py:28
  130.9 4.4 %collective-permute-start.20 = (f32[2,2,6,512]{3,2,1,0:T(8,128)}, f32[2,2,6,512]{3,2,1,0:T(8,128)S(1)}, u32[]{:S(2)}, u32[]{:S(2)}) collective-permute-start(f32[2,2,6,512]{3,2,1,0:T(8,128)} %bitcast.98), channel_id=1, source_target_pairs={{0,4},{4,8},{8,12},{1,5},{5,9},{9,13},{2,6},{6,10},{10,14},{3,7},{... | collective-permute-start | bytes 147464 | tf_op jit(solution)/shard_map/ppermute | solution.py:28
  139.1 5.1 %copy-start.17 = (f32[8]{0:T(128)S(1)}, f32[8]{0:T(128)}, u32[]{:S(2)}) copy-start(f32[8]{0:T(128)} %param.25) | copy-start | bytes 100
  139.1 5.1 %copy-start.18 = (s32[2]{0:T(128)S(1)}, s32[2]{0:T(128)}, u32[]{:S(2)}) copy-start(s32[2]{0:T(128)} %param.24) | copy-start | bytes 28
  139.1 12.2 %copy-start.7 = (f32[2,12,2,6,512]{4,2,3,1,0:T(2,128)S(1)}, f32[2,12,2,6,512]{4,2,3,1,0:T(2,128)}, u32[]{:S(2)}) copy-start(f32[2,12,2,6,512]{4,2,3,1,0:T(2,128)} %copy-done.6) | copy-start | bytes 1769476
  142.7 11.3 %copy-start.5 = (f32[2,12,2,6,512]{4,2,3,1,0:T(2,128)S(1)}, f32[2,12,2,6,512]{4,2,3,1,0:T(2,128)}, u32[]{:S(2)}) copy-start(f32[2,12,2,6,512]{4,2,3,1,0:T(2,128)} %copy-done.4) | copy-start | bytes 1769476
  142.7 8.5 %collective-permute-start.21 = (f32[2,2,6,512]{3,2,1,0:T(8,128)}, f32[2,2,6,512]{3,2,1,0:T(8,128)S(1)}, u32[]{:S(2)}, u32[]{:S(2)}) collective-permute-start(f32[2,2,6,512]{3,2,1,0:T(8,128)} %bitcast.93), channel_id=1, source_target_pairs={{12,0},{13,1},{14,2},{15,3},{28,16},{29,17},{30,18},{31,19}} | collective-permute-start | bytes 147464 | tf_op jit(solution)/shard_map/ppermute | solution.py:28
  144.4 9.6 %collective-permute-start.22 = (f32[2,2,6,512]{3,2,1,0:T(8,128)}, f32[2,2,6,512]{3,2,1,0:T(8,128)S(1)}, u32[]{:S(2)}, u32[]{:S(2)}) collective-permute-start(f32[2,2,6,512]{3,2,1,0:T(8,128)} %bitcast.94), channel_id=1, source_target_pairs={{8,0},{12,4},{9,1},{13,5},{10,2},{14,6},{11,3},{15,7},{24,16},{28,... | collective-permute-start | bytes 147464 | tf_op jit(solution)/shard_map/ppermute | solution.py:28
  145.7 8.6 %collective-permute-start.23 = (f32[2,2,6,512]{3,2,1,0:T(8,128)}, f32[2,2,6,512]{3,2,1,0:T(8,128)S(1)}, u32[]{:S(2)}, u32[]{:S(2)}) collective-permute-start(f32[2,2,6,512]{3,2,1,0:T(8,128)} %bitcast.95), channel_id=1, source_target_pairs={{4,0},{8,4},{12,8},{5,1},{9,5},{13,9},{6,2},{10,6},{14,10},{7,3},{... | collective-permute-start | bytes 147464 | tf_op jit(solution)/shard_map/ppermute | solution.py:28
  158.5 1.3 copy-start.14
  160.1 4.2 %collective-permute-start.24 = (f32[8,3,512]{2,0,1:T(8,128)S(1)}, f32[8,3,512]{2,0,1:T(8,128)S(1)}, u32[]{:S(2)}, u32[]{:S(2)}) collective-permute-start(f32[8,3,512]{2,0,1:T(8,128)S(1)} %bitcast.86), channel_id=1, source_target_pairs={{0,16},{16,0},{1,17},{17,1},{2,18},{18,2},{3,19},{19,3},{4,20},{20... | collective-permute-start | bytes 147464 | tf_op jit(solution)/shard_map/ppermute | solution.py:268

commit v8 on v7

--- a/solution.py
+++ b/solution.py
@@ -183,6 +183,36 @@
         in_specs=_vmem_specs(len(args)),
         out_specs=tuple(_vmem_specs(len(out_shape))),
     )(*args)
+
+
+def upper_then_lower(rhs, near_t, far_t, incoming, inverse, near, far):
+    count, conds = near_t.shape[0], near_t.shape[1]
+    carry = jax.ShapeDtypeStruct((2, 1) + rhs.shape[1:], jnp.float32)
+
+    def kernel(rhs_ref, nt_ref, ft_ref, inc_ref, d_ref, b_ref, a_ref, val_ref, carry_ref):
+        for c in range(conds):
+            last, before = inc_ref[0, 0, c], inc_ref[1, 0, c]
+            for i in range(count):
+                acc = _rows_times(nt_ref, (i, c), last) + _rows_times(ft_ref, (i, c), before)
+                before, last = last, rhs_ref[i, c] - acc
+                val_ref[i, c] = last
+            pending = None
+            partial_value = None
+            for i in range(count - 1, -1, -1):
+                r = val_ref[i, c] if pending is None else val_ref[i, c] - pending
+                now = _rows_times(d_ref, (i, c), r)
+                near_part = _rows_times(b_ref, (i, c), now)
+                pending = near_part if partial_value is None else partial_value + near_part
+                partial_value = _rows_times(a_ref, (i, c), now)
+            carry_ref[0, 0, c] = pending
+            carry_ref[1, 0, c] = partial_value
+
+    return pl.pallas_call(
+        kernel,
+        out_shape=(jax.ShapeDtypeStruct(rhs.shape, jnp.float32), carry),
+        in_specs=_vmem_specs(7),
+        out_specs=tuple(_vmem_specs(2)),
+    )(rhs, near_t, far_t, incoming, inverse, near, far)
 
 
 def carry_through(vector, response):
@@ -249,10 +279,11 @@
             "icvjq,cvqk->icvjk", grid, z_inverse, precision=lax.Precision.HIGHEST
         ).reshape(rhs.shape)
         yres = jnp.sum(y_inverse * zres[..., :, None, :], axis=-3)
-        _, offset = upper_pallas(yres, near_t, far_t, zeros, True)
+        (offset,) = upper_pallas(yres, near_t, far_t, zeros, False)
         entering = gathered_carry(offset[:, 0], upper_products, 1)
-        upper, _ = upper_pallas(yres, near_t, far_t, entering[:, None], True)
-        _, offset = lower_pallas(upper, inverse_diag, near_lower, far_lower, zeros, True)
+        upper, offset = upper_then_lower(
+            yres, near_t, far_t, entering[:, None], inverse_diag, near_lower, far_lower
+        )
         entering = gathered_carry(offset[:, 0], lower_products, -1)
         lower, _ = lower_pallas(upper, inverse_diag, near_lower, far_lower, entering[:, None], True)
         psi = (psi + 0.05 * lower) * keep

time: 166 us -> 164 us (0.988)
  Pallas kernels: 41.7 us -> 37.8 us
  waiting for transfers between devices: 31.3 us -> 33.1 us
    pallas_call x0 -> x2, Pallas kernels: none -> 9.6 us  [upper_then_lower(): pl.pallas_call(kernel, out_shape=(jax.ShapeDtypeStruct(rhs.shape, jnp.flo...]
    pallas_call x5 -> x3, Pallas kernels: 22.7 us -> 15.5 us  [lower_pallas(): pl.pallas_call(kernel, out_shape=tuple(out_shape), in_specs=_vmem_specs(l...]
    pallas_call x5 -> x3, Pallas kernels: 19 us -> 12.7 us  [upper_pallas(): pl.pallas_call(kernel, out_shape=tuple(out_shape), in_specs=_vmem_specs(l...]
    ppermute x16, waiting for transfers between devices: 28.8 us -> 30.7 us  [from_behind(): lax.ppermute(value, axis, [(source, source + steps) for source in range(f...]
  transfers between devices with their start and end apart: 25 -> 25, of which waited for: 8 -> 8; matrix products, arithmetic and copies ran while one was open for 14% -> 14% of each run, Pallas kernels for 15% -> 14%
where the time goes in v8:
time: 164 us; the launch traced here: 163 us
  starting transfers between devices  57.6 us (35%)
  Pallas kernels  37.8 us (23%)
  waiting for transfers between devices  33.1 us (20%)
  local copies, waits for them, and re-layouts  19.7 us (12%)
  other arithmetic  11.7 us (7%)
    ppermute x16, starting transfers between devices, from_behind(): lax.ppermute(value, axis, [(source, source + steps) for source in range(f...  34.6 us
    ppermute x16, waiting for transfers between devices, from_behind(): lax.ppermute(value, axis, [(source, source + steps) for source in range(f...  30.7 us
    ppermute x4, starting transfers between devices, extended(): before = lax.ppermute(last, axis, up)  16.4 us
    pallas_call x3, Pallas kernels, lower_pallas(): pl.pallas_call(kernel, out_shape=tuple(out_shape), in_specs=_vmem_specs(l...  15.5 us
    pallas_call x3, Pallas kernels, upper_pallas(): pl.pallas_call(kernel, out_shape=tuple(out_shape), in_specs=_vmem_specs(l...  12.7 us
    pallas_call x2, Pallas kernels, upper_then_lower(): pl.pallas_call(kernel, out_shape=(jax.ShapeDtypeStruct(rhs.shape, jnp.flo...  9.6 us
    unnamed x44, local copies, waits for them, and re-layouts  6.45 us
    ppermute x4, starting transfers between devices, extended(): after = lax.ppermute(first, axis, down)  5.15 us
  transfers between devices with their start and end apart: 25, of which 8 were waited for; matrix products, arithmetic and copies ran while one was open for 14% of the time, Pallas kernels for 14%

profile of v8, /device:TPU:0, one launch (start us, length us, event | category | flops | bytes accessed | tf_op | source)
XLA Modules:
  0.0 162.9 jit_solution(351748153730945302)
XLA Ops:
  0.6 1.0 copy.236
  1.8 1.3 collective-permute-start.2
  3.0 3.0 %collective-permute-start.3 = (f32[8,2,6,32]{3,2,1,0:T(8,128)S(1)}, f32[8,2,6,32]{3,2,1,0:T(8,128)S(1)}, u32[]{:S(2)}, u32[]{:S(2)}) collective-permute-start(f32[8,2,6,32]{3,2,1,0:T(8,128)S(1)} %get-tuple-element.33), channel_id=1, source_target_pairs={{0,1},{1,2},{2,3},{4,5},{5,6},{6,7},{8,9},{9,10},{10,11},{12,13},{... | collective-permute-start | bytes 36872 | tf_op jit(solution)/shard_map/ppermute | solution.py:19
  6.1 1.3 collective-permute-start
  7.4 5.6 %collective-permute-start.1 = (f32[1,2,6,512]{3,2,1,0:T(8,128)S(1)}, f32[1,2,6,512]{3,2,1,0:T(8,128)S(1)}, u32[]{:S(2)}, u32[]{:S(2)}) collective-permute-start(f32[1,2,6,512]{3,2,1,0:T(8,128)S(1)} %get-tuple-element.31), channel_id=1, source_target_pairs={{0,4},{4,8},{8,12},{1,5},{5,9},{9,13},{2,6},{6,10},{10,14},{3,7},{... | collective-permute-start | bytes 73736 | tf_op jit(solution)/shard_map/ppermute | solution.py:19
  13.0 4.0 %copy_bitcast_fusion = (f32[8,2,6,6,512]{4,3,2,1,0:T(8,128)}, f32[8,2,6,6,512]{4,3,2,1,0:T(8,128)}) fusion(f32[8,2,6,6,512]{4,1,3,2,0:T(2,128)} %param.16, f32[8,2,6,6,512]{4,1,3,2,0:T(2,128)} %param.15), kind=kLoop, calls=%fused_computation | loop fusion | bytes 4718592 | tf_op jit(solution)/shard_map/transpose | solution.py:262
  17.0 6.8 %shard_map.140 = f32[2,12,2,6,512]{4,3,2,1,0:T(8,128)} custom-call(f32[8,2,6,6,512]{4,3,2,1,0:T(8,128)} %get-tuple-element.35.refs_0_.refs_1_.nt_ref, f32[8,2,6,6,512]{4,3,2,1,0:T(8,128)} %get-tuple-element.34.refs_1_.refs_2_.ft_ref), custom_call_target="tpu_custom_call" | custom-call | tf_op jit(solution)/shard_map/pallas_call | solution.py:116
  23.9 2.5 %copy.213 = f32[2,12,2,6,512]{4,2,3,1,0:T(2,128)} copy(f32[2,12,2,6,512]{4,3,2,1,0:T(8,128)} %shard_map.140) | data formatting | bytes 1179648 | tf_op jit(solution)/shard_map/pallas_call | solution.py:116
  26.3 5.8 %collective-permute-start.5 = (f32[2,12,2,6,512]{4,2,3,1,0:T(2,128)}, f32[2,12,2,6,512]{4,2,3,1,0:T(2,128)}, u32[]{:S(2)}, u32[]{:S(2)}) collective-permute-start(f32[2,12,2,6,512]{4,2,3,1,0:T(2,128)} %copy.213), channel_id=1, source_target_pairs={{0,8},{4,12},{1,9},{5,13},{2,10},{6,14},{3,11},{7,15},{16,24},{20,... | collective-permute-start | bytes 1769480 | tf_op jit(solution)/shard_map/ppermute | solution.py:28
  32.1 1.3 collective-permute-start.4
  34.1 0.8 convolution_bitcast_fusion.1
  35.4 0.6 multiply_reduce_fusion.1
  36.0 0.8 copy.220.refs_0_.rhs_ref
  36.7 0.6 broadcast_in_dim.10.refs_3_
  37.4 3.0 %shard_map.141 = f32[2,1,2,6,512]{4,3,2,1,0:T(8,128)} custom-call(f32[8,2,6,512]{3,2,1,0:T(8,128)} %copy.220.refs_0_.rhs_ref, f32[8,2,6,6,512]{4,3,2,1,0:T(8,128)} %get-tuple-element.35.refs_0_.refs_1_.nt_ref, f32[8,2,6,6,512]{4,3,2,1,0:T(8,128)} %get-tuple-element.34.refs_1_.refs_2_.ft_ref, f32[2,1,2,6,512]{4,3,2,1,0:T(8,128)} %broadcast_in_dim.10.refs_3_), custom_call_target="tpu_custom_call" | custom-call | tf_op jit(solution)/shard_map/pallas_call | solution.py:116
  40.3 1.4 collective-permute-start.6
  41.8 1.4 copy.221.d_ref.refs_0_.refs_1_
  43.2 1.5 copy.222.b_ref.refs_1_.refs_2_
  44.7 1.4 copy.223.a_ref.refs_2_.refs_3_
  46.1 8.3 %shard_map.143 = f32[2,12,2,6,512]{4,3,2,1,0:T(8,128)} custom-call(f32[8,2,6,6,512]{4,3,2,1,0:T(8,128)} %copy.221.d_ref.refs_0_.refs_1_, f32[8,2,6,6,512]{4,3,2,1,0:T(8,128)} %copy.222.b_ref.refs_1_.refs_2_, f32[8,2,6,6,512]{4,3,2,1,0:T(8,128)} %copy.223.a_ref.refs_2_.refs_3_), custom_call_target="tpu_custom_call" | custom-call | tf_op jit(solution)/shard_map/pallas_call | solution.py:180
  54.4 2.4 %copy.227 = f32[2,12,2,6,512]{4,2,3,1,0:T(2,128)} copy(f32[2,12,2,6,512]{4,3,2,1,0:T(8,128)} %shard_map.143) | data formatting | bytes 1179648 | tf_op jit(solution)/shard_map/pallas_call | solution.py:180
  56.9 1.3 collective-permute-start.10
  58.1 1.3 collective-permute-start.9
  59.5 6.1 %collective-permute-start.7 = (f32[2,2,6,512]{3,2,1,0:T(8,128)S(1)}, f32[2,2,6,512]{3,2,1,0:T(8,128)S(1)}, u32[]{:S(2)}, u32[]{:S(2)}) collective-permute-start(f32[2,2,6,512]{3,2,1,0:T(8,128)S(1)} %bitcast.83), channel_id=1, source_target_pairs={{0,8},{4,12},{1,9},{5,13},{2,10},{6,14},{3,11},{7,15},{16,24},{20,... | collective-permute-start | bytes 147464 | tf_op jit(solution)/shard_map/ppermute | solution.py:28
  65.6 4.0 %collective-permute-start.8 = (f32[2,2,6,512]{3,2,1,0:T(8,128)S(1)}, f32[2,2,6,512]{3,2,1,0:T(8,128)S(1)}, u32[]{:S(2)}, u32[]{:S(2)}) collective-permute-start(f32[2,2,6,512]{3,2,1,0:T(8,128)S(1)} %bitcast.84), channel_id=1, source_target_pairs={{0,4},{4,8},{8,12},{1,5},{5,9},{9,13},{2,6},{6,10},{10,14},{3,7},{... | collective-permute-start | bytes 147464 | tf_op jit(solution)/shard_map/ppermute | solution.py:28
  69.6 1.3 multiply_reduce_fusion.10
  71.5 0.6 fusion.18.inc_ref
  72.1 4.8 %shard_map.142 = (f32[8,2,6,512]{3,2,1,0:T(8,128)}, f32[2,1,2,6,512]{4,3,2,1,0:T(8,128)}) custom-call(f32[8,2,6,512]{3,2,1,0:T(8,128)} %copy.220.refs_0_.rhs_ref, f32[8,2,6,6,512]{4,3,2,1,0:T(8,128)} %get-tuple-element.35.refs_0_.refs_1_.nt_ref, f32[8,2,6,6,512]{4,3,2,1,0:T(8,128)} %get-tuple-element.34.refs_1_.refs_2_.ft_ref, ...), custom_call_target="tpu_custom_call" | custom-call | tf_op jit(solution)/shard_map/pallas_call | solution.py:210
  76.9 1.3 collective-permute-start.11
  78.2 1.3 collective-permute-start.12
  79.5 1.3 collective-permute-start.13
  80.8 8.2 %collective-permute-done.11 = f32[2,2,6,512]{3,2,1,0:T(8,128)S(1)} collective-permute-done((f32[2,2,6,512]{3,2,1,0:T(8,128)}, f32[2,2,6,512]{3,2,1,0:T(8,128)S(1)}, u32[]{:S(2)}, u32[]{:S(2)}) %collective-permute-start.11) | collective-permute-done | bytes 49184 | tf_op jit(solution)/shard_map/ppermute | solution.py:28
  89.3 14.7 %collective-permute-done.12 = f32[2,2,6,512]{3,2,1,0:T(8,128)S(1)} collective-permute-done((f32[2,2,6,512]{3,2,1,0:T(8,128)}, f32[2,2,6,512]{3,2,1,0:T(8,128)S(1)}, u32[]{:S(2)}, u32[]{:S(2)}) %collective-permute-start.12) | collective-permute-done | bytes 49184 | tf_op jit(solution)/shard_map/ppermute | solution.py:28
  104.4 0.6 fusion.16.refs_4_
  105.0 3.6 %shard_map.144 = (f32[8,2,6,512]{3,2,1,0:T(8,128)}, f32[2,1,2,6,512]{4,3,2,1,0:T(8,128)}) custom-call(f32[8,2,6,512]{3,2,1,0:T(8,128)} %get-tuple-element.8.refs_0_, f32[8,2,6,6,512]{4,3,2,1,0:T(8,128)} %copy.221.d_ref.refs_0_.refs_1_, f32[8,2,6,6,512]{4,3,2,1,0:T(8,128)} %copy.222.b_ref.refs_1_.refs_2_, f32[8,2,6,6,512]{4,3,2,1,0:T(8,128)} %copy.223.a_ref.refs_2_.refs_3_, ...), custom_call_target="tpu_custom_call" | custom-call | tf_op jit(solution)/shard_map/pallas_call | solution.py:180
  108.7 1.1 add_multiply_fusion.1
  109.8 1.3 collective-permute-start.14
  111.1 4.5 %collective-permute-start.15 = (f32[1,2,6,512]{3,2,1,0:T(8,128)S(1)}, f32[1,2,6,512]{3,2,1,0:T(8,128)S(1)}, u32[]{:S(2)}, u32[]{:S(2)}) collective-permute-start(f32[1,2,6,512]{3,2,1,0:T(8,128)S(1)} %get-tuple-element.27), channel_id=1, source_target_pairs={{0,4},{4,8},{8,12},{1,5},{5,9},{9,13},{2,6},{6,10},{10,14},{3,7},{... | collective-permute-start | bytes 73736 | tf_op jit(solution)/shard_map/ppermute | solution.py:19
  115.7 1.3 collective-permute-start.16
  117.0 3.2 %collective-permute-start.17 = (f32[8,2,6,32]{3,2,1,0:T(8,128)S(1)}, f32[8,2,6,32]{3,2,1,0:T(8,128)S(1)}, u32[]{:S(2)}, u32[]{:S(2)}) collective-permute-start(f32[8,2,6,32]{3,2,1,0:T(8,128)S(1)} %get-tuple-element.29), channel_id=1, source_target_pairs={{0,1},{1,2},{2,3},{4,5},{5,6},{6,7},{8,9},{9,10},{10,11},{12,13},{... | collective-permute-start | bytes 36872 | tf_op jit(solution)/shard_map/ppermute | solution.py:19
  120.2 0.7 collective-permute-done.17
  121.5 0.8 convolution_bitcast_fusion
  122.8 0.6 multiply_reduce_fusion
  123.4 0.8 copy.245.refs_0_.rhs_ref
  124.2 2.9 %shard_map.145 = f32[2,1,2,6,512]{4,3,2,1,0:T(8,128)} custom-call(f32[8,2,6,512]{3,2,1,0:T(8,128)} %copy.245.refs_0_.rhs_ref, f32[8,2,6,6,512]{4,3,2,1,0:T(8,128)} %get-tuple-element.35.refs_0_.refs_1_.nt_ref, f32[8,2,6,6,512]{4,3,2,1,0:T(8,128)} %get-tuple-element.34.refs_1_.refs_2_.ft_ref, f32[2,1,2,6,512]{4,3,2,1,0:T(8,128)} %broadcast_in_dim.10.refs_3_), custom_call_target="tpu_custom_call" | custom-call | tf_op jit(solution)/shard_map/pallas_call | solution.py:116
  127.1 1.5 collective-permute-start.18
  128.6 2.2 %collective-permute-start.19 = (f32[2,2,6,512]{3,2,1,0:T(8,128)}, f32[2,2,6,512]{3,2,1,0:T(8,128)S(1)}, u32[]{:S(2)}, u32[]{:S(2)}) collective-permute-start(f32[2,2,6,512]{3,2,1,0:T(8,128)} %bitcast.86), channel_id=1, source_target_pairs={{0,8},{4,12},{1,9},{5,13},{2,10},{6,14},{3,11},{7,15},{16,24},{20,... | collective-permute-start | bytes 147464 | tf_op jit(solution)/shard_map/ppermute | solution.py:28
  130.8 1.8 %collective-permute-start.20 = (f32[2,2,6,512]{3,2,1,0:T(8,128)}, f32[2,2,6,512]{3,2,1,0:T(8,128)S(1)}, u32[]{:S(2)}, u32[]{:S(2)}) collective-permute-start(f32[2,2,6,512]{3,2,1,0:T(8,128)} %bitcast.87), channel_id=1, source_target_pairs={{0,4},{4,8},{8,12},{1,5},{5,9},{9,13},{2,6},{6,10},{10,14},{3,7},{... | collective-permute-start | bytes 147464 | tf_op jit(solution)/shard_map/ppermute | solution.py:28
  132.7 1.3 multiply_reduce_fusion.6
  134.4 0.9 collective-permute-done.20
  135.2 0.6 fusion.14.inc_ref
  135.9 4.8 %shard_map.146 = (f32[8,2,6,512]{3,2,1,0:T(8,128)}, f32[2,1,2,6,512]{4,3,2,1,0:T(8,128)}) custom-call(f32[8,2,6,512]{3,2,1,0:T(8,128)} %copy.245.refs_0_.rhs_ref, f32[8,2,6,6,512]{4,3,2,1,0:T(8,128)} %get-tuple-element.35.refs_0_.refs_1_.nt_ref, f32[8,2,6,6,512]{4,3,2,1,0:T(8,128)} %get-tuple-element.34.refs_1_.refs_2_.ft_ref, ...), custom_call_target="tpu_custom_call" | custom-call | tf_op jit(solution)/shard_map/pallas_call | solution.py:210
  140.7 1.4 collective-permute-start.21
  142.3 1.3 collective-permute-start.22
  143.6 1.3 collective-permute-start.23
  144.9 4.2 %collective-permute-done.21 = f32[2,2,6,512]{3,2,1,0:T(8,128)S(1)} collective-permute-done((f32[2,2,6,512]{3,2,1,0:T(8,128)}, f32[2,2,6,512]{3,2,1,0:T(8,128)S(1)}, u32[]{:S(2)}, u32[]{:S(2)}) %collective-permute-start.21) | collective-permute-done | bytes 49184 | tf_op jit(solution)/shard_map/ppermute | solution.py:28
  149.5 2.4 %collective-permute-done.22 = f32[2,2,6,512]{3,2,1,0:T(8,128)S(1)} collective-permute-done((f32[2,2,6,512]{3,2,1,0:T(8,128)}, f32[2,2,6,512]{3,2,1,0:T(8,128)S(1)}, u32[]{:S(2)}, u32[]{:S(2)}) %collective-permute-start.22) | collective-permute-done | bytes 49184 | tf_op jit(solution)/shard_map/ppermute | solution.py:28
  152.2 0.6 fusion.12.refs_4_
  152.9 3.6 %shard_map.147 = (f32[8,2,6,512]{3,2,1,0:T(8,128)}, f32[2,1,2,6,512]{4,3,2,1,0:T(8,128)}) custom-call(f32[8,2,6,512]{3,2,1,0:T(8,128)} %get-tuple-element.11.refs_0_, f32[8,2,6,6,512]{4,3,2,1,0:T(8,128)} %copy.221.d_ref.refs_0_.refs_1_, f32[8,2,6,6,512]{4,3,2,1,0:T(8,128)} %copy.222.b_ref.refs_1_.refs_2_, f32[8,2,6,6,512]{4,3,2,1,0:T(8,128)} %copy.223.a_ref.refs_2_.refs_3_, ...), custom_call_target="tpu_custom_call" | custom-call | tf_op jit(solution)/shard_map/pallas_call | solution.py:180
  156.5 1.1 multiply_bitcast_fusion
  158.1 1.6 collective-permute-start.24
  159.7 0.8 copy.256
  160.5 1.8 %collective-permute-done.24 = f32[8,3,512]{2,0,1:T(8,128)S(1)} collective-permute-done((f32[8,3,512]{2,0,1:T(8,128)S(1)}, f32[8,3,512]{2,0,1:T(8,128)S(1)}, u32[]{:S(2)}, u32[]{:S(2)}) %collective-permute-start.24) | collective-permute-done | bytes 49184 | tf_op jit(solution)/shard_map/ppermute | solution.py:299
  162.3 0.6 fusion.27
  (93 shorter events, 5.2 us)
Async XLA Ops:
  0.6 33.4 %copy-start = (f32[2,6,32,32]{3,2,1,0:T(8,128)S(1)}, f32[2,6,32,32]{3,2,1,0:T(8,128)}, u32[]{:S(2)}) copy-start(f32[2,6,32,32]{3,2,1,0:T(8,128)} %param.21) | copy-start | bytes 147460
  1.8 30.4 %collective-permute-start.2 = (f32[8,2,6,32]{3,2,1,0:T(8,128)S(1)}, f32[8,2,6,32]{3,2,1,0:T(8,128)S(1)}, u32[]{:S(2)}, u32[]{:S(2)}) collective-permute-start(f32[8,2,6,32]{3,2,1,0:T(8,128)S(1)} %get-tuple-element.32), channel_id=1, source_target_pairs={{1,0},{2,1},{3,2},{5,4},{6,5},{7,6},{9,8},{10,9},{11,10},{13,12},{... | collective-permute-start | bytes 36872 | tf_op jit(solution)/shard_map/ppermute | solution.py:20
  3.0 30.4 %collective-permute-start.3 = (f32[8,2,6,32]{3,2,1,0:T(8,128)S(1)}, f32[8,2,6,32]{3,2,1,0:T(8,128)S(1)}, u32[]{:S(2)}, u32[]{:S(2)}) collective-permute-start(f32[8,2,6,32]{3,2,1,0:T(8,128)S(1)} %get-tuple-element.33), channel_id=1, source_target_pairs={{0,1},{1,2},{2,3},{4,5},{5,6},{6,7},{8,9},{9,10},{10,11},{12,13},{... | collective-permute-start | bytes 36872 | tf_op jit(solution)/shard_map/ppermute | solution.py:19
  6.1 27.4 %collective-permute-start = (f32[1,2,6,512]{3,2,1,0:T(8,128)S(1)}, f32[1,2,6,512]{3,2,1,0:T(8,128)S(1)}, u32[]{:S(2)}, u32[]{:S(2)}) collective-permute-start(f32[1,2,6,512]{3,2,1,0:T(8,128)S(1)} %get-tuple-element.30), channel_id=1, source_target_pairs={{4,0},{8,4},{12,8},{5,1},{9,5},{13,9},{6,2},{10,6},{14,10},{7,3},{... | collective-permute-start | bytes 73736 | tf_op jit(solution)/shard_map/ppermute | solution.py:20
  7.4 26.1 %collective-permute-start.1 = (f32[1,2,6,512]{3,2,1,0:T(8,128)S(1)}, f32[1,2,6,512]{3,2,1,0:T(8,128)S(1)}, u32[]{:S(2)}, u32[]{:S(2)}) collective-permute-start(f32[1,2,6,512]{3,2,1,0:T(8,128)S(1)} %get-tuple-element.31), channel_id=1, source_target_pairs={{0,4},{4,8},{8,12},{1,5},{5,9},{9,13},{2,6},{6,10},{10,14},{3,7},{... | collective-permute-start | bytes 73736 | tf_op jit(solution)/shard_map/ppermute | solution.py:19
  23.9 9.6 %copy-start.11 = (f32[8,2,6,512]{3,1,2,0:T(2,128)S(1)}, f32[8,2,6,512]{3,1,2,0:T(2,128)}, u32[]{:S(2)}) copy-start(f32[8,2,6,512]{3,1,2,0:T(2,128)} %param.14) | copy-start | bytes 589828
  26.3 39.3 %collective-permute-start.5 = (f32[2,12,2,6,512]{4,2,3,1,0:T(2,128)}, f32[2,12,2,6,512]{4,2,3,1,0:T(2,128)}, u32[]{:S(2)}, u32[]{:S(2)}) collective-permute-start(f32[2,12,2,6,512]{4,2,3,1,0:T(2,128)} %copy.213), channel_id=1, source_target_pairs={{0,8},{4,12},{1,9},{5,13},{2,10},{6,14},{3,11},{7,15},{16,24},{20,... | collective-permute-start | bytes 1769480 | tf_op jit(solution)/shard_map/ppermute | solution.py:28
  32.1 38.9 %collective-permute-start.4 = (f32[2,12,2,6,512]{4,2,3,1,0:T(2,128)}, f32[2,12,2,6,512]{4,2,3,1,0:T(2,128)S(1)}, u32[]{:S(2)}, u32[]{:S(2)}) collective-permute-start(f32[2,12,2,6,512]{4,2,3,1,0:T(2,128)} %copy.213), channel_id=1, source_target_pairs={{0,4},{4,8},{8,12},{1,5},{5,9},{9,13},{2,6},{6,10},{10,14},{3,7},{... | collective-permute-start | bytes 1769480 | tf_op jit(solution)/shard_map/ppermute | solution.py:28
  34.1 1.3 copy-start.1
  37.4 4.4 %copy-start.8 = (f32[8,2,6,6,512]{4,1,3,2,0:T(2,128)S(1)}, f32[8,2,6,6,512]{4,1,3,2,0:T(2,128)}, u32[]{:S(2)}) copy-start(f32[8,2,6,6,512]{4,1,3,2,0:T(2,128)} %param.17) | copy-start | bytes 3538948
  40.3 2.9 %copy-start.9 = (f32[8,2,6,6,512]{4,1,3,2,0:T(2,128)S(1)}, f32[8,2,6,6,512]{4,1,3,2,0:T(2,128)}, u32[]{:S(2)}) copy-start(f32[8,2,6,6,512]{4,1,3,2,0:T(2,128)} %param.18) | copy-start | bytes 3538948
  40.3 19.1 %collective-permute-start.6 = (f32[2,2,6,512]{3,2,1,0:T(8,128)}, f32[2,2,6,512]{3,2,1,0:T(8,128)S(1)}, u32[]{:S(2)}, u32[]{:S(2)}) collective-permute-start(f32[2,2,6,512]{3,2,1,0:T(8,128)} %bitcast.82), channel_id=1, source_target_pairs={{0,12},{1,13},{2,14},{3,15},{16,28},{17,29},{18,30},{19,31}} | collective-permute-start | bytes 147464 | tf_op jit(solution)/shard_map/ppermute | solution.py:28
  43.2 1.5 copy-start.10
  54.4 5.0 %copy-start.15 = (f32[2,1,2,6,512]{4,3,2,1,0:T(8,128)S(1)}, f32[2,1,2,6,512]{4,3,2,1,0:T(8,128)}, u32[]{:S(2)}) copy-start(f32[2,1,2,6,512]{4,3,2,1,0:T(8,128)} %shard_map.141) | copy-start | bytes 147460
  56.9 32.2 %collective-permute-start.10 = (f32[2,12,2,6,512]{4,2,3,1,0:T(2,128)}, f32[2,12,2,6,512]{4,2,3,1,0:T(2,128)S(1)}, u32[]{:S(2)}, u32[]{:S(2)}) collective-permute-start(f32[2,12,2,6,512]{4,2,3,1,0:T(2,128)} %copy.227), channel_id=1, source_target_pairs={{8,0},{12,4},{9,1},{13,5},{10,2},{14,6},{11,3},{15,7},{24,16},{28,... | collective-permute-start | bytes 1769480 | tf_op jit(solution)/shard_map/ppermute | solution.py:28
  58.1 46.0 %collective-permute-start.9 = (f32[2,12,2,6,512]{4,2,3,1,0:T(2,128)}, f32[2,12,2,6,512]{4,2,3,1,0:T(2,128)S(1)}, u32[]{:S(2)}, u32[]{:S(2)}) collective-permute-start(f32[2,12,2,6,512]{4,2,3,1,0:T(2,128)} %copy.227), channel_id=1, source_target_pairs={{4,0},{8,4},{12,8},{5,1},{9,5},{13,9},{6,2},{10,6},{14,10},{7,3},{... | collective-permute-start | bytes 1769480 | tf_op jit(solution)/shard_map/ppermute | solution.py:28
  59.5 11.5 %collective-permute-start.7 = (f32[2,2,6,512]{3,2,1,0:T(8,128)S(1)}, f32[2,2,6,512]{3,2,1,0:T(8,128)S(1)}, u32[]{:S(2)}, u32[]{:S(2)}) collective-permute-start(f32[2,2,6,512]{3,2,1,0:T(8,128)S(1)} %bitcast.83), channel_id=1, source_target_pairs={{0,8},{4,12},{1,9},{5,13},{2,10},{6,14},{3,11},{7,15},{16,24},{20,... | collective-permute-start | bytes 147464 | tf_op jit(solution)/shard_map/ppermute | solution.py:28
  65.6 5.8 %collective-permute-start.8 = (f32[2,2,6,512]{3,2,1,0:T(8,128)S(1)}, f32[2,2,6,512]{3,2,1,0:T(8,128)S(1)}, u32[]{:S(2)}, u32[]{:S(2)}) collective-permute-start(f32[2,2,6,512]{3,2,1,0:T(8,128)S(1)} %bitcast.84), channel_id=1, source_target_pairs={{0,4},{4,8},{8,12},{1,5},{5,9},{9,13},{2,6},{6,10},{10,14},{3,7},{... | collective-permute-start | bytes 147464 | tf_op jit(solution)/shard_map/ppermute | solution.py:28
  71.0 5.9 %copy-start.2 = (f32[2,12,2,6,512]{4,2,3,1,0:T(2,128)}, f32[2,12,2,6,512]{4,2,3,1,0:T(2,128)S(1)}, u32[]{:S(2)}) copy-start(f32[2,12,2,6,512]{4,2,3,1,0:T(2,128)S(1)} %collective-permute-done.4) | copy-start | bytes 1769476
  72.1 6.1 %copy-start.16 = (s32[8,512]{1,0:T(8,128)S(1)}, s32[8,512]{1,0:T(8,128)}, u32[]{:S(2)}) copy-start(s32[8,512]{1,0:T(8,128)} %param.23) | copy-start | bytes 49156
  76.9 12.1 %collective-permute-start.11 = (f32[2,2,6,512]{3,2,1,0:T(8,128)}, f32[2,2,6,512]{3,2,1,0:T(8,128)S(1)}, u32[]{:S(2)}, u32[]{:S(2)}) collective-permute-start(f32[2,2,6,512]{3,2,1,0:T(8,128)} %bitcast.93), channel_id=1, source_target_pairs={{12,0},{13,1},{14,2},{15,3},{28,16},{29,17},{30,18},{31,19}} | collective-permute-start | bytes 147464 | tf_op jit(solution)/shard_map/ppermute | solution.py:28
  78.2 25.8 %collective-permute-start.12 = (f32[2,2,6,512]{3,2,1,0:T(8,128)}, f32[2,2,6,512]{3,2,1,0:T(8,128)S(1)}, u32[]{:S(2)}, u32[]{:S(2)}) collective-permute-start(f32[2,2,6,512]{3,2,1,0:T(8,128)} %bitcast.94), channel_id=1, source_target_pairs={{8,0},{12,4},{9,1},{13,5},{10,2},{14,6},{11,3},{15,7},{24,16},{28,... | collective-permute-start | bytes 147464 | tf_op jit(solution)/shard_map/ppermute | solution.py:28
  79.5 24.9 %collective-permute-start.13 = (f32[2,2,6,512]{3,2,1,0:T(8,128)}, f32[2,2,6,512]{3,2,1,0:T(8,128)S(1)}, u32[]{:S(2)}, u32[]{:S(2)}) collective-permute-start(f32[2,2,6,512]{3,2,1,0:T(8,128)} %bitcast.95), channel_id=1, source_target_pairs={{4,0},{8,4},{12,8},{5,1},{9,5},{13,9},{6,2},{10,6},{14,10},{7,3},{... | collective-permute-start | bytes 147464 | tf_op jit(solution)/shard_map/ppermute | solution.py:28
  89.1 19.6 %copy-start.6 = (f32[2,12,2,6,512]{4,2,3,1,0:T(2,128)}, f32[2,12,2,6,512]{4,2,3,1,0:T(2,128)S(1)}, u32[]{:S(2)}) copy-start(f32[2,12,2,6,512]{4,2,3,1,0:T(2,128)S(1)} %collective-permute-done.10) | copy-start | bytes 1769476
  104.1 4.6 %copy-start.4 = (f32[2,12,2,6,512]{4,2,3,1,0:T(2,128)}, f32[2,12,2,6,512]{4,2,3,1,0:T(2,128)S(1)}, u32[]{:S(2)}) copy-start(f32[2,12,2,6,512]{4,2,3,1,0:T(2,128)S(1)} %collective-permute-done.9) | copy-start | bytes 1769476
  105.0 3.6 %copy-start.13 = (f32[8,2,6,512]{3,1,2,0:T(2,128)S(1)}, f32[8,2,6,512]{3,1,2,0:T(2,128)}, u32[]{:S(2)}) copy-start(f32[8,2,6,512]{3,1,2,0:T(2,128)} %param.13) | copy-start | bytes 589828
  108.7 12.3 %copy-start.12 = (f32[8,2,6,512]{3,1,2,0:T(2,128)S(1)}, f32[8,2,6,512]{3,1,2,0:T(2,128)}, u32[]{:S(2)}) copy-start(f32[8,2,6,512]{3,1,2,0:T(2,128)} %param.14) | copy-start | bytes 589828
  109.8 11.2 %collective-permute-start.14 = (f32[1,2,6,512]{3,2,1,0:T(8,128)S(1)}, f32[1,2,6,512]{3,2,1,0:T(8,128)S(1)}, u32[]{:S(2)}, u32[]{:S(2)}) collective-permute-start(f32[1,2,6,512]{3,2,1,0:T(8,128)S(1)} %get-tuple-element.26), channel_id=1, source_target_pairs={{4,0},{8,4},{12,8},{5,1},{9,5},{13,9},{6,2},{10,6},{14,10},{7,3},{... | collective-permute-start | bytes 73736 | tf_op jit(solution)/shard_map/ppermute | solution.py:20
  111.1 9.9 %collective-permute-start.15 = (f32[1,2,6,512]{3,2,1,0:T(8,128)S(1)}, f32[1,2,6,512]{3,2,1,0:T(8,128)S(1)}, u32[]{:S(2)}, u32[]{:S(2)}) collective-permute-start(f32[1,2,6,512]{3,2,1,0:T(8,128)S(1)} %get-tuple-element.27), channel_id=1, source_target_pairs={{0,4},{4,8},{8,12},{1,5},{5,9},{9,13},{2,6},{6,10},{10,14},{3,7},{... | collective-permute-start | bytes 73736 | tf_op jit(solution)/shard_map/ppermute | solution.py:19
  115.7 4.5 %collective-permute-start.16 = (f32[8,2,6,32]{3,2,1,0:T(8,128)S(1)}, f32[8,2,6,32]{3,2,1,0:T(8,128)S(1)}, u32[]{:S(2)}, u32[]{:S(2)}) collective-permute-start(f32[8,2,6,32]{3,2,1,0:T(8,128)S(1)} %get-tuple-element.28), channel_id=1, source_target_pairs={{1,0},{2,1},{3,2},{5,4},{6,5},{7,6},{9,8},{10,9},{11,10},{13,12},{... | collective-permute-start | bytes 36872 | tf_op jit(solution)/shard_map/ppermute | solution.py:20
  117.0 3.9 %collective-permute-start.17 = (f32[8,2,6,32]{3,2,1,0:T(8,128)S(1)}, f32[8,2,6,32]{3,2,1,0:T(8,128)S(1)}, u32[]{:S(2)}, u32[]{:S(2)}) collective-permute-start(f32[8,2,6,32]{3,2,1,0:T(8,128)S(1)} %get-tuple-element.29), channel_id=1, source_target_pairs={{0,1},{1,2},{2,3},{4,5},{5,6},{6,7},{8,9},{9,10},{10,11},{12,13},{... | collective-permute-start | bytes 36872 | tf_op jit(solution)/shard_map/ppermute | solution.py:19
  127.1 7.0 %copy-start.3 = (f32[2,12,2,6,512]{4,2,3,1,0:T(2,128)S(1)}, f32[2,12,2,6,512]{4,2,3,1,0:T(2,128)}, u32[]{:S(2)}) copy-start(f32[2,12,2,6,512]{4,2,3,1,0:T(2,128)} %copy-done.2) | copy-start | bytes 1769476
  127.1 5.6 %collective-permute-start.18 = (f32[2,2,6,512]{3,2,1,0:T(8,128)}, f32[2,2,6,512]{3,2,1,0:T(8,128)S(1)}, u32[]{:S(2)}, u32[]{:S(2)}) collective-permute-start(f32[2,2,6,512]{3,2,1,0:T(8,128)} %bitcast.85), channel_id=1, source_target_pairs={{0,12},{1,13},{2,14},{3,15},{16,28},{17,29},{18,30},{19,31}} | collective-permute-start | bytes 147464 | tf_op jit(solution)/shard_map/ppermute | solution.py:28
  128.6 5.5 %collective-permute-start.19 = (f32[2,2,6,512]{3,2,1,0:T(8,128)}, f32[2,2,6,512]{3,2,1,0:T(8,128)S(1)}, u32[]{:S(2)}, u32[]{:S(2)}) collective-permute-start(f32[2,2,6,512]{3,2,1,0:T(8,128)} %bitcast.86), channel_id=1, source_target_pairs={{0,8},{4,12},{1,9},{5,13},{2,10},{6,14},{3,11},{7,15},{16,24},{20,... | collective-permute-start | bytes 147464 | tf_op jit(solution)/shard_map/ppermute | solution.py:28
  130.8 4.4 %collective-permute-start.20 = (f32[2,2,6,512]{3,2,1,0:T(8,128)}, f32[2,2,6,512]{3,2,1,0:T(8,128)S(1)}, u32[]{:S(2)}, u32[]{:S(2)}) collective-permute-start(f32[2,2,6,512]{3,2,1,0:T(8,128)} %bitcast.87), channel_id=1, source_target_pairs={{0,4},{4,8},{8,12},{1,5},{5,9},{9,13},{2,6},{6,10},{10,14},{3,7},{... | collective-permute-start | bytes 147464 | tf_op jit(solution)/shard_map/ppermute | solution.py:28
  135.9 6.3 %copy-start.17 = (f32[8]{0:T(128)S(1)}, f32[8]{0:T(128)}, u32[]{:S(2)}) copy-start(f32[8]{0:T(128)} %param.25) | copy-start | bytes 100
  135.9 6.3 %copy-start.18 = (s32[2]{0:T(128)S(1)}, s32[2]{0:T(128)}, u32[]{:S(2)}) copy-start(s32[2]{0:T(128)} %param.24) | copy-start | bytes 28
  135.9 13.3 %copy-start.7 = (f32[2,12,2,6,512]{4,2,3,1,0:T(2,128)S(1)}, f32[2,12,2,6,512]{4,2,3,1,0:T(2,128)}, u32[]{:S(2)}) copy-start(f32[2,12,2,6,512]{4,2,3,1,0:T(2,128)} %copy-done.6) | copy-start | bytes 1769476
  140.7 11.3 %copy-start.5 = (f32[2,12,2,6,512]{4,2,3,1,0:T(2,128)S(1)}, f32[2,12,2,6,512]{4,2,3,1,0:T(2,128)}, u32[]{:S(2)}) copy-start(f32[2,12,2,6,512]{4,2,3,1,0:T(2,128)} %copy-done.4) | copy-start | bytes 1769476
  140.7 8.5 %collective-permute-start.21 = (f32[2,2,6,512]{3,2,1,0:T(8,128)}, f32[2,2,6,512]{3,2,1,0:T(8,128)S(1)}, u32[]{:S(2)}, u32[]{:S(2)}) collective-permute-start(f32[2,2,6,512]{3,2,1,0:T(8,128)} %bitcast.96), channel_id=1, source_target_pairs={{12,0},{13,1},{14,2},{15,3},{28,16},{29,17},{30,18},{31,19}} | collective-permute-start | bytes 147464 | tf_op jit(solution)/shard_map/ppermute | solution.py:28
  142.3 9.6 %collective-permute-start.22 = (f32[2,2,6,512]{3,2,1,0:T(8,128)}, f32[2,2,6,512]{3,2,1,0:T(8,128)S(1)}, u32[]{:S(2)}, u32[]{:S(2)}) collective-permute-start(f32[2,2,6,512]{3,2,1,0:T(8,128)} %bitcast.97), channel_id=1, source_target_pairs={{8,0},{12,4},{9,1},{13,5},{10,2},{14,6},{11,3},{15,7},{24,16},{28,... | collective-permute-start | bytes 147464 | tf_op jit(solution)/shard_map/ppermute | solution.py:28
  143.6 8.6 %collective-permute-start.23 = (f32[2,2,6,512]{3,2,1,0:T(8,128)}, f32[2,2,6,512]{3,2,1,0:T(8,128)S(1)}, u32[]{:S(2)}, u32[]{:S(2)}) collective-permute-start(f32[2,2,6,512]{3,2,1,0:T(8,128)} %bitcast.98), channel_id=1, source_target_pairs={{4,0},{8,4},{12,8},{5,1},{9,5},{13,9},{6,2},{10,6},{14,10},{7,3},{... | collective-permute-start | bytes 147464 | tf_op jit(solution)/shard_map/ppermute | solution.py:28
  156.5 1.3 copy-start.14
  158.1 4.2 %collective-permute-start.24 = (f32[8,3,512]{2,0,1:T(8,128)S(1)}, f32[8,3,512]{2,0,1:T(8,128)S(1)}, u32[]{:S(2)}, u32[]{:S(2)}) collective-permute-start(f32[8,3,512]{2,0,1:T(8,128)S(1)} %bitcast.92), channel_id=1, source_target_pairs={{0,16},{16,0},{1,17},{17,1},{2,18},{18,2},{3,19},{19,3},{4,20},{20... | collective-permute-start | bytes 147464 | tf_op jit(solution)/shard_map/ppermute | solution.py:299

commit v9 on v8

--- a/solution.py
+++ b/solution.py
@@ -239,6 +239,19 @@
     return total
 
 
+def relayed_carry(vector, behind, steps):
+    count = lax.axis_size("gx")
+    if count == 1:
+        return jnp.zeros_like(vector)
+    nearest = from_behind(vector, "gx", steps)
+    if count == 2:
+        return nearest
+    total = nearest + carry_through(from_behind(vector, "gx", 2 * steps), behind)
+    for _ in range(count - 3):
+        total = nearest + carry_through(from_behind(total, "gx", steps), behind)
+    return total
+
+
 def on_device(
     psi_old,
     objective_grad,
@@ -265,7 +278,7 @@
     (response,) = lower_pallas(None, inverse_diag, near_lower, far_lower, units, False)
     reverse_matrix = response
     upper_products = shifted_operators(matrix, 1)
-    lower_products = shifted_operators(reverse_matrix, -1)
+    lower_behind = from_behind(reverse_matrix, "gx", -1)
     psi = psi_old
     for step in range(ITERS):
         stream_pad = extended(psi, (("gx", 0),), 1)
@@ -284,7 +297,7 @@
         upper, offset = upper_then_lower(
             yres, near_t, far_t, entering[:, None], inverse_diag, near_lower, far_lower
         )
-        entering = gathered_carry(offset[:, 0], lower_products, -1)
+        entering = relayed_carry(offset[:, 0], lower_behind, -1)
         lower, _ = lower_pallas(upper, inverse_diag, near_lower, far_lower, entering[:, None], True)
         psi = (psi + 0.05 * lower) * keep
     onehot = (cond_index[:, None] == jnp.arange(weight_table.shape[0])[None, :]).astype(jnp.float32)

time: 164 us -> 162 us (0.988)
  starting transfers between devices: 57.6 us -> 53.8 us
  other arithmetic: 11.7 us -> 13.9 us
    ppermute x16 -> x15, starting transfers between devices: 34.6 us -> 30.7 us  [from_behind(): lax.ppermute(value, axis, [(source, source + steps) for source in range(f...]
    reduce_sum x8, other arithmetic: 4.17 us -> 6.33 us  [carry_through(): return jnp.sum(jnp.sum(split * inputs, axis=2), axis=1)]
    ppermute x16 -> x15, waiting for transfers between devices: 30.7 us -> 29.1 us  [from_behind(): lax.ppermute(value, axis, [(source, source + steps) for source in range(f...]
    unnamed x44 -> x32, local copies, waits for them, and re-layouts: 6.45 us -> 6.38 us
  transfers between devices with their start and end apart: 25 -> 24, of which waited for: 8 -> 6; matrix products, arithmetic and copies ran while one was open for 14% -> 15% of each run, Pallas kernels for 14% -> 14%
where the time goes in v9:
time: 162 us; the launch traced here: 161 us
  starting transfers between devices  53.8 us (33%)
  Pallas kernels  37.7 us (23%)
  waiting for transfers between devices  31.6 us (20%)
  local copies, waits for them, and re-layouts  19.9 us (12%)
  other arithmetic  13.9 us (9%)
  matrix products  2.59 us (2%)
    ppermute x15, starting transfers between devices, from_behind(): lax.ppermute(value, axis, [(source, source + steps) for source in range(f...  30.7 us
    ppermute x15, waiting for transfers between devices, from_behind(): lax.ppermute(value, axis, [(source, source + steps) for source in range(f...  29.1 us
    ppermute x4, starting transfers between devices, extended(): before = lax.ppermute(last, axis, up)  16.4 us
    pallas_call x3, Pallas kernels, lower_pallas(): pl.pallas_call(kernel, out_shape=tuple(out_shape), in_specs=_vmem_specs(l...  15.5 us
    pallas_call x3, Pallas kernels, upper_pallas(): pl.pallas_call(kernel, out_shape=tuple(out_shape), in_specs=_vmem_specs(l...  12.7 us
    pallas_call x2, Pallas kernels, upper_then_lower(): pl.pallas_call(kernel, out_shape=(jax.ShapeDtypeStruct(rhs.shape, jnp.flo...  9.54 us
    unnamed x32, local copies, waits for them, and re-layouts  6.38 us
    reduce_sum x8, other arithmetic, carry_through(): return jnp.sum(jnp.sum(split * inputs, axis=2), axis=1)  6.33 us
  transfers between devices with their start and end apart: 24, of which 6 were waited for; matrix products, arithmetic and copies ran while one was open for 15% of the time, Pallas kernels for 14%

profile of v9, /device:TPU:0, one launch (start us, length us, event | category | flops | bytes accessed | tf_op | source)
XLA Modules:
  0.0 160.6 jit_solution(8892012937244983076)
XLA Ops:
  0.6 1.0 copy.233
  1.8 1.3 collective-permute-start.2
  3.0 3.0 %collective-permute-start.3 = (f32[8,2,6,32]{3,2,1,0:T(8,128)S(1)}, f32[8,2,6,32]{3,2,1,0:T(8,128)S(1)}, u32[]{:S(2)}, u32[]{:S(2)}) collective-permute-start(f32[8,2,6,32]{3,2,1,0:T(8,128)S(1)} %get-tuple-element.33), channel_id=1, source_target_pairs={{0,1},{1,2},{2,3},{4,5},{5,6},{6,7},{8,9},{9,10},{10,11},{12,13},{... | collective-permute-start | bytes 36872 | tf_op jit(solution)/shard_map/ppermute | solution.py:19
  6.1 1.3 collective-permute-start
  7.4 5.6 %collective-permute-start.1 = (f32[1,2,6,512]{3,2,1,0:T(8,128)S(1)}, f32[1,2,6,512]{3,2,1,0:T(8,128)S(1)}, u32[]{:S(2)}, u32[]{:S(2)}) collective-permute-start(f32[1,2,6,512]{3,2,1,0:T(8,128)S(1)} %get-tuple-element.31), channel_id=1, source_target_pairs={{0,4},{4,8},{8,12},{1,5},{5,9},{9,13},{2,6},{6,10},{10,14},{3,7},{... | collective-permute-start | bytes 73736 | tf_op jit(solution)/shard_map/ppermute | solution.py:19
  13.0 4.0 %copy_bitcast_fusion = (f32[8,2,6,6,512]{4,3,2,1,0:T(8,128)}, f32[8,2,6,6,512]{4,3,2,1,0:T(8,128)}) fusion(f32[8,2,6,6,512]{4,1,3,2,0:T(2,128)} %param.16, f32[8,2,6,6,512]{4,1,3,2,0:T(2,128)} %param.15), kind=kLoop, calls=%fused_computation | loop fusion | bytes 4718592 | tf_op jit(solution)/shard_map/transpose | solution.py:275
  17.0 6.8 %shard_map.140 = f32[2,12,2,6,512]{4,3,2,1,0:T(8,128)} custom-call(f32[8,2,6,6,512]{4,3,2,1,0:T(8,128)} %get-tuple-element.35.refs_0_.refs_1_.nt_ref, f32[8,2,6,6,512]{4,3,2,1,0:T(8,128)} %get-tuple-element.34.refs_1_.refs_2_.ft_ref), custom_call_target="tpu_custom_call" | custom-call | tf_op jit(solution)/shard_map/pallas_call | solution.py:116
  23.8 2.4 %copy.211 = f32[2,12,2,6,512]{4,2,3,1,0:T(2,128)} copy(f32[2,12,2,6,512]{4,3,2,1,0:T(8,128)} %shard_map.140) | data formatting | bytes 1179648 | tf_op jit(solution)/shard_map/pallas_call | solution.py:116
  26.3 5.7 %collective-permute-start.5 = (f32[2,12,2,6,512]{4,2,3,1,0:T(2,128)}, f32[2,12,2,6,512]{4,2,3,1,0:T(2,128)}, u32[]{:S(2)}, u32[]{:S(2)}) collective-permute-start(f32[2,12,2,6,512]{4,2,3,1,0:T(2,128)} %copy.211), channel_id=1, source_target_pairs={{0,8},{4,12},{1,9},{5,13},{2,10},{6,14},{3,11},{7,15},{16,24},{20,... | collective-permute-start | bytes 1769480 | tf_op jit(solution)/shard_map/ppermute | solution.py:28
  32.0 2.2 %collective-permute-start.4 = (f32[2,12,2,6,512]{4,2,3,1,0:T(2,128)}, f32[2,12,2,6,512]{4,2,3,1,0:T(2,128)}, u32[]{:S(2)}, u32[]{:S(2)}) collective-permute-start(f32[2,12,2,6,512]{4,2,3,1,0:T(2,128)} %copy.211), channel_id=1, source_target_pairs={{0,4},{4,8},{8,12},{1,5},{5,9},{9,13},{2,6},{6,10},{10,14},{3,7},{... | collective-permute-start | bytes 1769480 | tf_op jit(solution)/shard_map/ppermute | solution.py:28
  34.8 0.8 convolution_bitcast_fusion.1
  36.7 0.8 copy.218.refs_0_.rhs_ref
  37.5 0.6 broadcast_in_dim.10.refs_3_
  38.1 3.0 %shard_map.141 = f32[2,1,2,6,512]{4,3,2,1,0:T(8,128)} custom-call(f32[8,2,6,512]{3,2,1,0:T(8,128)} %copy.218.refs_0_.rhs_ref, f32[8,2,6,6,512]{4,3,2,1,0:T(8,128)} %get-tuple-element.35.refs_0_.refs_1_.nt_ref, f32[8,2,6,6,512]{4,3,2,1,0:T(8,128)} %get-tuple-element.34.refs_1_.refs_2_.ft_ref, f32[2,1,2,6,512]{4,3,2,1,0:T(8,128)} %broadcast_in_dim.10.refs_3_), custom_call_target="tpu_custom_call" | custom-call | tf_op jit(solution)/shard_map/pallas_call | solution.py:116
  41.1 1.4 collective-permute-start.6
  42.5 1.4 copy.219.d_ref.refs_0_.refs_1_
  43.9 1.4 copy.220.b_ref.refs_1_.refs_2_
  45.4 1.4 copy.221.a_ref.refs_2_.refs_3_
  46.8 8.3 %shard_map.143 = f32[2,12,2,6,512]{4,3,2,1,0:T(8,128)} custom-call(f32[8,2,6,6,512]{4,3,2,1,0:T(8,128)} %copy.219.d_ref.refs_0_.refs_1_, f32[8,2,6,6,512]{4,3,2,1,0:T(8,128)} %copy.220.b_ref.refs_1_.refs_2_, f32[8,2,6,6,512]{4,3,2,1,0:T(8,128)} %copy.221.a_ref.refs_2_.refs_3_), custom_call_target="tpu_custom_call" | custom-call | tf_op jit(solution)/shard_map/pallas_call | solution.py:180
  55.1 1.6 %copy.225 = f32[2,12,2,6,512]{4,2,3,1,0:T(2,128)S(1)} copy(f32[2,12,2,6,512]{4,3,2,1,0:T(8,128)} %shard_map.143) | data formatting | bytes 1179648 | tf_op jit(solution)/shard_map/pallas_call | solution.py:180
  56.7 1.3 collective-permute-start.10
  58.1 2.5 %collective-permute-start.7 = (f32[2,2,6,512]{3,2,1,0:T(8,128)S(1)}, f32[2,2,6,512]{3,2,1,0:T(8,128)S(1)}, u32[]{:S(2)}, u32[]{:S(2)}) collective-permute-start(f32[2,2,6,512]{3,2,1,0:T(8,128)S(1)} %bitcast.81), channel_id=1, source_target_pairs={{0,8},{4,12},{1,9},{5,13},{2,10},{6,14},{3,11},{7,15},{16,24},{20,... | collective-permute-start | bytes 147464 | tf_op jit(solution)/shard_map/ppermute | solution.py:28
  60.6 3.4 %collective-permute-start.8 = (f32[2,2,6,512]{3,2,1,0:T(8,128)S(1)}, f32[2,2,6,512]{3,2,1,0:T(8,128)S(1)}, u32[]{:S(2)}, u32[]{:S(2)}) collective-permute-start(f32[2,2,6,512]{3,2,1,0:T(8,128)S(1)} %bitcast.82), channel_id=1, source_target_pairs={{0,4},{4,8},{8,12},{1,5},{5,9},{9,13},{2,6},{6,10},{10,14},{3,7},{... | collective-permute-start | bytes 147464 | tf_op jit(solution)/shard_map/ppermute | solution.py:28
  64.0 1.3 multiply_reduce_fusion.10
  65.4 1.3 multiply_reduce_fusion.9
  66.8 0.6 fusion.16.inc_ref
  67.4 4.8 %shard_map.142 = (f32[8,2,6,512]{3,2,1,0:T(8,128)}, f32[2,1,2,6,512]{4,3,2,1,0:T(8,128)}) custom-call(f32[8,2,6,512]{3,2,1,0:T(8,128)} %copy.218.refs_0_.rhs_ref, f32[8,2,6,6,512]{4,3,2,1,0:T(8,128)} %get-tuple-element.35.refs_0_.refs_1_.nt_ref, f32[8,2,6,6,512]{4,3,2,1,0:T(8,128)} %get-tuple-element.34.refs_1_.refs_2_.ft_ref, ...), custom_call_target="tpu_custom_call" | custom-call | tf_op jit(solution)/shard_map/pallas_call | solution.py:210
  72.2 1.3 collective-permute-start.11
  73.4 1.3 collective-permute-start.9
  74.7 13.2 %collective-permute-done.11 = f32[2,2,6,512]{3,2,1,0:T(8,128)S(1)} collective-permute-done((f32[2,2,6,512]{3,2,1,0:T(8,128)}, f32[2,2,6,512]{3,2,1,0:T(8,128)S(1)}, u32[]{:S(2)}, u32[]{:S(2)}) %collective-permute-start.11) | collective-permute-done | bytes 49184 | tf_op jit(solution)/shard_map/ppermute | solution.py:28
  88.3 1.3 collective-permute-start.12
  89.6 4.8 %collective-permute-done.12 = f32[2,2,6,512]{3,2,1,0:T(8,128)S(1)} collective-permute-done((f32[2,2,6,512]{3,2,1,0:T(8,128)S(1)}, f32[2,2,6,512]{3,2,1,0:T(8,128)S(1)}, u32[]{:S(2)}, u32[]{:S(2)}) %collective-permute-start.12) | collective-permute-done | bytes 49184 | tf_op jit(solution)/shard_map/ppermute | solution.py:28
  94.8 0.6 fusion.15.refs_4_
  95.4 3.6 %shard_map.144 = (f32[8,2,6,512]{3,2,1,0:T(8,128)}, f32[2,1,2,6,512]{4,3,2,1,0:T(8,128)}) custom-call(f32[8,2,6,512]{3,2,1,0:T(8,128)} %get-tuple-element.8.refs_0_, f32[8,2,6,6,512]{4,3,2,1,0:T(8,128)} %copy.219.d_ref.refs_0_.refs_1_, f32[8,2,6,6,512]{4,3,2,1,0:T(8,128)} %copy.220.b_ref.refs_1_.refs_2_, f32[8,2,6,6,512]{4,3,2,1,0:T(8,128)} %copy.221.a_ref.refs_2_.refs_3_, ...), custom_call_target="tpu_custom_call" | custom-call | tf_op jit(solution)/shard_map/pallas_call | solution.py:180
  99.0 1.1 add_multiply_fusion.1
  100.1 1.3 collective-permute-start.13
  101.4 4.5 %collective-permute-start.14 = (f32[1,2,6,512]{3,2,1,0:T(8,128)S(1)}, f32[1,2,6,512]{3,2,1,0:T(8,128)S(1)}, u32[]{:S(2)}, u32[]{:S(2)}) collective-permute-start(f32[1,2,6,512]{3,2,1,0:T(8,128)S(1)} %get-tuple-element.27), channel_id=1, source_target_pairs={{0,4},{4,8},{8,12},{1,5},{5,9},{9,13},{2,6},{6,10},{10,14},{3,7},{... | collective-permute-start | bytes 73736 | tf_op jit(solution)/shard_map/ppermute | solution.py:19
  106.1 1.3 collective-permute-start.15
  107.4 3.2 %collective-permute-start.16 = (f32[8,2,6,32]{3,2,1,0:T(8,128)S(1)}, f32[8,2,6,32]{3,2,1,0:T(8,128)S(1)}, u32[]{:S(2)}, u32[]{:S(2)}) collective-permute-start(f32[8,2,6,32]{3,2,1,0:T(8,128)S(1)} %get-tuple-element.29), channel_id=1, source_target_pairs={{0,1},{1,2},{2,3},{4,5},{5,6},{6,7},{8,9},{9,10},{10,11},{12,13},{... | collective-permute-start | bytes 36872 | tf_op jit(solution)/shard_map/ppermute | solution.py:19
  110.6 0.7 collective-permute-done.16
  111.9 1.8 %convolution_bitcast_fusion = f32[8,2,6,16,32]{4,3,0,2,1:T(8,128)} fusion(f32[8,2,6,16,32]{4,3,0,2,1:T(8,128)S(1)} %reshape.49, f32[2,6,32,32]{3,2,1,0:T(8,128)S(1)} %copy-done), kind=kOutput, calls=%fused_computation.2 | convolution fusion | flops 18874368 | bytes 442368 | tf_op jit(solution)/shard_map/icvjq,cvqk->icvjk/dot_general | solution.py:291
  113.7 1.4 mul.178
  115.2 0.6 multiply_reduce_fusion
  115.8 0.8 copy.242.refs_0_.rhs_ref
  116.6 2.9 %shard_map.145 = f32[2,1,2,6,512]{4,3,2,1,0:T(8,128)} custom-call(f32[8,2,6,512]{3,2,1,0:T(8,128)} %copy.242.refs_0_.rhs_ref, f32[8,2,6,6,512]{4,3,2,1,0:T(8,128)} %get-tuple-element.35.refs_0_.refs_1_.nt_ref, f32[8,2,6,6,512]{4,3,2,1,0:T(8,128)} %get-tuple-element.34.refs_1_.refs_2_.ft_ref, f32[2,1,2,6,512]{4,3,2,1,0:T(8,128)} %broadcast_in_dim.10.refs_3_), custom_call_target="tpu_custom_call" | custom-call | tf_op jit(solution)/shard_map/pallas_call | solution.py:116
  119.5 2.7 %collective-permute-start.17 = (f32[2,2,6,512]{3,2,1,0:T(8,128)}, f32[2,2,6,512]{3,2,1,0:T(8,128)S(1)}, u32[]{:S(2)}, u32[]{:S(2)}) collective-permute-start(f32[2,2,6,512]{3,2,1,0:T(8,128)} %bitcast.83), channel_id=1, source_target_pairs={{0,12},{1,13},{2,14},{3,15},{16,28},{17,29},{18,30},{19,31}} | collective-permute-start | bytes 147464 | tf_op jit(solution)/shard_map/ppermute | solution.py:28
  122.2 1.8 %collective-permute-start.18 = (f32[2,2,6,512]{3,2,1,0:T(8,128)}, f32[2,2,6,512]{3,2,1,0:T(8,128)S(1)}, u32[]{:S(2)}, u32[]{:S(2)}) collective-permute-start(f32[2,2,6,512]{3,2,1,0:T(8,128)} %bitcast.84), channel_id=1, source_target_pairs={{0,8},{4,12},{1,9},{5,13},{2,10},{6,14},{3,11},{7,15},{16,24},{20,... | collective-permute-start | bytes 147464 | tf_op jit(solution)/shard_map/ppermute | solution.py:28
  124.0 1.9 %collective-permute-start.19 = (f32[2,2,6,512]{3,2,1,0:T(8,128)}, f32[2,2,6,512]{3,2,1,0:T(8,128)S(1)}, u32[]{:S(2)}, u32[]{:S(2)}) collective-permute-start(f32[2,2,6,512]{3,2,1,0:T(8,128)} %bitcast.85), channel_id=1, source_target_pairs={{0,4},{4,8},{8,12},{1,5},{5,9},{9,13},{2,6},{6,10},{10,14},{3,7},{... | collective-permute-start | bytes 147464 | tf_op jit(solution)/shard_map/ppermute | solution.py:28
  126.0 1.3 multiply_reduce_fusion.6
  127.4 1.3 multiply_reduce_fusion.5
  128.8 0.6 fusion.13.inc_ref
  129.4 4.8 %shard_map.146 = (f32[8,2,6,512]{3,2,1,0:T(8,128)}, f32[2,1,2,6,512]{4,3,2,1,0:T(8,128)}) custom-call(f32[8,2,6,512]{3,2,1,0:T(8,128)} %copy.242.refs_0_.rhs_ref, f32[8,2,6,6,512]{4,3,2,1,0:T(8,128)} %get-tuple-element.35.refs_0_.refs_1_.nt_ref, f32[8,2,6,6,512]{4,3,2,1,0:T(8,128)} %get-tuple-element.34.refs_1_.refs_2_.ft_ref, ...), custom_call_target="tpu_custom_call" | custom-call | tf_op jit(solution)/shard_map/pallas_call | solution.py:210
  134.2 1.3 collective-permute-start.21
  135.5 1.3 collective-permute-start.20
  136.8 6.3 %collective-permute-done.21 = f32[2,2,6,512]{3,2,1,0:T(8,128)S(1)} collective-permute-done((f32[2,2,6,512]{3,2,1,0:T(8,128)}, f32[2,2,6,512]{3,2,1,0:T(8,128)S(1)}, u32[]{:S(2)}, u32[]{:S(2)}) %collective-permute-start.21) | collective-permute-done | bytes 49184 | tf_op jit(solution)/shard_map/ppermute | solution.py:28
  143.5 1.3 collective-permute-start.22
  145.0 4.7 %collective-permute-done.22 = f32[2,2,6,512]{3,2,1,0:T(8,128)S(1)} collective-permute-done((f32[2,2,6,512]{3,2,1,0:T(8,128)S(1)}, f32[2,2,6,512]{3,2,1,0:T(8,128)S(1)}, u32[]{:S(2)}, u32[]{:S(2)}) %collective-permute-start.22) | collective-permute-done | bytes 49184 | tf_op jit(solution)/shard_map/ppermute | solution.py:28
  149.9 0.6 fusion.12.refs_4_
  150.6 3.6 %shard_map.147 = (f32[8,2,6,512]{3,2,1,0:T(8,128)}, f32[2,1,2,6,512]{4,3,2,1,0:T(8,128)}) custom-call(f32[8,2,6,512]{3,2,1,0:T(8,128)} %get-tuple-element.11.refs_0_, f32[8,2,6,6,512]{4,3,2,1,0:T(8,128)} %copy.219.d_ref.refs_0_.refs_1_, f32[8,2,6,6,512]{4,3,2,1,0:T(8,128)} %copy.220.b_ref.refs_1_.refs_2_, f32[8,2,6,6,512]{4,3,2,1,0:T(8,128)} %copy.221.a_ref.refs_2_.refs_3_, ...), custom_call_target="tpu_custom_call" | custom-call | tf_op jit(solution)/shard_map/pallas_call | solution.py:180
  154.1 1.1 multiply_bitcast_fusion
  155.8 1.6 collective-permute-start.23
  157.3 0.8 copy.253
  158.2 1.8 %collective-permute-done.23 = f32[8,3,512]{2,0,1:T(8,128)S(1)} collective-permute-done((f32[8,3,512]{2,0,1:T(8,128)S(1)}, f32[8,3,512]{2,0,1:T(8,128)S(1)}, u32[]{:S(2)}, u32[]{:S(2)}) %collective-permute-start.23) | collective-permute-done | bytes 49184 | tf_op jit(solution)/shard_map/ppermute | solution.py:312
  159.9 0.6 fusion.25
  (79 shorter events, 4.7 us)
Async XLA Ops:
  0.6 34.2 %copy-start = (f32[2,6,32,32]{3,2,1,0:T(8,128)S(1)}, f32[2,6,32,32]{3,2,1,0:T(8,128)}, u32[]{:S(2)}) copy-start(f32[2,6,32,32]{3,2,1,0:T(8,128)} %param.21) | copy-start | bytes 147460
  1.8 30.3 %collective-permute-start.2 = (f32[8,2,6,32]{3,2,1,0:T(8,128)S(1)}, f32[8,2,6,32]{3,2,1,0:T(8,128)S(1)}, u32[]{:S(2)}, u32[]{:S(2)}) collective-permute-start(f32[8,2,6,32]{3,2,1,0:T(8,128)S(1)} %get-tuple-element.32), channel_id=1, source_target_pairs={{1,0},{2,1},{3,2},{5,4},{6,5},{7,6},{9,8},{10,9},{11,10},{13,12},{... | collective-permute-start | bytes 36872 | tf_op jit(solution)/shard_map/ppermute | solution.py:20
  3.0 31.2 %collective-permute-start.3 = (f32[8,2,6,32]{3,2,1,0:T(8,128)S(1)}, f32[8,2,6,32]{3,2,1,0:T(8,128)S(1)}, u32[]{:S(2)}, u32[]{:S(2)}) collective-permute-start(f32[8,2,6,32]{3,2,1,0:T(8,128)S(1)} %get-tuple-element.33), channel_id=1, source_target_pairs={{0,1},{1,2},{2,3},{4,5},{5,6},{6,7},{8,9},{9,10},{10,11},{12,13},{... | collective-permute-start | bytes 36872 | tf_op jit(solution)/shard_map/ppermute | solution.py:19
  6.1 28.1 %collective-permute-start = (f32[1,2,6,512]{3,2,1,0:T(8,128)S(1)}, f32[1,2,6,512]{3,2,1,0:T(8,128)S(1)}, u32[]{:S(2)}, u32[]{:S(2)}) collective-permute-start(f32[1,2,6,512]{3,2,1,0:T(8,128)S(1)} %get-tuple-element.30), channel_id=1, source_target_pairs={{4,0},{8,4},{12,8},{5,1},{9,5},{13,9},{6,2},{10,6},{14,10},{7,3},{... | collective-permute-start | bytes 73736 | tf_op jit(solution)/shard_map/ppermute | solution.py:20
  7.4 26.8 %collective-permute-start.1 = (f32[1,2,6,512]{3,2,1,0:T(8,128)S(1)}, f32[1,2,6,512]{3,2,1,0:T(8,128)S(1)}, u32[]{:S(2)}, u32[]{:S(2)}) collective-permute-start(f32[1,2,6,512]{3,2,1,0:T(8,128)S(1)} %get-tuple-element.31), channel_id=1, source_target_pairs={{0,4},{4,8},{8,12},{1,5},{5,9},{9,13},{2,6},{6,10},{10,14},{3,7},{... | collective-permute-start | bytes 73736 | tf_op jit(solution)/shard_map/ppermute | solution.py:19
  23.8 10.4 %copy-start.5 = (f32[8,2,6,512]{3,1,2,0:T(2,128)S(1)}, f32[8,2,6,512]{3,1,2,0:T(2,128)}, u32[]{:S(2)}) copy-start(f32[8,2,6,512]{3,1,2,0:T(2,128)} %param.14) | copy-start | bytes 589828
  26.3 37.7 %collective-permute-start.5 = (f32[2,12,2,6,512]{4,2,3,1,0:T(2,128)}, f32[2,12,2,6,512]{4,2,3,1,0:T(2,128)}, u32[]{:S(2)}, u32[]{:S(2)}) collective-permute-start(f32[2,12,2,6,512]{4,2,3,1,0:T(2,128)} %copy.211), channel_id=1, source_target_pairs={{0,8},{4,12},{1,9},{5,13},{2,10},{6,14},{3,11},{7,15},{16,24},{20,... | collective-permute-start | bytes 1769480 | tf_op jit(solution)/shard_map/ppermute | solution.py:28
  32.0 33.4 %collective-permute-start.4 = (f32[2,12,2,6,512]{4,2,3,1,0:T(2,128)}, f32[2,12,2,6,512]{4,2,3,1,0:T(2,128)}, u32[]{:S(2)}, u32[]{:S(2)}) collective-permute-start(f32[2,12,2,6,512]{4,2,3,1,0:T(2,128)} %copy.211), channel_id=1, source_target_pairs={{0,4},{4,8},{8,12},{1,5},{5,9},{9,13},{2,6},{6,10},{10,14},{3,7},{... | collective-permute-start | bytes 1769480 | tf_op jit(solution)/shard_map/ppermute | solution.py:28
  34.8 1.3 copy-start.1
  38.1 4.4 %copy-start.2 = (f32[8,2,6,6,512]{4,1,3,2,0:T(2,128)S(1)}, f32[8,2,6,6,512]{4,1,3,2,0:T(2,128)}, u32[]{:S(2)}) copy-start(f32[8,2,6,6,512]{4,1,3,2,0:T(2,128)} %param.17) | copy-start | bytes 3538948
  41.1 2.9 %copy-start.3 = (f32[8,2,6,6,512]{4,1,3,2,0:T(2,128)S(1)}, f32[8,2,6,6,512]{4,1,3,2,0:T(2,128)}, u32[]{:S(2)}) copy-start(f32[8,2,6,6,512]{4,1,3,2,0:T(2,128)} %param.18) | copy-start | bytes 3538948
  41.1 19.5 %collective-permute-start.6 = (f32[2,2,6,512]{3,2,1,0:T(8,128)}, f32[2,2,6,512]{3,2,1,0:T(8,128)S(1)}, u32[]{:S(2)}, u32[]{:S(2)}) collective-permute-start(f32[2,2,6,512]{3,2,1,0:T(8,128)} %bitcast.80), channel_id=1, source_target_pairs={{0,12},{1,13},{2,14},{3,15},{16,28},{17,29},{18,30},{19,31}} | collective-permute-start | bytes 147464 | tf_op jit(solution)/shard_map/ppermute | solution.py:28
  43.9 1.5 copy-start.4
  55.1 2.9 %copy-start.9 = (f32[2,1,2,6,512]{4,3,2,1,0:T(8,128)S(1)}, f32[2,1,2,6,512]{4,3,2,1,0:T(8,128)}, u32[]{:S(2)}) copy-start(f32[2,1,2,6,512]{4,3,2,1,0:T(8,128)} %shard_map.141) | copy-start | bytes 147460
  56.7 31.3 %collective-permute-start.10 = (f32[2,12,2,6,512]{4,2,3,1,0:T(2,128)S(1)}, f32[2,12,2,6,512]{4,2,3,1,0:T(2,128)S(1)}, u32[]{:S(2)}, u32[]{:S(2)}) collective-permute-start(f32[2,12,2,6,512]{4,2,3,1,0:T(2,128)S(1)} %copy.225), channel_id=1, source_target_pairs={{4,0},{8,4},{12,8},{5,1},{9,5},{13,9},{6,2},{10,6},{14,10},{7,3},{... | collective-permute-start | bytes 1769480 | tf_op jit(solution)/shard_map/ppermute | solution.py:28
  58.1 7.3 %collective-permute-start.7 = (f32[2,2,6,512]{3,2,1,0:T(8,128)S(1)}, f32[2,2,6,512]{3,2,1,0:T(8,128)S(1)}, u32[]{:S(2)}, u32[]{:S(2)}) collective-permute-start(f32[2,2,6,512]{3,2,1,0:T(8,128)S(1)} %bitcast.81), channel_id=1, source_target_pairs={{0,8},{4,12},{1,9},{5,13},{2,10},{6,14},{3,11},{7,15},{16,24},{20,... | collective-permute-start | bytes 147464 | tf_op jit(solution)/shard_map/ppermute | solution.py:28
  60.6 6.2 %collective-permute-start.8 = (f32[2,2,6,512]{3,2,1,0:T(8,128)S(1)}, f32[2,2,6,512]{3,2,1,0:T(8,128)S(1)}, u32[]{:S(2)}, u32[]{:S(2)}) collective-permute-start(f32[2,2,6,512]{3,2,1,0:T(8,128)S(1)} %bitcast.82), channel_id=1, source_target_pairs={{0,4},{4,8},{8,12},{1,5},{5,9},{9,13},{2,6},{6,10},{10,14},{3,7},{... | collective-permute-start | bytes 147464 | tf_op jit(solution)/shard_map/ppermute | solution.py:28
  67.4 22.2 %copy-start.10 = (s32[8,512]{1,0:T(8,128)S(1)}, s32[8,512]{1,0:T(8,128)}, u32[]{:S(2)}) copy-start(s32[8,512]{1,0:T(8,128)} %param.23) | copy-start | bytes 49156
  72.2 15.8 %collective-permute-start.11 = (f32[2,2,6,512]{3,2,1,0:T(8,128)}, f32[2,2,6,512]{3,2,1,0:T(8,128)S(1)}, u32[]{:S(2)}, u32[]{:S(2)}) collective-permute-start(f32[2,2,6,512]{3,2,1,0:T(8,128)} %bitcast.93), channel_id=1, source_target_pairs={{8,0},{12,4},{9,1},{13,5},{10,2},{14,6},{11,3},{15,7},{24,16},{28,... | collective-permute-start | bytes 147464 | tf_op jit(solution)/shard_map/ppermute | solution.py:28
  73.4 14.8 %collective-permute-start.9 = (f32[2,2,6,512]{3,2,1,0:T(8,128)}, f32[2,2,6,512]{3,2,1,0:T(8,128)S(1)}, u32[]{:S(2)}, u32[]{:S(2)}) collective-permute-start(f32[2,2,6,512]{3,2,1,0:T(8,128)} %bitcast.94), channel_id=1, source_target_pairs={{4,0},{8,4},{12,8},{5,1},{9,5},{13,9},{6,2},{10,6},{14,10},{7,3},{... | collective-permute-start | bytes 147464 | tf_op jit(solution)/shard_map/ppermute | solution.py:28
  88.3 6.2 %collective-permute-start.12 = (f32[2,2,6,512]{3,2,1,0:T(8,128)S(1)}, f32[2,2,6,512]{3,2,1,0:T(8,128)S(1)}, u32[]{:S(2)}, u32[]{:S(2)}) collective-permute-start(f32[2,2,6,512]{3,2,1,0:T(8,128)S(1)} %copy_add_fusion.7), channel_id=1, source_target_pairs={{4,0},{8,4},{12,8},{5,1},{9,5},{13,9},{6,2},{10,6},{14,10},{7,3},{... | collective-permute-start | bytes 147464 | tf_op jit(solution)/shard_map/ppermute | solution.py:28
  95.4 3.6 %copy-start.7 = (f32[8,2,6,512]{3,1,2,0:T(2,128)S(1)}, f32[8,2,6,512]{3,1,2,0:T(2,128)}, u32[]{:S(2)}) copy-start(f32[8,2,6,512]{3,1,2,0:T(2,128)} %param.13) | copy-start | bytes 589828
  99.0 12.3 %copy-start.6 = (f32[8,2,6,512]{3,1,2,0:T(2,128)S(1)}, f32[8,2,6,512]{3,1,2,0:T(2,128)}, u32[]{:S(2)}) copy-start(f32[8,2,6,512]{3,1,2,0:T(2,128)} %param.14) | copy-start | bytes 589828
  100.1 11.2 %collective-permute-start.13 = (f32[1,2,6,512]{3,2,1,0:T(8,128)S(1)}, f32[1,2,6,512]{3,2,1,0:T(8,128)S(1)}, u32[]{:S(2)}, u32[]{:S(2)}) collective-permute-start(f32[1,2,6,512]{3,2,1,0:T(8,128)S(1)} %get-tuple-element.26), channel_id=1, source_target_pairs={{4,0},{8,4},{12,8},{5,1},{9,5},{13,9},{6,2},{10,6},{14,10},{7,3},{... | collective-permute-start | bytes 73736 | tf_op jit(solution)/shard_map/ppermute | solution.py:20
  101.4 9.9 %collective-permute-start.14 = (f32[1,2,6,512]{3,2,1,0:T(8,128)S(1)}, f32[1,2,6,512]{3,2,1,0:T(8,128)S(1)}, u32[]{:S(2)}, u32[]{:S(2)}) collective-permute-start(f32[1,2,6,512]{3,2,1,0:T(8,128)S(1)} %get-tuple-element.27), channel_id=1, source_target_pairs={{0,4},{4,8},{8,12},{1,5},{5,9},{9,13},{2,6},{6,10},{10,14},{3,7},{... | collective-permute-start | bytes 73736 | tf_op jit(solution)/shard_map/ppermute | solution.py:19
  106.1 4.5 %collective-permute-start.15 = (f32[8,2,6,32]{3,2,1,0:T(8,128)S(1)}, f32[8,2,6,32]{3,2,1,0:T(8,128)S(1)}, u32[]{:S(2)}, u32[]{:S(2)}) collective-permute-start(f32[8,2,6,32]{3,2,1,0:T(8,128)S(1)} %get-tuple-element.28), channel_id=1, source_target_pairs={{1,0},{2,1},{3,2},{5,4},{6,5},{7,6},{9,8},{10,9},{11,10},{13,12},{... | collective-permute-start | bytes 36872 | tf_op jit(solution)/shard_map/ppermute | solution.py:20
  107.4 3.9 %collective-permute-start.16 = (f32[8,2,6,32]{3,2,1,0:T(8,128)S(1)}, f32[8,2,6,32]{3,2,1,0:T(8,128)S(1)}, u32[]{:S(2)}, u32[]{:S(2)}) collective-permute-start(f32[8,2,6,32]{3,2,1,0:T(8,128)S(1)} %get-tuple-element.29), channel_id=1, source_target_pairs={{0,1},{1,2},{2,3},{4,5},{5,6},{6,7},{8,9},{9,10},{10,11},{12,13},{... | collective-permute-start | bytes 36872 | tf_op jit(solution)/shard_map/ppermute | solution.py:19
  119.5 6.5 %collective-permute-start.17 = (f32[2,2,6,512]{3,2,1,0:T(8,128)}, f32[2,2,6,512]{3,2,1,0:T(8,128)S(1)}, u32[]{:S(2)}, u32[]{:S(2)}) collective-permute-start(f32[2,2,6,512]{3,2,1,0:T(8,128)} %bitcast.83), channel_id=1, source_target_pairs={{0,12},{1,13},{2,14},{3,15},{16,28},{17,29},{18,30},{19,31}} | collective-permute-start | bytes 147464 | tf_op jit(solution)/shard_map/ppermute | solution.py:28
  122.2 5.2 %collective-permute-start.18 = (f32[2,2,6,512]{3,2,1,0:T(8,128)}, f32[2,2,6,512]{3,2,1,0:T(8,128)S(1)}, u32[]{:S(2)}, u32[]{:S(2)}) collective-permute-start(f32[2,2,6,512]{3,2,1,0:T(8,128)} %bitcast.84), channel_id=1, source_target_pairs={{0,8},{4,12},{1,9},{5,13},{2,10},{6,14},{3,11},{7,15},{16,24},{20,... | collective-permute-start | bytes 147464 | tf_op jit(solution)/shard_map/ppermute | solution.py:28
  124.0 4.7 %collective-permute-start.19 = (f32[2,2,6,512]{3,2,1,0:T(8,128)}, f32[2,2,6,512]{3,2,1,0:T(8,128)S(1)}, u32[]{:S(2)}, u32[]{:S(2)}) collective-permute-start(f32[2,2,6,512]{3,2,1,0:T(8,128)} %bitcast.85), channel_id=1, source_target_pairs={{0,4},{4,8},{8,12},{1,5},{5,9},{9,13},{2,6},{6,10},{10,14},{3,7},{... | collective-permute-start | bytes 147464 | tf_op jit(solution)/shard_map/ppermute | solution.py:28
  129.4 15.3 %copy-start.11 = (f32[8]{0:T(128)S(1)}, f32[8]{0:T(128)}, u32[]{:S(2)}) copy-start(f32[8]{0:T(128)} %param.25) | copy-start | bytes 100
  129.4 15.4 %copy-start.12 = (s32[2]{0:T(128)S(1)}, s32[2]{0:T(128)}, u32[]{:S(2)}) copy-start(s32[2]{0:T(128)} %param.24) | copy-start | bytes 28
  134.2 8.9 %collective-permute-start.21 = (f32[2,2,6,512]{3,2,1,0:T(8,128)}, f32[2,2,6,512]{3,2,1,0:T(8,128)S(1)}, u32[]{:S(2)}, u32[]{:S(2)}) collective-permute-start(f32[2,2,6,512]{3,2,1,0:T(8,128)} %bitcast.95), channel_id=1, source_target_pairs={{8,0},{12,4},{9,1},{13,5},{10,2},{14,6},{11,3},{15,7},{24,16},{28,... | collective-permute-start | bytes 147464 | tf_op jit(solution)/shard_map/ppermute | solution.py:28
  135.5 7.9 %collective-permute-start.20 = (f32[2,2,6,512]{3,2,1,0:T(8,128)}, f32[2,2,6,512]{3,2,1,0:T(8,128)S(1)}, u32[]{:S(2)}, u32[]{:S(2)}) collective-permute-start(f32[2,2,6,512]{3,2,1,0:T(8,128)} %bitcast.96), channel_id=1, source_target_pairs={{4,0},{8,4},{12,8},{5,1},{9,5},{13,9},{6,2},{10,6},{14,10},{7,3},{... | collective-permute-start | bytes 147464 | tf_op jit(solution)/shard_map/ppermute | solution.py:28
  143.5 6.2 %collective-permute-start.22 = (f32[2,2,6,512]{3,2,1,0:T(8,128)S(1)}, f32[2,2,6,512]{3,2,1,0:T(8,128)S(1)}, u32[]{:S(2)}, u32[]{:S(2)}) collective-permute-start(f32[2,2,6,512]{3,2,1,0:T(8,128)S(1)} %copy_add_fusion.3), channel_id=1, source_target_pairs={{4,0},{8,4},{12,8},{5,1},{9,5},{13,9},{6,2},{10,6},{14,10},{7,3},{... | collective-permute-start | bytes 147464 | tf_op jit(solution)/shard_map/ppermute | solution.py:28
  154.1 1.3 copy-start.8
  155.8 4.2 %collective-permute-start.23 = (f32[8,3,512]{2,0,1:T(8,128)S(1)}, f32[8,3,512]{2,0,1:T(8,128)S(1)}, u32[]{:S(2)}, u32[]{:S(2)}) collective-permute-start(f32[8,3,512]{2,0,1:T(8,128)S(1)} %bitcast.92), channel_id=1, source_target_pairs={{0,16},{16,0},{1,17},{17,1},{2,18},{18,2},{3,19},{19,3},{4,20},{20... | collective-permute-start | bytes 147464 | tf_op jit(solution)/shard_map/ppermute | solution.py:312

commit v10 on v9

--- a/solution.py
+++ b/solution.py
@@ -297,7 +297,14 @@
         upper, offset = upper_then_lower(
             yres, near_t, far_t, entering[:, None], inverse_diag, near_lower, far_lower
         )
-        entering = relayed_carry(offset[:, 0], lower_behind, -1)
+        if step == 0:
+            entering = jnp.zeros_like(offset[:, 0])
+            for _ in range(lax.axis_size("gx") - 1):
+                entering = from_behind(
+                    carry_through(entering, reverse_matrix) + offset[:, 0], "gx", -1
+                )
+        else:
+            entering = relayed_carry(offset[:, 0], lower_behind, -1)
         lower, _ = lower_pallas(upper, inverse_diag, near_lower, far_lower, entering[:, None], True)
         psi = (psi + 0.05 * lower) * keep
     onehot = (cond_index[:, None] == jnp.arange(weight_table.shape[0])[None, :]).astype(jnp.float32)

time: 162 us -> 174 us (1.074)
  waiting for transfers between devices: 31.6 us -> 44.4 us
    ppermute x15, waiting for transfers between devices: 29.1 us -> 41.9 us  [from_behind(): lax.ppermute(value, axis, [(source, source + steps) for source in range(f...]
    reduce_sum x8 -> x9, other arithmetic: 6.33 us -> 3.97 us  [carry_through(): return jnp.sum(jnp.sum(split * inputs, axis=2), axis=1)]
    unnamed x32 -> x42, local copies, waits for them, and re-layouts: 6.38 us -> 7.01 us
  transfers between devices with their start and end apart: 24 -> 24, of which waited for: 6 -> 10; matrix products, arithmetic and copies ran while one was open for 15% -> 13% of each run, Pallas kernels for 14% -> 13%
where the time goes in v10:
time: 174 us; the launch traced here: 173 us
  starting transfers between devices  53.6 us (31%)
  waiting for transfers between devices  44.4 us (26%)
  Pallas kernels  37.7 us (22%)
  local copies, waits for them, and re-layouts  20.6 us (12%)
  other arithmetic  12.6 us (7%)
  matrix products  2.59 us (1%)
    ppermute x15, waiting for transfers between devices, from_behind(): lax.ppermute(value, axis, [(source, source + steps) for source in range(f...  41.9 us
    ppermute x15, starting transfers between devices, from_behind(): lax.ppermute(value, axis, [(source, source + steps) for source in range(f...  29.9 us
    ppermute x4, starting transfers between devices, extended(): before = lax.ppermute(last, axis, up)  17 us
    pallas_call x3, Pallas kernels, lower_pallas(): pl.pallas_call(kernel, out_shape=tuple(out_shape), in_specs=_vmem_specs(l...  15.5 us
    pallas_call x3, Pallas kernels, upper_pallas(): pl.pallas_call(kernel, out_shape=tuple(out_shape), in_specs=_vmem_specs(l...  12.7 us
    pallas_call x2, Pallas kernels, upper_then_lower(): pl.pallas_call(kernel, out_shape=(jax.ShapeDtypeStruct(rhs.shape, jnp.flo...  9.54 us
    unnamed x42, local copies, waits for them, and re-layouts  7.01 us
    ppermute x4, starting transfers between devices, extended(): after = lax.ppermute(first, axis, down)  5.14 us
  transfers between devices with their start and end apart: 24, of which 10 were waited for; matrix products, arithmetic and copies ran while one was open for 13% of the time, Pallas kernels for 13%

profile of v10, /device:TPU:0, one launch (start us, length us, event | category | flops | bytes accessed | tf_op | source)
XLA Modules:
  0.0 172.7 jit_solution(11376939337697627298)
XLA Ops:
  0.6 1.0 copy.228
  2.3 1.3 collective-permute-start
  3.6 6.2 %collective-permute-start.1 = (f32[1,2,6,512]{3,2,1,0:T(8,128)}, f32[1,2,6,512]{3,2,1,0:T(8,128)}, u32[]{:S(2)}, u32[]{:S(2)}) collective-permute-start(f32[1,2,6,512]{3,2,1,0:T(8,128)} %get-tuple-element.31), channel_id=1, source_target_pairs={{0,4},{4,8},{8,12},{1,5},{5,9},{9,13},{2,6},{6,10},{10,14},{3,7},{... | collective-permute-start | bytes 73736 | tf_op jit(solution)/shard_map/ppermute | solution.py:19
  9.8 0.7 fusion.21
  10.5 1.3 collective-permute-start.2
  11.8 3.0 %collective-permute-start.3 = (f32[8,2,6,32]{3,2,1,0:T(8,128)}, f32[8,2,6,32]{3,2,1,0:T(8,128)S(1)}, u32[]{:S(2)}, u32[]{:S(2)}) collective-permute-start(f32[8,2,6,32]{3,2,1,0:T(8,128)} %get-tuple-element.33), channel_id=1, source_target_pairs={{0,1},{1,2},{2,3},{4,5},{5,6},{6,7},{8,9},{9,10},{10,11},{12,13},{... | collective-permute-start | bytes 36872 | tf_op jit(solution)/shard_map/ppermute | solution.py:19
  14.8 4.0 %copy_bitcast_fusion = (f32[8,2,6,6,512]{4,3,2,1,0:T(8,128)}, f32[8,2,6,6,512]{4,3,2,1,0:T(8,128)}) fusion(f32[8,2,6,6,512]{4,1,3,2,0:T(2,128)} %param.16, f32[8,2,6,6,512]{4,1,3,2,0:T(2,128)} %param.15), kind=kLoop, calls=%fused_computation | loop fusion | bytes 4718592 | tf_op jit(solution)/shard_map/transpose | solution.py:275
  18.8 6.9 %shard_map.140 = f32[2,12,2,6,512]{4,3,2,1,0:T(8,128)} custom-call(f32[8,2,6,6,512]{4,3,2,1,0:T(8,128)} %get-tuple-element.35.refs_0_.refs_1_.nt_ref, f32[8,2,6,6,512]{4,3,2,1,0:T(8,128)} %get-tuple-element.34.refs_1_.refs_2_.ft_ref), custom_call_target="tpu_custom_call" | custom-call | tf_op jit(solution)/shard_map/pallas_call | solution.py:116
  25.7 2.5 %copy.209 = f32[2,12,2,6,512]{4,2,3,1,0:T(2,128)} copy(f32[2,12,2,6,512]{4,3,2,1,0:T(8,128)} %shard_map.140) | data formatting | bytes 1179648 | tf_op jit(solution)/shard_map/pallas_call | solution.py:116
  28.2 5.1 %collective-permute-start.5 = (f32[2,12,2,6,512]{4,2,3,1,0:T(2,128)}, f32[2,12,2,6,512]{4,2,3,1,0:T(2,128)S(1)}, u32[]{:S(2)}, u32[]{:S(2)}) collective-permute-start(f32[2,12,2,6,512]{4,2,3,1,0:T(2,128)} %copy.209), channel_id=1, source_target_pairs={{0,8},{4,12},{1,9},{5,13},{2,10},{6,14},{3,11},{7,15},{16,24},{20,... | collective-permute-start | bytes 1769480 | tf_op jit(solution)/shard_map/ppermute | solution.py:28
  33.3 1.4 copy.217.d_ref.refs_0_.refs_1_
  34.7 1.4 copy.218.b_ref.refs_1_.refs_2_
  36.1 1.4 copy.219.a_ref.refs_2_.refs_3_
  37.6 8.3 %shard_map.143 = f32[2,12,2,6,512]{4,3,2,1,0:T(8,128)} custom-call(f32[8,2,6,6,512]{4,3,2,1,0:T(8,128)} %copy.217.d_ref.refs_0_.refs_1_, f32[8,2,6,6,512]{4,3,2,1,0:T(8,128)} %copy.218.b_ref.refs_1_.refs_2_, f32[8,2,6,6,512]{4,3,2,1,0:T(8,128)} %copy.219.a_ref.refs_2_.refs_3_), custom_call_target="tpu_custom_call" | custom-call | tf_op jit(solution)/shard_map/pallas_call | solution.py:180
  45.9 2.2 %collective-permute-start.4 = (f32[2,12,2,6,512]{4,2,3,1,0:T(2,128)}, f32[2,12,2,6,512]{4,2,3,1,0:T(2,128)}, u32[]{:S(2)}, u32[]{:S(2)}) collective-permute-start(f32[2,12,2,6,512]{4,2,3,1,0:T(2,128)} %copy.209), channel_id=1, source_target_pairs={{0,4},{4,8},{8,12},{1,5},{5,9},{9,13},{2,6},{6,10},{10,14},{3,7},{... | collective-permute-start | bytes 1769480 | tf_op jit(solution)/shard_map/ppermute | solution.py:28
  48.1 1.0 fusion
  49.5 0.8 convolution_bitcast_fusion.1
  51.3 0.8 copy.216.refs_0_.rhs_ref
  52.7 2.9 %shard_map.141 = f32[2,1,2,6,512]{4,3,2,1,0:T(8,128)} custom-call(f32[8,2,6,512]{3,2,1,0:T(8,128)} %copy.216.refs_0_.rhs_ref, f32[8,2,6,6,512]{4,3,2,1,0:T(8,128)} %get-tuple-element.35.refs_0_.refs_1_.nt_ref, f32[8,2,6,6,512]{4,3,2,1,0:T(8,128)} %get-tuple-element.34.refs_1_.refs_2_.ft_ref, f32[2,1,2,6,512]{4,3,2,1,0:T(8,128)} %broadcast_in_dim.10.refs_3_), custom_call_target="tpu_custom_call" | custom-call | tf_op jit(solution)/shard_map/pallas_call | solution.py:116
  55.7 1.3 collective-permute-start.6
  57.1 1.3 collective-permute-start.8
  58.4 1.3 collective-permute-start.7
  59.7 2.8 %collective-permute-done.6 = f32[2,2,6,512]{3,2,1,0:T(8,128)S(1)} collective-permute-done((f32[2,2,6,512]{3,2,1,0:T(8,128)}, f32[2,2,6,512]{3,2,1,0:T(8,128)S(1)}, u32[]{:S(2)}, u32[]{:S(2)}) %collective-permute-start.6) | collective-permute-done | bytes 49184 | tf_op jit(solution)/shard_map/ppermute | solution.py:28
  62.8 2.5 %collective-permute-done.7 = f32[2,2,6,512]{3,2,1,0:T(8,128)S(1)} collective-permute-done((f32[2,2,6,512]{3,2,1,0:T(8,128)}, f32[2,2,6,512]{3,2,1,0:T(8,128)S(1)}, u32[]{:S(2)}, u32[]{:S(2)}) %collective-permute-start.7) | collective-permute-done | bytes 49184 | tf_op jit(solution)/shard_map/ppermute | solution.py:28
  65.4 1.3 multiply_reduce_fusion.10
  67.4 4.8 %shard_map.142 = (f32[8,2,6,512]{3,2,1,0:T(8,128)}, f32[2,1,2,6,512]{4,3,2,1,0:T(8,128)}) custom-call(f32[8,2,6,512]{3,2,1,0:T(8,128)} %copy.216.refs_0_.rhs_ref, f32[8,2,6,6,512]{4,3,2,1,0:T(8,128)} %get-tuple-element.35.refs_0_.refs_1_.nt_ref, f32[8,2,6,6,512]{4,3,2,1,0:T(8,128)} %get-tuple-element.34.refs_1_.refs_2_.ft_ref, ...), custom_call_target="tpu_custom_call" | custom-call | tf_op jit(solution)/shard_map/pallas_call | solution.py:210
  72.2 0.9 bitcast_add_fusion.2
  73.1 1.3 collective-permute-start.9
  74.4 15.2 %collective-permute-done.9 = f32[2,2,6,512]{3,2,1,0:T(8,128)S(1)} collective-permute-done((f32[2,2,6,512]{3,2,1,0:T(8,128)S(1)}, f32[2,2,6,512]{3,2,1,0:T(8,128)S(1)}, u32[]{:S(2)}, u32[]{:S(2)}) %collective-permute-start.9) | collective-permute-done | bytes 49184 | tf_op jit(solution)/shard_map/ppermute | solution.py:28
  89.8 1.3 collective-permute-start.10
  91.1 4.9 %collective-permute-done.10 = f32[2,2,6,512]{3,2,1,0:T(8,128)S(1)} collective-permute-done((f32[2,2,6,512]{3,2,1,0:T(8,128)S(1)}, f32[2,2,6,512]{3,2,1,0:T(8,128)S(1)}, u32[]{:S(2)}, u32[]{:S(2)}) %collective-permute-start.10) | collective-permute-done | bytes 49184 | tf_op jit(solution)/shard_map/ppermute | solution.py:28
  96.1 1.3 collective-permute-start.11
  97.4 4.8 %collective-permute-done.11 = f32[2,2,6,512]{3,2,1,0:T(8,128)S(1)} collective-permute-done((f32[2,2,6,512]{3,2,1,0:T(8,128)S(1)}, f32[2,2,6,512]{3,2,1,0:T(8,128)S(1)}, u32[]{:S(2)}, u32[]{:S(2)}) %collective-permute-start.11) | collective-permute-done | bytes 49184 | tf_op jit(solution)/shard_map/ppermute | solution.py:28
  102.9 3.6 %shard_map.144 = (f32[8,2,6,512]{3,2,1,0:T(8,128)}, f32[2,1,2,6,512]{4,3,2,1,0:T(8,128)}) custom-call(f32[8,2,6,512]{3,2,1,0:T(8,128)} %get-tuple-element.8.refs_0_, f32[8,2,6,6,512]{4,3,2,1,0:T(8,128)} %copy.217.d_ref.refs_0_.refs_1_, f32[8,2,6,6,512]{4,3,2,1,0:T(8,128)} %copy.218.b_ref.refs_1_.refs_2_, f32[8,2,6,6,512]{4,3,2,1,0:T(8,128)} %copy.219.a_ref.refs_2_.refs_3_, ...), custom_call_target="tpu_custom_call" | custom-call | tf_op jit(solution)/shard_map/pallas_call | solution.py:180
  106.5 1.1 add_multiply_fusion.1
  107.6 1.3 collective-permute-start.12
  108.9 4.5 %collective-permute-start.13 = (f32[1,2,6,512]{3,2,1,0:T(8,128)S(1)}, f32[1,2,6,512]{3,2,1,0:T(8,128)S(1)}, u32[]{:S(2)}, u32[]{:S(2)}) collective-permute-start(f32[1,2,6,512]{3,2,1,0:T(8,128)S(1)} %get-tuple-element.27), channel_id=1, source_target_pairs={{0,4},{4,8},{8,12},{1,5},{5,9},{9,13},{2,6},{6,10},{10,14},{3,7},{... | collective-permute-start | bytes 73736 | tf_op jit(solution)/shard_map/ppermute | solution.py:19
  113.5 1.3 collective-permute-start.14
  114.8 3.2 %collective-permute-start.15 = (f32[8,2,6,32]{3,2,1,0:T(8,128)S(1)}, f32[8,2,6,32]{3,2,1,0:T(8,128)S(1)}, u32[]{:S(2)}, u32[]{:S(2)}) collective-permute-start(f32[8,2,6,32]{3,2,1,0:T(8,128)S(1)} %get-tuple-element.29), channel_id=1, source_target_pairs={{0,1},{1,2},{2,3},{4,5},{5,6},{6,7},{8,9},{9,10},{10,11},{12,13},{... | collective-permute-start | bytes 36872 | tf_op jit(solution)/shard_map/ppermute | solution.py:19
  118.1 0.7 collective-permute-done.15
  119.4 1.8 %convolution_bitcast_fusion = f32[8,2,6,16,32]{4,3,0,2,1:T(8,128)} fusion(f32[8,2,6,16,32]{4,3,0,2,1:T(8,128)S(1)} %reshape.50, f32[2,6,32,32]{3,2,1,0:T(8,128)S(1)} %copy-done), kind=kOutput, calls=%fused_computation.2 | convolution fusion | flops 18874368 | bytes 442368 | tf_op jit(solution)/shard_map/icvjq,cvqk->icvjk/dot_general | solution.py:291
  121.1 1.4 mul.187
  123.3 0.8 copy.237.refs_0_.rhs_ref
  124.1 2.9 %shard_map.145 = f32[2,1,2,6,512]{4,3,2,1,0:T(8,128)} custom-call(f32[8,2,6,512]{3,2,1,0:T(8,128)} %copy.237.refs_0_.rhs_ref, f32[8,2,6,6,512]{4,3,2,1,0:T(8,128)} %get-tuple-element.35.refs_0_.refs_1_.nt_ref, f32[8,2,6,6,512]{4,3,2,1,0:T(8,128)} %get-tuple-element.34.refs_1_.refs_2_.ft_ref, f32[2,1,2,6,512]{4,3,2,1,0:T(8,128)} %broadcast_in_dim.10.refs_3_), custom_call_target="tpu_custom_call" | custom-call | tf_op jit(solution)/shard_map/pallas_call | solution.py:116
  127.0 3.3 %collective-permute-start.16 = (f32[2,2,6,512]{3,2,1,0:T(8,128)}, f32[2,2,6,512]{3,2,1,0:T(8,128)S(1)}, u32[]{:S(2)}, u32[]{:S(2)}) collective-permute-start(f32[2,2,6,512]{3,2,1,0:T(8,128)} %bitcast.82), channel_id=1, source_target_pairs={{0,12},{1,13},{2,14},{3,15},{16,28},{17,29},{18,30},{19,31}} | collective-permute-start | bytes 147464 | tf_op jit(solution)/shard_map/ppermute | solution.py:28
  130.8 1.3 collective-permute-start.20
  132.1 4.5 %collective-permute-start.18 = (f32[2,2,6,512]{3,2,1,0:T(8,128)S(1)}, f32[2,2,6,512]{3,2,1,0:T(8,128)S(1)}, u32[]{:S(2)}, u32[]{:S(2)}) collective-permute-start(f32[2,2,6,512]{3,2,1,0:T(8,128)S(1)} %bitcast.83), channel_id=1, source_target_pairs={{0,4},{4,8},{8,12},{1,5},{5,9},{9,13},{2,6},{6,10},{10,14},{3,7},{... | collective-permute-start | bytes 147464 | tf_op jit(solution)/shard_map/ppermute | solution.py:28
  136.6 1.9 %collective-permute-start.17 = (f32[2,2,6,512]{3,2,1,0:T(8,128)S(1)}, f32[2,2,6,512]{3,2,1,0:T(8,128)S(1)}, u32[]{:S(2)}, u32[]{:S(2)}) collective-permute-start(f32[2,2,6,512]{3,2,1,0:T(8,128)S(1)} %bitcast.84), channel_id=1, source_target_pairs={{0,8},{4,12},{1,9},{5,13},{2,10},{6,14},{3,11},{7,15},{16,24},{20,... | collective-permute-start | bytes 147464 | tf_op jit(solution)/shard_map/ppermute | solution.py:28
  138.8 1.6 collective-permute-done.17
  140.5 1.3 multiply_reduce_fusion.8
  141.8 0.6 fusion.13.inc_ref
  142.5 4.8 %shard_map.146 = (f32[8,2,6,512]{3,2,1,0:T(8,128)}, f32[2,1,2,6,512]{4,3,2,1,0:T(8,128)}) custom-call(f32[8,2,6,512]{3,2,1,0:T(8,128)} %copy.237.refs_0_.rhs_ref, f32[8,2,6,6,512]{4,3,2,1,0:T(8,128)} %get-tuple-element.35.refs_0_.refs_1_.nt_ref, f32[8,2,6,6,512]{4,3,2,1,0:T(8,128)} %get-tuple-element.34.refs_1_.refs_2_.ft_ref, ...), custom_call_target="tpu_custom_call" | custom-call | tf_op jit(solution)/shard_map/pallas_call | solution.py:210
  147.3 1.3 collective-permute-start.21
  148.5 1.3 collective-permute-start.19
  149.8 5.5 %collective-permute-done.21 = f32[2,2,6,512]{3,2,1,0:T(8,128)S(1)} collective-permute-done((f32[2,2,6,512]{3,2,1,0:T(8,128)}, f32[2,2,6,512]{3,2,1,0:T(8,128)S(1)}, u32[]{:S(2)}, u32[]{:S(2)}) %collective-permute-start.21) | collective-permute-done | bytes 49184 | tf_op jit(solution)/shard_map/ppermute | solution.py:28
  155.6 1.3 collective-permute-start.22
  157.1 4.7 %collective-permute-done.22 = f32[2,2,6,512]{3,2,1,0:T(8,128)S(1)} collective-permute-done((f32[2,2,6,512]{3,2,1,0:T(8,128)S(1)}, f32[2,2,6,512]{3,2,1,0:T(8,128)S(1)}, u32[]{:S(2)}, u32[]{:S(2)}) %collective-permute-start.22) | collective-permute-done | bytes 49184 | tf_op jit(solution)/shard_map/ppermute | solution.py:28
  162.1 0.6 fusion.12.refs_4_
  162.7 3.6 %shard_map.147 = (f32[8,2,6,512]{3,2,1,0:T(8,128)}, f32[2,1,2,6,512]{4,3,2,1,0:T(8,128)}) custom-call(f32[8,2,6,512]{3,2,1,0:T(8,128)} %get-tuple-element.11.refs_0_, f32[8,2,6,6,512]{4,3,2,1,0:T(8,128)} %copy.217.d_ref.refs_0_.refs_1_, f32[8,2,6,6,512]{4,3,2,1,0:T(8,128)} %copy.218.b_ref.refs_1_.refs_2_, f32[8,2,6,6,512]{4,3,2,1,0:T(8,128)} %copy.219.a_ref.refs_2_.refs_3_, ...), custom_call_target="tpu_custom_call" | custom-call | tf_op jit(solution)/shard_map/pallas_call | solution.py:180
  166.3 1.1 multiply_bitcast_fusion
  167.9 1.6 collective-permute-start.23
  169.5 0.8 copy.249
  170.3 1.8 %collective-permute-done.23 = f32[8,3,512]{2,0,1:T(8,128)S(1)} collective-permute-done((f32[8,3,512]{2,0,1:T(8,128)S(1)}, f32[8,3,512]{2,0,1:T(8,128)S(1)}, u32[]{:S(2)}, u32[]{:S(2)}) %collective-permute-start.23) | collective-permute-done | bytes 49184 | tf_op jit(solution)/shard_map/ppermute | solution.py:319
  172.1 0.6 fusion.24
  (91 shorter events, 8.3 us)
Async XLA Ops:
  0.6 48.8 %copy-start = (f32[2,6,32,32]{3,2,1,0:T(8,128)S(1)}, f32[2,6,32,32]{3,2,1,0:T(8,128)}, u32[]{:S(2)}) copy-start(f32[2,6,32,32]{3,2,1,0:T(8,128)} %param.21) | copy-start | bytes 147460
  2.3 45.8 %collective-permute-start = (f32[1,2,6,512]{3,2,1,0:T(8,128)}, f32[1,2,6,512]{3,2,1,0:T(8,128)}, u32[]{:S(2)}, u32[]{:S(2)}) collective-permute-start(f32[1,2,6,512]{3,2,1,0:T(8,128)} %get-tuple-element.30), channel_id=1, source_target_pairs={{4,0},{8,4},{12,8},{5,1},{9,5},{13,9},{6,2},{10,6},{14,10},{7,3},{... | collective-permute-start | bytes 73736 | tf_op jit(solution)/shard_map/ppermute | solution.py:20
  3.6 44.5 %collective-permute-start.1 = (f32[1,2,6,512]{3,2,1,0:T(8,128)}, f32[1,2,6,512]{3,2,1,0:T(8,128)}, u32[]{:S(2)}, u32[]{:S(2)}) collective-permute-start(f32[1,2,6,512]{3,2,1,0:T(8,128)} %get-tuple-element.31), channel_id=1, source_target_pairs={{0,4},{4,8},{8,12},{1,5},{5,9},{9,13},{2,6},{6,10},{10,14},{3,7},{... | collective-permute-start | bytes 73736 | tf_op jit(solution)/shard_map/ppermute | solution.py:19
  10.5 35.4 %collective-permute-start.2 = (f32[8,2,6,32]{3,2,1,0:T(8,128)}, f32[8,2,6,32]{3,2,1,0:T(8,128)S(1)}, u32[]{:S(2)}, u32[]{:S(2)}) collective-permute-start(f32[8,2,6,32]{3,2,1,0:T(8,128)} %get-tuple-element.32), channel_id=1, source_target_pairs={{1,0},{2,1},{3,2},{5,4},{6,5},{7,6},{9,8},{10,9},{11,10},{13,12},{... | collective-permute-start | bytes 36872 | tf_op jit(solution)/shard_map/ppermute | solution.py:20
  11.8 36.3 %collective-permute-start.3 = (f32[8,2,6,32]{3,2,1,0:T(8,128)}, f32[8,2,6,32]{3,2,1,0:T(8,128)S(1)}, u32[]{:S(2)}, u32[]{:S(2)}) collective-permute-start(f32[8,2,6,32]{3,2,1,0:T(8,128)} %get-tuple-element.33), channel_id=1, source_target_pairs={{0,1},{1,2},{2,3},{4,5},{5,6},{6,7},{8,9},{9,10},{10,11},{12,13},{... | collective-permute-start | bytes 36872 | tf_op jit(solution)/shard_map/ppermute | solution.py:19
  25.7 7.6 %copy-start.5 = (f32[8,2,6,6,512]{4,1,3,2,0:T(2,128)S(1)}, f32[8,2,6,6,512]{4,1,3,2,0:T(2,128)}, u32[]{:S(2)}) copy-start(f32[8,2,6,6,512]{4,1,3,2,0:T(2,128)} %param.17) | copy-start | bytes 3538948
  28.2 6.5 %copy-start.6 = (f32[8,2,6,6,512]{4,1,3,2,0:T(2,128)S(1)}, f32[8,2,6,6,512]{4,1,3,2,0:T(2,128)}, u32[]{:S(2)}) copy-start(f32[8,2,6,6,512]{4,1,3,2,0:T(2,128)} %param.18) | copy-start | bytes 3538948
  28.2 34.4 %collective-permute-start.5 = (f32[2,12,2,6,512]{4,2,3,1,0:T(2,128)}, f32[2,12,2,6,512]{4,2,3,1,0:T(2,128)S(1)}, u32[]{:S(2)}, u32[]{:S(2)}) collective-permute-start(f32[2,12,2,6,512]{4,2,3,1,0:T(2,128)} %copy.209), channel_id=1, source_target_pairs={{0,8},{4,12},{1,9},{5,13},{2,10},{6,14},{3,11},{7,15},{16,24},{20,... | collective-permute-start | bytes 1769480 | tf_op jit(solution)/shard_map/ppermute | solution.py:28
  34.7 1.4 copy-start.7
  37.6 10.5 %copy-start.8 = (f32[8,2,6,512]{3,1,2,0:T(2,128)S(1)}, f32[8,2,6,512]{3,1,2,0:T(2,128)}, u32[]{:S(2)}) copy-start(f32[8,2,6,512]{3,1,2,0:T(2,128)} %param.14) | copy-start | bytes 589828
  45.9 19.5 %collective-permute-start.4 = (f32[2,12,2,6,512]{4,2,3,1,0:T(2,128)}, f32[2,12,2,6,512]{4,2,3,1,0:T(2,128)}, u32[]{:S(2)}, u32[]{:S(2)}) collective-permute-start(f32[2,12,2,6,512]{4,2,3,1,0:T(2,128)} %copy.209), channel_id=1, source_target_pairs={{0,4},{4,8},{8,12},{1,5},{5,9},{9,13},{2,6},{6,10},{10,14},{3,7},{... | collective-permute-start | bytes 1769480 | tf_op jit(solution)/shard_map/ppermute | solution.py:28
  49.5 1.3 copy-start.2
  52.7 4.2 %copy-start.1 = (f32[2,12,2,6,512]{4,3,2,1,0:T(8,128)S(1)}, f32[2,12,2,6,512]{4,3,2,1,0:T(8,128)}, u32[]{:S(2)}) copy-start(f32[2,12,2,6,512]{4,3,2,1,0:T(8,128)} %shard_map.143) | copy-start | bytes 1769476
  55.7 6.8 %collective-permute-start.6 = (f32[2,2,6,512]{3,2,1,0:T(8,128)}, f32[2,2,6,512]{3,2,1,0:T(8,128)S(1)}, u32[]{:S(2)}, u32[]{:S(2)}) collective-permute-start(f32[2,2,6,512]{3,2,1,0:T(8,128)} %bitcast.85), channel_id=1, source_target_pairs={{0,12},{1,13},{2,14},{3,15},{16,28},{17,29},{18,30},{19,31}} | collective-permute-start | bytes 147464 | tf_op jit(solution)/shard_map/ppermute | solution.py:28
  57.1 9.7 %collective-permute-start.8 = (f32[2,2,6,512]{3,2,1,0:T(8,128)}, f32[2,2,6,512]{3,2,1,0:T(8,128)S(1)}, u32[]{:S(2)}, u32[]{:S(2)}) collective-permute-start(f32[2,2,6,512]{3,2,1,0:T(8,128)} %bitcast.86), channel_id=1, source_target_pairs={{0,4},{4,8},{8,12},{1,5},{5,9},{9,13},{2,6},{6,10},{10,14},{3,7},{... | collective-permute-start | bytes 147464 | tf_op jit(solution)/shard_map/ppermute | solution.py:28
  58.4 7.0 %collective-permute-start.7 = (f32[2,2,6,512]{3,2,1,0:T(8,128)}, f32[2,2,6,512]{3,2,1,0:T(8,128)S(1)}, u32[]{:S(2)}, u32[]{:S(2)}) collective-permute-start(f32[2,2,6,512]{3,2,1,0:T(8,128)} %bitcast.87), channel_id=1, source_target_pairs={{0,8},{4,12},{1,9},{5,13},{2,10},{6,14},{3,11},{7,15},{16,24},{20,... | collective-permute-start | bytes 147464 | tf_op jit(solution)/shard_map/ppermute | solution.py:28
  62.5 9.6 %copy-start.3 = (f32[2,12,2,6,512]{4,2,3,1,0:T(2,128)}, f32[2,12,2,6,512]{4,2,3,1,0:T(2,128)S(1)}, u32[]{:S(2)}) copy-start(f32[2,12,2,6,512]{4,2,3,1,0:T(2,128)S(1)} %collective-permute-done.5) | copy-start | bytes 1769476
  72.2 17.6 %copy-start.11 = (f32[2,1,2,6,512]{4,3,2,1,0:T(8,128)S(1)}, f32[2,1,2,6,512]{4,3,2,1,0:T(8,128)}, u32[]{:S(2)}) copy-start(f32[2,1,2,6,512]{4,3,2,1,0:T(8,128)} %get-tuple-element.9) | copy-start | bytes 147460
  73.1 16.5 %collective-permute-start.9 = (f32[2,2,6,512]{3,2,1,0:T(8,128)S(1)}, f32[2,2,6,512]{3,2,1,0:T(8,128)S(1)}, u32[]{:S(2)}, u32[]{:S(2)}) collective-permute-start(f32[2,2,6,512]{3,2,1,0:T(8,128)S(1)} %bitcast_add_fusion.2), channel_id=1, source_target_pairs={{4,0},{8,4},{12,8},{5,1},{9,5},{13,9},{6,2},{10,6},{14,10},{7,3},{... | collective-permute-start | bytes 147464 | tf_op jit(solution)/shard_map/ppermute | solution.py:28
  89.6 7.8 %copy-start.15 = (s32[8,512]{1,0:T(8,128)S(1)}, s32[8,512]{1,0:T(8,128)}, u32[]{:S(2)}) copy-start(s32[8,512]{1,0:T(8,128)} %param.23) | copy-start | bytes 49156
  89.8 6.2 %collective-permute-start.10 = (f32[2,2,6,512]{3,2,1,0:T(8,128)S(1)}, f32[2,2,6,512]{3,2,1,0:T(8,128)S(1)}, u32[]{:S(2)}, u32[]{:S(2)}) collective-permute-start(f32[2,2,6,512]{3,2,1,0:T(8,128)S(1)} %bitcast_add_fusion.1), channel_id=1, source_target_pairs={{4,0},{8,4},{12,8},{5,1},{9,5},{13,9},{6,2},{10,6},{14,10},{7,3},{... | collective-permute-start | bytes 147464 | tf_op jit(solution)/shard_map/ppermute | solution.py:28
  96.1 6.2 %collective-permute-start.11 = (f32[2,2,6,512]{3,2,1,0:T(8,128)S(1)}, f32[2,2,6,512]{3,2,1,0:T(8,128)S(1)}, u32[]{:S(2)}, u32[]{:S(2)}) collective-permute-start(f32[2,2,6,512]{3,2,1,0:T(8,128)S(1)} %bitcast_add_fusion), channel_id=1, source_target_pairs={{4,0},{8,4},{12,8},{5,1},{9,5},{13,9},{6,2},{10,6},{14,10},{7,3},{... | collective-permute-start | bytes 147464 | tf_op jit(solution)/shard_map/ppermute | solution.py:28
  102.3 0.6 copy-start.14
  102.9 3.6 %copy-start.10 = (f32[8,2,6,512]{3,1,2,0:T(2,128)S(1)}, f32[8,2,6,512]{3,1,2,0:T(2,128)}, u32[]{:S(2)}) copy-start(f32[8,2,6,512]{3,1,2,0:T(2,128)} %param.13) | copy-start | bytes 589828
  106.5 12.3 %copy-start.9 = (f32[8,2,6,512]{3,1,2,0:T(2,128)S(1)}, f32[8,2,6,512]{3,1,2,0:T(2,128)}, u32[]{:S(2)}) copy-start(f32[8,2,6,512]{3,1,2,0:T(2,128)} %param.14) | copy-start | bytes 589828
  107.6 11.2 %collective-permute-start.12 = (f32[1,2,6,512]{3,2,1,0:T(8,128)S(1)}, f32[1,2,6,512]{3,2,1,0:T(8,128)S(1)}, u32[]{:S(2)}, u32[]{:S(2)}) collective-permute-start(f32[1,2,6,512]{3,2,1,0:T(8,128)S(1)} %get-tuple-element.26), channel_id=1, source_target_pairs={{4,0},{8,4},{12,8},{5,1},{9,5},{13,9},{6,2},{10,6},{14,10},{7,3},{... | collective-permute-start | bytes 73736 | tf_op jit(solution)/shard_map/ppermute | solution.py:20
  108.9 9.9 %collective-permute-start.13 = (f32[1,2,6,512]{3,2,1,0:T(8,128)S(1)}, f32[1,2,6,512]{3,2,1,0:T(8,128)S(1)}, u32[]{:S(2)}, u32[]{:S(2)}) collective-permute-start(f32[1,2,6,512]{3,2,1,0:T(8,128)S(1)} %get-tuple-element.27), channel_id=1, source_target_pairs={{0,4},{4,8},{8,12},{1,5},{5,9},{9,13},{2,6},{6,10},{10,14},{3,7},{... | collective-permute-start | bytes 73736 | tf_op jit(solution)/shard_map/ppermute | solution.py:19
  113.5 4.5 %collective-permute-start.14 = (f32[8,2,6,32]{3,2,1,0:T(8,128)S(1)}, f32[8,2,6,32]{3,2,1,0:T(8,128)S(1)}, u32[]{:S(2)}, u32[]{:S(2)}) collective-permute-start(f32[8,2,6,32]{3,2,1,0:T(8,128)S(1)} %get-tuple-element.28), channel_id=1, source_target_pairs={{1,0},{2,1},{3,2},{5,4},{6,5},{7,6},{9,8},{10,9},{11,10},{13,12},{... | collective-permute-start | bytes 36872 | tf_op jit(solution)/shard_map/ppermute | solution.py:20
  114.8 3.9 %collective-permute-start.15 = (f32[8,2,6,32]{3,2,1,0:T(8,128)S(1)}, f32[8,2,6,32]{3,2,1,0:T(8,128)S(1)}, u32[]{:S(2)}, u32[]{:S(2)}) collective-permute-start(f32[8,2,6,32]{3,2,1,0:T(8,128)S(1)} %get-tuple-element.29), channel_id=1, source_target_pairs={{0,1},{1,2},{2,3},{4,5},{5,6},{6,7},{8,9},{9,10},{10,11},{12,13},{... | collective-permute-start | bytes 36872 | tf_op jit(solution)/shard_map/ppermute | solution.py:19
  127.0 5.1 %copy-start.13 = (f32[2,1,2,6,512]{4,3,2,1,0:T(8,128)S(1)}, f32[2,1,2,6,512]{4,3,2,1,0:T(8,128)}, u32[]{:S(2)}) copy-start(f32[2,1,2,6,512]{4,3,2,1,0:T(8,128)} %shard_map.145) | copy-start | bytes 147460
  127.0 11.6 %copy-start.4 = (f32[2,12,2,6,512]{4,2,3,1,0:T(2,128)S(1)}, f32[2,12,2,6,512]{4,2,3,1,0:T(2,128)}, u32[]{:S(2)}) copy-start(f32[2,12,2,6,512]{4,2,3,1,0:T(2,128)} %copy-done.3) | copy-start | bytes 1769476
  127.0 11.6 %collective-permute-start.16 = (f32[2,2,6,512]{3,2,1,0:T(8,128)}, f32[2,2,6,512]{3,2,1,0:T(8,128)S(1)}, u32[]{:S(2)}, u32[]{:S(2)}) collective-permute-start(f32[2,2,6,512]{3,2,1,0:T(8,128)} %bitcast.82), channel_id=1, source_target_pairs={{0,12},{1,13},{2,14},{3,15},{16,28},{17,29},{18,30},{19,31}} | collective-permute-start | bytes 147464 | tf_op jit(solution)/shard_map/ppermute | solution.py:28
  130.8 24.6 %collective-permute-start.20 = (f32[2,12,2,6,512]{4,2,3,1,0:T(2,128)S(1)}, f32[2,12,2,6,512]{4,2,3,1,0:T(2,128)S(1)}, u32[]{:S(2)}, u32[]{:S(2)}) collective-permute-start(f32[2,12,2,6,512]{4,2,3,1,0:T(2,128)S(1)} %copy.241), channel_id=1, source_target_pairs={{4,0},{8,4},{12,8},{5,1},{9,5},{13,9},{6,2},{10,6},{14,10},{7,3},{... | collective-permute-start | bytes 1769480 | tf_op jit(solution)/shard_map/ppermute | solution.py:28
  132.1 9.7 %collective-permute-start.18 = (f32[2,2,6,512]{3,2,1,0:T(8,128)S(1)}, f32[2,2,6,512]{3,2,1,0:T(8,128)S(1)}, u32[]{:S(2)}, u32[]{:S(2)}) collective-permute-start(f32[2,2,6,512]{3,2,1,0:T(8,128)S(1)} %bitcast.83), channel_id=1, source_target_pairs={{0,4},{4,8},{8,12},{1,5},{5,9},{9,13},{2,6},{6,10},{10,14},{3,7},{... | collective-permute-start | bytes 147464 | tf_op jit(solution)/shard_map/ppermute | solution.py:28
  136.6 3.8 %collective-permute-start.17 = (f32[2,2,6,512]{3,2,1,0:T(8,128)S(1)}, f32[2,2,6,512]{3,2,1,0:T(8,128)S(1)}, u32[]{:S(2)}, u32[]{:S(2)}) collective-permute-start(f32[2,2,6,512]{3,2,1,0:T(8,128)S(1)} %bitcast.84), channel_id=1, source_target_pairs={{0,8},{4,12},{1,9},{5,13},{2,10},{6,14},{3,11},{7,15},{16,24},{20,... | collective-permute-start | bytes 147464 | tf_op jit(solution)/shard_map/ppermute | solution.py:28
  142.5 14.5 %copy-start.16 = (f32[8]{0:T(128)S(1)}, f32[8]{0:T(128)}, u32[]{:S(2)}) copy-start(f32[8]{0:T(128)} %param.25) | copy-start | bytes 100
  142.5 14.5 %copy-start.17 = (s32[2]{0:T(128)S(1)}, s32[2]{0:T(128)}, u32[]{:S(2)}) copy-start(s32[2]{0:T(128)} %param.24) | copy-start | bytes 28
  147.3 8.0 %collective-permute-start.21 = (f32[2,2,6,512]{3,2,1,0:T(8,128)}, f32[2,2,6,512]{3,2,1,0:T(8,128)S(1)}, u32[]{:S(2)}, u32[]{:S(2)}) collective-permute-start(f32[2,2,6,512]{3,2,1,0:T(8,128)} %bitcast.96), channel_id=1, source_target_pairs={{8,0},{12,4},{9,1},{13,5},{10,2},{14,6},{11,3},{15,7},{24,16},{28,... | collective-permute-start | bytes 147464 | tf_op jit(solution)/shard_map/ppermute | solution.py:28
  148.5 7.1 %collective-permute-start.19 = (f32[2,2,6,512]{3,2,1,0:T(8,128)}, f32[2,2,6,512]{3,2,1,0:T(8,128)S(1)}, u32[]{:S(2)}, u32[]{:S(2)}) collective-permute-start(f32[2,2,6,512]{3,2,1,0:T(8,128)} %bitcast.97), channel_id=1, source_target_pairs={{4,0},{8,4},{12,8},{5,1},{9,5},{13,9},{6,2},{10,6},{14,10},{7,3},{... | collective-permute-start | bytes 147464 | tf_op jit(solution)/shard_map/ppermute | solution.py:28
  155.6 6.2 %collective-permute-start.22 = (f32[2,2,6,512]{3,2,1,0:T(8,128)S(1)}, f32[2,2,6,512]{3,2,1,0:T(8,128)S(1)}, u32[]{:S(2)}, u32[]{:S(2)}) collective-permute-start(f32[2,2,6,512]{3,2,1,0:T(8,128)S(1)} %copy_add_fusion.3), channel_id=1, source_target_pairs={{4,0},{8,4},{12,8},{5,1},{9,5},{13,9},{6,2},{10,6},{14,10},{7,3},{... | collective-permute-start | bytes 147464 | tf_op jit(solution)/shard_map/ppermute | solution.py:28
  166.3 1.3 copy-start.12
  167.9 4.2 %collective-permute-start.23 = (f32[8,3,512]{2,0,1:T(8,128)S(1)}, f32[8,3,512]{2,0,1:T(8,128)S(1)}, u32[]{:S(2)}, u32[]{:S(2)}) collective-permute-start(f32[8,3,512]{2,0,1:T(8,128)S(1)} %bitcast.95), channel_id=1, source_target_pairs={{0,16},{16,0},{1,17},{17,1},{2,18},{18,2},{3,19},{19,3},{4,20},{20... | collective-permute-start | bytes 147464 | tf_op jit(solution)/shard_map/ppermute | solution.py:319

commit v11 on v9

--- a/solution.py
+++ b/solution.py
@@ -279,7 +279,7 @@
     reverse_matrix = response
     upper_products = shifted_operators(matrix, 1)
     lower_behind = from_behind(reverse_matrix, "gx", -1)
-    psi = psi_old
+    psi, _, _ = lax.optimization_barrier((psi_old, matrix, reverse_matrix))
     for step in range(ITERS):
         stream_pad = extended(psi, (("gx", 0),), 1)
         span_pad = extended(psi, (("gy", 3),), NZ)

time: 162 us -> 173 us (1.068)
  waiting for transfers between devices: 31.6 us -> 47.4 us
  local copies, waits for them, and re-layouts: 19.9 us -> 17 us
  starting transfers between devices: 53.8 us -> 51.7 us
    ppermute x15, waiting for transfers between devices: 29.1 us -> 45 us  [from_behind(): lax.ppermute(value, axis, [(source, source + steps) for source in range(f...]
    ppermute x15, starting transfers between devices: 30.7 us -> 28.5 us  [from_behind(): lax.ppermute(value, axis, [(source, source + steps) for source in range(f...]
    unnamed x32 -> x39, local copies, waits for them, and re-layouts: 6.38 us -> 7.48 us
  transfers between devices with their start and end apart: 24 -> 24, of which waited for: 6 -> 7; matrix products, arithmetic and copies ran while one was open for 15% -> 8% of each run, Pallas kernels for 14% -> 4%
where the time goes in v11:
time: 173 us; the launch traced here: 172 us
  starting transfers between devices  51.7 us (30%)
  waiting for transfers between devices  47.4 us (27%)
  Pallas kernels  37.8 us (22%)
  local copies, waits for them, and re-layouts  17 us (10%)
  other arithmetic  13.9 us (8%)
  matrix products  2.56 us (1%)
    ppermute x15, waiting for transfers between devices, from_behind(): lax.ppermute(value, axis, [(source, source + steps) for source in range(f...  45 us
    ppermute x15, starting transfers between devices, from_behind(): lax.ppermute(value, axis, [(source, source + steps) for source in range(f...  28.5 us
    ppermute x4, starting transfers between devices, extended(): before = lax.ppermute(last, axis, up)  16.4 us
    pallas_call x3, Pallas kernels, lower_pallas(): pl.pallas_call(kernel, out_shape=tuple(out_shape), in_specs=_vmem_specs(l...  15.5 us
    pallas_call x3, Pallas kernels, upper_pallas(): pl.pallas_call(kernel, out_shape=tuple(out_shape), in_specs=_vmem_specs(l...  12.7 us
    pallas_call x2, Pallas kernels, upper_then_lower(): pl.pallas_call(kernel, out_shape=(jax.ShapeDtypeStruct(rhs.shape, jnp.flo...  9.54 us
    unnamed x39, local copies, waits for them, and re-layouts  7.48 us
    reduce_sum x8, other arithmetic, carry_through(): return jnp.sum(jnp.sum(split * inputs, axis=2), axis=1)  6.33 us
  transfers between devices with their start and end apart: 24, of which 7 were waited for; matrix products, arithmetic and copies ran while one was open for 8% of the time, Pallas kernels for 4%

profile of v11, /device:TPU:0, one launch (start us, length us, event | category | flops | bytes accessed | tf_op | source)
XLA Modules:
  0.0 171.7 jit_solution(17901884568048086734)
XLA Ops:
  0.7 2.8 %copy.199.refs_0_.d_ref.refs_1_ = f32[8,2,6,6,512]{4,3,2,1,0:T(8,128)} copy(f32[8,2,6,6,512]{4,1,3,2,0:T(2,128)} %param.17) | data formatting | bytes 2359296 | tf_op args[4]
  3.5 1.4 copy.200.refs_1_.b_ref.refs_2_
  4.9 1.4 copy.201.refs_2_.a_ref.refs_3_
  6.3 0.8 copy-done.7
  7.1 2.4 %copy_bitcast_fusion = (f32[8,2,6,6,512]{4,3,2,1,0:T(8,128)}, f32[8,2,6,6,512]{4,3,2,1,0:T(8,128)}) fusion(f32[8,2,6,6,512]{4,1,3,2,0:T(2,128)S(1)} %copy-done.6, f32[8,2,6,6,512]{4,1,3,2,0:T(2,128)S(1)} %copy-done.7), kind=kLoop, calls=%fused_computation | loop fusion | bytes 4718592 | tf_op jit(solution)/shard_map/transpose | solution.py:275
  9.5 6.9 %shard_map.140 = f32[2,12,2,6,512]{4,3,2,1,0:T(8,128)} custom-call(f32[8,2,6,6,512]{4,3,2,1,0:T(8,128)} %get-tuple-element.37.refs_0_.refs_1_.nt_ref, f32[8,2,6,6,512]{4,3,2,1,0:T(8,128)} %get-tuple-element.36.refs_1_.refs_2_.ft_ref), custom_call_target="tpu_custom_call" | custom-call | tf_op jit(solution)/shard_map/pallas_call | solution.py:116
  16.4 8.3 %shard_map.141 = f32[2,12,2,6,512]{4,3,2,1,0:T(8,128)} custom-call(f32[8,2,6,6,512]{4,3,2,1,0:T(8,128)} %copy.199.refs_0_.d_ref.refs_1_, f32[8,2,6,6,512]{4,3,2,1,0:T(8,128)} %copy.200.refs_1_.b_ref.refs_2_, f32[8,2,6,6,512]{4,3,2,1,0:T(8,128)} %copy.201.refs_2_.a_ref.refs_3_), custom_call_target="tpu_custom_call" | custom-call | tf_op jit(solution)/shard_map/pallas_call | solution.py:180
  24.8 1.4 collective-permute-start
  26.2 5.6 %collective-permute-start.1 = (f32[1,2,6,512]{3,2,1,0:T(8,128)S(1)}, f32[1,2,6,512]{3,2,1,0:T(8,128)S(1)}, u32[]{:S(2)}, u32[]{:S(2)}) collective-permute-start(f32[1,2,6,512]{3,2,1,0:T(8,128)S(1)} %get-tuple-element.33), channel_id=1, source_target_pairs={{0,4},{4,8},{8,12},{1,5},{5,9},{9,13},{2,6},{6,10},{10,14},{3,7},{... | collective-permute-start | bytes 73736 | tf_op jit(solution)/shard_map/ppermute | solution.py:19
  31.9 1.3 collective-permute-start.2
  33.2 3.0 %collective-permute-start.3 = (f32[8,2,6,32]{3,2,1,0:T(8,128)S(1)}, f32[8,2,6,32]{3,2,1,0:T(8,128)S(1)}, u32[]{:S(2)}, u32[]{:S(2)}) collective-permute-start(f32[8,2,6,32]{3,2,1,0:T(8,128)S(1)} %get-tuple-element.35), channel_id=1, source_target_pairs={{0,1},{1,2},{2,3},{4,5},{5,6},{6,7},{8,9},{9,10},{10,11},{12,13},{... | collective-permute-start | bytes 36872 | tf_op jit(solution)/shard_map/ppermute | solution.py:19
  36.2 1.3 copy.214
  37.5 5.7 %collective-permute-start.5 = (f32[2,12,2,6,512]{4,2,3,1,0:T(2,128)}, f32[2,12,2,6,512]{4,2,3,1,0:T(2,128)}, u32[]{:S(2)}, u32[]{:S(2)}) collective-permute-start(f32[2,12,2,6,512]{4,2,3,1,0:T(2,128)} %copy.214), channel_id=1, source_target_pairs={{0,8},{4,12},{1,9},{5,13},{2,10},{6,14},{3,11},{7,15},{16,24},{20,... | collective-permute-start | bytes 1769480 | tf_op jit(solution)/shard_map/ppermute | solution.py:28
  43.2 2.2 %collective-permute-start.4 = (f32[2,12,2,6,512]{4,2,3,1,0:T(2,128)}, f32[2,12,2,6,512]{4,2,3,1,0:T(2,128)}, u32[]{:S(2)}, u32[]{:S(2)}) collective-permute-start(f32[2,12,2,6,512]{4,2,3,1,0:T(2,128)} %copy.214), channel_id=1, source_target_pairs={{0,4},{4,8},{8,12},{1,5},{5,9},{9,13},{2,6},{6,10},{10,14},{3,7},{... | collective-permute-start | bytes 1769480 | tf_op jit(solution)/shard_map/ppermute | solution.py:28
  46.0 0.8 convolution_bitcast_fusion.1
  47.9 0.8 copy.221.refs_0_.rhs_ref
  48.7 0.6 broadcast_in_dim.10.refs_3_
  49.3 2.9 %shard_map.142 = f32[2,1,2,6,512]{4,3,2,1,0:T(8,128)} custom-call(f32[8,2,6,512]{3,2,1,0:T(8,128)} %copy.221.refs_0_.rhs_ref, f32[8,2,6,6,512]{4,3,2,1,0:T(8,128)} %get-tuple-element.37.refs_0_.refs_1_.nt_ref, f32[8,2,6,6,512]{4,3,2,1,0:T(8,128)} %get-tuple-element.36.refs_1_.refs_2_.ft_ref, f32[2,1,2,6,512]{4,3,2,1,0:T(8,128)} %broadcast_in_dim.10.refs_3_), custom_call_target="tpu_custom_call" | custom-call | tf_op jit(solution)/shard_map/pallas_call | solution.py:116
  52.2 1.4 collective-permute-start.6
  54.1 1.3 collective-permute-start.10
  55.5 2.5 %collective-permute-start.7 = (f32[2,2,6,512]{3,2,1,0:T(8,128)S(1)}, f32[2,2,6,512]{3,2,1,0:T(8,128)S(1)}, u32[]{:S(2)}, u32[]{:S(2)}) collective-permute-start(f32[2,2,6,512]{3,2,1,0:T(8,128)S(1)} %bitcast.81), channel_id=1, source_target_pairs={{0,8},{4,12},{1,9},{5,13},{2,10},{6,14},{3,11},{7,15},{16,24},{20,... | collective-permute-start | bytes 147464 | tf_op jit(solution)/shard_map/ppermute | solution.py:28
  58.0 12.4 %collective-permute-done.6 = f32[2,2,6,512]{3,2,1,0:T(8,128)S(1)} collective-permute-done((f32[2,2,6,512]{3,2,1,0:T(8,128)}, f32[2,2,6,512]{3,2,1,0:T(8,128)S(1)}, u32[]{:S(2)}, u32[]{:S(2)}) %collective-permute-start.6) | collective-permute-done | bytes 49184 | tf_op jit(solution)/shard_map/ppermute | solution.py:28
  70.4 1.3 collective-permute-start.8
  71.7 1.3 multiply_reduce_fusion.10
  73.2 1.3 multiply_reduce_fusion.9
  74.5 0.6 fusion.16.inc_ref
  75.2 4.8 %shard_map.143 = (f32[8,2,6,512]{3,2,1,0:T(8,128)}, f32[2,1,2,6,512]{4,3,2,1,0:T(8,128)}) custom-call(f32[8,2,6,512]{3,2,1,0:T(8,128)} %copy.221.refs_0_.rhs_ref, f32[8,2,6,6,512]{4,3,2,1,0:T(8,128)} %get-tuple-element.37.refs_0_.refs_1_.nt_ref, f32[8,2,6,6,512]{4,3,2,1,0:T(8,128)} %get-tuple-element.36.refs_1_.refs_2_.ft_ref, ...), custom_call_target="tpu_custom_call" | custom-call | tf_op jit(solution)/shard_map/pallas_call | solution.py:210
  79.9 1.3 collective-permute-start.11
  81.2 1.3 collective-permute-start.9
  82.5 16.7 %collective-permute-done.11 = f32[2,2,6,512]{3,2,1,0:T(8,128)S(1)} collective-permute-done((f32[2,2,6,512]{3,2,1,0:T(8,128)}, f32[2,2,6,512]{3,2,1,0:T(8,128)S(1)}, u32[]{:S(2)}, u32[]{:S(2)}) %collective-permute-start.11) | collective-permute-done | bytes 49184 | tf_op jit(solution)/shard_map/ppermute | solution.py:28
  99.5 1.3 collective-permute-start.12
  100.8 4.8 %collective-permute-done.12 = f32[2,2,6,512]{3,2,1,0:T(8,128)S(1)} collective-permute-done((f32[2,2,6,512]{3,2,1,0:T(8,128)S(1)}, f32[2,2,6,512]{3,2,1,0:T(8,128)S(1)}, u32[]{:S(2)}, u32[]{:S(2)}) %collective-permute-start.12) | collective-permute-done | bytes 49184 | tf_op jit(solution)/shard_map/ppermute | solution.py:28
  106.0 0.6 fusion.15.refs_4_
  106.6 3.6 %shard_map.144 = (f32[8,2,6,512]{3,2,1,0:T(8,128)}, f32[2,1,2,6,512]{4,3,2,1,0:T(8,128)}) custom-call(f32[8,2,6,512]{3,2,1,0:T(8,128)} %get-tuple-element.10.refs_0_, f32[8,2,6,6,512]{4,3,2,1,0:T(8,128)} %copy.199.refs_0_.d_ref.refs_1_, f32[8,2,6,6,512]{4,3,2,1,0:T(8,128)} %copy.200.refs_1_.b_ref.refs_2_, f32[8,2,6,6,512]{4,3,2,1,0:T(8,128)} %copy.201.refs_2_.a_ref.refs_3_, ...), custom_call_target="tpu_custom_call" | custom-call | tf_op jit(solution)/shard_map/pallas_call | solution.py:180
  110.3 1.1 add_multiply_fusion.1
  111.3 1.3 collective-permute-start.13
  112.6 4.5 %collective-permute-start.14 = (f32[1,2,6,512]{3,2,1,0:T(8,128)S(1)}, f32[1,2,6,512]{3,2,1,0:T(8,128)S(1)}, u32[]{:S(2)}, u32[]{:S(2)}) collective-permute-start(f32[1,2,6,512]{3,2,1,0:T(8,128)S(1)} %get-tuple-element.29), channel_id=1, source_target_pairs={{0,4},{4,8},{8,12},{1,5},{5,9},{9,13},{2,6},{6,10},{10,14},{3,7},{... | collective-permute-start | bytes 73736 | tf_op jit(solution)/shard_map/ppermute | solution.py:19
  117.3 1.3 collective-permute-start.15
  118.6 3.2 %collective-permute-start.16 = (f32[8,2,6,32]{3,2,1,0:T(8,128)S(1)}, f32[8,2,6,32]{3,2,1,0:T(8,128)S(1)}, u32[]{:S(2)}, u32[]{:S(2)}) collective-permute-start(f32[8,2,6,32]{3,2,1,0:T(8,128)S(1)} %get-tuple-element.31), channel_id=1, source_target_pairs={{0,1},{1,2},{2,3},{4,5},{5,6},{6,7},{8,9},{9,10},{10,11},{12,13},{... | collective-permute-start | bytes 36872 | tf_op jit(solution)/shard_map/ppermute | solution.py:19
  121.8 0.7 collective-permute-done.16
  123.1 1.8 %convolution_bitcast_fusion = f32[8,2,6,16,32]{4,3,0,2,1:T(8,128)} fusion(f32[8,2,6,16,32]{4,3,0,2,1:T(8,128)S(1)} %reshape.49, f32[2,6,32,32]{3,2,1,0:T(8,128)S(1)} %copy-done), kind=kOutput, calls=%fused_computation.2 | convolution fusion | flops 18874368 | bytes 442368 | tf_op jit(solution)/shard_map/icvjq,cvqk->icvjk/dot_general | solution.py:291
  124.9 1.4 mul.178
  126.4 0.6 multiply_reduce_fusion
  127.0 0.8 copy.242.refs_0_.rhs_ref
  127.8 2.9 %shard_map.145 = f32[2,1,2,6,512]{4,3,2,1,0:T(8,128)} custom-call(f32[8,2,6,512]{3,2,1,0:T(8,128)} %copy.242.refs_0_.rhs_ref, f32[8,2,6,6,512]{4,3,2,1,0:T(8,128)} %get-tuple-element.37.refs_0_.refs_1_.nt_ref, f32[8,2,6,6,512]{4,3,2,1,0:T(8,128)} %get-tuple-element.36.refs_1_.refs_2_.ft_ref, f32[2,1,2,6,512]{4,3,2,1,0:T(8,128)} %broadcast_in_dim.10.refs_3_), custom_call_target="tpu_custom_call" | custom-call | tf_op jit(solution)/shard_map/pallas_call | solution.py:116
  130.7 2.6 %collective-permute-start.17 = (f32[2,2,6,512]{3,2,1,0:T(8,128)}, f32[2,2,6,512]{3,2,1,0:T(8,128)S(1)}, u32[]{:S(2)}, u32[]{:S(2)}) collective-permute-start(f32[2,2,6,512]{3,2,1,0:T(8,128)} %bitcast.83), channel_id=1, source_target_pairs={{0,12},{1,13},{2,14},{3,15},{16,28},{17,29},{18,30},{19,31}} | collective-permute-start | bytes 147464 | tf_op jit(solution)/shard_map/ppermute | solution.py:28
  133.3 1.8 %collective-permute-start.18 = (f32[2,2,6,512]{3,2,1,0:T(8,128)}, f32[2,2,6,512]{3,2,1,0:T(8,128)S(1)}, u32[]{:S(2)}, u32[]{:S(2)}) collective-permute-start(f32[2,2,6,512]{3,2,1,0:T(8,128)} %bitcast.84), channel_id=1, source_target_pairs={{0,8},{4,12},{1,9},{5,13},{2,10},{6,14},{3,11},{7,15},{16,24},{20,... | collective-permute-start | bytes 147464 | tf_op jit(solution)/shard_map/ppermute | solution.py:28
  135.2 1.9 %collective-permute-start.19 = (f32[2,2,6,512]{3,2,1,0:T(8,128)}, f32[2,2,6,512]{3,2,1,0:T(8,128)S(1)}, u32[]{:S(2)}, u32[]{:S(2)}) collective-permute-start(f32[2,2,6,512]{3,2,1,0:T(8,128)} %bitcast.85), channel_id=1, source_target_pairs={{0,4},{4,8},{8,12},{1,5},{5,9},{9,13},{2,6},{6,10},{10,14},{3,7},{... | collective-permute-start | bytes 147464 | tf_op jit(solution)/shard_map/ppermute | solution.py:28
  137.1 1.3 multiply_reduce_fusion.6
  138.6 1.3 multiply_reduce_fusion.5
  139.9 0.6 fusion.13.inc_ref
  140.6 4.8 %shard_map.146 = (f32[8,2,6,512]{3,2,1,0:T(8,128)}, f32[2,1,2,6,512]{4,3,2,1,0:T(8,128)}) custom-call(f32[8,2,6,512]{3,2,1,0:T(8,128)} %copy.242.refs_0_.rhs_ref, f32[8,2,6,6,512]{4,3,2,1,0:T(8,128)} %get-tuple-element.37.refs_0_.refs_1_.nt_ref, f32[8,2,6,6,512]{4,3,2,1,0:T(8,128)} %get-tuple-element.36.refs_1_.refs_2_.ft_ref, ...), custom_call_target="tpu_custom_call" | custom-call | tf_op jit(solution)/shard_map/pallas_call | solution.py:210
  145.3 1.3 collective-permute-start.21
  146.6 1.3 collective-permute-start.20
  147.9 6.3 %collective-permute-done.21 = f32[2,2,6,512]{3,2,1,0:T(8,128)S(1)} collective-permute-done((f32[2,2,6,512]{3,2,1,0:T(8,128)}, f32[2,2,6,512]{3,2,1,0:T(8,128)S(1)}, u32[]{:S(2)}, u32[]{:S(2)}) %collective-permute-start.21) | collective-permute-done | bytes 49184 | tf_op jit(solution)/shard_map/ppermute | solution.py:28
  154.6 1.3 collective-permute-start.22
  156.1 4.7 %collective-permute-done.22 = f32[2,2,6,512]{3,2,1,0:T(8,128)S(1)} collective-permute-done((f32[2,2,6,512]{3,2,1,0:T(8,128)S(1)}, f32[2,2,6,512]{3,2,1,0:T(8,128)S(1)}, u32[]{:S(2)}, u32[]{:S(2)}) %collective-permute-start.22) | collective-permute-done | bytes 49184 | tf_op jit(solution)/shard_map/ppermute | solution.py:28
  161.0 0.6 fusion.12.refs_4_
  161.7 3.6 %shard_map.147 = (f32[8,2,6,512]{3,2,1,0:T(8,128)}, f32[2,1,2,6,512]{4,3,2,1,0:T(8,128)}) custom-call(f32[8,2,6,512]{3,2,1,0:T(8,128)} %get-tuple-element.13.refs_0_, f32[8,2,6,6,512]{4,3,2,1,0:T(8,128)} %copy.199.refs_0_.d_ref.refs_1_, f32[8,2,6,6,512]{4,3,2,1,0:T(8,128)} %copy.200.refs_1_.b_ref.refs_2_, f32[8,2,6,6,512]{4,3,2,1,0:T(8,128)} %copy.201.refs_2_.a_ref.refs_3_, ...), custom_call_target="tpu_custom_call" | custom-call | tf_op jit(solution)/shard_map/pallas_call | solution.py:180
  165.3 1.1 multiply_bitcast_fusion
  166.9 1.6 collective-permute-start.23
  168.4 0.8 copy.253
  169.3 1.8 %collective-permute-done.23 = f32[8,3,512]{2,0,1:T(8,128)S(1)} collective-permute-done((f32[8,3,512]{2,0,1:T(8,128)S(1)}, f32[8,3,512]{2,0,1:T(8,128)S(1)}, u32[]{:S(2)}, u32[]{:S(2)}) %collective-permute-start.23) | collective-permute-done | bytes 49184 | tf_op jit(solution)/shard_map/ppermute | solution.py:312
  171.0 0.6 fusion.25
  (87 shorter events, 5.2 us)
Async XLA Ops:
  0.6 45.4 %copy-start = (f32[2,6,32,32]{3,2,1,0:T(8,128)S(1)}, f32[2,6,32,32]{3,2,1,0:T(8,128)}, u32[]{:S(2)}) copy-start(f32[2,6,32,32]{3,2,1,0:T(8,128)} %param.21) | copy-start | bytes 147460
  0.6 2.8 %copy-start.4 = (f32[8,2,6,6,512]{4,1,3,2,0:T(2,128)S(1)}, f32[8,2,6,6,512]{4,1,3,2,0:T(2,128)}, u32[]{:S(2)}) copy-start(f32[8,2,6,6,512]{4,1,3,2,0:T(2,128)} %param.18) | copy-start | bytes 3538948
  3.5 1.4 copy-start.5
  4.9 1.4 copy-start.6
  4.9 2.2 %copy-start.7 = (f32[8,2,6,6,512]{4,1,3,2,0:T(2,128)S(1)}, f32[8,2,6,6,512]{4,1,3,2,0:T(2,128)}, u32[]{:S(2)}) copy-start(f32[8,2,6,6,512]{4,1,3,2,0:T(2,128)} %param.15) | copy-start | bytes 3538948
  16.4 8.3 %copy-start.10 = (f32[8,2,6,512]{3,1,2,0:T(2,128)S(1)}, f32[8,2,6,512]{3,1,2,0:T(2,128)}, u32[]{:S(2)}) copy-start(f32[8,2,6,512]{3,1,2,0:T(2,128)} %param.13) | copy-start | bytes 589828
  24.7 11.5 %copy-start.3 = (f32[2,12,2,6,512]{4,3,2,1,0:T(8,128)S(1)}, f32[2,12,2,6,512]{4,3,2,1,0:T(8,128)}, u32[]{:S(2)}) copy-start(f32[2,12,2,6,512]{4,3,2,1,0:T(8,128)} %shard_map.140) | copy-start | bytes 1769476
  24.7 20.7 %copy-start.8 = (f32[8,2,6,512]{3,1,2,0:T(2,128)S(1)}, f32[8,2,6,512]{3,1,2,0:T(2,128)}, u32[]{:S(2)}) copy-start(f32[8,2,6,512]{3,1,2,0:T(2,128)} %param.14) | copy-start | bytes 589828
  24.8 20.7 %collective-permute-start = (f32[1,2,6,512]{3,2,1,0:T(8,128)S(1)}, f32[1,2,6,512]{3,2,1,0:T(8,128)S(1)}, u32[]{:S(2)}, u32[]{:S(2)}) collective-permute-start(f32[1,2,6,512]{3,2,1,0:T(8,128)S(1)} %get-tuple-element.32), channel_id=1, source_target_pairs={{4,0},{8,4},{12,8},{5,1},{9,5},{13,9},{6,2},{10,6},{14,10},{7,3},{... | collective-permute-start | bytes 73736 | tf_op jit(solution)/shard_map/ppermute | solution.py:20
  26.2 19.2 %collective-permute-start.1 = (f32[1,2,6,512]{3,2,1,0:T(8,128)S(1)}, f32[1,2,6,512]{3,2,1,0:T(8,128)S(1)}, u32[]{:S(2)}, u32[]{:S(2)}) collective-permute-start(f32[1,2,6,512]{3,2,1,0:T(8,128)S(1)} %get-tuple-element.33), channel_id=1, source_target_pairs={{0,4},{4,8},{8,12},{1,5},{5,9},{9,13},{2,6},{6,10},{10,14},{3,7},{... | collective-permute-start | bytes 73736 | tf_op jit(solution)/shard_map/ppermute | solution.py:19
  31.9 11.4 %collective-permute-start.2 = (f32[8,2,6,32]{3,2,1,0:T(8,128)S(1)}, f32[8,2,6,32]{3,2,1,0:T(8,128)S(1)}, u32[]{:S(2)}, u32[]{:S(2)}) collective-permute-start(f32[8,2,6,32]{3,2,1,0:T(8,128)S(1)} %get-tuple-element.34), channel_id=1, source_target_pairs={{1,0},{2,1},{3,2},{5,4},{6,5},{7,6},{9,8},{10,9},{11,10},{13,12},{... | collective-permute-start | bytes 36872 | tf_op jit(solution)/shard_map/ppermute | solution.py:20
  33.2 12.2 %collective-permute-start.3 = (f32[8,2,6,32]{3,2,1,0:T(8,128)S(1)}, f32[8,2,6,32]{3,2,1,0:T(8,128)S(1)}, u32[]{:S(2)}, u32[]{:S(2)}) collective-permute-start(f32[8,2,6,32]{3,2,1,0:T(8,128)S(1)} %get-tuple-element.35), channel_id=1, source_target_pairs={{0,1},{1,2},{2,3},{4,5},{5,6},{6,7},{8,9},{9,10},{10,11},{12,13},{... | collective-permute-start | bytes 36872 | tf_op jit(solution)/shard_map/ppermute | solution.py:19
  37.5 34.2 %collective-permute-start.5 = (f32[2,12,2,6,512]{4,2,3,1,0:T(2,128)}, f32[2,12,2,6,512]{4,2,3,1,0:T(2,128)}, u32[]{:S(2)}, u32[]{:S(2)}) collective-permute-start(f32[2,12,2,6,512]{4,2,3,1,0:T(2,128)} %copy.214), channel_id=1, source_target_pairs={{0,8},{4,12},{1,9},{5,13},{2,10},{6,14},{3,11},{7,15},{16,24},{20,... | collective-permute-start | bytes 1769480 | tf_op jit(solution)/shard_map/ppermute | solution.py:28
  43.2 29.9 %collective-permute-start.4 = (f32[2,12,2,6,512]{4,2,3,1,0:T(2,128)}, f32[2,12,2,6,512]{4,2,3,1,0:T(2,128)}, u32[]{:S(2)}, u32[]{:S(2)}) collective-permute-start(f32[2,12,2,6,512]{4,2,3,1,0:T(2,128)} %copy.214), channel_id=1, source_target_pairs={{0,4},{4,8},{8,12},{1,5},{5,9},{9,13},{2,6},{6,10},{10,14},{3,7},{... | collective-permute-start | bytes 1769480 | tf_op jit(solution)/shard_map/ppermute | solution.py:28
  46.0 1.3 copy-start.1
  49.3 4.4 %copy-start.2 = (f32[2,12,2,6,512]{4,3,2,1,0:T(8,128)S(1)}, f32[2,12,2,6,512]{4,3,2,1,0:T(8,128)}, u32[]{:S(2)}) copy-start(f32[2,12,2,6,512]{4,3,2,1,0:T(8,128)} %shard_map.141) | copy-start | bytes 1769476
  52.2 3.2 %copy-start.13 = (f32[2,1,2,6,512]{4,3,2,1,0:T(8,128)S(1)}, f32[2,1,2,6,512]{4,3,2,1,0:T(8,128)}, u32[]{:S(2)}) copy-start(f32[2,1,2,6,512]{4,3,2,1,0:T(8,128)} %shard_map.142) | copy-start | bytes 147460
  52.2 18.2 %collective-permute-start.6 = (f32[2,2,6,512]{3,2,1,0:T(8,128)}, f32[2,2,6,512]{3,2,1,0:T(8,128)S(1)}, u32[]{:S(2)}, u32[]{:S(2)}) collective-permute-start(f32[2,2,6,512]{3,2,1,0:T(8,128)} %bitcast.80), channel_id=1, source_target_pairs={{0,12},{1,13},{2,14},{3,15},{16,28},{17,29},{18,30},{19,31}} | collective-permute-start | bytes 147464 | tf_op jit(solution)/shard_map/ppermute | solution.py:28
  54.1 45.1 %collective-permute-start.10 = (f32[2,12,2,6,512]{4,2,3,1,0:T(2,128)S(1)}, f32[2,12,2,6,512]{4,2,3,1,0:T(2,128)S(1)}, u32[]{:S(2)}, u32[]{:S(2)}) collective-permute-start(f32[2,12,2,6,512]{4,2,3,1,0:T(2,128)S(1)} %copy.225), channel_id=1, source_target_pairs={{4,0},{8,4},{12,8},{5,1},{9,5},{13,9},{6,2},{10,6},{14,10},{7,3},{... | collective-permute-start | bytes 1769480 | tf_op jit(solution)/shard_map/ppermute | solution.py:28
  55.5 17.6 %collective-permute-start.7 = (f32[2,2,6,512]{3,2,1,0:T(8,128)S(1)}, f32[2,2,6,512]{3,2,1,0:T(8,128)S(1)}, u32[]{:S(2)}, u32[]{:S(2)}) collective-permute-start(f32[2,2,6,512]{3,2,1,0:T(8,128)S(1)} %bitcast.81), channel_id=1, source_target_pairs={{0,8},{4,12},{1,9},{5,13},{2,10},{6,14},{3,11},{7,15},{16,24},{20,... | collective-permute-start | bytes 147464 | tf_op jit(solution)/shard_map/ppermute | solution.py:28
  70.4 4.1 %collective-permute-start.8 = (f32[2,2,6,512]{3,2,1,0:T(8,128)S(1)}, f32[2,2,6,512]{3,2,1,0:T(8,128)S(1)}, u32[]{:S(2)}, u32[]{:S(2)}) collective-permute-start(f32[2,2,6,512]{3,2,1,0:T(8,128)S(1)} %bitcast.82), channel_id=1, source_target_pairs={{0,4},{4,8},{8,12},{1,5},{5,9},{9,13},{2,6},{6,10},{10,14},{3,7},{... | collective-permute-start | bytes 147464 | tf_op jit(solution)/shard_map/ppermute | solution.py:28
  75.2 25.7 %copy-start.14 = (s32[8,512]{1,0:T(8,128)S(1)}, s32[8,512]{1,0:T(8,128)}, u32[]{:S(2)}) copy-start(s32[8,512]{1,0:T(8,128)} %param.23) | copy-start | bytes 49156
  79.9 19.3 %collective-permute-start.11 = (f32[2,2,6,512]{3,2,1,0:T(8,128)}, f32[2,2,6,512]{3,2,1,0:T(8,128)S(1)}, u32[]{:S(2)}, u32[]{:S(2)}) collective-permute-start(f32[2,2,6,512]{3,2,1,0:T(8,128)} %bitcast.93), channel_id=1, source_target_pairs={{8,0},{12,4},{9,1},{13,5},{10,2},{14,6},{11,3},{15,7},{24,16},{28,... | collective-permute-start | bytes 147464 | tf_op jit(solution)/shard_map/ppermute | solution.py:28
  81.2 18.3 %collective-permute-start.9 = (f32[2,2,6,512]{3,2,1,0:T(8,128)}, f32[2,2,6,512]{3,2,1,0:T(8,128)S(1)}, u32[]{:S(2)}, u32[]{:S(2)}) collective-permute-start(f32[2,2,6,512]{3,2,1,0:T(8,128)} %bitcast.94), channel_id=1, source_target_pairs={{4,0},{8,4},{12,8},{5,1},{9,5},{13,9},{6,2},{10,6},{14,10},{7,3},{... | collective-permute-start | bytes 147464 | tf_op jit(solution)/shard_map/ppermute | solution.py:28
  99.5 6.2 %collective-permute-start.12 = (f32[2,2,6,512]{3,2,1,0:T(8,128)S(1)}, f32[2,2,6,512]{3,2,1,0:T(8,128)S(1)}, u32[]{:S(2)}, u32[]{:S(2)}) collective-permute-start(f32[2,2,6,512]{3,2,1,0:T(8,128)S(1)} %copy_add_fusion.7), channel_id=1, source_target_pairs={{4,0},{8,4},{12,8},{5,1},{9,5},{13,9},{6,2},{10,6},{14,10},{7,3},{... | collective-permute-start | bytes 147464 | tf_op jit(solution)/shard_map/ppermute | solution.py:28
  106.6 3.6 %copy-start.11 = (f32[8,2,6,512]{3,1,2,0:T(2,128)S(1)}, f32[8,2,6,512]{3,1,2,0:T(2,128)}, u32[]{:S(2)}) copy-start(f32[8,2,6,512]{3,1,2,0:T(2,128)} %param.13) | copy-start | bytes 589828
  110.3 12.3 %copy-start.9 = (f32[8,2,6,512]{3,1,2,0:T(2,128)S(1)}, f32[8,2,6,512]{3,1,2,0:T(2,128)}, u32[]{:S(2)}) copy-start(f32[8,2,6,512]{3,1,2,0:T(2,128)} %param.14) | copy-start | bytes 589828
  111.3 11.2 %collective-permute-start.13 = (f32[1,2,6,512]{3,2,1,0:T(8,128)S(1)}, f32[1,2,6,512]{3,2,1,0:T(8,128)S(1)}, u32[]{:S(2)}, u32[]{:S(2)}) collective-permute-start(f32[1,2,6,512]{3,2,1,0:T(8,128)S(1)} %get-tuple-element.28), channel_id=1, source_target_pairs={{4,0},{8,4},{12,8},{5,1},{9,5},{13,9},{6,2},{10,6},{14,10},{7,3},{... | collective-permute-start | bytes 73736 | tf_op jit(solution)/shard_map/ppermute | solution.py:20
  112.6 9.9 %collective-permute-start.14 = (f32[1,2,6,512]{3,2,1,0:T(8,128)S(1)}, f32[1,2,6,512]{3,2,1,0:T(8,128)S(1)}, u32[]{:S(2)}, u32[]{:S(2)}) collective-permute-start(f32[1,2,6,512]{3,2,1,0:T(8,128)S(1)} %get-tuple-element.29), channel_id=1, source_target_pairs={{0,4},{4,8},{8,12},{1,5},{5,9},{9,13},{2,6},{6,10},{10,14},{3,7},{... | collective-permute-start | bytes 73736 | tf_op jit(solution)/shard_map/ppermute | solution.py:19
  117.3 4.5 %collective-permute-start.15 = (f32[8,2,6,32]{3,2,1,0:T(8,128)S(1)}, f32[8,2,6,32]{3,2,1,0:T(8,128)S(1)}, u32[]{:S(2)}, u32[]{:S(2)}) collective-permute-start(f32[8,2,6,32]{3,2,1,0:T(8,128)S(1)} %get-tuple-element.30), channel_id=1, source_target_pairs={{1,0},{2,1},{3,2},{5,4},{6,5},{7,6},{9,8},{10,9},{11,10},{13,12},{... | collective-permute-start | bytes 36872 | tf_op jit(solution)/shard_map/ppermute | solution.py:20
  118.6 3.9 %collective-permute-start.16 = (f32[8,2,6,32]{3,2,1,0:T(8,128)S(1)}, f32[8,2,6,32]{3,2,1,0:T(8,128)S(1)}, u32[]{:S(2)}, u32[]{:S(2)}) collective-permute-start(f32[8,2,6,32]{3,2,1,0:T(8,128)S(1)} %get-tuple-element.31), channel_id=1, source_target_pairs={{0,1},{1,2},{2,3},{4,5},{5,6},{6,7},{8,9},{9,10},{10,11},{12,13},{... | collective-permute-start | bytes 36872 | tf_op jit(solution)/shard_map/ppermute | solution.py:19
  130.7 6.4 %collective-permute-start.17 = (f32[2,2,6,512]{3,2,1,0:T(8,128)}, f32[2,2,6,512]{3,2,1,0:T(8,128)S(1)}, u32[]{:S(2)}, u32[]{:S(2)}) collective-permute-start(f32[2,2,6,512]{3,2,1,0:T(8,128)} %bitcast.83), channel_id=1, source_target_pairs={{0,12},{1,13},{2,14},{3,15},{16,28},{17,29},{18,30},{19,31}} | collective-permute-start | bytes 147464 | tf_op jit(solution)/shard_map/ppermute | solution.py:28
  133.3 5.2 %collective-permute-start.18 = (f32[2,2,6,512]{3,2,1,0:T(8,128)}, f32[2,2,6,512]{3,2,1,0:T(8,128)S(1)}, u32[]{:S(2)}, u32[]{:S(2)}) collective-permute-start(f32[2,2,6,512]{3,2,1,0:T(8,128)} %bitcast.84), channel_id=1, source_target_pairs={{0,8},{4,12},{1,9},{5,13},{2,10},{6,14},{3,11},{7,15},{16,24},{20,... | collective-permute-start | bytes 147464 | tf_op jit(solution)/shard_map/ppermute | solution.py:28
  135.2 4.7 %collective-permute-start.19 = (f32[2,2,6,512]{3,2,1,0:T(8,128)}, f32[2,2,6,512]{3,2,1,0:T(8,128)S(1)}, u32[]{:S(2)}, u32[]{:S(2)}) collective-permute-start(f32[2,2,6,512]{3,2,1,0:T(8,128)} %bitcast.85), channel_id=1, source_target_pairs={{0,4},{4,8},{8,12},{1,5},{5,9},{9,13},{2,6},{6,10},{10,14},{3,7},{... | collective-permute-start | bytes 147464 | tf_op jit(solution)/shard_map/ppermute | solution.py:28
  140.6 15.3 %copy-start.15 = (f32[8]{0:T(128)S(1)}, f32[8]{0:T(128)}, u32[]{:S(2)}) copy-start(f32[8]{0:T(128)} %param.25) | copy-start | bytes 100
  140.6 15.3 %copy-start.16 = (s32[2]{0:T(128)S(1)}, s32[2]{0:T(128)}, u32[]{:S(2)}) copy-start(s32[2]{0:T(128)} %param.24) | copy-start | bytes 28
  145.3 8.9 %collective-permute-start.21 = (f32[2,2,6,512]{3,2,1,0:T(8,128)}, f32[2,2,6,512]{3,2,1,0:T(8,128)S(1)}, u32[]{:S(2)}, u32[]{:S(2)}) collective-permute-start(f32[2,2,6,512]{3,2,1,0:T(8,128)} %bitcast.95), channel_id=1, source_target_pairs={{8,0},{12,4},{9,1},{13,5},{10,2},{14,6},{11,3},{15,7},{24,16},{28,... | collective-permute-start | bytes 147464 | tf_op jit(solution)/shard_map/ppermute | solution.py:28
  146.6 7.9 %collective-permute-start.20 = (f32[2,2,6,512]{3,2,1,0:T(8,128)}, f32[2,2,6,512]{3,2,1,0:T(8,128)S(1)}, u32[]{:S(2)}, u32[]{:S(2)}) collective-permute-start(f32[2,2,6,512]{3,2,1,0:T(8,128)} %bitcast.96), channel_id=1, source_target_pairs={{4,0},{8,4},{12,8},{5,1},{9,5},{13,9},{6,2},{10,6},{14,10},{7,3},{... | collective-permute-start | bytes 147464 | tf_op jit(solution)/shard_map/ppermute | solution.py:28
  154.6 6.2 %collective-permute-start.22 = (f32[2,2,6,512]{3,2,1,0:T(8,128)S(1)}, f32[2,2,6,512]{3,2,1,0:T(8,128)S(1)}, u32[]{:S(2)}, u32[]{:S(2)}) collective-permute-start(f32[2,2,6,512]{3,2,1,0:T(8,128)S(1)} %copy_add_fusion.3), channel_id=1, source_target_pairs={{4,0},{8,4},{12,8},{5,1},{9,5},{13,9},{6,2},{10,6},{14,10},{7,3},{... | collective-permute-start | bytes 147464 | tf_op jit(solution)/shard_map/ppermute | solution.py:28
  165.3 1.3 copy-start.12
  166.9 4.2 %collective-permute-start.23 = (f32[8,3,512]{2,0,1:T(8,128)S(1)}, f32[8,3,512]{2,0,1:T(8,128)S(1)}, u32[]{:S(2)}, u32[]{:S(2)}) collective-permute-start(f32[8,3,512]{2,0,1:T(8,128)S(1)} %bitcast.92), channel_id=1, source_target_pairs={{0,16},{16,0},{1,17},{17,1},{2,18},{18,2},{3,19},{19,3},{4,20},{20... | collective-permute-start | bytes 147464 | tf_op jit(solution)/shard_map/ppermute | solution.py:312

commit v12 on v9

--- a/solution.py
+++ b/solution.py
@@ -185,6 +185,26 @@
     )(*args)
 
 
+def lower_update(rhs, inverse, near, far, incoming, psi, keep):
+    count, conds = inverse.shape[0], inverse.shape[1]
+
+    def kernel(rhs_ref, d_ref, b_ref, a_ref, inc_ref, psi_ref, keep_ref, out_ref):
+        for c in range(conds):
+            pending, partial_value = inc_ref[0, 0, c], inc_ref[1, 0, c]
+            for i in range(count - 1, -1, -1):
+                now = _rows_times(d_ref, (i, c), rhs_ref[i, c] - pending)
+                pending = partial_value + _rows_times(b_ref, (i, c), now)
+                partial_value = _rows_times(a_ref, (i, c), now)
+                out_ref[i, c] = (psi_ref[i, c] + 0.05 * now) * keep_ref[i : i + 1, :]
+
+    return pl.pallas_call(
+        kernel,
+        out_shape=jax.ShapeDtypeStruct(psi.shape, jnp.float32),
+        in_specs=_vmem_specs(7),
+        out_specs=pl.BlockSpec(memory_space=pltpu.VMEM),
+    )(rhs, inverse, near, far, incoming, psi, keep)
+
+
 def upper_then_lower(rhs, near_t, far_t, incoming, inverse, near, far):
     count, conds = near_t.shape[0], near_t.shape[1]
     carry = jax.ShapeDtypeStruct((2, 1) + rhs.shape[1:], jnp.float32)
@@ -267,7 +287,7 @@
     cond_index,
     weight_table,
 ):
-    keep = (1.0 - wall_mask.astype(jnp.float32))[:, None, None, :]
+    keep_rows = 1.0 - wall_mask.astype(jnp.float32)
     carry_shape = psi_old.shape[1:]
     zeros = jnp.zeros((2, 1) + carry_shape, jnp.float32)
     units = (2, 2 * carry_shape[1]) + carry_shape
@@ -298,8 +318,9 @@
             yres, near_t, far_t, entering[:, None], inverse_diag, near_lower, far_lower
         )
         entering = relayed_carry(offset[:, 0], lower_behind, -1)
-        lower, _ = lower_pallas(upper, inverse_diag, near_lower, far_lower, entering[:, None], True)
-        psi = (psi + 0.05 * lower) * keep
+        psi = lower_update(
+            upper, inverse_diag, near_lower, far_lower, entering[:, None], psi, keep_rows
+        )
     onehot = (cond_index[:, None] == jnp.arange(weight_table.shape[0])[None, :]).astype(jnp.float32)
     weights = jnp.sum(onehot * weight_table[None, :], axis=1)
     local_sens = jnp.einsum(

time: 162 us -> 162 us (level)
    pallas_call x0 -> x2, Pallas kernels: none -> 7.34 us  [lower_update(): pl.pallas_call(kernel, out_shape=jax.ShapeDtypeStruct(psi.shape, jnp.floa...]
    pallas_call x3 -> x1, Pallas kernels: 15.5 us -> 8.28 us  [lower_pallas(): pl.pallas_call(kernel, out_shape=tuple(out_shape), in_specs=_vmem_specs(l...]
    sub x2, other arithmetic: 0.45 us -> 2.1 us  [on_device(): rhs = objective_grad + 0.5 * beside_all - 2.0 * psi]
    slice x4, local copies, waits for them, and re-layouts: 0.18 us -> 1.82 us  [extended(): first = lax.slice_in_dim(value, 0, width, axis=dim)]
    unnamed x32 -> x34, local copies, waits for them, and re-layouts: 6.38 us -> 6.38 us
  transfers between devices with their start and end apart: 24 -> 24, of which waited for: 6 -> 6; matrix products, arithmetic and copies ran while one was open for 15% -> 16% of each run, Pallas kernels for 14% -> 14%
where the time goes in v12:
time: 162 us; the launch traced here: 161 us
  starting transfers between devices  53.7 us (33%)
  Pallas kernels  37.8 us (23%)
  waiting for transfers between devices  31 us (19%)
  local copies, waits for them, and re-layouts  20.4 us (13%)
  other arithmetic  15.1 us (9%)
    ppermute x15, starting transfers between devices, from_behind(): lax.ppermute(value, axis, [(source, source + steps) for source in range(f...  30.7 us
    ppermute x15, waiting for transfers between devices, from_behind(): lax.ppermute(value, axis, [(source, source + steps) for source in range(f...  28.5 us
    ppermute x4, starting transfers between devices, extended(): before = lax.ppermute(last, axis, up)  16.4 us
    pallas_call x3, Pallas kernels, upper_pallas(): pl.pallas_call(kernel, out_shape=tuple(out_shape), in_specs=_vmem_specs(l...  12.7 us
    pallas_call x2, Pallas kernels, upper_then_lower(): pl.pallas_call(kernel, out_shape=(jax.ShapeDtypeStruct(rhs.shape, jnp.flo...  9.54 us
    pallas_call x1, Pallas kernels, lower_pallas(): pl.pallas_call(kernel, out_shape=tuple(out_shape), in_specs=_vmem_specs(l...  8.28 us
    pallas_call x2, Pallas kernels, lower_update(): pl.pallas_call(kernel, out_shape=jax.ShapeDtypeStruct(psi.shape, jnp.floa...  7.34 us
    unnamed x34, local copies, waits for them, and re-layouts  6.38 us
  transfers between devices with their start and end apart: 24, of which 6 were waited for; matrix products, arithmetic and copies ran while one was open for 16% of the time, Pallas kernels for 14%

profile of v12, /device:TPU:0, one launch (start us, length us, event | category | flops | bytes accessed | tf_op | source)
XLA Modules:
  0.0 160.9 jit_solution(222639024654544610)
XLA Ops:
  0.6 1.0 copy.198.psi_ref
  1.8 1.3 collective-permute-start.2
  3.1 3.0 %collective-permute-start.3 = (f32[8,2,6,32]{3,2,1,0:T(8,128)S(1)}, f32[8,2,6,32]{3,2,1,0:T(8,128)S(1)}, u32[]{:S(2)}, u32[]{:S(2)}) collective-permute-start(f32[8,2,6,32]{3,2,1,0:T(8,128)S(1)} %get-tuple-element.27), channel_id=1, source_target_pairs={{0,1},{1,2},{2,3},{4,5},{5,6},{6,7},{8,9},{9,10},{10,11},{12,13},{... | collective-permute-start | bytes 36872 | tf_op jit(solution)/shard_map/ppermute | solution.py:19
  6.1 1.3 collective-permute-start
  7.4 5.6 %collective-permute-start.1 = (f32[1,2,6,512]{3,2,1,0:T(8,128)S(1)}, f32[1,2,6,512]{3,2,1,0:T(8,128)S(1)}, u32[]{:S(2)}, u32[]{:S(2)}) collective-permute-start(f32[1,2,6,512]{3,2,1,0:T(8,128)S(1)} %get-tuple-element.25), channel_id=1, source_target_pairs={{0,4},{4,8},{8,12},{1,5},{5,9},{9,13},{2,6},{6,10},{10,14},{3,7},{... | collective-permute-start | bytes 73736 | tf_op jit(solution)/shard_map/ppermute | solution.py:19
  13.0 4.0 %copy_bitcast_fusion = (f32[8,2,6,6,512]{4,3,2,1,0:T(8,128)}, f32[8,2,6,6,512]{4,3,2,1,0:T(8,128)}) fusion(f32[8,2,6,6,512]{4,1,3,2,0:T(2,128)} %param.16, f32[8,2,6,6,512]{4,1,3,2,0:T(2,128)} %param.15), kind=kLoop, calls=%fused_computation | loop fusion | bytes 4718592 | tf_op jit(solution)/shard_map/transpose | solution.py:295
  17.0 6.8 %shard_map.140 = f32[2,12,2,6,512]{4,3,2,1,0:T(8,128)} custom-call(f32[8,2,6,6,512]{4,3,2,1,0:T(8,128)} %get-tuple-element.29.refs_0_.refs_1_.nt_ref, f32[8,2,6,6,512]{4,3,2,1,0:T(8,128)} %get-tuple-element.28.refs_1_.refs_2_.ft_ref), custom_call_target="tpu_custom_call" | custom-call | tf_op jit(solution)/shard_map/pallas_call | solution.py:116
  23.9 2.4 %copy.211 = f32[2,12,2,6,512]{4,2,3,1,0:T(2,128)} copy(f32[2,12,2,6,512]{4,3,2,1,0:T(8,128)} %shard_map.140) | data formatting | bytes 1179648 | tf_op jit(solution)/shard_map/pallas_call | solution.py:116
  26.3 5.7 %collective-permute-start.5 = (f32[2,12,2,6,512]{4,2,3,1,0:T(2,128)}, f32[2,12,2,6,512]{4,2,3,1,0:T(2,128)}, u32[]{:S(2)}, u32[]{:S(2)}) collective-permute-start(f32[2,12,2,6,512]{4,2,3,1,0:T(2,128)} %copy.211), channel_id=1, source_target_pairs={{0,8},{4,12},{1,9},{5,13},{2,10},{6,14},{3,11},{7,15},{16,24},{20,... | collective-permute-start | bytes 1769480 | tf_op jit(solution)/shard_map/ppermute | solution.py:28
  32.0 2.2 %collective-permute-start.4 = (f32[2,12,2,6,512]{4,2,3,1,0:T(2,128)}, f32[2,12,2,6,512]{4,2,3,1,0:T(2,128)}, u32[]{:S(2)}, u32[]{:S(2)}) collective-permute-start(f32[2,12,2,6,512]{4,2,3,1,0:T(2,128)} %copy.211), channel_id=1, source_target_pairs={{0,4},{4,8},{8,12},{1,5},{5,9},{9,13},{2,6},{6,10},{10,14},{3,7},{... | collective-permute-start | bytes 1769480 | tf_op jit(solution)/shard_map/ppermute | solution.py:28
  34.9 0.8 convolution_bitcast_fusion.1
  36.7 0.8 copy.218.refs_0_.rhs_ref
  37.5 0.6 broadcast_in_dim.10.refs_3_
  38.1 3.0 %shard_map.141 = f32[2,1,2,6,512]{4,3,2,1,0:T(8,128)} custom-call(f32[8,2,6,512]{3,2,1,0:T(8,128)} %copy.218.refs_0_.rhs_ref, f32[8,2,6,6,512]{4,3,2,1,0:T(8,128)} %get-tuple-element.29.refs_0_.refs_1_.nt_ref, f32[8,2,6,6,512]{4,3,2,1,0:T(8,128)} %get-tuple-element.28.refs_1_.refs_2_.ft_ref, f32[2,1,2,6,512]{4,3,2,1,0:T(8,128)} %broadcast_in_dim.10.refs_3_), custom_call_target="tpu_custom_call" | custom-call | tf_op jit(solution)/shard_map/pallas_call | solution.py:116
  41.1 1.4 collective-permute-start.6
  42.5 1.4 copy.219.d_ref.refs_0_
  44.0 1.4 copy.220.b_ref.refs_1_
  45.4 1.4 copy.221.a_ref.refs_2_
  46.9 8.3 %shard_map.143 = f32[2,12,2,6,512]{4,3,2,1,0:T(8,128)} custom-call(f32[8,2,6,6,512]{4,3,2,1,0:T(8,128)} %copy.219.d_ref.refs_0_, f32[8,2,6,6,512]{4,3,2,1,0:T(8,128)} %copy.220.b_ref.refs_1_, f32[8,2,6,6,512]{4,3,2,1,0:T(8,128)} %copy.221.a_ref.refs_2_), custom_call_target="tpu_custom_call" | custom-call | tf_op jit(solution)/shard_map/pallas_call | solution.py:180
  55.1 1.6 %copy.225 = f32[2,12,2,6,512]{4,2,3,1,0:T(2,128)S(1)} copy(f32[2,12,2,6,512]{4,3,2,1,0:T(8,128)} %shard_map.143) | data formatting | bytes 1179648 | tf_op jit(solution)/shard_map/pallas_call | solution.py:180
  56.8 1.3 collective-permute-start.10
  58.1 2.5 %collective-permute-start.7 = (f32[2,2,6,512]{3,2,1,0:T(8,128)S(1)}, f32[2,2,6,512]{3,2,1,0:T(8,128)S(1)}, u32[]{:S(2)}, u32[]{:S(2)}) collective-permute-start(f32[2,2,6,512]{3,2,1,0:T(8,128)S(1)} %bitcast.81), channel_id=1, source_target_pairs={{0,8},{4,12},{1,9},{5,13},{2,10},{6,14},{3,11},{7,15},{16,24},{20,... | collective-permute-start | bytes 147464 | tf_op jit(solution)/shard_map/ppermute | solution.py:28
  60.6 3.3 %collective-permute-start.8 = (f32[2,2,6,512]{3,2,1,0:T(8,128)S(1)}, f32[2,2,6,512]{3,2,1,0:T(8,128)S(1)}, u32[]{:S(2)}, u32[]{:S(2)}) collective-permute-start(f32[2,2,6,512]{3,2,1,0:T(8,128)S(1)} %bitcast.82), channel_id=1, source_target_pairs={{0,4},{4,8},{8,12},{1,5},{5,9},{9,13},{2,6},{6,10},{10,14},{3,7},{... | collective-permute-start | bytes 147464 | tf_op jit(solution)/shard_map/ppermute | solution.py:28
  64.0 1.3 multiply_reduce_fusion.10
  65.4 1.3 multiply_reduce_fusion.9
  66.8 0.6 fusion.16.inc_ref
  67.4 4.8 %shard_map.142 = (f32[8,2,6,512]{3,2,1,0:T(8,128)}, f32[2,1,2,6,512]{4,3,2,1,0:T(8,128)}) custom-call(f32[8,2,6,512]{3,2,1,0:T(8,128)} %copy.218.refs_0_.rhs_ref, f32[8,2,6,6,512]{4,3,2,1,0:T(8,128)} %get-tuple-element.29.refs_0_.refs_1_.nt_ref, f32[8,2,6,6,512]{4,3,2,1,0:T(8,128)} %get-tuple-element.28.refs_1_.refs_2_.ft_ref, ...), custom_call_target="tpu_custom_call" | custom-call | tf_op jit(solution)/shard_map/pallas_call | solution.py:230
  72.2 1.3 collective-permute-start.11
  73.5 1.3 collective-permute-start.9
  74.8 13.2 %collective-permute-done.11 = f32[2,2,6,512]{3,2,1,0:T(8,128)S(1)} collective-permute-done((f32[2,2,6,512]{3,2,1,0:T(8,128)}, f32[2,2,6,512]{3,2,1,0:T(8,128)S(1)}, u32[]{:S(2)}, u32[]{:S(2)}) %collective-permute-start.11) | collective-permute-done | bytes 49184 | tf_op jit(solution)/shard_map/ppermute | solution.py:28
  88.3 1.3 collective-permute-start.12
  90.2 4.2 %collective-permute-done.12 = f32[2,2,6,512]{3,2,1,0:T(8,128)S(1)} collective-permute-done((f32[2,2,6,512]{3,2,1,0:T(8,128)S(1)}, f32[2,2,6,512]{3,2,1,0:T(8,128)S(1)}, u32[]{:S(2)}, u32[]{:S(2)}) %collective-permute-start.12) | collective-permute-done | bytes 49184 | tf_op jit(solution)/shard_map/ppermute | solution.py:28
  94.8 0.6 fusion.15.inc_ref
  95.4 3.7 %shard_map.144.psi_ref = f32[8,2,6,512]{3,2,1,0:T(8,128)} custom-call(f32[8,2,6,512]{3,2,1,0:T(8,128)} %get-tuple-element.6.rhs_ref, f32[8,2,6,6,512]{4,3,2,1,0:T(8,128)} %copy.219.d_ref.refs_0_, f32[8,2,6,6,512]{4,3,2,1,0:T(8,128)} %copy.220.b_ref.refs_1_, f32[8,2,6,6,512]{4,3,2,1,0:T(8,128)} %copy.221.a_ref.refs_2_, f32[2,1,2,6,512]{4,3,2,1,0:T(8,128)} %fusion.15.inc_ref, ...), custom_call_target="tpu_custom_call" | custom-call | tf_op jit(solution)/shard_map/pallas_call | solution.py:200
  99.1 0.8 fusion.19
  99.9 1.3 collective-permute-start.13
  101.2 4.5 %collective-permute-start.14 = (f32[1,2,6,512]{3,2,1,0:T(8,128)S(1)}, f32[1,2,6,512]{3,2,1,0:T(8,128)S(1)}, u32[]{:S(2)}, u32[]{:S(2)}) collective-permute-start(f32[1,2,6,512]{3,2,1,0:T(8,128)S(1)} %get-tuple-element.21), channel_id=1, source_target_pairs={{0,4},{4,8},{8,12},{1,5},{5,9},{9,13},{2,6},{6,10},{10,14},{3,7},{... | collective-permute-start | bytes 73736 | tf_op jit(solution)/shard_map/ppermute | solution.py:19
  105.7 1.0 fusion.20
  106.7 1.3 collective-permute-start.15
  108.0 3.2 %collective-permute-start.16 = (f32[8,2,6,32]{3,2,1,0:T(8,128)S(1)}, f32[8,2,6,32]{3,2,1,0:T(8,128)S(1)}, u32[]{:S(2)}, u32[]{:S(2)}) collective-permute-start(f32[8,2,6,32]{3,2,1,0:T(8,128)S(1)} %get-tuple-element.23), channel_id=1, source_target_pairs={{0,1},{1,2},{2,3},{4,5},{5,6},{6,7},{8,9},{9,10},{10,11},{12,13},{... | collective-permute-start | bytes 36872 | tf_op jit(solution)/shard_map/ppermute | solution.py:19
  111.2 0.7 collective-permute-done.16
  111.9 1.9 %fusion = f32[8,2,6,512]{3,2,1,0:T(8,128)S(1)} fusion(f32[8,2,6,512]{3,1,2,0:T(2,128)S(1)} %copy-done.8, f32[8,2,6,512]{3,2,1,0:T(8,128)} %shard_map.144.psi_ref, f32[8,2,6,32]{3,2,1,0:T(8,128)S(1)} %collective-permute-done.16, f32[8,2,6,32]{3,2,1,0:T(8,128)S(1)} %collective-permute-done.15, f32[1,2,6,512]{3,2,1,0:T(8,128)S(1)} %collective-permute-done.14, ...), kind=kLoop, calls=%fused_computation.17 | loop fusion | flops 540672 | bytes 663552 | tf_op jit(solution)/shard_map/sub | solution.py:309
  114.1 0.8 convolution_bitcast_fusion
  116.0 0.8 copy.242.refs_0_.rhs_ref
  116.8 2.9 %shard_map.145 = f32[2,1,2,6,512]{4,3,2,1,0:T(8,128)} custom-call(f32[8,2,6,512]{3,2,1,0:T(8,128)} %copy.242.refs_0_.rhs_ref, f32[8,2,6,6,512]{4,3,2,1,0:T(8,128)} %get-tuple-element.29.refs_0_.refs_1_.nt_ref, f32[8,2,6,6,512]{4,3,2,1,0:T(8,128)} %get-tuple-element.28.refs_1_.refs_2_.ft_ref, f32[2,1,2,6,512]{4,3,2,1,0:T(8,128)} %broadcast_in_dim.10.refs_3_), custom_call_target="tpu_custom_call" | custom-call | tf_op jit(solution)/shard_map/pallas_call | solution.py:116
  119.7 2.7 %collective-permute-start.17 = (f32[2,2,6,512]{3,2,1,0:T(8,128)}, f32[2,2,6,512]{3,2,1,0:T(8,128)S(1)}, u32[]{:S(2)}, u32[]{:S(2)}) collective-permute-start(f32[2,2,6,512]{3,2,1,0:T(8,128)} %bitcast.83), channel_id=1, source_target_pairs={{0,12},{1,13},{2,14},{3,15},{16,28},{17,29},{18,30},{19,31}} | collective-permute-start | bytes 147464 | tf_op jit(solution)/shard_map/ppermute | solution.py:28
  122.4 1.8 %collective-permute-start.18 = (f32[2,2,6,512]{3,2,1,0:T(8,128)}, f32[2,2,6,512]{3,2,1,0:T(8,128)S(1)}, u32[]{:S(2)}, u32[]{:S(2)}) collective-permute-start(f32[2,2,6,512]{3,2,1,0:T(8,128)} %bitcast.84), channel_id=1, source_target_pairs={{0,8},{4,12},{1,9},{5,13},{2,10},{6,14},{3,11},{7,15},{16,24},{20,... | collective-permute-start | bytes 147464 | tf_op jit(solution)/shard_map/ppermute | solution.py:28
  124.3 1.9 %collective-permute-start.19 = (f32[2,2,6,512]{3,2,1,0:T(8,128)}, f32[2,2,6,512]{3,2,1,0:T(8,128)S(1)}, u32[]{:S(2)}, u32[]{:S(2)}) collective-permute-start(f32[2,2,6,512]{3,2,1,0:T(8,128)} %bitcast.85), channel_id=1, source_target_pairs={{0,4},{4,8},{8,12},{1,5},{5,9},{9,13},{2,6},{6,10},{10,14},{3,7},{... | collective-permute-start | bytes 147464 | tf_op jit(solution)/shard_map/ppermute | solution.py:28
  126.2 1.3 multiply_reduce_fusion.6
  127.7 1.3 multiply_reduce_fusion.5
  129.0 0.6 fusion.13.inc_ref
  129.7 4.8 %shard_map.146 = (f32[8,2,6,512]{3,2,1,0:T(8,128)}, f32[2,1,2,6,512]{4,3,2,1,0:T(8,128)}) custom-call(f32[8,2,6,512]{3,2,1,0:T(8,128)} %copy.242.refs_0_.rhs_ref, f32[8,2,6,6,512]{4,3,2,1,0:T(8,128)} %get-tuple-element.29.refs_0_.refs_1_.nt_ref, f32[8,2,6,6,512]{4,3,2,1,0:T(8,128)} %get-tuple-element.28.refs_1_.refs_2_.ft_ref, ...), custom_call_target="tpu_custom_call" | custom-call | tf_op jit(solution)/shard_map/pallas_call | solution.py:230
  134.4 1.3 collective-permute-start.21
  135.7 1.3 collective-permute-start.20
  137.0 6.3 %collective-permute-done.21 = f32[2,2,6,512]{3,2,1,0:T(8,128)S(1)} collective-permute-done((f32[2,2,6,512]{3,2,1,0:T(8,128)}, f32[2,2,6,512]{3,2,1,0:T(8,128)S(1)}, u32[]{:S(2)}, u32[]{:S(2)}) %collective-permute-start.21) | collective-permute-done | bytes 49184 | tf_op jit(solution)/shard_map/ppermute | solution.py:28
  143.7 1.3 collective-permute-start.22
  145.2 4.7 %collective-permute-done.22 = f32[2,2,6,512]{3,2,1,0:T(8,128)S(1)} collective-permute-done((f32[2,2,6,512]{3,2,1,0:T(8,128)S(1)}, f32[2,2,6,512]{3,2,1,0:T(8,128)S(1)}, u32[]{:S(2)}, u32[]{:S(2)}) %collective-permute-start.22) | collective-permute-done | bytes 49184 | tf_op jit(solution)/shard_map/ppermute | solution.py:28
  150.1 0.6 fusion.12.inc_ref
  150.8 3.7 %shard_map.147 = f32[8,2,6,512]{3,2,1,0:T(8,128)} custom-call(f32[8,2,6,512]{3,2,1,0:T(8,128)} %get-tuple-element.8.rhs_ref, f32[8,2,6,6,512]{4,3,2,1,0:T(8,128)} %copy.219.d_ref.refs_0_, f32[8,2,6,6,512]{4,3,2,1,0:T(8,128)} %copy.220.b_ref.refs_1_, f32[8,2,6,6,512]{4,3,2,1,0:T(8,128)} %copy.221.a_ref.refs_2_, f32[2,1,2,6,512]{4,3,2,1,0:T(8,128)} %fusion.12.inc_ref, ...), custom_call_target="tpu_custom_call" | custom-call | tf_op jit(solution)/shard_map/pallas_call | solution.py:200
  154.5 1.1 multiply_bitcast_fusion
  156.1 1.6 collective-permute-start.23
  157.7 0.8 copy.253
  158.5 1.8 %collective-permute-done.23 = f32[8,3,512]{2,0,1:T(8,128)S(1)} collective-permute-done((f32[8,3,512]{2,0,1:T(8,128)S(1)}, f32[8,3,512]{2,0,1:T(8,128)S(1)}, u32[]{:S(2)}, u32[]{:S(2)}) %collective-permute-start.23) | collective-permute-done | bytes 49184 | tf_op jit(solution)/shard_map/ppermute | solution.py:333
  160.3 0.6 fusion.25
  (80 shorter events, 5.9 us)
Async XLA Ops:
  0.6 34.2 %copy-start = (f32[2,6,32,32]{3,2,1,0:T(8,128)S(1)}, f32[2,6,32,32]{3,2,1,0:T(8,128)}, u32[]{:S(2)}) copy-start(f32[2,6,32,32]{3,2,1,0:T(8,128)} %param.21) | copy-start | bytes 147460
  1.7 32.6 %copy-start.2 = (f32[8,2,6,512]{3,2,1,0:T(8,128)}, f32[8,2,6,512]{3,2,1,0:T(8,128)S(1)}, u32[]{:S(2)}) copy-start(f32[8,2,6,512]{3,2,1,0:T(8,128)S(1)} %copy.198.psi_ref) | copy-start | bytes 589828
  1.8 30.3 %collective-permute-start.2 = (f32[8,2,6,32]{3,2,1,0:T(8,128)S(1)}, f32[8,2,6,32]{3,2,1,0:T(8,128)S(1)}, u32[]{:S(2)}, u32[]{:S(2)}) collective-permute-start(f32[8,2,6,32]{3,2,1,0:T(8,128)S(1)} %get-tuple-element.26), channel_id=1, source_target_pairs={{1,0},{2,1},{3,2},{5,4},{6,5},{7,6},{9,8},{10,9},{11,10},{13,12},{... | collective-permute-start | bytes 36872 | tf_op jit(solution)/shard_map/ppermute | solution.py:20
  3.1 31.2 %collective-permute-start.3 = (f32[8,2,6,32]{3,2,1,0:T(8,128)S(1)}, f32[8,2,6,32]{3,2,1,0:T(8,128)S(1)}, u32[]{:S(2)}, u32[]{:S(2)}) collective-permute-start(f32[8,2,6,32]{3,2,1,0:T(8,128)S(1)} %get-tuple-element.27), channel_id=1, source_target_pairs={{0,1},{1,2},{2,3},{4,5},{5,6},{6,7},{8,9},{9,10},{10,11},{12,13},{... | collective-permute-start | bytes 36872 | tf_op jit(solution)/shard_map/ppermute | solution.py:19
  6.1 28.1 %collective-permute-start = (f32[1,2,6,512]{3,2,1,0:T(8,128)S(1)}, f32[1,2,6,512]{3,2,1,0:T(8,128)S(1)}, u32[]{:S(2)}, u32[]{:S(2)}) collective-permute-start(f32[1,2,6,512]{3,2,1,0:T(8,128)S(1)} %get-tuple-element.24), channel_id=1, source_target_pairs={{4,0},{8,4},{12,8},{5,1},{9,5},{13,9},{6,2},{10,6},{14,10},{7,3},{... | collective-permute-start | bytes 73736 | tf_op jit(solution)/shard_map/ppermute | solution.py:20
  7.4 26.8 %collective-permute-start.1 = (f32[1,2,6,512]{3,2,1,0:T(8,128)S(1)}, f32[1,2,6,512]{3,2,1,0:T(8,128)S(1)}, u32[]{:S(2)}, u32[]{:S(2)}) collective-permute-start(f32[1,2,6,512]{3,2,1,0:T(8,128)S(1)} %get-tuple-element.25), channel_id=1, source_target_pairs={{0,4},{4,8},{8,12},{1,5},{5,9},{9,13},{2,6},{6,10},{10,14},{3,7},{... | collective-permute-start | bytes 73736 | tf_op jit(solution)/shard_map/ppermute | solution.py:19
  23.9 10.4 %copy-start.7 = (f32[8,2,6,512]{3,1,2,0:T(2,128)S(1)}, f32[8,2,6,512]{3,1,2,0:T(2,128)}, u32[]{:S(2)}) copy-start(f32[8,2,6,512]{3,1,2,0:T(2,128)} %param.14) | copy-start | bytes 589828
  26.3 37.7 %collective-permute-start.5 = (f32[2,12,2,6,512]{4,2,3,1,0:T(2,128)}, f32[2,12,2,6,512]{4,2,3,1,0:T(2,128)}, u32[]{:S(2)}, u32[]{:S(2)}) collective-permute-start(f32[2,12,2,6,512]{4,2,3,1,0:T(2,128)} %copy.211), channel_id=1, source_target_pairs={{0,8},{4,12},{1,9},{5,13},{2,10},{6,14},{3,11},{7,15},{16,24},{20,... | collective-permute-start | bytes 1769480 | tf_op jit(solution)/shard_map/ppermute | solution.py:28
  32.0 33.4 %collective-permute-start.4 = (f32[2,12,2,6,512]{4,2,3,1,0:T(2,128)}, f32[2,12,2,6,512]{4,2,3,1,0:T(2,128)}, u32[]{:S(2)}, u32[]{:S(2)}) collective-permute-start(f32[2,12,2,6,512]{4,2,3,1,0:T(2,128)} %copy.211), channel_id=1, source_target_pairs={{0,4},{4,8},{8,12},{1,5},{5,9},{9,13},{2,6},{6,10},{10,14},{3,7},{... | collective-permute-start | bytes 1769480 | tf_op jit(solution)/shard_map/ppermute | solution.py:28
  34.8 1.3 copy-start.1
  38.1 4.4 %copy-start.4 = (f32[8,2,6,6,512]{4,1,3,2,0:T(2,128)S(1)}, f32[8,2,6,6,512]{4,1,3,2,0:T(2,128)}, u32[]{:S(2)}) copy-start(f32[8,2,6,6,512]{4,1,3,2,0:T(2,128)} %param.17) | copy-start | bytes 3538948
  41.1 2.9 %copy-start.5 = (f32[8,2,6,6,512]{4,1,3,2,0:T(2,128)S(1)}, f32[8,2,6,6,512]{4,1,3,2,0:T(2,128)}, u32[]{:S(2)}) copy-start(f32[8,2,6,6,512]{4,1,3,2,0:T(2,128)} %param.18) | copy-start | bytes 3538948
  41.1 19.5 %collective-permute-start.6 = (f32[2,2,6,512]{3,2,1,0:T(8,128)}, f32[2,2,6,512]{3,2,1,0:T(8,128)S(1)}, u32[]{:S(2)}, u32[]{:S(2)}) collective-permute-start(f32[2,2,6,512]{3,2,1,0:T(8,128)} %bitcast.80), channel_id=1, source_target_pairs={{0,12},{1,13},{2,14},{3,15},{16,28},{17,29},{18,30},{19,31}} | collective-permute-start | bytes 147464 | tf_op jit(solution)/shard_map/ppermute | solution.py:28
  44.0 1.4 copy-start.6
  55.1 2.9 %copy-start.10 = (f32[2,1,2,6,512]{4,3,2,1,0:T(8,128)S(1)}, f32[2,1,2,6,512]{4,3,2,1,0:T(8,128)}, u32[]{:S(2)}) copy-start(f32[2,1,2,6,512]{4,3,2,1,0:T(8,128)} %shard_map.141) | copy-start | bytes 147460
  56.8 31.3 %collective-permute-start.10 = (f32[2,12,2,6,512]{4,2,3,1,0:T(2,128)S(1)}, f32[2,12,2,6,512]{4,2,3,1,0:T(2,128)S(1)}, u32[]{:S(2)}, u32[]{:S(2)}) collective-permute-start(f32[2,12,2,6,512]{4,2,3,1,0:T(2,128)S(1)} %copy.225), channel_id=1, source_target_pairs={{4,0},{8,4},{12,8},{5,1},{9,5},{13,9},{6,2},{10,6},{14,10},{7,3},{... | collective-permute-start | bytes 1769480 | tf_op jit(solution)/shard_map/ppermute | solution.py:28
  58.1 7.3 %collective-permute-start.7 = (f32[2,2,6,512]{3,2,1,0:T(8,128)S(1)}, f32[2,2,6,512]{3,2,1,0:T(8,128)S(1)}, u32[]{:S(2)}, u32[]{:S(2)}) collective-permute-start(f32[2,2,6,512]{3,2,1,0:T(8,128)S(1)} %bitcast.81), channel_id=1, source_target_pairs={{0,8},{4,12},{1,9},{5,13},{2,10},{6,14},{3,11},{7,15},{16,24},{20,... | collective-permute-start | bytes 147464 | tf_op jit(solution)/shard_map/ppermute | solution.py:28
  60.6 6.2 %collective-permute-start.8 = (f32[2,2,6,512]{3,2,1,0:T(8,128)S(1)}, f32[2,2,6,512]{3,2,1,0:T(8,128)S(1)}, u32[]{:S(2)}, u32[]{:S(2)}) collective-permute-start(f32[2,2,6,512]{3,2,1,0:T(8,128)S(1)} %bitcast.82), channel_id=1, source_target_pairs={{0,4},{4,8},{8,12},{1,5},{5,9},{9,13},{2,6},{6,10},{10,14},{3,7},{... | collective-permute-start | bytes 147464 | tf_op jit(solution)/shard_map/ppermute | solution.py:28
  67.4 22.2 %copy-start.11 = (s32[8,512]{1,0:T(8,128)S(1)}, s32[8,512]{1,0:T(8,128)}, u32[]{:S(2)}) copy-start(s32[8,512]{1,0:T(8,128)} %param.23) | copy-start | bytes 49156
  72.2 15.8 %collective-permute-start.11 = (f32[2,2,6,512]{3,2,1,0:T(8,128)}, f32[2,2,6,512]{3,2,1,0:T(8,128)S(1)}, u32[]{:S(2)}, u32[]{:S(2)}) collective-permute-start(f32[2,2,6,512]{3,2,1,0:T(8,128)} %bitcast.93), channel_id=1, source_target_pairs={{8,0},{12,4},{9,1},{13,5},{10,2},{14,6},{11,3},{15,7},{24,16},{28,... | collective-permute-start | bytes 147464 | tf_op jit(solution)/shard_map/ppermute | solution.py:28
  73.5 14.8 %collective-permute-start.9 = (f32[2,2,6,512]{3,2,1,0:T(8,128)}, f32[2,2,6,512]{3,2,1,0:T(8,128)S(1)}, u32[]{:S(2)}, u32[]{:S(2)}) collective-permute-start(f32[2,2,6,512]{3,2,1,0:T(8,128)} %bitcast.94), channel_id=1, source_target_pairs={{4,0},{8,4},{12,8},{5,1},{9,5},{13,9},{6,2},{10,6},{14,10},{7,3},{... | collective-permute-start | bytes 147464 | tf_op jit(solution)/shard_map/ppermute | solution.py:28
  88.3 6.2 %collective-permute-start.12 = (f32[2,2,6,512]{3,2,1,0:T(8,128)S(1)}, f32[2,2,6,512]{3,2,1,0:T(8,128)S(1)}, u32[]{:S(2)}, u32[]{:S(2)}) collective-permute-start(f32[2,2,6,512]{3,2,1,0:T(8,128)S(1)} %copy_add_fusion.7), channel_id=1, source_target_pairs={{4,0},{8,4},{12,8},{5,1},{9,5},{13,9},{6,2},{10,6},{14,10},{7,3},{... | collective-permute-start | bytes 147464 | tf_op jit(solution)/shard_map/ppermute | solution.py:28
  95.4 16.5 %copy-start.8 = (f32[8,2,6,512]{3,1,2,0:T(2,128)S(1)}, f32[8,2,6,512]{3,1,2,0:T(2,128)}, u32[]{:S(2)}) copy-start(f32[8,2,6,512]{3,1,2,0:T(2,128)} %param.14) | copy-start | bytes 589828
  99.9 12.0 %collective-permute-start.13 = (f32[1,2,6,512]{3,2,1,0:T(8,128)S(1)}, f32[1,2,6,512]{3,2,1,0:T(8,128)S(1)}, u32[]{:S(2)}, u32[]{:S(2)}) collective-permute-start(f32[1,2,6,512]{3,2,1,0:T(8,128)S(1)} %get-tuple-element.20), channel_id=1, source_target_pairs={{4,0},{8,4},{12,8},{5,1},{9,5},{13,9},{6,2},{10,6},{14,10},{7,3},{... | collective-permute-start | bytes 73736 | tf_op jit(solution)/shard_map/ppermute | solution.py:20
  101.2 10.7 %collective-permute-start.14 = (f32[1,2,6,512]{3,2,1,0:T(8,128)S(1)}, f32[1,2,6,512]{3,2,1,0:T(8,128)S(1)}, u32[]{:S(2)}, u32[]{:S(2)}) collective-permute-start(f32[1,2,6,512]{3,2,1,0:T(8,128)S(1)} %get-tuple-element.21), channel_id=1, source_target_pairs={{0,4},{4,8},{8,12},{1,5},{5,9},{9,13},{2,6},{6,10},{10,14},{3,7},{... | collective-permute-start | bytes 73736 | tf_op jit(solution)/shard_map/ppermute | solution.py:19
  106.7 4.5 %collective-permute-start.15 = (f32[8,2,6,32]{3,2,1,0:T(8,128)S(1)}, f32[8,2,6,32]{3,2,1,0:T(8,128)S(1)}, u32[]{:S(2)}, u32[]{:S(2)}) collective-permute-start(f32[8,2,6,32]{3,2,1,0:T(8,128)S(1)} %get-tuple-element.22), channel_id=1, source_target_pairs={{1,0},{2,1},{3,2},{5,4},{6,5},{7,6},{9,8},{10,9},{11,10},{13,12},{... | collective-permute-start | bytes 36872 | tf_op jit(solution)/shard_map/ppermute | solution.py:20
  108.0 3.9 %collective-permute-start.16 = (f32[8,2,6,32]{3,2,1,0:T(8,128)S(1)}, f32[8,2,6,32]{3,2,1,0:T(8,128)S(1)}, u32[]{:S(2)}, u32[]{:S(2)}) collective-permute-start(f32[8,2,6,32]{3,2,1,0:T(8,128)S(1)} %get-tuple-element.23), channel_id=1, source_target_pairs={{0,1},{1,2},{2,3},{4,5},{5,6},{6,7},{8,9},{9,10},{10,11},{12,13},{... | collective-permute-start | bytes 36872 | tf_op jit(solution)/shard_map/ppermute | solution.py:19
  119.7 6.5 %collective-permute-start.17 = (f32[2,2,6,512]{3,2,1,0:T(8,128)}, f32[2,2,6,512]{3,2,1,0:T(8,128)S(1)}, u32[]{:S(2)}, u32[]{:S(2)}) collective-permute-start(f32[2,2,6,512]{3,2,1,0:T(8,128)} %bitcast.83), channel_id=1, source_target_pairs={{0,12},{1,13},{2,14},{3,15},{16,28},{17,29},{18,30},{19,31}} | collective-permute-start | bytes 147464 | tf_op jit(solution)/shard_map/ppermute | solution.py:28
  122.4 5.2 %collective-permute-start.18 = (f32[2,2,6,512]{3,2,1,0:T(8,128)}, f32[2,2,6,512]{3,2,1,0:T(8,128)S(1)}, u32[]{:S(2)}, u32[]{:S(2)}) collective-permute-start(f32[2,2,6,512]{3,2,1,0:T(8,128)} %bitcast.84), channel_id=1, source_target_pairs={{0,8},{4,12},{1,9},{5,13},{2,10},{6,14},{3,11},{7,15},{16,24},{20,... | collective-permute-start | bytes 147464 | tf_op jit(solution)/shard_map/ppermute | solution.py:28
  124.3 4.7 %collective-permute-start.19 = (f32[2,2,6,512]{3,2,1,0:T(8,128)}, f32[2,2,6,512]{3,2,1,0:T(8,128)S(1)}, u32[]{:S(2)}, u32[]{:S(2)}) collective-permute-start(f32[2,2,6,512]{3,2,1,0:T(8,128)} %bitcast.85), channel_id=1, source_target_pairs={{0,4},{4,8},{8,12},{1,5},{5,9},{9,13},{2,6},{6,10},{10,14},{3,7},{... | collective-permute-start | bytes 147464 | tf_op jit(solution)/shard_map/ppermute | solution.py:28
  129.6 15.3 %copy-start.12 = (f32[8]{0:T(128)S(1)}, f32[8]{0:T(128)}, u32[]{:S(2)}) copy-start(f32[8]{0:T(128)} %param.25) | copy-start | bytes 100
  129.6 15.4 %copy-start.13 = (s32[2]{0:T(128)S(1)}, s32[2]{0:T(128)}, u32[]{:S(2)}) copy-start(s32[2]{0:T(128)} %param.24) | copy-start | bytes 28
  134.4 8.9 %collective-permute-start.21 = (f32[2,2,6,512]{3,2,1,0:T(8,128)}, f32[2,2,6,512]{3,2,1,0:T(8,128)S(1)}, u32[]{:S(2)}, u32[]{:S(2)}) collective-permute-start(f32[2,2,6,512]{3,2,1,0:T(8,128)} %bitcast.95), channel_id=1, source_target_pairs={{8,0},{12,4},{9,1},{13,5},{10,2},{14,6},{11,3},{15,7},{24,16},{28,... | collective-permute-start | bytes 147464 | tf_op jit(solution)/shard_map/ppermute | solution.py:28
  135.7 7.9 %collective-permute-start.20 = (f32[2,2,6,512]{3,2,1,0:T(8,128)}, f32[2,2,6,512]{3,2,1,0:T(8,128)S(1)}, u32[]{:S(2)}, u32[]{:S(2)}) collective-permute-start(f32[2,2,6,512]{3,2,1,0:T(8,128)} %bitcast.96), channel_id=1, source_target_pairs={{4,0},{8,4},{12,8},{5,1},{9,5},{13,9},{6,2},{10,6},{14,10},{7,3},{... | collective-permute-start | bytes 147464 | tf_op jit(solution)/shard_map/ppermute | solution.py:28
  143.7 6.2 %collective-permute-start.22 = (f32[2,2,6,512]{3,2,1,0:T(8,128)S(1)}, f32[2,2,6,512]{3,2,1,0:T(8,128)S(1)}, u32[]{:S(2)}, u32[]{:S(2)}) collective-permute-start(f32[2,2,6,512]{3,2,1,0:T(8,128)S(1)} %copy_add_fusion.3), channel_id=1, source_target_pairs={{4,0},{8,4},{12,8},{5,1},{9,5},{13,9},{6,2},{10,6},{14,10},{7,3},{... | collective-permute-start | bytes 147464 | tf_op jit(solution)/shard_map/ppermute | solution.py:28
  154.5 1.3 copy-start.9
  154.5 3.2 %copy-start.3 = (f32[8,2,6,512]{3,2,1,0:T(8,128)S(1)}, f32[8,2,6,512]{3,2,1,0:T(8,128)}, u32[]{:S(2)}) copy-start(f32[8,2,6,512]{3,2,1,0:T(8,128)} %shard_map.147) | copy-start | bytes 589828
  156.1 4.2 %collective-permute-start.23 = (f32[8,3,512]{2,0,1:T(8,128)S(1)}, f32[8,3,512]{2,0,1:T(8,128)S(1)}, u32[]{:S(2)}, u32[]{:S(2)}) collective-permute-start(f32[8,3,512]{2,0,1:T(8,128)S(1)} %bitcast.92), channel_id=1, source_target_pairs={{0,16},{16,0},{1,17},{17,1},{2,18},{18,2},{3,19},{19,3},{4,20},{20... | collective-permute-start | bytes 147464 | tf_op jit(solution)/shard_map/ppermute | solution.py:333

commit v13 on v12

--- a/solution.py
+++ b/solution.py
@@ -298,10 +298,21 @@
     (response,) = lower_pallas(None, inverse_diag, near_lower, far_lower, units, False)
     reverse_matrix = response
     upper_products = shifted_operators(matrix, 1)
-    lower_behind = from_behind(reverse_matrix, "gx", -1)
     psi = psi_old
     for step in range(ITERS):
-        stream_pad = extended(psi, (("gx", 0),), 1)
+        if step == 0:
+            size = lax.axis_size("gx")
+            up = [(i, i + 1) for i in range(size - 1)]
+            down = [(j, i) for i, j in up]
+            first = psi[:1]
+            bundle = jnp.concatenate([first.reshape(-1), reverse_matrix.reshape(-1)])
+            bundle = lax.ppermute(bundle, "gx", down)
+            after = bundle[: first.size].reshape(first.shape)
+            lower_behind = bundle[first.size :].reshape(reverse_matrix.shape)
+            before = lax.ppermute(psi[-1:], "gx", up)
+            stream_pad = jnp.concatenate([before, psi, after], axis=0)
+        else:
+            stream_pad = extended(psi, (("gx", 0),), 1)
         span_pad = extended(psi, (("gy", 3),), NZ)
         beside_all = (
             stream_pad[2:] + stream_pad[:-2] + span_pad[..., 2 * NZ :] + span_pad[..., : -2 * NZ]

time: 162 us -> 181 us (1.12)
  waiting for transfers between devices: 31 us -> 51.4 us
  starting transfers between devices: 53.7 us -> 49.1 us
  local copies, waits for them, and re-layouts: 20.4 us -> 23.9 us
    ppermute x15 -> x14, waiting for transfers between devices: 28.5 us -> 48.9 us  [from_behind(): lax.ppermute(value, axis, [(source, source + steps) for source in range(f...]
    ppermute x0 -> x2, starting transfers between devices: none -> 7.45 us  [the longest x1 6.17 us: on_device(): before = lax.ppermute(psi[-1:], 'gx', up)]
    ppermute x15 -> x14, starting transfers between devices: 30.7 us -> 24.8 us  [from_behind(): lax.ppermute(value, axis, [(source, source + steps) for source in range(f...]
    ppermute x4 -> x3, starting transfers between devices: 16.4 us -> 11.4 us  [extended(): before = lax.ppermute(last, axis, up)]
    reduce_sum x8, other arithmetic: 6.33 us -> 3.57 us  [carry_through(): return jnp.sum(jnp.sum(split * inputs, axis=2), axis=1)]
    unnamed x34 -> x38, local copies, waits for them, and re-layouts: 6.38 us -> 7.73 us
    ppermute x4 -> x3, starting transfers between devices: 5.14 us -> 3.85 us  [extended(): after = lax.ppermute(first, axis, down)]
  transfers between devices with their start and end apart: 24 -> 23, of which waited for: 6 -> 9; matrix products, arithmetic and copies ran while one was open for 16% -> 10% of each run, Pallas kernels for 14% -> 5%
where the time goes in v13:
time: 181 us; the launch traced here: 180 us
  waiting for transfers between devices  51.4 us (28%)
  starting transfers between devices  49.1 us (27%)
  Pallas kernels  37.7 us (21%)
  local copies, waits for them, and re-layouts  23.9 us (13%)
  other arithmetic  13.8 us (8%)
  matrix products  2.59 us (1%)
    ppermute x14, waiting for transfers between devices, from_behind(): lax.ppermute(value, axis, [(source, source + steps) for source in range(f...  48.9 us
    ppermute x14, starting transfers between devices, from_behind(): lax.ppermute(value, axis, [(source, source + steps) for source in range(f...  24.8 us
    pallas_call x3, Pallas kernels, upper_pallas(): pl.pallas_call(kernel, out_shape=tuple(out_shape), in_specs=_vmem_specs(l...  12.7 us
    ppermute x3, starting transfers between devices, extended(): before = lax.ppermute(last, axis, up)  11.4 us
    pallas_call x2, Pallas kernels, upper_then_lower(): pl.pallas_call(kernel, out_shape=(jax.ShapeDtypeStruct(rhs.shape, jnp.flo...  9.52 us
    pallas_call x1, Pallas kernels, lower_pallas(): pl.pallas_call(kernel, out_shape=tuple(out_shape), in_specs=_vmem_specs(l...  8.21 us
    unnamed x38, local copies, waits for them, and re-layouts  7.73 us
    pallas_call x2, Pallas kernels, lower_update(): pl.pallas_call(kernel, out_shape=jax.ShapeDtypeStruct(psi.shape, jnp.floa...  7.27 us
  transfers between devices with their start and end apart: 23, of which 9 were waited for; matrix products, arithmetic and copies ran while one was open for 10% of the time, Pallas kernels for 5%

profile of v13, /device:TPU:0, one launch (start us, length us, event | category | flops | bytes accessed | tf_op | source)
XLA Modules:
  0.0 179.7 jit_solution(10242703701592177714)
XLA Ops:
  0.7 2.8 %copy.195.refs_0_.d_ref = f32[8,2,6,6,512]{4,3,2,1,0:T(8,128)} copy(f32[8,2,6,6,512]{4,1,3,2,0:T(2,128)} %param.17) | data formatting | bytes 2359296 | tf_op args[4]
  3.5 1.4 copy.196.refs_1_.b_ref
  4.9 1.4 copy.197.refs_2_.a_ref
  6.3 8.2 %shard_map.140 = f32[2,12,2,6,512]{4,3,2,1,0:T(8,128)} custom-call(f32[8,2,6,6,512]{4,3,2,1,0:T(8,128)} %copy.195.refs_0_.d_ref, f32[8,2,6,6,512]{4,3,2,1,0:T(8,128)} %copy.196.refs_1_.b_ref, f32[8,2,6,6,512]{4,3,2,1,0:T(8,128)} %copy.197.refs_2_.a_ref), custom_call_target="tpu_custom_call" | custom-call | tf_op jit(solution)/shard_map/pallas_call | solution.py:180
  14.6 1.3 reshape.51
  15.9 0.9 pad_maximum_fusion
  16.9 1.3 collective-permute-start
  18.2 1.0 copy.198.psi_ref
  19.2 0.7 fusion.19
  19.9 1.3 collective-permute-start.2
  21.2 3.7 %collective-permute-start.3 = (f32[8,2,6,32]{3,2,1,0:T(8,128)}, f32[8,2,6,32]{3,2,1,0:T(8,128)}, u32[]{:S(2)}, u32[]{:S(2)}) collective-permute-start(f32[8,2,6,32]{3,2,1,0:T(8,128)} %get-tuple-element.25), channel_id=1, source_target_pairs={{0,1},{1,2},{2,3},{4,5},{5,6},{6,7},{8,9},{9,10},{10,11},{12,13},{... | collective-permute-start | bytes 36872 | tf_op jit(solution)/shard_map/ppermute | solution.py:19
  25.4 6.2 %collective-permute-start.1 = (f32[1,2,6,512]{3,2,1,0:T(8,128)}, f32[1,2,6,512]{3,2,1,0:T(8,128)}, u32[]{:S(2)}, u32[]{:S(2)}) collective-permute-start(f32[1,2,6,512]{3,2,1,0:T(8,128)} %slice.92), channel_id=1, source_target_pairs={{0,4},{4,8},{8,12},{1,5},{5,9},{9,13},{2,6},{6,10},{10,14},{3,7},{... | collective-permute-start | bytes 73736 | tf_op jit(solution)/shard_map/ppermute | solution.py:312
  31.6 2.4 %copy_bitcast_fusion = (f32[8,2,6,6,512]{4,3,2,1,0:T(8,128)}, f32[8,2,6,6,512]{4,3,2,1,0:T(8,128)}) fusion(f32[8,2,6,6,512]{4,1,3,2,0:T(2,128)S(1)} %copy-done.7, f32[8,2,6,6,512]{4,1,3,2,0:T(2,128)S(1)} %copy-done.8), kind=kLoop, calls=%fused_computation | loop fusion | bytes 4718592 | tf_op jit(solution)/shard_map/transpose | solution.py:295
  34.0 6.9 %shard_map.141 = f32[2,12,2,6,512]{4,3,2,1,0:T(8,128)} custom-call(f32[8,2,6,6,512]{4,3,2,1,0:T(8,128)} %get-tuple-element.27.refs_0_.refs_1_.nt_ref, f32[8,2,6,6,512]{4,3,2,1,0:T(8,128)} %get-tuple-element.26.refs_1_.refs_2_.ft_ref), custom_call_target="tpu_custom_call" | custom-call | tf_op jit(solution)/shard_map/pallas_call | solution.py:116
  40.9 2.4 %copy.211 = f32[2,12,2,6,512]{4,2,3,1,0:T(2,128)} copy(f32[2,12,2,6,512]{4,3,2,1,0:T(8,128)} %shard_map.141) | data formatting | bytes 1179648 | tf_op jit(solution)/shard_map/pallas_call | solution.py:116
  43.4 5.2 %collective-permute-start.5 = (f32[2,12,2,6,512]{4,2,3,1,0:T(2,128)}, f32[2,12,2,6,512]{4,2,3,1,0:T(2,128)}, u32[]{:S(2)}, u32[]{:S(2)}) collective-permute-start(f32[2,12,2,6,512]{4,2,3,1,0:T(2,128)} %copy.211), channel_id=1, source_target_pairs={{0,8},{4,12},{1,9},{5,13},{2,10},{6,14},{3,11},{7,15},{16,24},{20,... | collective-permute-start | bytes 1769480 | tf_op jit(solution)/shard_map/ppermute | solution.py:28
  48.6 1.3 collective-permute-start.4
  50.0 1.1 fusion.1
  51.5 0.8 convolution_bitcast_fusion.1
  53.4 0.8 copy.218.refs_0_.rhs_ref
  54.7 2.9 %shard_map.142 = f32[2,1,2,6,512]{4,3,2,1,0:T(8,128)} custom-call(f32[8,2,6,512]{3,2,1,0:T(8,128)} %copy.218.refs_0_.rhs_ref, f32[8,2,6,6,512]{4,3,2,1,0:T(8,128)} %get-tuple-element.27.refs_0_.refs_1_.nt_ref, f32[8,2,6,6,512]{4,3,2,1,0:T(8,128)} %get-tuple-element.26.refs_1_.refs_2_.ft_ref, f32[2,1,2,6,512]{4,3,2,1,0:T(8,128)} %broadcast_in_dim.10.refs_3_), custom_call_target="tpu_custom_call" | custom-call | tf_op jit(solution)/shard_map/pallas_call | solution.py:116
  57.6 1.3 collective-permute-start.6
  58.9 1.3 collective-permute-start.7
  60.2 1.3 collective-permute-start.8
  61.5 14.4 %collective-permute-done.6 = f32[2,2,6,512]{3,2,1,0:T(8,128)S(1)} collective-permute-done((f32[2,2,6,512]{3,2,1,0:T(8,128)}, f32[2,2,6,512]{3,2,1,0:T(8,128)S(1)}, u32[]{:S(2)}, u32[]{:S(2)}) %collective-permute-start.6) | collective-permute-done | bytes 49184 | tf_op jit(solution)/shard_map/ppermute | solution.py:28
  76.0 1.3 multiply_reduce_fusion.10
  78.0 0.6 fusion.14.inc_ref
  78.7 4.8 %shard_map.143 = (f32[8,2,6,512]{3,2,1,0:T(8,128)}, f32[2,1,2,6,512]{4,3,2,1,0:T(8,128)}) custom-call(f32[8,2,6,512]{3,2,1,0:T(8,128)} %copy.218.refs_0_.rhs_ref, f32[8,2,6,6,512]{4,3,2,1,0:T(8,128)} %get-tuple-element.27.refs_0_.refs_1_.nt_ref, f32[8,2,6,6,512]{4,3,2,1,0:T(8,128)} %get-tuple-element.26.refs_1_.refs_2_.ft_ref, ...), custom_call_target="tpu_custom_call" | custom-call | tf_op jit(solution)/shard_map/pallas_call | solution.py:230
  83.4 1.4 collective-permute-start.10
  85.0 1.3 collective-permute-start.9
  86.3 18.2 %collective-permute-done.10 = f32[2,2,6,512]{3,2,1,0:T(8,128)S(1)} collective-permute-done((f32[2,2,6,512]{3,2,1,0:T(8,128)}, f32[2,2,6,512]{3,2,1,0:T(8,128)S(1)}, u32[]{:S(2)}, u32[]{:S(2)}) %collective-permute-start.10) | collective-permute-done | bytes 49184 | tf_op jit(solution)/shard_map/ppermute | solution.py:28
  104.6 1.3 collective-permute-start.11
  106.6 4.2 %collective-permute-done.11 = f32[2,2,6,512]{3,2,1,0:T(8,128)S(1)} collective-permute-done((f32[2,2,6,512]{3,2,1,0:T(8,128)S(1)}, f32[2,2,6,512]{3,2,1,0:T(8,128)S(1)}, u32[]{:S(2)}, u32[]{:S(2)}) %collective-permute-start.11) | collective-permute-done | bytes 49184 | tf_op jit(solution)/shard_map/ppermute | solution.py:28
  111.6 3.6 %shard_map.144.psi_ref = f32[8,2,6,512]{3,2,1,0:T(8,128)} custom-call(f32[8,2,6,512]{3,2,1,0:T(8,128)} %get-tuple-element.6.rhs_ref, f32[8,2,6,6,512]{4,3,2,1,0:T(8,128)} %copy.195.refs_0_.d_ref, f32[8,2,6,6,512]{4,3,2,1,0:T(8,128)} %copy.196.refs_1_.b_ref, f32[8,2,6,6,512]{4,3,2,1,0:T(8,128)} %copy.197.refs_2_.a_ref, ...), custom_call_target="tpu_custom_call" | custom-call | tf_op jit(solution)/shard_map/pallas_call | solution.py:200
  115.2 0.8 fusion.17
  116.0 1.3 collective-permute-start.12
  117.3 4.5 %collective-permute-start.13 = (f32[1,2,6,512]{3,2,1,0:T(8,128)S(1)}, f32[1,2,6,512]{3,2,1,0:T(8,128)S(1)}, u32[]{:S(2)}, u32[]{:S(2)}) collective-permute-start(f32[1,2,6,512]{3,2,1,0:T(8,128)S(1)} %get-tuple-element.21), channel_id=1, source_target_pairs={{0,4},{4,8},{8,12},{1,5},{5,9},{9,13},{2,6},{6,10},{10,14},{3,7},{... | collective-permute-start | bytes 73736 | tf_op jit(solution)/shard_map/ppermute | solution.py:19
  121.9 1.0 fusion.18
  122.8 1.3 collective-permute-start.14
  124.1 3.2 %collective-permute-start.15 = (f32[8,2,6,32]{3,2,1,0:T(8,128)S(1)}, f32[8,2,6,32]{3,2,1,0:T(8,128)S(1)}, u32[]{:S(2)}, u32[]{:S(2)}) collective-permute-start(f32[8,2,6,32]{3,2,1,0:T(8,128)S(1)} %get-tuple-element.23), channel_id=1, source_target_pairs={{0,1},{1,2},{2,3},{4,5},{5,6},{6,7},{8,9},{9,10},{10,11},{12,13},{... | collective-permute-start | bytes 36872 | tf_op jit(solution)/shard_map/ppermute | solution.py:19
  127.3 0.7 collective-permute-done.15
  128.0 1.6 fusion
  129.6 0.8 copy.229
  130.4 1.1 reshape.53
  131.6 1.8 convolution_bitcast_fusion
  133.4 1.4 mul.141
  135.5 0.8 copy.236.refs_0_.rhs_ref
  136.3 2.9 %shard_map.145 = f32[2,1,2,6,512]{4,3,2,1,0:T(8,128)} custom-call(f32[8,2,6,512]{3,2,1,0:T(8,128)} %copy.236.refs_0_.rhs_ref, f32[8,2,6,6,512]{4,3,2,1,0:T(8,128)} %get-tuple-element.27.refs_0_.refs_1_.nt_ref, f32[8,2,6,6,512]{4,3,2,1,0:T(8,128)} %get-tuple-element.26.refs_1_.refs_2_.ft_ref, f32[2,1,2,6,512]{4,3,2,1,0:T(8,128)} %broadcast_in_dim.10.refs_3_), custom_call_target="tpu_custom_call" | custom-call | tf_op jit(solution)/shard_map/pallas_call | solution.py:116
  139.2 2.7 %collective-permute-start.16 = (f32[2,2,6,512]{3,2,1,0:T(8,128)}, f32[2,2,6,512]{3,2,1,0:T(8,128)S(1)}, u32[]{:S(2)}, u32[]{:S(2)}) collective-permute-start(f32[2,2,6,512]{3,2,1,0:T(8,128)} %bitcast.75), channel_id=1, source_target_pairs={{0,12},{1,13},{2,14},{3,15},{16,28},{17,29},{18,30},{19,31}} | collective-permute-start | bytes 147464 | tf_op jit(solution)/shard_map/ppermute | solution.py:28
  141.9 1.8 %collective-permute-start.17 = (f32[2,2,6,512]{3,2,1,0:T(8,128)}, f32[2,2,6,512]{3,2,1,0:T(8,128)S(1)}, u32[]{:S(2)}, u32[]{:S(2)}) collective-permute-start(f32[2,2,6,512]{3,2,1,0:T(8,128)} %bitcast.76), channel_id=1, source_target_pairs={{0,8},{4,12},{1,9},{5,13},{2,10},{6,14},{3,11},{7,15},{16,24},{20,... | collective-permute-start | bytes 147464 | tf_op jit(solution)/shard_map/ppermute | solution.py:28
  143.7 1.9 %collective-permute-start.18 = (f32[2,2,6,512]{3,2,1,0:T(8,128)}, f32[2,2,6,512]{3,2,1,0:T(8,128)S(1)}, u32[]{:S(2)}, u32[]{:S(2)}) collective-permute-start(f32[2,2,6,512]{3,2,1,0:T(8,128)} %bitcast.77), channel_id=1, source_target_pairs={{0,4},{4,8},{8,12},{1,5},{5,9},{9,13},{2,6},{6,10},{10,14},{3,7},{... | collective-permute-start | bytes 147464 | tf_op jit(solution)/shard_map/ppermute | solution.py:28
  145.7 1.3 multiply_reduce_fusion.8
  147.8 0.6 fusion.12.inc_ref
  148.5 4.8 %shard_map.146 = (f32[8,2,6,512]{3,2,1,0:T(8,128)}, f32[2,1,2,6,512]{4,3,2,1,0:T(8,128)}) custom-call(f32[8,2,6,512]{3,2,1,0:T(8,128)} %copy.236.refs_0_.rhs_ref, f32[8,2,6,6,512]{4,3,2,1,0:T(8,128)} %get-tuple-element.27.refs_0_.refs_1_.nt_ref, f32[8,2,6,6,512]{4,3,2,1,0:T(8,128)} %get-tuple-element.26.refs_1_.refs_2_.ft_ref, ...), custom_call_target="tpu_custom_call" | custom-call | tf_op jit(solution)/shard_map/pallas_call | solution.py:230
  153.3 1.4 collective-permute-start.20
  154.7 1.3 collective-permute-start.19
  156.0 6.5 %collective-permute-done.20 = f32[2,2,6,512]{3,2,1,0:T(8,128)S(1)} collective-permute-done((f32[2,2,6,512]{3,2,1,0:T(8,128)}, f32[2,2,6,512]{3,2,1,0:T(8,128)S(1)}, u32[]{:S(2)}, u32[]{:S(2)}) %collective-permute-start.20) | collective-permute-done | bytes 49184 | tf_op jit(solution)/shard_map/ppermute | solution.py:28
  162.7 1.3 collective-permute-start.21
  164.2 4.7 %collective-permute-done.21 = f32[2,2,6,512]{3,2,1,0:T(8,128)S(1)} collective-permute-done((f32[2,2,6,512]{3,2,1,0:T(8,128)S(1)}, f32[2,2,6,512]{3,2,1,0:T(8,128)S(1)}, u32[]{:S(2)}, u32[]{:S(2)}) %collective-permute-start.21) | collective-permute-done | bytes 49184 | tf_op jit(solution)/shard_map/ppermute | solution.py:28
  169.7 3.6 %shard_map.147 = f32[8,2,6,512]{3,2,1,0:T(8,128)} custom-call(f32[8,2,6,512]{3,2,1,0:T(8,128)} %get-tuple-element.8.rhs_ref, f32[8,2,6,6,512]{4,3,2,1,0:T(8,128)} %copy.195.refs_0_.d_ref, f32[8,2,6,6,512]{4,3,2,1,0:T(8,128)} %copy.196.refs_1_.b_ref, f32[8,2,6,6,512]{4,3,2,1,0:T(8,128)} %copy.197.refs_2_.a_ref, f32[2,1,2,6,512]{4,3,2,1,0:T(8,128)} %add_bitcast_fusion.inc_ref, ...), custom_call_target="tpu_custom_call" | custom-call | tf_op jit(solution)/shard_map/pallas_call | solution.py:200
  173.3 1.1 multiply_bitcast_fusion
  174.9 1.6 collective-permute-start.22
  176.5 0.8 copy.245
  177.3 1.8 collective-permute-done.22
  (92 shorter events, 8.9 us)
Async XLA Ops:
  0.6 50.8 %copy-start = (f32[2,6,32,32]{3,2,1,0:T(8,128)S(1)}, f32[2,6,32,32]{3,2,1,0:T(8,128)}, u32[]{:S(2)}) copy-start(f32[2,6,32,32]{3,2,1,0:T(8,128)} %param.21) | copy-start | bytes 147460
  0.6 2.8 %copy-start.5 = (f32[8,2,6,6,512]{4,1,3,2,0:T(2,128)S(1)}, f32[8,2,6,6,512]{4,1,3,2,0:T(2,128)}, u32[]{:S(2)}) copy-start(f32[8,2,6,6,512]{4,1,3,2,0:T(2,128)} %param.18) | copy-start | bytes 3538948
  3.5 1.4 copy-start.6
  14.6 1.3 slice-start.1
  14.6 17.1 %copy-start.8 = (f32[8,2,6,6,512]{4,1,3,2,0:T(2,128)S(1)}, f32[8,2,6,6,512]{4,1,3,2,0:T(2,128)}, u32[]{:S(2)}) copy-start(f32[8,2,6,6,512]{4,1,3,2,0:T(2,128)} %param.15) | copy-start | bytes 3538948
  15.9 15.7 %copy-start.7 = (f32[8,2,6,6,512]{4,1,3,2,0:T(2,128)S(1)}, f32[8,2,6,6,512]{4,1,3,2,0:T(2,128)}, u32[]{:S(2)}) copy-start(f32[8,2,6,6,512]{4,1,3,2,0:T(2,128)} %param.16) | copy-start | bytes 3538948
  16.9 31.7 %collective-permute-start = (f32[153600]{0:T(1024)}, f32[153600]{0:T(1024)S(1)}, u32[]{:S(2)}, u32[]{:S(2)}) collective-permute-start(f32[153600]{0:T(1024)} %pad_maximum_fusion), channel_id=1, source_target_pairs={{4,0},{8,4},{12,8},{5,1},{9,5},{13,9},{6,2},{10,6},{14,10},{7,3},{... | collective-permute-start | bytes 1843208 | tf_op jit(solution)/shard_map/ppermute | solution.py:309
  19.2 30.8 %copy-start.2 = (f32[8,2,6,512]{3,2,1,0:T(8,128)}, f32[8,2,6,512]{3,2,1,0:T(8,128)S(1)}, u32[]{:S(2)}) copy-start(f32[8,2,6,512]{3,2,1,0:T(8,128)S(1)} %copy.198.psi_ref) | copy-start | bytes 589828
  19.9 30.1 %collective-permute-start.2 = (f32[8,2,6,32]{3,2,1,0:T(8,128)}, f32[8,2,6,32]{3,2,1,0:T(8,128)}, u32[]{:S(2)}, u32[]{:S(2)}) collective-permute-start(f32[8,2,6,32]{3,2,1,0:T(8,128)} %get-tuple-element.24), channel_id=1, source_target_pairs={{1,0},{2,1},{3,2},{5,4},{6,5},{7,6},{9,8},{10,9},{11,10},{13,12},{... | collective-permute-start | bytes 36872 | tf_op jit(solution)/shard_map/ppermute | solution.py:20
  21.2 28.8 %collective-permute-start.3 = (f32[8,2,6,32]{3,2,1,0:T(8,128)}, f32[8,2,6,32]{3,2,1,0:T(8,128)}, u32[]{:S(2)}, u32[]{:S(2)}) collective-permute-start(f32[8,2,6,32]{3,2,1,0:T(8,128)} %get-tuple-element.25), channel_id=1, source_target_pairs={{0,1},{1,2},{2,3},{4,5},{5,6},{6,7},{8,9},{9,10},{10,11},{12,13},{... | collective-permute-start | bytes 36872 | tf_op jit(solution)/shard_map/ppermute | solution.py:19
  25.4 24.5 %collective-permute-start.1 = (f32[1,2,6,512]{3,2,1,0:T(8,128)}, f32[1,2,6,512]{3,2,1,0:T(8,128)}, u32[]{:S(2)}, u32[]{:S(2)}) collective-permute-start(f32[1,2,6,512]{3,2,1,0:T(8,128)} %slice.92), channel_id=1, source_target_pairs={{0,4},{4,8},{8,12},{1,5},{5,9},{9,13},{2,6},{6,10},{10,14},{3,7},{... | collective-permute-start | bytes 73736 | tf_op jit(solution)/shard_map/ppermute | solution.py:312
  40.9 9.0 %copy-start.9 = (f32[8,2,6,512]{3,1,2,0:T(2,128)S(1)}, f32[8,2,6,512]{3,1,2,0:T(2,128)}, u32[]{:S(2)}) copy-start(f32[8,2,6,512]{3,1,2,0:T(2,128)} %param.14) | copy-start | bytes 589828
  43.4 32.6 %collective-permute-start.5 = (f32[2,12,2,6,512]{4,2,3,1,0:T(2,128)}, f32[2,12,2,6,512]{4,2,3,1,0:T(2,128)}, u32[]{:S(2)}, u32[]{:S(2)}) collective-permute-start(f32[2,12,2,6,512]{4,2,3,1,0:T(2,128)} %copy.211), channel_id=1, source_target_pairs={{0,8},{4,12},{1,9},{5,13},{2,10},{6,14},{3,11},{7,15},{16,24},{20,... | collective-permute-start | bytes 1769480 | tf_op jit(solution)/shard_map/ppermute | solution.py:28
  48.6 2.5 %copy-start.4 = (f32[153600]{0:T(1024)}, f32[153600]{0:T(1024)S(1)}, u32[]{:S(2)}) copy-start(f32[153600]{0:T(1024)S(1)} %collective-permute-done) | copy-start | bytes 1843204
  48.6 28.8 %collective-permute-start.4 = (f32[2,12,2,6,512]{4,2,3,1,0:T(2,128)}, f32[2,12,2,6,512]{4,2,3,1,0:T(2,128)S(1)}, u32[]{:S(2)}, u32[]{:S(2)}) collective-permute-start(f32[2,12,2,6,512]{4,2,3,1,0:T(2,128)} %copy.211), channel_id=1, source_target_pairs={{0,4},{4,8},{8,12},{1,5},{5,9},{9,13},{2,6},{6,10},{10,14},{3,7},{... | collective-permute-start | bytes 1769480 | tf_op jit(solution)/shard_map/ppermute | solution.py:28
  51.5 1.3 copy-start.1
  57.6 18.3 %collective-permute-start.6 = (f32[2,2,6,512]{3,2,1,0:T(8,128)}, f32[2,2,6,512]{3,2,1,0:T(8,128)S(1)}, u32[]{:S(2)}, u32[]{:S(2)}) collective-permute-start(f32[2,2,6,512]{3,2,1,0:T(8,128)} %bitcast.72), channel_id=1, source_target_pairs={{0,12},{1,13},{2,14},{3,15},{16,28},{17,29},{18,30},{19,31}} | collective-permute-start | bytes 147464 | tf_op jit(solution)/shard_map/ppermute | solution.py:28
  58.9 18.4 %collective-permute-start.7 = (f32[2,2,6,512]{3,2,1,0:T(8,128)}, f32[2,2,6,512]{3,2,1,0:T(8,128)S(1)}, u32[]{:S(2)}, u32[]{:S(2)}) collective-permute-start(f32[2,2,6,512]{3,2,1,0:T(8,128)} %bitcast.73), channel_id=1, source_target_pairs={{0,8},{4,12},{1,9},{5,13},{2,10},{6,14},{3,11},{7,15},{16,24},{20,... | collective-permute-start | bytes 147464 | tf_op jit(solution)/shard_map/ppermute | solution.py:28
  60.2 17.8 %collective-permute-start.8 = (f32[2,2,6,512]{3,2,1,0:T(8,128)}, f32[2,2,6,512]{3,2,1,0:T(8,128)S(1)}, u32[]{:S(2)}, u32[]{:S(2)}) collective-permute-start(f32[2,2,6,512]{3,2,1,0:T(8,128)} %bitcast.74), channel_id=1, source_target_pairs={{0,4},{4,8},{8,12},{1,5},{5,9},{9,13},{2,6},{6,10},{10,14},{3,7},{... | collective-permute-start | bytes 147464 | tf_op jit(solution)/shard_map/ppermute | solution.py:28
  83.4 1.4 slice-start
  83.4 1.5 copy-start.13
  83.4 21.0 %collective-permute-start.10 = (f32[2,2,6,512]{3,2,1,0:T(8,128)}, f32[2,2,6,512]{3,2,1,0:T(8,128)S(1)}, u32[]{:S(2)}, u32[]{:S(2)}) collective-permute-start(f32[2,2,6,512]{3,2,1,0:T(8,128)} %bitcast.85), channel_id=1, source_target_pairs={{8,0},{12,4},{9,1},{13,5},{10,2},{14,6},{11,3},{15,7},{24,16},{28,... | collective-permute-start | bytes 147464 | tf_op jit(solution)/shard_map/ppermute | solution.py:28
  84.9 21.1 %copy-start.12 = (s32[8,512]{1,0:T(8,128)S(1)}, s32[8,512]{1,0:T(8,128)}, u32[]{:S(2)}) copy-start(s32[8,512]{1,0:T(8,128)} %param.23) | copy-start | bytes 49156
  85.0 19.6 %collective-permute-start.9 = (f32[2,2,6,512]{3,2,1,0:T(8,128)S(1)}, f32[2,2,6,512]{3,2,1,0:T(8,128)S(1)}, u32[]{:S(2)}, u32[]{:S(2)}) collective-permute-start(f32[2,2,6,512]{3,2,1,0:T(8,128)S(1)} %bitcast.86), channel_id=1, source_target_pairs={{4,0},{8,4},{12,8},{5,1},{9,5},{13,9},{6,2},{10,6},{14,10},{7,3},{... | collective-permute-start | bytes 147464 | tf_op jit(solution)/shard_map/ppermute | solution.py:28
  104.6 6.2 %collective-permute-start.11 = (f32[2,2,6,512]{3,2,1,0:T(8,128)S(1)}, f32[2,2,6,512]{3,2,1,0:T(8,128)S(1)}, u32[]{:S(2)}, u32[]{:S(2)}) collective-permute-start(f32[2,2,6,512]{3,2,1,0:T(8,128)S(1)} %add.57), channel_id=1, source_target_pairs={{4,0},{8,4},{12,8},{5,1},{9,5},{13,9},{6,2},{10,6},{14,10},{7,3},{... | collective-permute-start | bytes 147464 | tf_op jit(solution)/shard_map/ppermute | solution.py:28
  111.6 16.5 %copy-start.10 = (f32[8,2,6,512]{3,1,2,0:T(2,128)S(1)}, f32[8,2,6,512]{3,1,2,0:T(2,128)}, u32[]{:S(2)}) copy-start(f32[8,2,6,512]{3,1,2,0:T(2,128)} %param.14) | copy-start | bytes 589828
  116.0 12.0 %collective-permute-start.12 = (f32[1,2,6,512]{3,2,1,0:T(8,128)S(1)}, f32[1,2,6,512]{3,2,1,0:T(8,128)S(1)}, u32[]{:S(2)}, u32[]{:S(2)}) collective-permute-start(f32[1,2,6,512]{3,2,1,0:T(8,128)S(1)} %get-tuple-element.20), channel_id=1, source_target_pairs={{4,0},{8,4},{12,8},{5,1},{9,5},{13,9},{6,2},{10,6},{14,10},{7,3},{... | collective-permute-start | bytes 73736 | tf_op jit(solution)/shard_map/ppermute | solution.py:20
  117.3 10.7 %collective-permute-start.13 = (f32[1,2,6,512]{3,2,1,0:T(8,128)S(1)}, f32[1,2,6,512]{3,2,1,0:T(8,128)S(1)}, u32[]{:S(2)}, u32[]{:S(2)}) collective-permute-start(f32[1,2,6,512]{3,2,1,0:T(8,128)S(1)} %get-tuple-element.21), channel_id=1, source_target_pairs={{0,4},{4,8},{8,12},{1,5},{5,9},{9,13},{2,6},{6,10},{10,14},{3,7},{... | collective-permute-start | bytes 73736 | tf_op jit(solution)/shard_map/ppermute | solution.py:19
  122.8 4.5 %collective-permute-start.14 = (f32[8,2,6,32]{3,2,1,0:T(8,128)S(1)}, f32[8,2,6,32]{3,2,1,0:T(8,128)S(1)}, u32[]{:S(2)}, u32[]{:S(2)}) collective-permute-start(f32[8,2,6,32]{3,2,1,0:T(8,128)S(1)} %get-tuple-element.22), channel_id=1, source_target_pairs={{1,0},{2,1},{3,2},{5,4},{6,5},{7,6},{9,8},{10,9},{11,10},{13,12},{... | collective-permute-start | bytes 36872 | tf_op jit(solution)/shard_map/ppermute | solution.py:20
  124.1 3.9 %collective-permute-start.15 = (f32[8,2,6,32]{3,2,1,0:T(8,128)S(1)}, f32[8,2,6,32]{3,2,1,0:T(8,128)S(1)}, u32[]{:S(2)}, u32[]{:S(2)}) collective-permute-start(f32[8,2,6,32]{3,2,1,0:T(8,128)S(1)} %get-tuple-element.23), channel_id=1, source_target_pairs={{0,1},{1,2},{2,3},{4,5},{5,6},{6,7},{8,9},{9,10},{10,11},{12,13},{... | collective-permute-start | bytes 36872 | tf_op jit(solution)/shard_map/ppermute | solution.py:19
  139.2 6.5 %collective-permute-start.16 = (f32[2,2,6,512]{3,2,1,0:T(8,128)}, f32[2,2,6,512]{3,2,1,0:T(8,128)S(1)}, u32[]{:S(2)}, u32[]{:S(2)}) collective-permute-start(f32[2,2,6,512]{3,2,1,0:T(8,128)} %bitcast.75), channel_id=1, source_target_pairs={{0,12},{1,13},{2,14},{3,15},{16,28},{17,29},{18,30},{19,31}} | collective-permute-start | bytes 147464 | tf_op jit(solution)/shard_map/ppermute | solution.py:28
  141.9 5.2 %collective-permute-start.17 = (f32[2,2,6,512]{3,2,1,0:T(8,128)}, f32[2,2,6,512]{3,2,1,0:T(8,128)S(1)}, u32[]{:S(2)}, u32[]{:S(2)}) collective-permute-start(f32[2,2,6,512]{3,2,1,0:T(8,128)} %bitcast.76), channel_id=1, source_target_pairs={{0,8},{4,12},{1,9},{5,13},{2,10},{6,14},{3,11},{7,15},{16,24},{20,... | collective-permute-start | bytes 147464 | tf_op jit(solution)/shard_map/ppermute | solution.py:28
  143.7 4.1 %collective-permute-start.18 = (f32[2,2,6,512]{3,2,1,0:T(8,128)}, f32[2,2,6,512]{3,2,1,0:T(8,128)S(1)}, u32[]{:S(2)}, u32[]{:S(2)}) collective-permute-start(f32[2,2,6,512]{3,2,1,0:T(8,128)} %bitcast.77), channel_id=1, source_target_pairs={{0,4},{4,8},{8,12},{1,5},{5,9},{9,13},{2,6},{6,10},{10,14},{3,7},{... | collective-permute-start | bytes 147464 | tf_op jit(solution)/shard_map/ppermute | solution.py:28
  153.3 10.8 %copy-start.14 = (f32[8]{0:T(128)S(1)}, f32[8]{0:T(128)}, u32[]{:S(2)}) copy-start(f32[8]{0:T(128)} %param.25) | copy-start | bytes 100
  153.3 10.8 %copy-start.15 = (s32[2]{0:T(128)S(1)}, s32[2]{0:T(128)}, u32[]{:S(2)}) copy-start(s32[2]{0:T(128)} %param.24) | copy-start | bytes 28
  153.3 9.3 %collective-permute-start.20 = (f32[2,2,6,512]{3,2,1,0:T(8,128)}, f32[2,2,6,512]{3,2,1,0:T(8,128)S(1)}, u32[]{:S(2)}, u32[]{:S(2)}) collective-permute-start(f32[2,2,6,512]{3,2,1,0:T(8,128)} %bitcast.87), channel_id=1, source_target_pairs={{8,0},{12,4},{9,1},{13,5},{10,2},{14,6},{11,3},{15,7},{24,16},{28,... | collective-permute-start | bytes 147464 | tf_op jit(solution)/shard_map/ppermute | solution.py:28
  154.7 8.0 %collective-permute-start.19 = (f32[2,2,6,512]{3,2,1,0:T(8,128)}, f32[2,2,6,512]{3,2,1,0:T(8,128)S(1)}, u32[]{:S(2)}, u32[]{:S(2)}) collective-permute-start(f32[2,2,6,512]{3,2,1,0:T(8,128)} %bitcast.88), channel_id=1, source_target_pairs={{4,0},{8,4},{12,8},{5,1},{9,5},{13,9},{6,2},{10,6},{14,10},{7,3},{... | collective-permute-start | bytes 147464 | tf_op jit(solution)/shard_map/ppermute | solution.py:28
  162.7 6.2 %collective-permute-start.21 = (f32[2,2,6,512]{3,2,1,0:T(8,128)S(1)}, f32[2,2,6,512]{3,2,1,0:T(8,128)S(1)}, u32[]{:S(2)}, u32[]{:S(2)}) collective-permute-start(f32[2,2,6,512]{3,2,1,0:T(8,128)S(1)} %add.65), channel_id=1, source_target_pairs={{4,0},{8,4},{12,8},{5,1},{9,5},{13,9},{6,2},{10,6},{14,10},{7,3},{... | collective-permute-start | bytes 147464 | tf_op jit(solution)/shard_map/ppermute | solution.py:28
  173.3 1.3 copy-start.11
  173.3 3.2 %copy-start.3 = (f32[8,2,6,512]{3,2,1,0:T(8,128)S(1)}, f32[8,2,6,512]{3,2,1,0:T(8,128)}, u32[]{:S(2)}) copy-start(f32[8,2,6,512]{3,2,1,0:T(8,128)} %shard_map.147) | copy-start | bytes 589828
  174.9 4.2 %collective-permute-start.22 = (f32[8,3,512]{2,0,1:T(8,128)S(1)}, f32[8,3,512]{2,0,1:T(8,128)S(1)}, u32[]{:S(2)}, u32[]{:S(2)}) collective-permute-start(f32[8,3,512]{2,0,1:T(8,128)S(1)} %bitcast.84), channel_id=1, source_target_pairs={{0,16},{16,0},{1,17},{17,1},{2,18},{18,2},{3,19},{19,3},{4,20},{20... | collective-permute-start | bytes 147464 | tf_op jit(solution)/shard_map/ppermute | solution.py:344
